TPU v7x, 32 devices: a whole 2x2x4 slice. The times are simulated.
32 devices in a mesh: sum: 8 (over z, x), mode: 4 (over y, core).
Axes of the slice: x: 2, y: 2, z: 4, core: 2. Of those that a mesh axis runs over, the one named last changes fastest.
Arguments:
- left_cores: bfloat16 [8, 512, 64, 512], P('sum', None, 'mode'), may hold values from -80 to 80, as said below
- right_cores: bfloat16 [8, 512, 64, 512], P('sum', None, 'mode'), may hold values from -6 to 6
- sketch: bfloat16 [64, 512, 512], P('mode'), may hold values from -0.03125 to 0.03125
Outputs:
- basis_core: float32 [512, 64, 512], P('sum', 'mode')
- carries: float32 [8, 512, 512], P('sum')
Inputs may be any that keep to these rules, and one draw needn't show every extreme that they name: `left_cores`: independent entries; each row (summand, left rank, mode index) has its own scale.
All inputs are finite; a program needn't handle non-finite values.
Results may differ from a plain program's by a relative error of at most 0.0035.
Values may be sent and summed in bfloat16 or wider, within the bound.
No kernel may reach another device: no remote copies, remote signals or barrier semaphores. Data moves between devices by JAX's collectives and lax.ppermute only.
A program may use at most 128 MiB of HBM per device.

v0:
```python
import math

import jax
import jax.numpy as jnp
from jax import lax
from jax.sharding import PartitionSpec as P

R_IN = 512
MODES = 64


def orthonormal(sketched, gram):
    lower = jnp.linalg.cholesky(gram)
    return lax.linalg.triangular_solve(
        lower, sketched, left_side=False, lower=True, transpose_a=True
    )


def per_device(left_cores, right_cores, sketch):
    sum_local, rows_in, mode_local, rank_width = left_cores.shape
    target = sketch.shape[2]
    flat_sketch = sketch.reshape(-1, target)
    flat_right = right_cores.reshape(sum_local * rank_width, -1)
    partial_map = jnp.dot(flat_right, flat_sketch, preferred_element_type=jnp.float32).reshape(
        sum_local, rank_width, target
    )
    mapped = lax.psum(partial_map, "mode").astype(jnp.bfloat16)
    flat_left = left_cores.reshape(sum_local, rows_in * mode_local, rank_width)
    local_sum = jnp.einsum("skr,srp->kp", flat_left, mapped, preferred_element_type=jnp.float32)
    local_sum = local_sum.reshape(rows_in, mode_local, target)
    factor = math.sqrt(R_IN * MODES)
    share = lax.psum_scatter(local_sum, "sum", scatter_dimension=0, tiled=True)
    flat_share = share.reshape(-1, target)
    gram_part = jnp.dot(flat_share.T, flat_share, precision=lax.Precision.HIGHEST)
    gram = lax.psum(gram_part, ("sum", "mode"))
    basis = orthonormal(flat_share, gram)
    block = basis.reshape(share.shape)
    rounded = block.astype(jnp.bfloat16)
    pieces = lax.all_gather(rounded, "sum", axis=0, tiled=True)
    count = pieces.shape[0]
    chosen = left_cores
    chosen = chosen.reshape(sum_local, count * mode_local, rank_width)
    partial_carry = jnp.einsum(
        "kp,skr->spr", pieces.reshape(-1, target), chosen, preferred_element_type=jnp.float32
    )
    carries = lax.psum(partial_carry, "mode")
    return (block * factor, carries)


def solution(mesh):
    in_specs = (P("sum", None, "mode", None), P("sum", None, "mode", None), P("mode", None, None))
    out_specs = (P("sum", "mode", None), P("sum", None, None))
    return jax.shard_map(
        per_device, mesh=mesh, in_specs=in_specs, out_specs=out_specs, check_vma=False
    )
```

profile of v0, /device:TPU:0, one launch (start us, length us, event | category | flops | bytes accessed | tf_op | source)
XLA Modules:
  0.0 864.9 jit_solution(7836462655036602845)
XLA Ops:
  7.2 16.4 %copy.36 = bf16[64,8,16,512]{3,1,2,0:T(8,128)(2,1)} copy(bf16[64,8,16,512]{3,2,1,0:T(8,128)(2,1)} %bitcast.87) | data formatting | bytes 16777216
  23.6 9.4 %convolution_bitcast_fusion.3 = f32[1,512,512]{2,1,0:T(8,128)S(1)} fusion(bf16[512,8192]{1,0:T(8,128)(2,1)} %bitcast.88, bf16[8192,512]{1,0:T(8,128)(2,1)} %bitcast.91), kind=kOutput, calls=%fused_computation.13 | convolution fusion | flops 4294967296 | bytes 17825792 | tf_op jit(solution)/shard_map/dot_general | solution.py:24
  33.0 28.3 %all-reduce.8 = bf16[1,512,512]{2,1,0:T(8,128)(2,1)S(1)} all-reduce(f32[1,512,512]{2,1,0:T(8,128)S(1)} %convolution_bitcast_fusion.3), channel_id=1, replica_groups=mesh['sum'=8,'mode'=4] {'mode'}, use_global_device_ids=true, to_apply=%region_0.0 | all-reduce | flops 262144 | bytes 1572864 | tf_op jit(solution)/shard_map/psum | solution.py:27
  61.3 27.3 %convolution_bitcast_fusion = f32[512,16,512]{0,2,1:T(8,128)} fusion(bf16[512,16,512]{2,1,0:T(8,128)(2,1)} %bitcast.81, bf16[1,512,512]{2,1,0:T(8,128)(2,1)S(1)} %all-reduce.8), kind=kOutput, calls=%fused_computation.2 | convolution fusion | flops 4294967296 | bytes 25690112 | tf_op jit(solution)/shard_map/skr,srp->kp/dot_general | solution.py:29
  88.7 20.2 %copy.23 = f32[512,16,512]{2,1,0:T(8,128)} copy(f32[512,16,512]{0,2,1:T(8,128)} %convolution_bitcast_fusion) | data formatting | bytes 33554432 | tf_op jit(solution)/shard_map/skr,srp->kp/dot_general | solution.py:29
  108.9 11.2 %all-reduce.5.cloned.1.call-start = ((), (), s32[]{:S(2)}) async-start(), calls=%async_computation.2 | async-start | bytes 2097152 | tf_op jit(solution)/shard_map/psum | solution.py:35
  120.1 271.5 %reduce-scatter.2.cloned.1.call-done = f32[64,16,512]{2,1,0:T(8,128)} async-done(((f32[512,16,512]{2,1,0:T(8,128)}), f32[64,16,512]{2,1,0:T(8,128)}) %reduce-scatter.2.cloned.1.call-update) | async-done | bytes 2097168 | tf_op jit(solution)/shard_map/reduce_scatter | solution.py:32
  391.6 6.7 convolution_bitcast_fusion.2
  398.4 129.0 %all-reduce.5.cloned.1.call-done = f32[512,512]{0,1:T(8,128)} async-done(((f32[512,512]{0,1:T(8,128)}), f32[512,512]{0,1:T(8,128)}) %all-reduce.5.cloned.1.call-update) | async-done | bytes 1048592 | tf_op jit(solution)/shard_map/psum | solution.py:35
  527.4 1.6 copy.27
  530.2 11.7 %cholesky.104 = f32[128,128]{1,0:T(8,128)S(1)} custom-call(f32[128,128]{1,0:T(8,128)S(1)} %cholesky.266), custom_call_target="Cholesky" | custom-call | tf_op jit(solution)/shard_map/jit(cholesky)/cholesky | solution.py:13
  542.0 9.8 %custom-call.30 = f32[1,128,128]{1,2,0:T(8,128)S(1)} custom-call(f32[1,128,128]{2,1,0:T(8,128)S(1)} %get-tuple-element.31), custom_call_target="InvertDiagBlocksLowerTriangular" | custom-call | tf_op jit(solution)/shard_map/jit(cholesky)/cholesky | solution.py:13
  554.5 11.7 %cholesky.217 = f32[128,128]{1,0:T(8,128)S(1)} custom-call(f32[128,128]{1,0:T(8,128)S(1)} %cholesky.270), custom_call_target="Cholesky" | custom-call | tf_op jit(solution)/shard_map/jit(cholesky)/cholesky | solution.py:13
  566.2 10.2 %custom-call.31 = f32[1,128,128]{1,2,0:T(8,128)S(1)} custom-call(f32[1,128,128]{2,1,0:T(8,128)S(1)} %get-tuple-element.28), custom_call_target="InvertDiagBlocksLowerTriangular" | custom-call | tf_op jit(solution)/shard_map/jit(cholesky)/cholesky | solution.py:13
  578.0 11.7 %cholesky.238 = f32[128,128]{1,0:T(8,128)S(1)} custom-call(f32[128,128]{1,0:T(8,128)S(1)} %cholesky.275), custom_call_target="Cholesky" | custom-call | tf_op jit(solution)/shard_map/jit(cholesky)/cholesky | solution.py:13
  590.4 9.8 %custom-call.32 = f32[1,128,128]{1,2,0:T(8,128)S(1)} custom-call(f32[1,128,128]{2,1,0:T(8,128)S(1)} %get-tuple-element.25), custom_call_target="InvertDiagBlocksLowerTriangular" | custom-call | tf_op jit(solution)/shard_map/jit(cholesky)/cholesky | solution.py:13
  601.7 11.7 %cholesky.255 = f32[128,128]{1,0:T(8,128)S(1)} custom-call(f32[128,128]{1,0:T(8,128)S(1)} %convolution_subtract_fusion.4), custom_call_target="Cholesky" | custom-call | tf_op jit(solution)/shard_map/jit(cholesky)/cholesky | solution.py:13
  618.5 14.2 %while.1 = (s32[]{:T(128)}, f32[512,512]{1,0:T(8,128)}, s32[4,2]{0,1:T(2,128)S(1)}, f32[4,128,128]{2,1,0:T(8,128)}, s32[]{:T(128)}) while((s32[]{:T(128)}, f32[512,512]{1,0:T(8,128)}, s32[4,2]{0,1:T(2,128)S(1)}, f32[4,128,128]{2,1,0:T(8,128)}, s32[]{:T(128)}) %tuple.32), condition=%wide.while_cond, body=%wide.while_body.sunk | while | flops 2 | bytes 132705 | solution.py:14
  619.2 2.9 bitcast_dynamic-update-slice_fusion.2
  622.8 2.9 bitcast_dynamic-update-slice_fusion.2
  626.3 2.9 bitcast_dynamic-update-slice_fusion.2
  629.9 2.8 bitcast_dynamic-update-slice_fusion.2
  632.7 40.1 %custom-call.33 = f32[4,128,128]{1,2,0:T(8,128)S(1)} custom-call(f32[4,128,128]{2,1,0:T(8,128)} %get-tuple-element.9), custom_call_target="InvertDiagBlocksLowerTriangular" | custom-call | tf_op jit(solution)/shard_map/triangular_solve | solution.py:14
  673.5 1.8 convolution_subtract_fusion.1
  675.9 2.7 convolution_subtract_fusion
  679.3 3.8 fusion.7
  686.4 123.8 %all-gather.2.cloned.1.call-done = bf16[512,16,512]{2,1,0:T(8,128)(2,1)} async-done(((bf16[64,16,512]{2,1,0:T(8,128)(2,1)}), bf16[512,16,512]{2,1,0:T(8,128)(2,1)}) %all-gather.2.cloned.1.call-update) | async-done | bytes 8388624 | tf_op jit(solution)/shard_map/all_gather | solution.py:39
  810.2 11.2 %convolution_bitcast_fusion.1 = f32[1,512,512]{2,1,0:T(8,128)} fusion(bf16[8192,512]{1,0:T(8,128)(2,1)} %bitcast.92, bf16[8192,512]{1,0:T(8,128)(2,1)} %bitcast.82), kind=kOutput, calls=%fused_computation.11 | convolution fusion | flops 4294967296 | bytes 17825792 | tf_op jit(solution)/shard_map/kp,skr->spr/dot_general | solution.py:43
  821.4 1.5 fusion.11
  822.9 1.8 copy.28
  824.7 31.2 %all-reduce.7.cloned.1.call-done = f32[1,512,512]{2,1,0:T(8,128)} async-done(((f32[1,512,512]{2,1,0:T(8,128)}), f32[1,512,512]{2,1,0:T(8,128)}) %all-reduce.7.cloned.1.call-update) | async-done | bytes 1048592 | tf_op jit(solution)/shard_map/psum | solution.py:46
  855.9 2.3 copy.58
  (53 shorter events, 18.1 us)
Async XLA Ops:
  7.2 384.4 %reduce-scatter.2.cloned.1.call-start = ((), (), s32[]{:S(2)}) async-start(), calls=%async_computation.1 | async-start | bytes 18874368 | tf_op jit(solution)/shard_map/reduce_scatter | solution.py:32
  108.9 418.4 %all-reduce.5.cloned.1.call-start = ((), (), s32[]{:S(2)}) async-start(), calls=%async_computation.2 | async-start | bytes 2097152 | tf_op jit(solution)/shard_map/psum | solution.py:35
  398.3 411.9 %all-gather.2.cloned.1.call-start = ((), (), s32[]{:S(2)}) async-start(), calls=%async_computation.3 | async-start | bytes 9437184 | tf_op jit(solution)/shard_map/all_gather | solution.py:39
  527.4 1.7 copy-start.3
  529.3 1.0 copy-start.4
  578.0 94.9 %copy-start = (f32[64,16,512]{2,1,0:T(8,128)S(1)}, f32[64,16,512]{2,1,0:T(8,128)}, u32[]{:S(2)}) copy-start(f32[64,16,512]{2,1,0:T(8,128)} %reduce-scatter.2.cloned.1.call-done) | copy-start | bytes 6291460
  679.3 4.5 copy-start.1
  683.8 0.8 copy-start.2
  686.1 169.8 %all-reduce.7.cloned.1.call-start = ((), (), s32[]{:S(2)}) async-start(), calls=%async_computation.4 | async-start | bytes 2097152 | tf_op jit(solution)/shard_map/psum | solution.py:46
Sparse Core Ops, SparseCore 0:
  109.0 282.4 reduce-scatter.1
  398.4 128.8 all-reduce.4
  686.2 123.9 all-gather.1
  821.6 34.2 all-reduce.6
where the time goes:
time: 875 us; the launch traced here: 865 us
  waiting for transfers between devices  555 us (63%)
  other arithmetic  122 us (14%)
  matrix products  71.1 us (8%)
  local copies, waits for them, and re-layouts  59.7 us (7%)
  blocking collectives  28.3 us (3%)
  between operations  16.8 us (2%)
  starting transfers between devices  11.5 us (1%)
    reduce_scatter x1, waiting for transfers between devices, per_device(): share = lax.psum_scatter(local_sum, 'sum', scatter_dimension=0, tiled=True)  271 us
    psum x1, waiting for transfers between devices, per_device(): gram = lax.psum(gram_part, ('sum', 'mode'))  129 us
    all_gather x1, waiting for transfers between devices, per_device(): pieces = lax.all_gather(rounded, 'sum', axis=0, tiled=True)  124 us
    another operation x14, other arithmetic, orthonormal(): lower = jnp.linalg.cholesky(gram)  78.8 us
    another operation x3, other arithmetic, orthonormal(): lax.linalg.triangular_solve(lower, sketched, left_side=False, lower=True,...  41.4 us
    psum x1, waiting for transfers between devices, per_device(): carries = lax.psum(partial_carry, 'mode')  31.2 us
    psum x1, blocking collectives, per_device(): mapped = lax.psum(partial_map, 'mode').astype(jnp.bfloat16)  28.3 us
    dot_general x1, matrix products, per_device(): jnp.einsum('skr,srp->kp', flat_left, mapped, preferred_element_type=jnp.f...  27.3 us
  transfers between devices with their start and end apart: 4, of which 4 were waited for; matrix products, arithmetic and copies ran while one was open for 0% of the time, Pallas kernels for 0%

commit v1 on v0

v1 whole, which is shorter than its diff:
```python
import math

import jax
import jax.numpy as jnp
from jax import lax
from jax.experimental.layout import Layout, with_layout_constraint
from jax.sharding import PartitionSpec as P

R_IN = 512
MODES = 64
BLOCK = 128

HI = lax.Precision.HIGHEST


def mm(a, b):
    return jnp.dot(a, b, precision=HI, preferred_element_type=jnp.float32)


def orthonormal(sketched, gram):
    n = gram.shape[0]
    b = min(BLOCK, n)
    nb = n // b
    eye = jnp.eye(b, dtype=jnp.float32)
    inverses = []
    panels = []
    trailing = gram
    for k in range(nb):
        diag = trailing[:b, :b]
        lkk = jnp.linalg.cholesky(diag)
        ikk = lax.linalg.triangular_solve(lkk, eye, left_side=True, lower=True)
        inverses.append(ikk)
        if k < nb - 1:
            panel = mm(trailing[b:, :b], ikk.T)
            panels.append(panel)
            trailing = trailing[b:, b:] - mm(panel, panel.T)
    blocks = []
    for k in range(nb):
        rhs = sketched[:, k * b:(k + 1) * b]
        if k > 0:
            done = jnp.concatenate(blocks, axis=1)
            lrow = jnp.concatenate(
                [panels[j][(k - j - 1) * b:(k - j) * b] for j in range(k)], axis=1
            )
            rhs = rhs - mm(done, lrow.T)
        blocks.append(mm(rhs, inverses[k].T))
    return jnp.concatenate(blocks, axis=1)


def per_device(left_cores, right_cores, sketch):
    sum_local, rows_in, mode_local, rank_width = left_cores.shape
    target = sketch.shape[2]
    partial_map = lax.dot_general(
        right_cores, sketch, (((2, 3), (0, 1)), ((), ())), preferred_element_type=jnp.float32
    )
    mapped = lax.psum(partial_map, "mode").astype(jnp.bfloat16)
    local_sum = lax.dot_general(
        left_cores, mapped, (((0, 3), (0, 1)), ((), ())), preferred_element_type=jnp.float32
    )
    local_sum = with_layout_constraint(local_sum, Layout(major_to_minor=(0, 1, 2)))
    factor = math.sqrt(R_IN * MODES)
    share = lax.psum_scatter(local_sum, "sum", scatter_dimension=0, tiled=True)
    flat_share = share.reshape(-1, target)
    gram_part = jnp.dot(flat_share.T, flat_share, precision=HI)
    gram = lax.psum(gram_part, ("sum", "mode"))
    basis = orthonormal(flat_share, gram)
    block = basis.reshape(share.shape)
    rounded = block.astype(jnp.bfloat16)
    pieces = lax.all_gather(rounded, "sum", axis=0, tiled=True)
    partial_carry = lax.dot_general(
        pieces, left_cores, (((0, 1), (1, 2)), ((), ())), preferred_element_type=jnp.float32
    )
    partial_carry = jnp.transpose(partial_carry, (1, 0, 2))
    carries = lax.psum(partial_carry, "mode")
    return (block * factor, carries)


def solution(mesh):
    in_specs = (P("sum", None, "mode", None), P("sum", None, "mode", None), P("mode", None, None))
    out_specs = (P("sum", "mode", None), P("sum", None, None))
    return jax.shard_map(
        per_device, mesh=mesh, in_specs=in_specs, out_specs=out_specs, check_vma=False
    )
```

time: 875 us -> 796 us (0.910)
  local copies, waits for them, and re-layouts: 59.7 us -> 8.84 us
  other arithmetic: 122 us -> 103 us
  waiting for transfers between devices: 555 us -> 566 us
  starting transfers between devices: 11.5 us -> 0.67 us
    dot_general x1 -> x0, local copies, waits for them, and re-layouts: 20.2 us -> none  [per_device(): jnp.einsum('skr,srp->kp', flat_left, mapped, preferred_element_type=jnp.f...]
    another operation x17 -> x20, other arithmetic: 120 us -> 100 us  [the longest x8 50.5 us: orthonormal(): ikk = lax.linalg.triangular_solve(lkk, eye, left_side=True, lower=True)]
    unnamed x12 -> x9, local copies, waits for them, and re-layouts: 20.4 us -> 3.06 us
    another operation x13 -> x4, matrix products: 16.3 us -> 1.14 us  [orthonormal(): ikk = lax.linalg.triangular_solve(lkk, eye, left_side=True, lower=True)]
    another operation x17 -> x0, local copies, waits for them, and re-layouts: 14.3 us -> none
    dot_general x4 -> x17, matrix products: 54.7 us -> 66.7 us  [the longest x1 18.2 us: per_device(): lax.dot_general(pieces, left_cores, (((0, 1), (1, 2)), ((), ())), preferr...]
    psum x1, starting transfers between devices: 11.2 us -> 0.3 us  [per_device(): gram = lax.psum(gram_part, ('sum', 'mode'))]
    reduce_scatter x1, waiting for transfers between devices: 271 us -> 282 us  [per_device(): share = lax.psum_scatter(local_sum, 'sum', scatter_dimension=0, tiled=True)]
where the time goes in v1:
time: 796 us; the launch traced here: 789 us
  waiting for transfers between devices  566 us (71%)
  other arithmetic  103 us (13%)
  matrix products  67.8 us (9%)
  blocking collectives  28 us (4%)
  between operations  14.6 us (2%)
  local copies, waits for them, and re-layouts  8.84 us (1%)
    reduce_scatter x1, waiting for transfers between devices, per_device(): share = lax.psum_scatter(local_sum, 'sum', scatter_dimension=0, tiled=True)  282 us
    psum x1, waiting for transfers between devices, per_device(): gram = lax.psum(gram_part, ('sum', 'mode'))  129 us
    all_gather x1, waiting for transfers between devices, per_device(): pieces = lax.all_gather(rounded, 'sum', axis=0, tiled=True)  124 us
    another operation x8, other arithmetic, orthonormal(): ikk = lax.linalg.triangular_solve(lkk, eye, left_side=True, lower=True)  50.5 us
    another operation x12, other arithmetic, orthonormal(): lkk = jnp.linalg.cholesky(diag)  49.8 us
    psum x1, waiting for transfers between devices, per_device(): carries = lax.psum(partial_carry, 'mode')  31.2 us
    psum x1, blocking collectives, per_device(): mapped = lax.psum(partial_map, 'mode').astype(jnp.bfloat16)  28 us
    dot_general x1, matrix products, per_device(): lax.dot_general(pieces, left_cores, (((0, 1), (1, 2)), ((), ())), preferr...  18.2 us
  transfers between devices with their start and end apart: 4, of which 4 were waited for; matrix products, arithmetic and copies ran while one was open for 0% of the time, Pallas kernels for 0%

profile of v1, /device:TPU:0, one launch (start us, length us, event | category | flops | bytes accessed | tf_op | source)
XLA Modules:
  0.0 789.0 jit_solution(3310593755060591880)
XLA Ops:
  7.2 17.1 %fusion.10 = f32[1,512,512]{2,1,0:T(8,128)S(1)} fusion(bf16[16,512,512]{2,1,0:T(8,128)(2,1)} %param.8, bf16[512,16,512]{2,1,0:T(8,128)(2,1)} %bitcast.84), kind=kOutput, calls=%fused_computation.13 | convolution fusion | flops 4294967296 | bytes 17825792 | tf_op jit(solution)/shard_map/dot_general | solution.py:53
  24.3 28.0 %all-reduce.7 = bf16[1,512,512]{2,1,0:T(8,128)(2,1)S(1)} all-reduce(f32[1,512,512]{2,1,0:T(8,128)S(1)} %fusion.10), channel_id=1, replica_groups=mesh['sum'=8,'mode'=4] {'mode'}, use_global_device_ids=true, to_apply=%region_0.0 | all-reduce | flops 262144 | bytes 1572864 | tf_op jit(solution)/shard_map/psum | solution.py:56
  52.3 11.6 %convolution_bitcast_fusion = f32[512,16,512]{2,1,0:T(8,128)} fusion(bf16[1,512,512]{2,1,0:T(8,128)(2,1)S(1)} %all-reduce.7, bf16[1,512,16,512]{3,2,1,0:T(8,128)(2,1)} %param.6), kind=kOutput, calls=%fused_computation | convolution fusion | flops 4294967296 | bytes 25690112 | tf_op jit(solution)/shard_map/dot_general | solution.py:57
  64.3 282.3 %reduce-scatter.2.cloned.1.call-done = f32[64,16,512]{2,1,0:T(8,128)} async-done(((f32[512,16,512]{2,1,0:T(8,128)}), f32[64,16,512]{2,1,0:T(8,128)}) %reduce-scatter.2.cloned.1.call-update) | async-done | bytes 2097168 | tf_op jit(solution)/shard_map/reduce_scatter | solution.py:62
  346.6 6.7 convolution_bitcast_fusion.1
  353.4 129.0 %all-reduce.4.cloned.1.call-done = f32[512,512]{0,1:T(8,128)} async-done(((f32[512,512]{0,1:T(8,128)}), f32[512,512]{0,1:T(8,128)}) %all-reduce.4.cloned.1.call-update) | async-done | bytes 1048592 | tf_op jit(solution)/shard_map/psum | solution.py:65
  482.4 0.8 slice.79
  483.3 0.9 fusion.62
  484.2 11.7 %cholesky.74 = f32[128,128]{1,0:T(8,128)S(1)} custom-call(f32[128,128]{1,0:T(8,128)S(1)} %fusion.62), custom_call_target="Cholesky" | custom-call | tf_op jit(solution)/shard_map/jit(cholesky)/cholesky | solution.py:30
  497.2 9.8 %custom-call.8 = f32[1,128,128]{1,2,0:T(8,128)S(1)} custom-call(f32[1,128,128]{2,1,0:T(8,128)S(1)} %fusion.48), custom_call_target="InvertDiagBlocksLowerTriangular" | custom-call | tf_op jit(solution)/shard_map/triangular_solve/custom-call.0 | solution.py:31
  507.4 1.2 fusion.28
  508.6 1.7 convolution_subtract_fusion
  510.5 11.7 %cholesky.85 = f32[128,128]{1,0:T(8,128)S(1)} custom-call(f32[128,128]{1,0:T(8,128)S(1)} %fusion.60), custom_call_target="Cholesky" | custom-call | tf_op jit(solution)/shard_map/jit(cholesky)/cholesky | solution.py:30
  523.5 18.5 %custom-call.9 = f32[1,128,128]{1,2,0:T(8,128)S(1)} custom-call(f32[1,128,128]{2,1,0:T(8,128)S(1)} %fusion.49), custom_call_target="InvertDiagBlocksLowerTriangular" | custom-call | tf_op jit(solution)/shard_map/triangular_solve/custom-call.0 | solution.py:31
  543.1 0.7 fusion.66
  543.9 11.7 %cholesky.96 = f32[128,128]{1,0:T(8,128)S(1)} custom-call(f32[128,128]{1,0:T(8,128)S(1)} %fusion.58), custom_call_target="Cholesky" | custom-call | tf_op jit(solution)/shard_map/jit(cholesky)/cholesky | solution.py:30
  555.6 0.7 compare_reduce_fusion.1
  556.9 9.8 %custom-call.10 = f32[1,128,128]{1,2,0:T(8,128)S(1)} custom-call(f32[1,128,128]{2,1,0:T(8,128)S(1)} %fusion.50), custom_call_target="InvertDiagBlocksLowerTriangular" | custom-call | tf_op jit(solution)/shard_map/triangular_solve/custom-call.0 | solution.py:31
  567.6 11.9 %cholesky.107 = f32[128,128]{1,0:T(8,128)S(1)} custom-call(f32[128,128]{1,0:T(8,128)S(1)} %fusion.56), custom_call_target="Cholesky" | custom-call | tf_op jit(solution)/shard_map/jit(cholesky)/cholesky | solution.py:30
  579.6 0.7 compare_reduce_fusion
  580.9 9.8 %custom-call.11 = f32[1,128,128]{1,2,0:T(8,128)S(1)} custom-call(f32[1,128,128]{2,1,0:T(8,128)S(1)} %fusion.51), custom_call_target="InvertDiagBlocksLowerTriangular" | custom-call | tf_op jit(solution)/shard_map/triangular_solve/custom-call.0 | solution.py:31
  591.6 1.0 convolution_subtract_fusion.2
  593.3 2.7 convolution_subtract_fusion.1
  596.6 2.8 fusion.16
  600.0 0.8 copy-done.2
  601.5 1.5 copy.36
  603.4 123.7 %all-gather.2.cloned.1.call-done = bf16[512,16,512]{2,0,1:T(8,128)(2,1)} async-done(((bf16[64,16,512]{2,0,1:T(8,128)(2,1)}), bf16[512,16,512]{2,0,1:T(8,128)(2,1)}) %all-gather.2.cloned.1.call-update) | async-done | bytes 8388624 | tf_op jit(solution)/shard_map/all_gather | solution.py:69
  727.1 18.2 %fusion.13 = f32[1,512,512]{2,1,0:T(8,128)} fusion(bf16[512,16,512]{2,0,1:T(8,128)(2,1)} %all-gather.2.cloned.1.call-done, bf16[512,16,512]{2,1,0:T(8,128)(2,1)} %bitcast.85), kind=kOutput, calls=%fused_computation.14 | convolution fusion | flops 4294967296 | bytes 17825792 | tf_op jit(solution)/shard_map/dot_general | solution.py:70
  745.3 1.5 fusion.20
  746.8 1.8 copy.34
  748.6 31.2 %all-reduce.6.cloned.1.call-done = f32[1,512,512]{2,1,0:T(8,128)} async-done(((f32[1,512,512]{2,1,0:T(8,128)}), f32[1,512,512]{2,1,0:T(8,128)}) %all-reduce.6.cloned.1.call-update) | async-done | bytes 1048592 | tf_op jit(solution)/shard_map/psum | solution.py:74
  779.8 2.3 copy.59
  (48 shorter events, 10.7 us)
Async XLA Ops:
  7.2 339.5 %reduce-scatter.2.cloned.1.call-start = ((), (), s32[]{:S(2)}) async-start(), calls=%async_computation.1 | async-start | bytes 18874368 | tf_op jit(solution)/shard_map/reduce_scatter | solution.py:62
  64.0 418.4 %all-reduce.4.cloned.1.call-start = ((), (), s32[]{:S(2)}) async-start(), calls=%async_computation.2 | async-start | bytes 2097152 | tf_op jit(solution)/shard_map/psum | solution.py:65
  353.4 373.8 %all-gather.2.cloned.1.call-start = ((), (), s32[]{:S(2)}) async-start(), calls=%async_computation.3 | async-start | bytes 9437184 | tf_op jit(solution)/shard_map/all_gather | solution.py:69
  510.4 80.6 %copy-start = (f32[64,16,512]{2,1,0:T(8,128)S(1)}, f32[64,16,512]{2,1,0:T(8,128)}, u32[]{:S(2)}) copy-start(f32[64,16,512]{2,1,0:T(8,128)} %reduce-scatter.2.cloned.1.call-done) | copy-start | bytes 6291460
  592.6 3.9 copy-start.3
  596.6 3.4 copy-start.1
  600.0 0.8 copy-start.2
  603.1 176.7 %all-reduce.6.cloned.1.call-start = ((), (), s32[]{:S(2)}) async-start(), calls=%async_computation.4 | async-start | bytes 2097152 | tf_op jit(solution)/shard_map/psum | solution.py:74
Sparse Core Ops, SparseCore 0:
  64.1 282.4 reduce-scatter.1
  353.5 128.8 all-reduce.3
  603.2 123.8 all-gather.1
  745.4 34.2 all-reduce.5

commit v2 on v1

--- a/solution.py
+++ b/solution.py
@@ -62,7 +62,7 @@
     share = lax.psum_scatter(local_sum, "sum", scatter_dimension=0, tiled=True)
     flat_share = share.reshape(-1, target)
     gram_part = jnp.dot(flat_share.T, flat_share, precision=HI)
-    gram = lax.psum(gram_part, ("sum", "mode"))
+    gram = lax.psum(lax.psum(gram_part, "mode"), "sum")
     basis = orthonormal(flat_share, gram)
     block = basis.reshape(share.shape)
     rounded = block.astype(jnp.bfloat16)

time: 796 us -> 785 us (0.986)
  waiting for transfers between devices: 566 us -> 555 us
    psum x1 -> x2, waiting for transfers between devices: 129 us -> 117 us  [per_device(): gram = lax.psum(lax.psum(gram_part, 'mode'), 'sum')]
  transfers between devices with their start and end apart: 4 -> 5, of which waited for: 4 -> 5; matrix products, arithmetic and copies ran while one was open for 0% -> 0% of each run, Pallas kernels for 0% -> 0%
where the time goes in v2:
time: 785 us; the launch traced here: 778 us
  waiting for transfers between devices  555 us (71%)
  other arithmetic  103 us (13%)
  matrix products  67.8 us (9%)
  blocking collectives  28 us (4%)
  between operations  14.6 us (2%)
  local copies, waits for them, and re-layouts  8.84 us (1%)
    reduce_scatter x1, waiting for transfers between devices, per_device(): share = lax.psum_scatter(local_sum, 'sum', scatter_dimension=0, tiled=True)  282 us
    all_gather x1, waiting for transfers between devices, per_device(): pieces = lax.all_gather(rounded, 'sum', axis=0, tiled=True)  124 us
    psum x2, waiting for transfers between devices, per_device(): gram = lax.psum(lax.psum(gram_part, 'mode'), 'sum')  117 us
    another operation x8, other arithmetic, orthonormal(): ikk = lax.linalg.triangular_solve(lkk, eye, left_side=True, lower=True)  50.5 us
    another operation x12, other arithmetic, orthonormal(): lkk = jnp.linalg.cholesky(diag)  49.8 us
    psum x1, waiting for transfers between devices, per_device(): carries = lax.psum(partial_carry, 'mode')  31.2 us
    psum x1, blocking collectives, per_device(): mapped = lax.psum(partial_map, 'mode').astype(jnp.bfloat16)  28 us
    dot_general x1, matrix products, per_device(): lax.dot_general(pieces, left_cores, (((0, 1), (1, 2)), ((), ())), preferr...  18.2 us
  transfers between devices with their start and end apart: 5, of which 5 were waited for; matrix products, arithmetic and copies ran while one was open for 0% of the time, Pallas kernels for 0%

profile of v2, /device:TPU:0, one launch (start us, length us, event | category | flops | bytes accessed | tf_op | source)
XLA Modules:
  0.0 777.8 jit_solution(4699825983358824691)
XLA Ops:
  7.2 17.1 %fusion.10 = f32[1,512,512]{2,1,0:T(8,128)S(1)} fusion(bf16[16,512,512]{2,1,0:T(8,128)(2,1)} %param.8, bf16[512,16,512]{2,1,0:T(8,128)(2,1)} %bitcast.84), kind=kOutput, calls=%fused_computation.13 | convolution fusion | flops 4294967296 | bytes 17825792 | tf_op jit(solution)/shard_map/dot_general | solution.py:53
  24.3 28.0 %all-reduce.10 = bf16[1,512,512]{2,1,0:T(8,128)(2,1)S(1)} all-reduce(f32[1,512,512]{2,1,0:T(8,128)S(1)} %fusion.10), channel_id=1, replica_groups=mesh['sum'=8,'mode'=4] {'mode'}, use_global_device_ids=true, to_apply=%region_0.0 | all-reduce | flops 262144 | bytes 1572864 | tf_op jit(solution)/shard_map/psum | solution.py:56
  52.3 11.6 %convolution_bitcast_fusion = f32[512,16,512]{2,1,0:T(8,128)} fusion(bf16[1,512,512]{2,1,0:T(8,128)(2,1)S(1)} %all-reduce.10, bf16[1,512,16,512]{3,2,1,0:T(8,128)(2,1)} %param.6), kind=kOutput, calls=%fused_computation | convolution fusion | flops 4294967296 | bytes 25690112 | tf_op jit(solution)/shard_map/dot_general | solution.py:57
  64.3 282.3 %reduce-scatter.2.cloned.1.call-done = f32[64,16,512]{2,1,0:T(8,128)} async-done(((f32[512,16,512]{2,1,0:T(8,128)}), f32[64,16,512]{2,1,0:T(8,128)}) %reduce-scatter.2.cloned.1.call-update) | async-done | bytes 2097168 | tf_op jit(solution)/shard_map/reduce_scatter | solution.py:62
  346.6 6.7 convolution_bitcast_fusion.1
  353.4 35.2 %all-reduce.5.cloned.1.call-done = f32[512,512]{0,1:T(8,128)} async-done(((f32[512,512]{0,1:T(8,128)}), f32[512,512]{0,1:T(8,128)}) %all-reduce.5.cloned.1.call-update) | async-done | bytes 1048592 | tf_op jit(solution)/shard_map/psum | solution.py:65
  388.7 81.9 %all-reduce.7.cloned.1.call-done = f32[512,512]{0,1:T(8,128)} async-done(((f32[512,512]{0,1:T(8,128)}), f32[512,512]{0,1:T(8,128)}) %all-reduce.7.cloned.1.call-update) | async-done | bytes 1048592 | tf_op jit(solution)/shard_map/psum | solution.py:65
  470.6 0.8 slice.79
  471.5 0.9 fusion.62
  472.4 11.7 %cholesky.74 = f32[128,128]{1,0:T(8,128)S(1)} custom-call(f32[128,128]{1,0:T(8,128)S(1)} %fusion.62), custom_call_target="Cholesky" | custom-call | tf_op jit(solution)/shard_map/jit(cholesky)/cholesky | solution.py:30
  485.4 9.8 %custom-call.8 = f32[1,128,128]{1,2,0:T(8,128)S(1)} custom-call(f32[1,128,128]{2,1,0:T(8,128)S(1)} %fusion.48), custom_call_target="InvertDiagBlocksLowerTriangular" | custom-call | tf_op jit(solution)/shard_map/triangular_solve/custom-call.0 | solution.py:31
  495.5 1.2 fusion.28
  496.8 1.7 convolution_subtract_fusion
  498.7 11.7 %cholesky.85 = f32[128,128]{1,0:T(8,128)S(1)} custom-call(f32[128,128]{1,0:T(8,128)S(1)} %fusion.60), custom_call_target="Cholesky" | custom-call | tf_op jit(solution)/shard_map/jit(cholesky)/cholesky | solution.py:30
  511.7 18.5 %custom-call.9 = f32[1,128,128]{1,2,0:T(8,128)S(1)} custom-call(f32[1,128,128]{2,1,0:T(8,128)S(1)} %fusion.49), custom_call_target="InvertDiagBlocksLowerTriangular" | custom-call | tf_op jit(solution)/shard_map/triangular_solve/custom-call.0 | solution.py:31
  531.3 0.7 fusion.66
  532.0 11.7 %cholesky.96 = f32[128,128]{1,0:T(8,128)S(1)} custom-call(f32[128,128]{1,0:T(8,128)S(1)} %fusion.58), custom_call_target="Cholesky" | custom-call | tf_op jit(solution)/shard_map/jit(cholesky)/cholesky | solution.py:30
  543.8 0.7 compare_reduce_fusion.1
  545.1 9.8 %custom-call.10 = f32[1,128,128]{1,2,0:T(8,128)S(1)} custom-call(f32[1,128,128]{2,1,0:T(8,128)S(1)} %fusion.50), custom_call_target="InvertDiagBlocksLowerTriangular" | custom-call | tf_op jit(solution)/shard_map/triangular_solve/custom-call.0 | solution.py:31
  555.8 11.9 %cholesky.107 = f32[128,128]{1,0:T(8,128)S(1)} custom-call(f32[128,128]{1,0:T(8,128)S(1)} %fusion.56), custom_call_target="Cholesky" | custom-call | tf_op jit(solution)/shard_map/jit(cholesky)/cholesky | solution.py:30
  569.1 9.8 %custom-call.11 = f32[1,128,128]{1,2,0:T(8,128)S(1)} custom-call(f32[1,128,128]{2,1,0:T(8,128)S(1)} %fusion.51), custom_call_target="InvertDiagBlocksLowerTriangular" | custom-call | tf_op jit(solution)/shard_map/triangular_solve/custom-call.0 | solution.py:31
  579.8 1.0 convolution_subtract_fusion.2
  581.4 2.7 convolution_subtract_fusion.1
  584.8 2.8 fusion.16
  588.2 0.8 copy-done.2
  589.7 1.5 copy.36
  591.6 124.4 %all-gather.2.cloned.1.call-done = bf16[512,16,512]{2,0,1:T(8,128)(2,1)} async-done(((bf16[64,16,512]{2,0,1:T(8,128)(2,1)}), bf16[512,16,512]{2,0,1:T(8,128)(2,1)}) %all-gather.2.cloned.1.call-update) | async-done | bytes 8388624 | tf_op jit(solution)/shard_map/all_gather | solution.py:69
  716.0 18.2 %fusion.13 = f32[1,512,512]{2,1,0:T(8,128)} fusion(bf16[512,16,512]{2,0,1:T(8,128)(2,1)} %all-gather.2.cloned.1.call-done, bf16[512,16,512]{2,1,0:T(8,128)(2,1)} %bitcast.85), kind=kOutput, calls=%fused_computation.14 | convolution fusion | flops 4294967296 | bytes 17825792 | tf_op jit(solution)/shard_map/dot_general | solution.py:70
  734.1 1.5 fusion.20
  735.6 1.8 copy.34
  737.4 31.2 %all-reduce.9.cloned.1.call-done = f32[1,512,512]{2,1,0:T(8,128)} async-done(((f32[1,512,512]{2,1,0:T(8,128)}), f32[1,512,512]{2,1,0:T(8,128)}) %all-reduce.9.cloned.1.call-update) | async-done | bytes 1048592 | tf_op jit(solution)/shard_map/psum | solution.py:74
  768.6 2.3 copy.60
  (51 shorter events, 11.4 us)
Async XLA Ops:
  7.2 339.5 %reduce-scatter.2.cloned.1.call-start = ((), (), s32[]{:S(2)}) async-start(), calls=%async_computation.1 | async-start | bytes 18874368 | tf_op jit(solution)/shard_map/reduce_scatter | solution.py:62
  64.0 324.6 %all-reduce.5.cloned.1.call-start = ((), (), s32[]{:S(2)}) async-start(), calls=%async_computation.2 | async-start | bytes 2097152 | tf_op jit(solution)/shard_map/psum | solution.py:65
  353.4 117.2 %all-reduce.7.cloned.1.call-start = ((), (), s32[]{:S(2)}) async-start(), calls=%async_computation.3 | async-start | bytes 2097152 | tf_op jit(solution)/shard_map/psum | solution.py:65
  388.7 327.3 %all-gather.2.cloned.1.call-start = ((), (), s32[]{:S(2)}) async-start(), calls=%async_computation.4 | async-start | bytes 9437184 | tf_op jit(solution)/shard_map/all_gather | solution.py:69
  498.6 80.6 %copy-start = (f32[64,16,512]{2,1,0:T(8,128)S(1)}, f32[64,16,512]{2,1,0:T(8,128)}, u32[]{:S(2)}) copy-start(f32[64,16,512]{2,1,0:T(8,128)} %reduce-scatter.2.cloned.1.call-done) | copy-start | bytes 6291460
  580.8 3.9 copy-start.3
  584.7 3.4 copy-start.1
  588.2 0.8 copy-start.2
  591.3 177.3 %all-reduce.9.cloned.1.call-start = ((), (), s32[]{:S(2)}) async-start(), calls=%async_computation.5 | async-start | bytes 2097152 | tf_op jit(solution)/shard_map/psum | solution.py:74
Sparse Core Ops, SparseCore 0:
  64.1 282.4 reduce-scatter.1
  353.5 35.1 all-reduce.4
  392.2 78.3 all-reduce.6
  591.4 124.4 all-gather.1
  734.3 34.2 all-reduce.8

commit v3 on v2

--- a/solution.py
+++ b/solution.py
@@ -1,3 +1,4 @@
+import functools
 import math
 
 import jax
@@ -47,7 +48,65 @@
     return jnp.concatenate(blocks, axis=1)
 
 
-def per_device(left_cores, right_cores, sketch):
+def ring_order(mesh):
+    n = mesh.shape["sum"]
+    plain = list(range(n))
+    try:
+        coords = [tuple(int(c) for c in mesh.devices[i, 0].coords) for i in range(n)]
+    except (AttributeError, TypeError, IndexError):
+        return plain
+    axes = [d for d in range(len(coords[0])) if len({c[d] for c in coords}) > 1]
+    if len(axes) != 2:
+        return plain
+    values = [sorted({c[d] for c in coords}) for d in axes]
+    if len(values[0]) % 2:
+        axes, values = axes[::-1], values[::-1]
+    if len(values[0]) % 2 or len(values[0]) * len(values[1]) != n:
+        return plain
+    where = {(c[axes[0]], c[axes[1]]): i for i, c in enumerate(coords)}
+    first, second = values
+    cells = [(a, second[0]) for a in first]
+    for row, a in enumerate(reversed(first)):
+        cols = second[1:] if row % 2 == 0 else second[1:][::-1]
+        cells.extend((a, b) for b in cols)
+    if len(set(cells)) != n or any(cell not in where for cell in cells):
+        return plain
+    return [where[cell] for cell in cells]
+
+
+def ring_reduce_scatter(local, ring):
+    n = len(ring)
+    rows = local.shape[0] // n
+    half = rows // 2
+    pos = [0] * n
+    for p, i in enumerate(ring):
+        pos[i] = p
+    me = lax.axis_index("sum")
+    fwd = [(ring[p], ring[(p + 1) % n]) for p in range(n)]
+    bwd = [(ring[p], ring[(p - 1) % n]) for p in range(n)]
+
+    def table(shift, sign):
+        return jnp.asarray(
+            [[ring[(pos[i] + sign * (shift + t)) % n] for i in range(n)] for t in range(n)],
+            dtype=jnp.int32,
+        )
+
+    fwd_blocks = table(1, -1)
+    bwd_blocks = table(1, 1)
+
+    def piece(block, offset, size):
+        start = block * rows + offset
+        return lax.dynamic_slice_in_dim(local, start, size, axis=0)
+
+    acc_f = piece(fwd_blocks[0, me], 0, half)
+    acc_b = piece(bwd_blocks[0, me], half, rows - half)
+    for t in range(1, n):
+        acc_f = lax.ppermute(acc_f, "sum", fwd) + piece(fwd_blocks[t, me], 0, half)
+        acc_b = lax.ppermute(acc_b, "sum", bwd) + piece(bwd_blocks[t, me], half, rows - half)
+    return jnp.concatenate([acc_f, acc_b], axis=0)
+
+
+def per_device(ring, left_cores, right_cores, sketch):
     sum_local, rows_in, mode_local, rank_width = left_cores.shape
     target = sketch.shape[2]
     partial_map = lax.dot_general(
@@ -59,7 +118,7 @@
     )
     local_sum = with_layout_constraint(local_sum, Layout(major_to_minor=(0, 1, 2)))
     factor = math.sqrt(R_IN * MODES)
-    share = lax.psum_scatter(local_sum, "sum", scatter_dimension=0, tiled=True)
+    share = ring_reduce_scatter(local_sum, ring)
     flat_share = share.reshape(-1, target)
     gram_part = jnp.dot(flat_share.T, flat_share, precision=HI)
     gram = lax.psum(lax.psum(gram_part, "mode"), "sum")
@@ -78,6 +137,7 @@
 def solution(mesh):
     in_specs = (P("sum", None, "mode", None), P("sum", None, "mode", None), P("mode", None, None))
     out_specs = (P("sum", "mode", None), P("sum", None, None))
+    ring = ring_order(mesh)
     return jax.shard_map(
-        per_device, mesh=mesh, in_specs=in_specs, out_specs=out_specs, check_vma=False
+        functools.partial(per_device, ring), mesh=mesh, in_specs=in_specs, out_specs=out_specs, check_vma=False
     )

time: 785 us -> 702 us (0.89)
  waiting for transfers between devices: 555 us -> 428 us
  starting transfers between devices: 0.71 us -> 16.5 us
  other arithmetic: 103 us -> 118 us
  between operations: 14.6 us -> 24.7 us
    reduce_scatter x1 -> x0, waiting for transfers between devices: 282 us -> none  [per_device(): share = lax.psum_scatter(local_sum, 'sum', scatter_dimension=0, tiled=True)]
    ppermute x0 -> x14, waiting for transfers between devices: none -> 157 us  [the longest x7 132 us: ring_reduce_scatter(): acc_f = lax.ppermute(acc_f, 'sum', fwd) + piece(fwd_blocks[t, me], 0, half)]
    add x0 -> x8, other arithmetic: none -> 21.9 us  [the longest x7 20.4 us: ring_reduce_scatter(): acc_f = lax.ppermute(acc_f, 'sum', fwd) + piece(fwd_blocks[t, me], 0, half)]
    ppermute x0 -> x14, starting transfers between devices: none -> 15.6 us  [the longest x7 8.61 us: ring_reduce_scatter(): acc_f = lax.ppermute(acc_f, 'sum', fwd) + piece(fwd_blocks[t, me], 0, half)]
    another operation x8, other arithmetic: 50.5 us -> 41.9 us  [orthonormal(): ikk = lax.linalg.triangular_solve(lkk, eye, left_side=True, lower=True)]
  transfers between devices with their start and end apart: 5 -> 18, of which waited for: 5 -> 18; matrix products, arithmetic and copies ran while one was open for 0% -> 1% of each run, Pallas kernels for 0% -> 0%
where the time goes in v3:
time: 702 us; the launch traced here: 693 us
  waiting for transfers between devices  428 us (61%)
  other arithmetic  118 us (17%)
  matrix products  65.6 us (9%)
  blocking collectives  28 us (4%)
  between operations  24.7 us (4%)
  starting transfers between devices  16.5 us (2%)
  local copies, waits for them, and re-layouts  12.5 us (2%)
    ppermute x7, waiting for transfers between devices, ring_reduce_scatter(): acc_f = lax.ppermute(acc_f, 'sum', fwd) + piece(fwd_blocks[t, me], 0, half)  132 us
    all_gather x1, waiting for transfers between devices, per_device(): pieces = lax.all_gather(rounded, 'sum', axis=0, tiled=True)  124 us
    psum x2, waiting for transfers between devices, per_device(): gram = lax.psum(lax.psum(gram_part, 'mode'), 'sum')  115 us
    another operation x12, other arithmetic, orthonormal(): lkk = jnp.linalg.cholesky(diag)  49.8 us
    another operation x8, other arithmetic, orthonormal(): ikk = lax.linalg.triangular_solve(lkk, eye, left_side=True, lower=True)  41.9 us
    psum x1, waiting for transfers between devices, per_device(): carries = lax.psum(partial_carry, 'mode')  31.2 us
    psum x1, blocking collectives, per_device(): mapped = lax.psum(partial_map, 'mode').astype(jnp.bfloat16)  28 us
    ppermute x7, waiting for transfers between devices, ring_reduce_scatter(): lax.ppermute(acc_b, 'sum', bwd)  24.9 us
  transfers between devices with their start and end apart: 18, of which 18 were waited for; matrix products, arithmetic and copies ran while one was open for 1% of the time, Pallas kernels for 0%

profile of v3, /device:TPU:0, one launch (start us, length us, event | category | flops | bytes accessed | tf_op | source)
XLA Modules:
  0.0 692.5 jit_solution(9236064500363184354)
XLA Ops:
  9.5 17.1 %fusion.10 = f32[1,512,512]{2,1,0:T(8,128)S(1)} fusion(bf16[16,512,512]{2,1,0:T(8,128)(2,1)} %param.10, bf16[512,16,512]{2,1,0:T(8,128)(2,1)} %bitcast.103), kind=kOutput, calls=%fused_computation.14 | convolution fusion | flops 4294967296 | bytes 17825792 | tf_op jit(solution)/shard_map/dot_general | solution.py:112
  26.6 28.0 %all-reduce.10 = bf16[1,512,512]{2,1,0:T(8,128)(2,1)S(1)} all-reduce(f32[1,512,512]{2,1,0:T(8,128)S(1)} %fusion.10), channel_id=1, replica_groups=mesh['sum'=8,'mode'=4] {'mode'}, use_global_device_ids=true, to_apply=%region_0.0 | all-reduce | flops 262144 | bytes 1572864 | tf_op jit(solution)/shard_map/psum | solution.py:115
  54.6 11.6 %convolution_bitcast_fusion = f32[512,16,512]{2,1,0:T(8,128)} fusion(bf16[1,512,512]{2,1,0:T(8,128)(2,1)S(1)} %all-reduce.10, bf16[1,512,16,512]{3,2,1,0:T(8,128)(2,1)} %param.8), kind=kOutput, calls=%fused_computation | convolution fusion | flops 4294967296 | bytes 25690112 | tf_op jit(solution)/shard_map/dot_general | solution.py:116
  70.4 22.6 %collective-permute-done = f32[32,16,512]{2,1,0:T(8,128)S(1)} collective-permute-done((f32[32,16,512]{2,1,0:T(8,128)S(1)}, f32[32,16,512]{2,1,0:T(8,128)S(1)}, u32[]{:S(2)}, u32[]{:S(2)}) %collective-permute-start) | collective-permute-done | bytes 1048608 | tf_op jit(solution)/shard_map/ppermute | solution.py:104
  93.0 2.8 dynamic-slice_add_fusion.13
  99.2 21.3 %collective-permute-done.1 = f32[32,16,512]{2,1,0:T(8,128)S(1)} collective-permute-done((f32[32,16,512]{2,1,0:T(8,128)S(1)}, f32[32,16,512]{2,1,0:T(8,128)S(1)}, u32[]{:S(2)}, u32[]{:S(2)}) %collective-permute-start.1) | collective-permute-done | bytes 1048608 | tf_op jit(solution)/shard_map/ppermute | solution.py:104
  121.9 3.0 dynamic-slice_add_fusion.12
  128.2 20.1 %collective-permute-done.2 = f32[32,16,512]{2,1,0:T(8,128)S(1)} collective-permute-done((f32[32,16,512]{2,1,0:T(8,128)S(1)}, f32[32,16,512]{2,1,0:T(8,128)S(1)}, u32[]{:S(2)}, u32[]{:S(2)}) %collective-permute-start.2) | collective-permute-done | bytes 1048608 | tf_op jit(solution)/shard_map/ppermute | solution.py:104
  149.8 3.0 dynamic-slice_add_fusion.11
  156.3 18.7 %collective-permute-done.3 = f32[32,16,512]{2,1,0:T(8,128)S(1)} collective-permute-done((f32[32,16,512]{2,1,0:T(8,128)S(1)}, f32[32,16,512]{2,1,0:T(8,128)S(1)}, u32[]{:S(2)}, u32[]{:S(2)}) %collective-permute-start.3) | collective-permute-done | bytes 1048608 | tf_op jit(solution)/shard_map/ppermute | solution.py:104
  176.7 3.0 dynamic-slice_add_fusion.10
  183.0 17.7 %collective-permute-done.4 = f32[32,16,512]{2,1,0:T(8,128)S(1)} collective-permute-done((f32[32,16,512]{2,1,0:T(8,128)S(1)}, f32[32,16,512]{2,1,0:T(8,128)S(1)}, u32[]{:S(2)}, u32[]{:S(2)}) %collective-permute-start.4) | collective-permute-done | bytes 1048608 | tf_op jit(solution)/shard_map/ppermute | solution.py:104
  202.2 3.0 dynamic-slice_add_fusion.9
  208.5 16.5 %collective-permute-done.5 = f32[32,16,512]{2,1,0:T(8,128)S(1)} collective-permute-done((f32[32,16,512]{2,1,0:T(8,128)S(1)}, f32[32,16,512]{2,1,0:T(8,128)S(1)}, u32[]{:S(2)}, u32[]{:S(2)}) %collective-permute-start.5) | collective-permute-done | bytes 1048608 | tf_op jit(solution)/shard_map/ppermute | solution.py:104
  225.6 3.3 dynamic-slice_add_fusion.8
  232.2 15.3 %collective-permute-done.6 = f32[32,16,512]{2,1,0:T(8,128)S(1)} collective-permute-done((f32[32,16,512]{2,1,0:T(8,128)S(1)}, f32[32,16,512]{2,1,0:T(8,128)S(1)}, u32[]{:S(2)}, u32[]{:S(2)}) %collective-permute-start.6) | collective-permute-done | bytes 1048608 | tf_op jit(solution)/shard_map/ppermute | solution.py:104
  247.4 2.9 collective-permute-done.12
  255.1 15.3 %collective-permute-done.13 = f32[32,16,512]{2,1,0:T(8,128)S(1)} collective-permute-done((f32[32,16,512]{2,1,0:T(8,128)S(1)}, f32[32,16,512]{2,1,0:T(8,128)S(1)}, u32[]{:S(2)}, u32[]{:S(2)}) %collective-permute-start.13) | collective-permute-done | bytes 1048608 | tf_op jit(solution)/shard_map/ppermute | solution.py:105
  271.8 4.5 convolution_bitcast_fusion.1
  276.4 34.5 %all-reduce.5.cloned.1.call-done = f32[512,512]{0,1:T(8,128)} async-done(((f32[512,512]{0,1:T(8,128)}), f32[512,512]{0,1:T(8,128)}) %all-reduce.5.cloned.1.call-update) | async-done | bytes 1048592 | tf_op jit(solution)/shard_map/psum | solution.py:124
  312.9 80.4 %all-reduce.7.cloned.1.call-done = f32[512,512]{0,1:T(8,128)} async-done(((f32[512,512]{0,1:T(8,128)}), f32[512,512]{0,1:T(8,128)}) %all-reduce.7.cloned.1.call-update) | async-done | bytes 1048592 | tf_op jit(solution)/shard_map/psum | solution.py:124
  395.0 11.7 %cholesky.74 = f32[128,128]{1,0:T(8,128)S(1)} custom-call(f32[128,128]{1,0:T(8,128)S(1)} %fusion.64), custom_call_target="Cholesky" | custom-call | tf_op jit(solution)/shard_map/jit(cholesky)/cholesky | solution.py:31
  408.1 9.8 %custom-call.8 = f32[1,128,128]{1,2,0:T(8,128)S(1)} custom-call(f32[1,128,128]{2,1,0:T(8,128)S(1)} %fusion.49), custom_call_target="InvertDiagBlocksLowerTriangular" | custom-call | tf_op jit(solution)/shard_map/triangular_solve/custom-call.0 | solution.py:32
  421.3 11.7 %cholesky.85 = f32[128,128]{1,0:T(8,128)S(1)} custom-call(f32[128,128]{1,0:T(8,128)S(1)} %fusion.62), custom_call_target="Cholesky" | custom-call | tf_op jit(solution)/shard_map/jit(cholesky)/cholesky | solution.py:31
  434.4 9.9 %custom-call.9 = f32[1,128,128]{1,2,0:T(8,128)S(1)} custom-call(f32[1,128,128]{2,1,0:T(8,128)S(1)} %fusion.50), custom_call_target="InvertDiagBlocksLowerTriangular" | custom-call | tf_op jit(solution)/shard_map/triangular_solve/custom-call.0 | solution.py:32
  446.7 11.7 %cholesky.96 = f32[128,128]{1,0:T(8,128)S(1)} custom-call(f32[128,128]{1,0:T(8,128)S(1)} %fusion.60), custom_call_target="Cholesky" | custom-call | tf_op jit(solution)/shard_map/jit(cholesky)/cholesky | solution.py:31
  459.8 9.8 %custom-call.10 = f32[1,128,128]{1,2,0:T(8,128)S(1)} custom-call(f32[1,128,128]{2,1,0:T(8,128)S(1)} %fusion.51), custom_call_target="InvertDiagBlocksLowerTriangular" | custom-call | tf_op jit(solution)/shard_map/triangular_solve/custom-call.0 | solution.py:32
  470.5 11.9 %cholesky.107 = f32[128,128]{1,0:T(8,128)S(1)} custom-call(f32[128,128]{1,0:T(8,128)S(1)} %fusion.58), custom_call_target="Cholesky" | custom-call | tf_op jit(solution)/shard_map/jit(cholesky)/cholesky | solution.py:31
  483.8 9.8 %custom-call.11 = f32[1,128,128]{1,2,0:T(8,128)S(1)} custom-call(f32[1,128,128]{2,1,0:T(8,128)S(1)} %fusion.52), custom_call_target="InvertDiagBlocksLowerTriangular" | custom-call | tf_op jit(solution)/shard_map/triangular_solve/custom-call.0 | solution.py:32
  506.3 124.4 %all-gather.2.cloned.1.call-done = bf16[512,16,512]{2,0,1:T(8,128)(2,1)} async-done(((bf16[64,16,512]{2,0,1:T(8,128)(2,1)}), bf16[512,16,512]{2,0,1:T(8,128)(2,1)}) %all-gather.2.cloned.1.call-update) | async-done | bytes 8388624 | tf_op jit(solution)/shard_map/all_gather | solution.py:128
  630.7 18.2 %fusion.13 = f32[1,512,512]{2,1,0:T(8,128)} fusion(bf16[512,16,512]{2,0,1:T(8,128)(2,1)} %all-gather.2.cloned.1.call-done, bf16[512,16,512]{2,1,0:T(8,128)(2,1)} %bitcast.104), kind=kOutput, calls=%fused_computation.15 | convolution fusion | flops 4294967296 | bytes 17825792 | tf_op jit(solution)/shard_map/dot_general | solution.py:129
  652.1 31.2 %all-reduce.9.cloned.1.call-done = f32[1,512,512]{2,1,0:T(8,128)} async-done(((f32[1,512,512]{2,1,0:T(8,128)}), f32[1,512,512]{2,1,0:T(8,128)}) %all-reduce.9.cloned.1.call-update) | async-done | bytes 1048592 | tf_op jit(solution)/shard_map/psum | solution.py:133
  (90 shorter events, 63.0 us)
Async XLA Ops:
  7.2 303.7 %all-reduce.5.cloned.1.call-start = ((), (), s32[]{:S(2)}) async-start(), calls=%async_computation | async-start | bytes 2097152 | tf_op jit(solution)/shard_map/psum | solution.py:124
  67.6 25.5 %collective-permute-start = (f32[32,16,512]{2,1,0:T(8,128)S(1)}, f32[32,16,512]{2,1,0:T(8,128)S(1)}, u32[]{:S(2)}, u32[]{:S(2)}) collective-permute-start(f32[32,16,512]{2,1,0:T(8,128)S(1)} %constant_dynamic-slice_fusion.2), channel_id=1, source_target_pairs={{0,4},{4,12},{12,20},{20,28},{28,24},{24,16},{16,8},{8,0},{1,5},{5... | collective-permute-start | bytes 3145736 | tf_op jit(solution)/shard_map/ppermute | solution.py:104
  95.9 24.6 %collective-permute-start.1 = (f32[32,16,512]{2,1,0:T(8,128)S(1)}, f32[32,16,512]{2,1,0:T(8,128)S(1)}, u32[]{:S(2)}, u32[]{:S(2)}) collective-permute-start(f32[32,16,512]{2,1,0:T(8,128)S(1)} %get-tuple-element.18), channel_id=1, source_target_pairs={{0,4},{4,12},{12,20},{20,28},{28,24},{24,16},{16,8},{8,0},{1,5},{5... | collective-permute-start | bytes 3145736 | tf_op jit(solution)/shard_map/ppermute | solution.py:104
  97.4 24.5 %collective-permute-start.7 = (f32[32,16,512]{2,1,0:T(8,128)}, f32[32,16,512]{2,1,0:T(8,128)S(1)}, u32[]{:S(2)}, u32[]{:S(2)}) collective-permute-start(f32[32,16,512]{2,1,0:T(8,128)} %get-tuple-element.19), channel_id=1, source_target_pairs={{0,8},{4,0},{12,4},{20,12},{28,20},{24,28},{16,24},{8,16},{1,9},{5... | collective-permute-start | bytes 3145736 | tf_op jit(solution)/shard_map/ppermute | solution.py:105
  124.9 23.4 %collective-permute-start.2 = (f32[32,16,512]{2,1,0:T(8,128)S(1)}, f32[32,16,512]{2,1,0:T(8,128)S(1)}, u32[]{:S(2)}, u32[]{:S(2)}) collective-permute-start(f32[32,16,512]{2,1,0:T(8,128)S(1)} %get-tuple-element.16), channel_id=1, source_target_pairs={{0,4},{4,12},{12,20},{20,28},{28,24},{24,16},{16,8},{8,0},{1,5},{5... | collective-permute-start | bytes 3145736 | tf_op jit(solution)/shard_map/ppermute | solution.py:104
  126.5 23.3 %collective-permute-start.8 = (f32[32,16,512]{2,1,0:T(8,128)}, f32[32,16,512]{2,1,0:T(8,128)S(1)}, u32[]{:S(2)}, u32[]{:S(2)}) collective-permute-start(f32[32,16,512]{2,1,0:T(8,128)} %get-tuple-element.17), channel_id=1, source_target_pairs={{0,8},{4,0},{12,4},{20,12},{28,20},{24,28},{16,24},{8,16},{1,9},{5... | collective-permute-start | bytes 3145736 | tf_op jit(solution)/shard_map/ppermute | solution.py:105
  152.8 22.2 %collective-permute-start.3 = (f32[32,16,512]{2,1,0:T(8,128)S(1)}, f32[32,16,512]{2,1,0:T(8,128)S(1)}, u32[]{:S(2)}, u32[]{:S(2)}) collective-permute-start(f32[32,16,512]{2,1,0:T(8,128)S(1)} %get-tuple-element.14), channel_id=1, source_target_pairs={{0,4},{4,12},{12,20},{20,28},{28,24},{24,16},{16,8},{8,0},{1,5},{5... | collective-permute-start | bytes 3145736 | tf_op jit(solution)/shard_map/ppermute | solution.py:104
  154.4 22.3 %collective-permute-start.9 = (f32[32,16,512]{2,1,0:T(8,128)}, f32[32,16,512]{2,1,0:T(8,128)S(1)}, u32[]{:S(2)}, u32[]{:S(2)}) collective-permute-start(f32[32,16,512]{2,1,0:T(8,128)} %get-tuple-element.15), channel_id=1, source_target_pairs={{0,8},{4,0},{12,4},{20,12},{28,20},{24,28},{16,24},{8,16},{1,9},{5... | collective-permute-start | bytes 3145736 | tf_op jit(solution)/shard_map/ppermute | solution.py:105
  179.7 21.0 %collective-permute-start.4 = (f32[32,16,512]{2,1,0:T(8,128)S(1)}, f32[32,16,512]{2,1,0:T(8,128)S(1)}, u32[]{:S(2)}, u32[]{:S(2)}) collective-permute-start(f32[32,16,512]{2,1,0:T(8,128)S(1)} %get-tuple-element.12), channel_id=1, source_target_pairs={{0,4},{4,12},{12,20},{20,28},{28,24},{24,16},{16,8},{8,0},{1,5},{5... | collective-permute-start | bytes 3145736 | tf_op jit(solution)/shard_map/ppermute | solution.py:104
  181.3 20.9 %collective-permute-start.10 = (f32[32,16,512]{2,1,0:T(8,128)}, f32[32,16,512]{2,1,0:T(8,128)S(1)}, u32[]{:S(2)}, u32[]{:S(2)}) collective-permute-start(f32[32,16,512]{2,1,0:T(8,128)} %get-tuple-element.13), channel_id=1, source_target_pairs={{0,8},{4,0},{12,4},{20,12},{28,20},{24,28},{16,24},{8,16},{1,9},{5... | collective-permute-start | bytes 3145736 | tf_op jit(solution)/shard_map/ppermute | solution.py:105
  205.2 19.8 %collective-permute-start.5 = (f32[32,16,512]{2,1,0:T(8,128)S(1)}, f32[32,16,512]{2,1,0:T(8,128)S(1)}, u32[]{:S(2)}, u32[]{:S(2)}) collective-permute-start(f32[32,16,512]{2,1,0:T(8,128)S(1)} %get-tuple-element.10), channel_id=1, source_target_pairs={{0,4},{4,12},{12,20},{20,28},{28,24},{24,16},{16,8},{8,0},{1,5},{5... | collective-permute-start | bytes 3145736 | tf_op jit(solution)/shard_map/ppermute | solution.py:104
  205.7 19.9 %collective-permute-start.11 = (f32[32,16,512]{2,1,0:T(8,128)}, f32[32,16,512]{2,1,0:T(8,128)}, u32[]{:S(2)}, u32[]{:S(2)}) collective-permute-start(f32[32,16,512]{2,1,0:T(8,128)} %get-tuple-element.11), channel_id=1, source_target_pairs={{0,8},{4,0},{12,4},{20,12},{28,20},{24,28},{16,24},{8,16},{1,9},{5... | collective-permute-start | bytes 3145736 | tf_op jit(solution)/shard_map/ppermute | solution.py:105
  228.9 18.6 %collective-permute-start.6 = (f32[32,16,512]{2,1,0:T(8,128)S(1)}, f32[32,16,512]{2,1,0:T(8,128)S(1)}, u32[]{:S(2)}, u32[]{:S(2)}) collective-permute-start(f32[32,16,512]{2,1,0:T(8,128)S(1)} %get-tuple-element.8), channel_id=1, source_target_pairs={{0,4},{4,12},{12,20},{20,28},{28,24},{24,16},{16,8},{8,0},{1,5},{5... | collective-permute-start | bytes 3145736 | tf_op jit(solution)/shard_map/ppermute | solution.py:104
  229.2 21.1 %collective-permute-start.12 = (f32[32,16,512]{2,1,0:T(8,128)}, f32[32,16,512]{2,1,0:T(8,128)}, u32[]{:S(2)}, u32[]{:S(2)}) collective-permute-start(f32[32,16,512]{2,1,0:T(8,128)} %get-tuple-element.9), channel_id=1, source_target_pairs={{0,8},{4,0},{12,4},{20,12},{28,20},{24,28},{16,24},{8,16},{1,9},{5... | collective-permute-start | bytes 3145736 | tf_op jit(solution)/shard_map/ppermute | solution.py:105
  252.7 23.6 %copy-start.2 = (f32[32,16,512]{2,1,0:T(8,128)}, f32[32,16,512]{2,1,0:T(8,128)S(1)}, u32[]{:S(2)}) copy-start(f32[32,16,512]{2,1,0:T(8,128)S(1)} %get-tuple-element.6) | copy-start | bytes 3145732
  252.7 17.6 %collective-permute-start.13 = (f32[32,16,512]{2,1,0:T(8,128)S(1)}, f32[32,16,512]{2,1,0:T(8,128)S(1)}, u32[]{:S(2)}, u32[]{:S(2)}) collective-permute-start(f32[32,16,512]{2,1,0:T(8,128)S(1)} %get-tuple-element.7), channel_id=1, source_target_pairs={{0,8},{4,0},{12,4},{20,12},{28,20},{24,28},{16,24},{8,16},{1,9},{5... | collective-permute-start | bytes 3145736 | tf_op jit(solution)/shard_map/ppermute | solution.py:105
  276.3 116.9 %all-reduce.7.cloned.1.call-start = ((), (), s32[]{:S(2)}) async-start(), calls=%async_computation.1 | async-start | bytes 2097152 | tf_op jit(solution)/shard_map/psum | solution.py:124
  310.9 319.7 %all-gather.2.cloned.1.call-start = ((), (), s32[]{:S(2)}) async-start(), calls=%async_computation.2 | async-start | bytes 9437184 | tf_op jit(solution)/shard_map/all_gather | solution.py:128
  495.5 4.0 copy-start.3
  495.5 4.0 copy-start.4
  499.5 3.4 copy-start
  502.9 0.8 copy-start.1
  506.0 177.3 %all-reduce.9.cloned.1.call-start = ((), (), s32[]{:S(2)}) async-start(), calls=%async_computation.3 | async-start | bytes 2097152 | tf_op jit(solution)/shard_map/psum | solution.py:133
Sparse Core Ops, SparseCore 0:
  276.4 34.4 all-reduce.4
  314.8 78.3 all-reduce.6
  506.1 124.4 all-gather.1
  648.9 34.2 all-reduce.8

commit v4 on v3

--- a/solution.py
+++ b/solution.py
@@ -106,6 +106,41 @@
     return jnp.concatenate([acc_f, acc_b], axis=0)
 
 
+def ring_gather_carries(own, left_cores, ring):
+    n = len(ring)
+    rows = own.shape[0]
+    half = rows // 2
+    pos = [0] * n
+    for p, i in enumerate(ring):
+        pos[i] = p
+    me = lax.axis_index("sum")
+    fwd = [(ring[p], ring[(p + 1) % n]) for p in range(n)]
+    bwd = [(ring[p], ring[(p - 1) % n]) for p in range(n)]
+    fwd_blocks = jnp.asarray(
+        [[ring[(pos[i] - t) % n] for i in range(n)] for t in range(n)], dtype=jnp.int32
+    )
+    bwd_blocks = jnp.asarray(
+        [[ring[(pos[i] + t) % n] for i in range(n)] for t in range(n)], dtype=jnp.int32
+    )
+
+    def term(piece, block, offset):
+        start = block * rows + offset
+        lhs = lax.dynamic_slice_in_dim(left_cores, start, piece.shape[0], axis=1)
+        return lax.dot_general(
+            piece, lhs, (((0, 1), (1, 2)), ((), ())), preferred_element_type=jnp.float32
+        )
+
+    hold_f = own[:half]
+    hold_b = own[half:]
+    total = term(hold_f, fwd_blocks[0, me], 0) + term(hold_b, bwd_blocks[0, me], half)
+    for t in range(1, n):
+        hold_f = lax.ppermute(hold_f, "sum", fwd)
+        hold_b = lax.ppermute(hold_b, "sum", bwd)
+        total = total + term(hold_f, fwd_blocks[t, me], 0)
+        total = total + term(hold_b, bwd_blocks[t, me], half)
+    return jnp.transpose(total, (1, 0, 2))
+
+
 def per_device(ring, left_cores, right_cores, sketch):
     sum_local, rows_in, mode_local, rank_width = left_cores.shape
     target = sketch.shape[2]
@@ -125,11 +160,7 @@
     basis = orthonormal(flat_share, gram)
     block = basis.reshape(share.shape)
     rounded = block.astype(jnp.bfloat16)
-    pieces = lax.all_gather(rounded, "sum", axis=0, tiled=True)
-    partial_carry = lax.dot_general(
-        pieces, left_cores, (((0, 1), (1, 2)), ((), ())), preferred_element_type=jnp.float32
-    )
-    partial_carry = jnp.transpose(partial_carry, (1, 0, 2))
+    partial_carry = ring_gather_carries(rounded, left_cores, ring)
     carries = lax.psum(partial_carry, "mode")
     return (block * factor, carries)
 

time: 702 us -> 650 us (0.926)
  waiting for transfers between devices: 428 us -> 350 us
  starting transfers between devices: 16.5 us -> 30 us
  between operations: 24.7 us -> 34.9 us
  local copies, waits for them, and re-layouts: 12.5 us -> 19.6 us
    all_gather x1 -> x0, waiting for transfers between devices: 124 us -> none  [per_device(): pieces = lax.all_gather(rounded, 'sum', axis=0, tiled=True)]
    ppermute x0 -> x14, waiting for transfers between devices: none -> 59.4 us  [the longest x7 59.3 us: ring_gather_carries(): hold_b = lax.ppermute(hold_b, 'sum', bwd)]
    ppermute x7, waiting for transfers between devices: 132 us -> 83.4 us  [ring_reduce_scatter(): acc_f = lax.ppermute(acc_f, 'sum', fwd) + piece(fwd_blocks[t, me], 0, half)]
    ppermute x7, waiting for transfers between devices: 24.9 us -> 73.3 us  [ring_reduce_scatter(): lax.ppermute(acc_b, 'sum', bwd)]
    psum x2, waiting for transfers between devices: 115 us -> 100 us  [per_device(): gram = lax.psum(lax.psum(gram_part, 'mode'), 'sum')]
    ppermute x0 -> x14, starting transfers between devices: none -> 14.6 us  [the longest x7 13 us: ring_gather_carries(): hold_f = lax.ppermute(hold_f, 'sum', fwd)]
    dot_general x1 -> x16, matrix products: 18.2 us -> 13.6 us  [term(): lax.dot_general(piece, lhs, (((0, 1), (1, 2)), ((), ())), preferred_eleme...]
  transfers between devices with their start and end apart: 18 -> 31, of which waited for: 18 -> 24; matrix products, arithmetic and copies ran while one was open for 1% -> 3% of each run, Pallas kernels for 0% -> 0%
where the time goes in v4:
time: 650 us; the launch traced here: 640 us
  waiting for transfers between devices  350 us (54%)
  other arithmetic  114 us (18%)
  matrix products  64.9 us (10%)
  between operations  34.9 us (5%)
  starting transfers between devices  30 us (5%)
  blocking collectives  28 us (4%)
  local copies, waits for them, and re-layouts  19.6 us (3%)
    psum x2, waiting for transfers between devices, per_device(): gram = lax.psum(lax.psum(gram_part, 'mode'), 'sum')  100 us
    ppermute x7, waiting for transfers between devices, ring_reduce_scatter(): acc_f = lax.ppermute(acc_f, 'sum', fwd) + piece(fwd_blocks[t, me], 0, half)  83.4 us
    ppermute x7, waiting for transfers between devices, ring_reduce_scatter(): lax.ppermute(acc_b, 'sum', bwd)  73.3 us
    ppermute x7, waiting for transfers between devices, ring_gather_carries(): hold_b = lax.ppermute(hold_b, 'sum', bwd)  59.3 us
    another operation x12, other arithmetic, orthonormal(): lkk = jnp.linalg.cholesky(diag)  49.7 us
    another operation x8, other arithmetic, orthonormal(): ikk = lax.linalg.triangular_solve(lkk, eye, left_side=True, lower=True)  41.9 us
    psum x1, waiting for transfers between devices, per_device(): carries = lax.psum(partial_carry, 'mode')  33.5 us
    psum x1, blocking collectives, per_device(): mapped = lax.psum(partial_map, 'mode').astype(jnp.bfloat16)  28 us
  transfers between devices with their start and end apart: 31, of which 24 were waited for; matrix products, arithmetic and copies ran while one was open for 3% of the time, Pallas kernels for 0%

profile of v4, /device:TPU:0, one launch (start us, length us, event | category | flops | bytes accessed | tf_op | source)
XLA Modules:
  0.0 640.5 jit_solution(14722976330813283843)
XLA Ops:
  9.5 17.1 %fusion.9 = f32[1,512,512]{2,1,0:T(8,128)S(1)} fusion(bf16[16,512,512]{2,1,0:T(8,128)(2,1)} %param.12, bf16[512,16,512]{2,1,0:T(8,128)(2,1)} %bitcast.257), kind=kOutput, calls=%fused_computation.29 | convolution fusion | flops 4294967296 | bytes 17825792 | tf_op jit(solution)/shard_map/dot_general | solution.py:147
  26.6 28.0 %all-reduce.10 = bf16[1,512,512]{2,1,0:T(8,128)(2,1)S(1)} all-reduce(f32[1,512,512]{2,1,0:T(8,128)S(1)} %fusion.9), channel_id=1, replica_groups=mesh['sum'=8,'mode'=4] {'mode'}, use_global_device_ids=true, to_apply=%region_0.0 | all-reduce | flops 262144 | bytes 1572864 | tf_op jit(solution)/shard_map/psum | solution.py:150
  54.6 11.7 %convolution_bitcast_fusion = f32[512,16,512]{2,1,0:T(8,128)} fusion(bf16[1,512,16,512]{3,2,1,0:T(8,128)(2,1)} %param.10, bf16[1,512,512]{2,1,0:T(8,128)(2,1)S(1)} %all-reduce.10), kind=kOutput, calls=%fused_computation | convolution fusion | flops 4294967296 | bytes 25690112 | tf_op jit(solution)/shard_map/dot_general | solution.py:151
  70.4 22.7 %collective-permute-done = f32[32,16,512]{2,1,0:T(8,128)S(1)} collective-permute-done((f32[32,16,512]{2,1,0:T(8,128)S(1)}, f32[32,16,512]{2,1,0:T(8,128)S(1)}, u32[]{:S(2)}, u32[]{:S(2)}) %collective-permute-start) | collective-permute-done | bytes 1048608 | tf_op jit(solution)/shard_map/ppermute | solution.py:104
  98.2 21.4 %collective-permute-done.1 = f32[32,16,512]{2,1,0:T(8,128)S(1)} collective-permute-done((f32[32,16,512]{2,1,0:T(8,128)S(1)}, f32[32,16,512]{2,1,0:T(8,128)S(1)}, u32[]{:S(2)}, u32[]{:S(2)}) %collective-permute-start.1) | collective-permute-done | bytes 1048608 | tf_op jit(solution)/shard_map/ppermute | solution.py:104
  126.6 20.1 %collective-permute-done.2 = f32[32,16,512]{2,1,0:T(8,128)S(1)} collective-permute-done((f32[32,16,512]{2,1,0:T(8,128)S(1)}, f32[32,16,512]{2,1,0:T(8,128)S(1)}, u32[]{:S(2)}, u32[]{:S(2)}) %collective-permute-start.2) | collective-permute-done | bytes 1048608 | tf_op jit(solution)/shard_map/ppermute | solution.py:104
  153.8 18.8 %collective-permute-done.3 = f32[32,16,512]{2,1,0:T(8,128)S(1)} collective-permute-done((f32[32,16,512]{2,1,0:T(8,128)S(1)}, f32[32,16,512]{2,1,0:T(8,128)S(1)}, u32[]{:S(2)}, u32[]{:S(2)}) %collective-permute-start.3) | collective-permute-done | bytes 1048608 | tf_op jit(solution)/shard_map/ppermute | solution.py:104
  180.1 17.6 %collective-permute-done.10 = f32[32,16,512]{2,1,0:T(8,128)S(1)} collective-permute-done((f32[32,16,512]{2,1,0:T(8,128)S(1)}, f32[32,16,512]{2,1,0:T(8,128)S(1)}, u32[]{:S(2)}, u32[]{:S(2)}) %collective-permute-start.10) | collective-permute-done | bytes 1048608 | tf_op jit(solution)/shard_map/ppermute | solution.py:105
  203.6 16.7 %collective-permute-done.11 = f32[32,16,512]{2,1,0:T(8,128)S(1)} collective-permute-done((f32[32,16,512]{2,1,0:T(8,128)S(1)}, f32[32,16,512]{2,1,0:T(8,128)S(1)}, u32[]{:S(2)}, u32[]{:S(2)}) %collective-permute-start.11) | collective-permute-done | bytes 1048608 | tf_op jit(solution)/shard_map/ppermute | solution.py:105
  227.0 17.6 %collective-permute-done.12 = f32[32,16,512]{2,1,0:T(8,128)S(1)} collective-permute-done((f32[32,16,512]{2,1,0:T(8,128)}, f32[32,16,512]{2,1,0:T(8,128)S(1)}, u32[]{:S(2)}, u32[]{:S(2)}) %collective-permute-start.12) | collective-permute-done | bytes 1048608 | tf_op jit(solution)/shard_map/ppermute | solution.py:105
  248.4 17.0 %collective-permute-done.13 = f32[32,16,512]{2,1,0:T(8,128)S(1)} collective-permute-done((f32[32,16,512]{2,1,0:T(8,128)S(1)}, f32[32,16,512]{2,1,0:T(8,128)S(1)}, u32[]{:S(2)}, u32[]{:S(2)}) %collective-permute-start.13) | collective-permute-done | bytes 1048608 | tf_op jit(solution)/shard_map/ppermute | solution.py:105
  266.9 4.5 convolution_bitcast_fusion.17
  271.5 35.4 %all-reduce.5.cloned.1.call-done = f32[512,512]{0,1:T(8,128)} async-done(((f32[512,512]{0,1:T(8,128)}), f32[512,512]{0,1:T(8,128)}) %all-reduce.5.cloned.1.call-update) | async-done | bytes 1048592 | tf_op jit(solution)/shard_map/psum | solution.py:159
  318.1 6.2 constant_dynamic-slice_fusion.1
  324.7 64.6 %all-reduce.7.cloned.1.call-done = f32[512,512]{0,1:T(8,128)} async-done(((f32[512,512]{0,1:T(8,128)}), f32[512,512]{0,1:T(8,128)}) %all-reduce.7.cloned.1.call-update) | async-done | bytes 1048592 | tf_op jit(solution)/shard_map/psum | solution.py:159
  391.0 11.7 %cholesky.74 = f32[128,128]{1,0:T(8,128)S(1)} custom-call(f32[128,128]{1,0:T(8,128)S(1)} %fusion.108), custom_call_target="Cholesky" | custom-call | tf_op jit(solution)/shard_map/jit(cholesky)/cholesky | solution.py:31
  404.1 9.8 %custom-call.8 = f32[1,128,128]{1,2,0:T(8,128)S(1)} custom-call(f32[1,128,128]{2,1,0:T(8,128)S(1)} %fusion.93), custom_call_target="InvertDiagBlocksLowerTriangular" | custom-call | tf_op jit(solution)/shard_map/triangular_solve/custom-call.0 | solution.py:32
  419.6 11.9 %cholesky.85 = f32[128,128]{1,0:T(8,128)S(1)} custom-call(f32[128,128]{1,0:T(8,128)S(1)} %fusion.106), custom_call_target="Cholesky" | custom-call | tf_op jit(solution)/shard_map/jit(cholesky)/cholesky | solution.py:31
  432.9 9.8 %custom-call.9 = f32[1,128,128]{1,2,0:T(8,128)S(1)} custom-call(f32[1,128,128]{2,1,0:T(8,128)S(1)} %fusion.94), custom_call_target="InvertDiagBlocksLowerTriangular" | custom-call | tf_op jit(solution)/shard_map/triangular_solve/custom-call.0 | solution.py:32
  448.6 11.7 %cholesky.96 = f32[128,128]{1,0:T(8,128)S(1)} custom-call(f32[128,128]{1,0:T(8,128)S(1)} %fusion.104), custom_call_target="Cholesky" | custom-call | tf_op jit(solution)/shard_map/jit(cholesky)/cholesky | solution.py:31
  461.6 9.8 %custom-call.10 = f32[1,128,128]{1,2,0:T(8,128)S(1)} custom-call(f32[1,128,128]{2,1,0:T(8,128)S(1)} %fusion.95), custom_call_target="InvertDiagBlocksLowerTriangular" | custom-call | tf_op jit(solution)/shard_map/triangular_solve/custom-call.0 | solution.py:32
  476.7 11.7 %cholesky.107 = f32[128,128]{1,0:T(8,128)S(1)} custom-call(f32[128,128]{1,0:T(8,128)S(1)} %fusion.102), custom_call_target="Cholesky" | custom-call | tf_op jit(solution)/shard_map/jit(cholesky)/cholesky | solution.py:31
  489.7 9.8 %custom-call.11 = f32[1,128,128]{1,2,0:T(8,128)S(1)} custom-call(f32[1,128,128]{2,1,0:T(8,128)S(1)} %fusion.96), custom_call_target="InvertDiagBlocksLowerTriangular" | custom-call | tf_op jit(solution)/shard_map/triangular_solve/custom-call.0 | solution.py:32
  499.8 3.7 fusion.3
  512.8 8.8 %collective-permute-done.15 = bf16[32,16,512]{2,0,1:T(8,128)(2,1)S(1)} collective-permute-done((bf16[32,16,512]{2,0,1:T(8,128)(2,1)S(1)}, bf16[32,16,512]{2,0,1:T(8,128)(2,1)S(1)}, u32[]{:S(2)}, u32[]{:S(2)}) %collective-permute-start.15) | collective-permute-done | bytes 524320 | tf_op jit(solution)/shard_map/ppermute | solution.py:138
  524.8 9.0 %collective-permute-done.17 = bf16[32,16,512]{2,0,1:T(8,128)(2,1)S(1)} collective-permute-done((bf16[32,16,512]{2,0,1:T(8,128)(2,1)S(1)}, bf16[32,16,512]{2,0,1:T(8,128)(2,1)S(1)}, u32[]{:S(2)}, u32[]{:S(2)}) %collective-permute-start.17) | collective-permute-done | bytes 524320 | tf_op jit(solution)/shard_map/ppermute | solution.py:138
  537.1 8.8 %collective-permute-done.19 = bf16[32,16,512]{2,0,1:T(8,128)(2,1)S(1)} collective-permute-done((bf16[32,16,512]{2,0,1:T(8,128)(2,1)S(1)}, bf16[32,16,512]{2,0,1:T(8,128)(2,1)S(1)}, u32[]{:S(2)}, u32[]{:S(2)}) %collective-permute-start.19) | collective-permute-done | bytes 524320 | tf_op jit(solution)/shard_map/ppermute | solution.py:138
  549.2 8.8 %collective-permute-done.21 = bf16[32,16,512]{2,0,1:T(8,128)(2,1)S(1)} collective-permute-done((bf16[32,16,512]{2,0,1:T(8,128)(2,1)S(1)}, bf16[32,16,512]{2,0,1:T(8,128)(2,1)S(1)}, u32[]{:S(2)}, u32[]{:S(2)}) %collective-permute-start.21) | collective-permute-done | bytes 524320 | tf_op jit(solution)/shard_map/ppermute | solution.py:138
  561.2 8.8 %collective-permute-done.23 = bf16[32,16,512]{2,0,1:T(8,128)(2,1)S(1)} collective-permute-done((bf16[32,16,512]{2,0,1:T(8,128)(2,1)S(1)}, bf16[32,16,512]{2,0,1:T(8,128)(2,1)S(1)}, u32[]{:S(2)}, u32[]{:S(2)}) %collective-permute-start.23) | collective-permute-done | bytes 524320 | tf_op jit(solution)/shard_map/ppermute | solution.py:138
  573.3 9.3 %collective-permute-done.25 = bf16[32,16,512]{2,0,1:T(8,128)(2,1)S(1)} collective-permute-done((bf16[32,16,512]{2,0,1:T(8,128)(2,1)S(1)}, bf16[32,16,512]{2,0,1:T(8,128)(2,1)S(1)}, u32[]{:S(2)}, u32[]{:S(2)}) %collective-permute-start.25) | collective-permute-done | bytes 524320 | tf_op jit(solution)/shard_map/ppermute | solution.py:138
  585.9 5.9 collective-permute-done.27
  597.7 33.5 %all-reduce.9.cloned.1.call-done = f32[1,512,512]{2,1,0:T(8,128)} async-done(((f32[1,512,512]{2,1,0:T(8,128)}), f32[1,512,512]{2,1,0:T(8,128)}) %all-reduce.9.cloned.1.call-update) | async-done | bytes 1048592 | tf_op jit(solution)/shard_map/psum | solution.py:164
  (167 shorter events, 103.5 us)
Async XLA Ops:
  7.2 299.8 %all-reduce.5.cloned.1.call-start = ((), (), s32[]{:S(2)}) async-start(), calls=%async_computation | async-start | bytes 2097152 | tf_op jit(solution)/shard_map/psum | solution.py:159
  67.6 25.5 %collective-permute-start = (f32[32,16,512]{2,1,0:T(8,128)S(1)}, f32[32,16,512]{2,1,0:T(8,128)S(1)}, u32[]{:S(2)}, u32[]{:S(2)}) collective-permute-start(f32[32,16,512]{2,1,0:T(8,128)S(1)} %constant_dynamic-slice_fusion.18), channel_id=1, source_target_pairs={{0,4},{4,12},{12,20},{20,28},{28,24},{24,16},{16,8},{8,0},{1,5},{5... | collective-permute-start | bytes 3145736 | tf_op jit(solution)/shard_map/ppermute | solution.py:104
  95.0 24.7 %collective-permute-start.1 = (f32[32,16,512]{2,1,0:T(8,128)S(1)}, f32[32,16,512]{2,1,0:T(8,128)S(1)}, u32[]{:S(2)}, u32[]{:S(2)}) collective-permute-start(f32[32,16,512]{2,1,0:T(8,128)S(1)} %get-tuple-element.18), channel_id=1, source_target_pairs={{0,4},{4,12},{12,20},{20,28},{28,24},{24,16},{16,8},{8,0},{1,5},{5... | collective-permute-start | bytes 3145736 | tf_op jit(solution)/shard_map/ppermute | solution.py:104
  96.5 24.4 %collective-permute-start.7 = (f32[32,16,512]{2,1,0:T(8,128)S(1)}, f32[32,16,512]{2,1,0:T(8,128)}, u32[]{:S(2)}, u32[]{:S(2)}) collective-permute-start(f32[32,16,512]{2,1,0:T(8,128)S(1)} %get-tuple-element.19), channel_id=1, source_target_pairs={{0,8},{4,0},{12,4},{20,12},{28,20},{24,28},{16,24},{8,16},{1,9},{5... | collective-permute-start | bytes 3145736 | tf_op jit(solution)/shard_map/ppermute | solution.py:105
  123.2 23.5 %collective-permute-start.2 = (f32[32,16,512]{2,1,0:T(8,128)S(1)}, f32[32,16,512]{2,1,0:T(8,128)S(1)}, u32[]{:S(2)}, u32[]{:S(2)}) collective-permute-start(f32[32,16,512]{2,1,0:T(8,128)S(1)} %get-tuple-element.16), channel_id=1, source_target_pairs={{0,4},{4,12},{12,20},{20,28},{28,24},{24,16},{16,8},{8,0},{1,5},{5... | collective-permute-start | bytes 3145736 | tf_op jit(solution)/shard_map/ppermute | solution.py:104
  124.8 23.2 %collective-permute-start.8 = (f32[32,16,512]{2,1,0:T(8,128)S(1)}, f32[32,16,512]{2,1,0:T(8,128)}, u32[]{:S(2)}, u32[]{:S(2)}) collective-permute-start(f32[32,16,512]{2,1,0:T(8,128)S(1)} %get-tuple-element.17), channel_id=1, source_target_pairs={{0,8},{4,0},{12,4},{20,12},{28,20},{24,28},{16,24},{8,16},{1,9},{5... | collective-permute-start | bytes 3145736 | tf_op jit(solution)/shard_map/ppermute | solution.py:105
  150.4 22.3 %collective-permute-start.3 = (f32[32,16,512]{2,1,0:T(8,128)S(1)}, f32[32,16,512]{2,1,0:T(8,128)S(1)}, u32[]{:S(2)}, u32[]{:S(2)}) collective-permute-start(f32[32,16,512]{2,1,0:T(8,128)S(1)} %get-tuple-element.14), channel_id=1, source_target_pairs={{0,4},{4,12},{12,20},{20,28},{28,24},{24,16},{16,8},{8,0},{1,5},{5... | collective-permute-start | bytes 3145736 | tf_op jit(solution)/shard_map/ppermute | solution.py:104
  152.1 22.2 %collective-permute-start.9 = (f32[32,16,512]{2,1,0:T(8,128)S(1)}, f32[32,16,512]{2,1,0:T(8,128)}, u32[]{:S(2)}, u32[]{:S(2)}) collective-permute-start(f32[32,16,512]{2,1,0:T(8,128)S(1)} %get-tuple-element.15), channel_id=1, source_target_pairs={{0,8},{4,0},{12,4},{20,12},{28,20},{24,28},{16,24},{8,16},{1,9},{5... | collective-permute-start | bytes 3145736 | tf_op jit(solution)/shard_map/ppermute | solution.py:105
  176.7 21.1 %collective-permute-start.10 = (f32[32,16,512]{2,1,0:T(8,128)S(1)}, f32[32,16,512]{2,1,0:T(8,128)S(1)}, u32[]{:S(2)}, u32[]{:S(2)}) collective-permute-start(f32[32,16,512]{2,1,0:T(8,128)S(1)} %get-tuple-element.13), channel_id=1, source_target_pairs={{0,8},{4,0},{12,4},{20,12},{28,20},{24,28},{16,24},{8,16},{1,9},{5... | collective-permute-start | bytes 3145736 | tf_op jit(solution)/shard_map/ppermute | solution.py:105
  177.1 20.8 %collective-permute-start.4 = (f32[32,16,512]{2,1,0:T(8,128)S(1)}, f32[32,16,512]{2,1,0:T(8,128)}, u32[]{:S(2)}, u32[]{:S(2)}) collective-permute-start(f32[32,16,512]{2,1,0:T(8,128)S(1)} %get-tuple-element.12), channel_id=1, source_target_pairs={{0,4},{4,12},{12,20},{20,28},{28,24},{24,16},{16,8},{8,0},{1,5},{5... | collective-permute-start | bytes 3145736 | tf_op jit(solution)/shard_map/ppermute | solution.py:104
  200.2 20.0 %collective-permute-start.11 = (f32[32,16,512]{2,1,0:T(8,128)S(1)}, f32[32,16,512]{2,1,0:T(8,128)S(1)}, u32[]{:S(2)}, u32[]{:S(2)}) collective-permute-start(f32[32,16,512]{2,1,0:T(8,128)S(1)} %get-tuple-element.11), channel_id=1, source_target_pairs={{0,8},{4,0},{12,4},{20,12},{28,20},{24,28},{16,24},{8,16},{1,9},{5... | collective-permute-start | bytes 3145736 | tf_op jit(solution)/shard_map/ppermute | solution.py:105
  200.8 19.7 %collective-permute-start.5 = (f32[32,16,512]{2,1,0:T(8,128)S(1)}, f32[32,16,512]{2,1,0:T(8,128)}, u32[]{:S(2)}, u32[]{:S(2)}) collective-permute-start(f32[32,16,512]{2,1,0:T(8,128)S(1)} %get-tuple-element.10), channel_id=1, source_target_pairs={{0,4},{4,12},{12,20},{20,28},{28,24},{24,16},{16,8},{8,0},{1,5},{5... | collective-permute-start | bytes 3145736 | tf_op jit(solution)/shard_map/ppermute | solution.py:104
  223.8 20.8 %collective-permute-start.12 = (f32[32,16,512]{2,1,0:T(8,128)}, f32[32,16,512]{2,1,0:T(8,128)S(1)}, u32[]{:S(2)}, u32[]{:S(2)}) collective-permute-start(f32[32,16,512]{2,1,0:T(8,128)} %get-tuple-element.9), channel_id=1, source_target_pairs={{0,8},{4,0},{12,4},{20,12},{28,20},{24,28},{16,24},{8,16},{1,9},{5... | collective-permute-start | bytes 3145736 | tf_op jit(solution)/shard_map/ppermute | solution.py:105
  225.1 19.6 %collective-permute-start.6 = (f32[32,16,512]{2,1,0:T(8,128)S(1)}, f32[32,16,512]{2,1,0:T(8,128)}, u32[]{:S(2)}, u32[]{:S(2)}) collective-permute-start(f32[32,16,512]{2,1,0:T(8,128)S(1)} %get-tuple-element.8), channel_id=1, source_target_pairs={{0,4},{4,12},{12,20},{20,28},{28,24},{24,16},{16,8},{8,0},{1,5},{5... | collective-permute-start | bytes 3145736 | tf_op jit(solution)/shard_map/ppermute | solution.py:104
  247.0 18.5 %collective-permute-start.13 = (f32[32,16,512]{2,1,0:T(8,128)S(1)}, f32[32,16,512]{2,1,0:T(8,128)S(1)}, u32[]{:S(2)}, u32[]{:S(2)}) collective-permute-start(f32[32,16,512]{2,1,0:T(8,128)S(1)} %get-tuple-element.7), channel_id=1, source_target_pairs={{0,8},{4,0},{12,4},{20,12},{28,20},{24,28},{16,24},{8,16},{1,9},{5... | collective-permute-start | bytes 3145736 | tf_op jit(solution)/shard_map/ppermute | solution.py:105
  266.9 40.5 %copy-start.19 = (s32[8,8]{1,0:T(8,128)S(1)}, s32[8,8]{1,0:T(8,128)}, u32[]{:S(2)}) copy-start(s32[8,8]{1,0:T(8,128)} %constant.152.clone) | copy-start | bytes 772
  271.4 117.8 %all-reduce.7.cloned.1.call-start = ((), (), s32[]{:S(2)}) async-start(), calls=%async_computation.1 | async-start | bytes 2097152 | tf_op jit(solution)/shard_map/psum | solution.py:159
  306.9 324.3 %all-reduce.9.cloned.1.call-start = ((), (), s32[]{:S(2)}) async-start(), calls=%async_computation.2 | async-start | bytes 2097152 | tf_op jit(solution)/shard_map/psum | solution.py:164
  508.5 13.0 %collective-permute-start.15 = (bf16[32,16,512]{2,0,1:T(8,128)(2,1)S(1)}, bf16[32,16,512]{2,0,1:T(8,128)(2,1)S(1)}, u32[]{:S(2)}, u32[]{:S(2)}) collective-permute-start(bf16[32,16,512]{2,0,1:T(8,128)(2,1)S(1)} %copy.65), channel_id=1, source_target_pairs={{0,8},{4,0},{12,4},{20,12},{28,20},{24,28},{16,24},{8,16},{1,9},{5... | collective-permute-start | bytes 1572872 | tf_op jit(solution)/shard_map/ppermute | solution.py:138
  509.7 12.9 %collective-permute-start.14 = (bf16[32,16,512]{2,0,1:T(8,128)(2,1)S(1)}, bf16[32,16,512]{2,0,1:T(8,128)(2,1)S(1)}, u32[]{:S(2)}, u32[]{:S(2)}) collective-permute-start(bf16[32,16,512]{2,0,1:T(8,128)(2,1)S(1)} %copy.63), channel_id=1, source_target_pairs={{0,4},{4,12},{12,20},{20,28},{28,24},{24,16},{16,8},{8,0},{1,5},{5... | collective-permute-start | bytes 1572872 | tf_op jit(solution)/shard_map/ppermute | solution.py:137
  521.5 12.2 %collective-permute-start.17 = (bf16[32,16,512]{2,0,1:T(8,128)(2,1)S(1)}, bf16[32,16,512]{2,0,1:T(8,128)(2,1)S(1)}, u32[]{:S(2)}, u32[]{:S(2)}) collective-permute-start(bf16[32,16,512]{2,0,1:T(8,128)(2,1)S(1)} %collective-permute-done.15), channel_id=1, source_target_pairs={{0,8},{4,0},{12,4},{20,12},{28,20},{24,28},{16,24},{8,16},{1,9},{5... | collective-permute-start | bytes 1572872 | tf_op jit(solution)/shard_map/ppermute | solution.py:138
  522.7 11.8 %collective-permute-start.16 = (bf16[32,16,512]{2,0,1:T(8,128)(2,1)S(1)}, bf16[32,16,512]{2,0,1:T(8,128)(2,1)S(1)}, u32[]{:S(2)}, u32[]{:S(2)}) collective-permute-start(bf16[32,16,512]{2,0,1:T(8,128)(2,1)S(1)} %collective-permute-done.14), channel_id=1, source_target_pairs={{0,4},{4,12},{12,20},{20,28},{28,24},{24,16},{16,8},{8,0},{1,5},{5... | collective-permute-start | bytes 1572872 | tf_op jit(solution)/shard_map/ppermute | solution.py:137
  533.8 12.1 %collective-permute-start.19 = (bf16[32,16,512]{2,0,1:T(8,128)(2,1)S(1)}, bf16[32,16,512]{2,0,1:T(8,128)(2,1)S(1)}, u32[]{:S(2)}, u32[]{:S(2)}) collective-permute-start(bf16[32,16,512]{2,0,1:T(8,128)(2,1)S(1)} %collective-permute-done.17), channel_id=1, source_target_pairs={{0,8},{4,0},{12,4},{20,12},{28,20},{24,28},{16,24},{8,16},{1,9},{5... | collective-permute-start | bytes 1572872 | tf_op jit(solution)/shard_map/ppermute | solution.py:138
  534.5 12.0 %collective-permute-start.18 = (bf16[32,16,512]{2,0,1:T(8,128)(2,1)S(1)}, bf16[32,16,512]{2,0,1:T(8,128)(2,1)S(1)}, u32[]{:S(2)}, u32[]{:S(2)}) collective-permute-start(bf16[32,16,512]{2,0,1:T(8,128)(2,1)S(1)} %collective-permute-done.16), channel_id=1, source_target_pairs={{0,4},{4,12},{12,20},{20,28},{28,24},{24,16},{16,8},{8,0},{1,5},{5... | collective-permute-start | bytes 1572872 | tf_op jit(solution)/shard_map/ppermute | solution.py:137
  545.9 12.1 %collective-permute-start.21 = (bf16[32,16,512]{2,0,1:T(8,128)(2,1)S(1)}, bf16[32,16,512]{2,0,1:T(8,128)(2,1)S(1)}, u32[]{:S(2)}, u32[]{:S(2)}) collective-permute-start(bf16[32,16,512]{2,0,1:T(8,128)(2,1)S(1)} %collective-permute-done.19), channel_id=1, source_target_pairs={{0,8},{4,0},{12,4},{20,12},{28,20},{24,28},{16,24},{8,16},{1,9},{5... | collective-permute-start | bytes 1572872 | tf_op jit(solution)/shard_map/ppermute | solution.py:138
  546.5 12.1 %collective-permute-start.20 = (bf16[32,16,512]{2,0,1:T(8,128)(2,1)S(1)}, bf16[32,16,512]{2,0,1:T(8,128)(2,1)S(1)}, u32[]{:S(2)}, u32[]{:S(2)}) collective-permute-start(bf16[32,16,512]{2,0,1:T(8,128)(2,1)S(1)} %collective-permute-done.18), channel_id=1, source_target_pairs={{0,4},{4,12},{12,20},{20,28},{28,24},{24,16},{16,8},{8,0},{1,5},{5... | collective-permute-start | bytes 1572872 | tf_op jit(solution)/shard_map/ppermute | solution.py:137
  558.0 12.1 %collective-permute-start.23 = (bf16[32,16,512]{2,0,1:T(8,128)(2,1)S(1)}, bf16[32,16,512]{2,0,1:T(8,128)(2,1)S(1)}, u32[]{:S(2)}, u32[]{:S(2)}) collective-permute-start(bf16[32,16,512]{2,0,1:T(8,128)(2,1)S(1)} %collective-permute-done.21), channel_id=1, source_target_pairs={{0,8},{4,0},{12,4},{20,12},{28,20},{24,28},{16,24},{8,16},{1,9},{5... | collective-permute-start | bytes 1572872 | tf_op jit(solution)/shard_map/ppermute | solution.py:138
  558.6 12.1 %collective-permute-start.22 = (bf16[32,16,512]{2,0,1:T(8,128)(2,1)S(1)}, bf16[32,16,512]{2,0,1:T(8,128)(2,1)S(1)}, u32[]{:S(2)}, u32[]{:S(2)}) collective-permute-start(bf16[32,16,512]{2,0,1:T(8,128)(2,1)S(1)} %collective-permute-done.20), channel_id=1, source_target_pairs={{0,4},{4,12},{12,20},{20,28},{28,24},{24,16},{16,8},{8,0},{1,5},{5... | collective-permute-start | bytes 1572872 | tf_op jit(solution)/shard_map/ppermute | solution.py:137
  570.0 12.6 %collective-permute-start.25 = (bf16[32,16,512]{2,0,1:T(8,128)(2,1)S(1)}, bf16[32,16,512]{2,0,1:T(8,128)(2,1)S(1)}, u32[]{:S(2)}, u32[]{:S(2)}) collective-permute-start(bf16[32,16,512]{2,0,1:T(8,128)(2,1)S(1)} %collective-permute-done.23), channel_id=1, source_target_pairs={{0,8},{4,0},{12,4},{20,12},{28,20},{24,28},{16,24},{8,16},{1,9},{5... | collective-permute-start | bytes 1572872 | tf_op jit(solution)/shard_map/ppermute | solution.py:138
  570.7 12.6 %collective-permute-start.24 = (bf16[32,16,512]{2,0,1:T(8,128)(2,1)S(1)}, bf16[32,16,512]{2,0,1:T(8,128)(2,1)S(1)}, u32[]{:S(2)}, u32[]{:S(2)}) collective-permute-start(bf16[32,16,512]{2,0,1:T(8,128)(2,1)S(1)} %collective-permute-done.22), channel_id=1, source_target_pairs={{0,4},{4,12},{12,20},{20,28},{28,24},{24,16},{16,8},{8,0},{1,5},{5... | collective-permute-start | bytes 1572872 | tf_op jit(solution)/shard_map/ppermute | solution.py:137
  582.6 9.2 %collective-permute-start.27 = (bf16[32,16,512]{2,0,1:T(8,128)(2,1)S(1)}, bf16[32,16,512]{2,0,1:T(8,128)(2,1)S(1)}, u32[]{:S(2)}, u32[]{:S(2)}) collective-permute-start(bf16[32,16,512]{2,0,1:T(8,128)(2,1)S(1)} %collective-permute-done.25), channel_id=1, source_target_pairs={{0,8},{4,0},{12,4},{20,12},{28,20},{24,28},{16,24},{8,16},{1,9},{5... | collective-permute-start | bytes 1572872 | tf_op jit(solution)/shard_map/ppermute | solution.py:138
  583.2 9.2 %collective-permute-start.26 = (bf16[32,16,512]{2,0,1:T(8,128)(2,1)S(1)}, bf16[32,16,512]{2,0,1:T(8,128)(2,1)S(1)}, u32[]{:S(2)}, u32[]{:S(2)}) collective-permute-start(bf16[32,16,512]{2,0,1:T(8,128)(2,1)S(1)} %collective-permute-done.24), channel_id=1, source_target_pairs={{0,4},{4,12},{12,20},{20,28},{28,24},{24,16},{16,8},{8,0},{1,5},{5... | collective-permute-start | bytes 1572872 | tf_op jit(solution)/shard_map/ppermute | solution.py:137
  (20 other events, 160.6 us)
Sparse Core Ops, SparseCore 0:
  271.6 35.3 all-reduce.4
  310.8 78.3 all-reduce.6
  594.6 36.6 all-reduce.8

commit v5 on v4

--- a/solution.py
+++ b/solution.py
@@ -141,6 +141,36 @@
     return jnp.transpose(total, (1, 0, 2))
 
 
+def ring_all_gather(own, ring):
+    n = len(ring)
+    rows = own.shape[0]
+    half = rows // 2
+    pos = [0] * n
+    for p, i in enumerate(ring):
+        pos[i] = p
+    me = lax.axis_index("sum")
+    fwd = [(ring[p], ring[(p + 1) % n]) for p in range(n)]
+    bwd = [(ring[p], ring[(p - 1) % n]) for p in range(n)]
+    fwd_blocks = jnp.asarray(
+        [[ring[(pos[i] - t) % n] for i in range(n)] for t in range(n)], dtype=jnp.int32
+    )
+    bwd_blocks = jnp.asarray(
+        [[ring[(pos[i] + t) % n] for i in range(n)] for t in range(n)], dtype=jnp.int32
+    )
+    out = jnp.zeros((n * rows,) + own.shape[1:], own.dtype)
+    hold_f = own[:half]
+    hold_b = own[half:]
+    for t in range(n):
+        if t:
+            hold_f = lax.ppermute(hold_f, "sum", fwd)
+            hold_b = lax.ppermute(hold_b, "sum", bwd)
+        out = lax.dynamic_update_slice_in_dim(out, hold_f, fwd_blocks[t, me] * rows, axis=0)
+        out = lax.dynamic_update_slice_in_dim(
+            out, hold_b, bwd_blocks[t, me] * rows + half, axis=0
+        )
+    return out
+
+
 def per_device(ring, left_cores, right_cores, sketch):
     sum_local, rows_in, mode_local, rank_width = left_cores.shape
     target = sketch.shape[2]
@@ -156,7 +186,8 @@
     share = ring_reduce_scatter(local_sum, ring)
     flat_share = share.reshape(-1, target)
     gram_part = jnp.dot(flat_share.T, flat_share, precision=HI)
-    gram = lax.psum(lax.psum(gram_part, "mode"), "sum")
+    gram_mode = lax.psum(gram_part, "mode")
+    gram = ring_all_gather(ring_reduce_scatter(gram_mode, ring), ring)
     basis = orthonormal(flat_share, gram)
     block = basis.reshape(share.shape)
     rounded = block.astype(jnp.bfloat16)

time: 650 us -> 724 us (1.11)
  local copies, waits for them, and re-layouts: 19.6 us -> 58.6 us
  starting transfers between devices: 30 us -> 59.3 us
    psum x2 -> x1, waiting for transfers between devices: 100 us -> 35.1 us  [per_device(): gram_mode = lax.psum(gram_part, 'mode')]
    dynamic_update_slice x0 -> x16, local copies, waits for them, and re-layouts: none -> 39.7 us  [the longest x8 21 us: ring_all_gather(): lax.dynamic_update_slice_in_dim(out, hold_b, bwd_blocks[t, me] * rows + h...]
    ppermute x7 -> x14, waiting for transfers between devices: 83.4 us -> 123 us  [ring_reduce_scatter(): acc_f = lax.ppermute(acc_f, 'sum', fwd) + piece(fwd_blocks[t, me], 0, half)]
    ppermute x0 -> x14, waiting for transfers between devices: none -> 23.9 us  [the longest x7 23.7 us: ring_all_gather(): hold_f = lax.ppermute(hold_f, 'sum', fwd)]
    ppermute x0 -> x14, starting transfers between devices: none -> 14.7 us  [the longest x7 11.3 us: ring_all_gather(): hold_b = lax.ppermute(hold_b, 'sum', bwd)]
    ppermute x7, starting transfers between devices: 13 us -> 2.31 us  [ring_gather_carries(): hold_f = lax.ppermute(hold_f, 'sum', fwd)]
    ppermute x7, starting transfers between devices: 1.59 us -> 12 us  [ring_gather_carries(): hold_b = lax.ppermute(hold_b, 'sum', bwd)]
    ppermute x7 -> x14, starting transfers between devices: 10.3 us -> 18.3 us  [ring_reduce_scatter(): acc_f = lax.ppermute(acc_f, 'sum', fwd) + piece(fwd_blocks[t, me], 0, half)]
  transfers between devices with their start and end apart: 31 -> 58, of which waited for: 24 -> 48; matrix products, arithmetic and copies ran while one was open for 3% -> 8% of each run, Pallas kernels for 0% -> 0%
where the time goes in v5:
time: 724 us; the launch traced here: 714 us
  waiting for transfers between devices  348 us (48%)
  other arithmetic  121 us (17%)
  matrix products  63.7 us (9%)
  starting transfers between devices  59.3 us (8%)
  local copies, waits for them, and re-layouts  58.6 us (8%)
  between operations  35.6 us (5%)
  blocking collectives  27.9 us (4%)
    ppermute x14, waiting for transfers between devices, ring_reduce_scatter(): acc_f = lax.ppermute(acc_f, 'sum', fwd) + piece(fwd_blocks[t, me], 0, half)  123 us
    ppermute x14, waiting for transfers between devices, ring_reduce_scatter(): lax.ppermute(acc_b, 'sum', bwd)  78.6 us
    ppermute x7, waiting for transfers between devices, ring_gather_carries(): hold_b = lax.ppermute(hold_b, 'sum', bwd)  51.7 us
    another operation x12, other arithmetic, orthonormal(): lkk = jnp.linalg.cholesky(diag)  49.6 us
    another operation x8, other arithmetic, orthonormal(): ikk = lax.linalg.triangular_solve(lkk, eye, left_side=True, lower=True)  42 us
    psum x1, waiting for transfers between devices, per_device(): gram_mode = lax.psum(gram_part, 'mode')  35.1 us
    psum x1, waiting for transfers between devices, per_device(): carries = lax.psum(partial_carry, 'mode')  31.3 us
    psum x1, blocking collectives, per_device(): mapped = lax.psum(partial_map, 'mode').astype(jnp.bfloat16)  27.9 us
  transfers between devices with their start and end apart: 58, of which 48 were waited for; matrix products, arithmetic and copies ran while one was open for 8% of the time, Pallas kernels for 0%

profile of v5, /device:TPU:0, one launch (start us, length us, event | category | flops | bytes accessed | tf_op | source)
XLA Modules:
  0.0 713.8 jit_solution(4655082007455247105)
XLA Ops:
  9.6 17.1 %fusion.9 = f32[1,512,512]{2,1,0:T(8,128)S(1)} fusion(bf16[16,512,512]{2,1,0:T(8,128)(2,1)} %param.16, bf16[512,16,512]{2,1,0:T(8,128)(2,1)} %bitcast.257), kind=kOutput, calls=%fused_computation.29 | convolution fusion | flops 4294967296 | bytes 17825792 | tf_op jit(solution)/shard_map/dot_general | solution.py:177
  26.7 27.9 %all-reduce.7 = bf16[1,512,512]{2,1,0:T(8,128)(2,1)S(1)} all-reduce(f32[1,512,512]{2,1,0:T(8,128)S(1)} %fusion.9), channel_id=1, replica_groups=mesh['sum'=8,'mode'=4] {'mode'}, use_global_device_ids=true, to_apply=%region_0.0 | all-reduce | flops 262144 | bytes 1572864 | tf_op jit(solution)/shard_map/psum | solution.py:180
  54.6 11.6 %convolution_bitcast_fusion = f32[512,16,512]{2,1,0:T(8,128)} fusion(bf16[1,512,16,512]{3,2,1,0:T(8,128)(2,1)} %param.14, bf16[1,512,512]{2,1,0:T(8,128)(2,1)S(1)} %all-reduce.7), kind=kOutput, calls=%fused_computation | convolution fusion | flops 4294967296 | bytes 25690112 | tf_op jit(solution)/shard_map/dot_general | solution.py:181
  70.4 22.5 %collective-permute-done = f32[32,16,512]{2,1,0:T(8,128)S(1)} collective-permute-done((f32[32,16,512]{2,1,0:T(8,128)S(1)}, f32[32,16,512]{2,1,0:T(8,128)S(1)}, u32[]{:S(2)}, u32[]{:S(2)}) %collective-permute-start) | collective-permute-done | bytes 1048608 | tf_op jit(solution)/shard_map/ppermute | solution.py:104
  99.0 21.7 %collective-permute-done.1 = f32[32,16,512]{2,1,0:T(8,128)S(1)} collective-permute-done((f32[32,16,512]{2,1,0:T(8,128)}, f32[32,16,512]{2,1,0:T(8,128)S(1)}, u32[]{:S(2)}, u32[]{:S(2)}) %collective-permute-start.1) | collective-permute-done | bytes 1048608 | tf_op jit(solution)/shard_map/ppermute | solution.py:104
  128.0 20.3 %collective-permute-done.2 = f32[32,16,512]{2,1,0:T(8,128)S(1)} collective-permute-done((f32[32,16,512]{2,1,0:T(8,128)}, f32[32,16,512]{2,1,0:T(8,128)S(1)}, u32[]{:S(2)}, u32[]{:S(2)}) %collective-permute-start.2) | collective-permute-done | bytes 1048608 | tf_op jit(solution)/shard_map/ppermute | solution.py:104
  155.9 19.0 %collective-permute-done.3 = f32[32,16,512]{2,1,0:T(8,128)S(1)} collective-permute-done((f32[32,16,512]{2,1,0:T(8,128)}, f32[32,16,512]{2,1,0:T(8,128)S(1)}, u32[]{:S(2)}, u32[]{:S(2)}) %collective-permute-start.3) | collective-permute-done | bytes 1048608 | tf_op jit(solution)/shard_map/ppermute | solution.py:104
  182.3 17.9 %collective-permute-done.10 = f32[32,16,512]{2,1,0:T(8,128)S(1)} collective-permute-done((f32[32,16,512]{2,1,0:T(8,128)}, f32[32,16,512]{2,1,0:T(8,128)S(1)}, u32[]{:S(2)}, u32[]{:S(2)}) %collective-permute-start.10) | collective-permute-done | bytes 1048608 | tf_op jit(solution)/shard_map/ppermute | solution.py:105
  206.5 17.0 %collective-permute-done.11 = f32[32,16,512]{2,1,0:T(8,128)S(1)} collective-permute-done((f32[32,16,512]{2,1,0:T(8,128)}, f32[32,16,512]{2,1,0:T(8,128)S(1)}, u32[]{:S(2)}, u32[]{:S(2)}) %collective-permute-start.11) | collective-permute-done | bytes 1048608 | tf_op jit(solution)/shard_map/ppermute | solution.py:105
  230.9 16.2 %collective-permute-done.12 = f32[32,16,512]{2,1,0:T(8,128)S(1)} collective-permute-done((f32[32,16,512]{2,1,0:T(8,128)}, f32[32,16,512]{2,1,0:T(8,128)S(1)}, u32[]{:S(2)}, u32[]{:S(2)}) %collective-permute-start.12) | collective-permute-done | bytes 1048608 | tf_op jit(solution)/shard_map/ppermute | solution.py:105
  253.0 16.5 %collective-permute-done.13 = f32[32,16,512]{2,1,0:T(8,128)S(1)} collective-permute-done((f32[32,16,512]{2,1,0:T(8,128)}, f32[32,16,512]{2,1,0:T(8,128)S(1)}, u32[]{:S(2)}, u32[]{:S(2)}) %collective-permute-start.13) | collective-permute-done | bytes 1048608 | tf_op jit(solution)/shard_map/ppermute | solution.py:105
  275.6 35.1 %all-reduce.4.cloned.1.call-done = f32[512,512]{0,1:T(8,128)} async-done(((f32[512,512]{0,1:T(8,128)}), f32[512,512]{0,1:T(8,128)}) %all-reduce.4.cloned.1.call-update) | async-done | bytes 1048592 | tf_op jit(solution)/shard_map/psum | solution.py:189
  314.1 5.8 collective-permute-done.14
  340.9 6.2 collective-permute-done.17
  352.1 6.3 collective-permute-done.18
  376.5 6.8 collective-permute-done.28
  385.6 6.4 collective-permute-done.30
  420.6 6.1 constant_dynamic-slice_fusion.15
  471.6 11.7 %cholesky.74 = f32[128,128]{1,0:T(8,128)S(1)} custom-call(f32[128,128]{1,0:T(8,128)S(1)} %fusion.108), custom_call_target="Cholesky" | custom-call | tf_op jit(solution)/shard_map/jit(cholesky)/cholesky | solution.py:31
  484.7 9.8 %custom-call.8 = f32[1,128,128]{1,2,0:T(8,128)S(1)} custom-call(f32[1,128,128]{2,1,0:T(8,128)S(1)} %fusion.93), custom_call_target="InvertDiagBlocksLowerTriangular" | custom-call | tf_op jit(solution)/shard_map/triangular_solve/custom-call.0 | solution.py:32
  497.6 11.7 %cholesky.85 = f32[128,128]{1,0:T(8,128)S(1)} custom-call(f32[128,128]{1,0:T(8,128)S(1)} %fusion.106), custom_call_target="Cholesky" | custom-call | tf_op jit(solution)/shard_map/jit(cholesky)/cholesky | solution.py:31
  510.7 9.9 %custom-call.9 = f32[1,128,128]{1,2,0:T(8,128)S(1)} custom-call(f32[1,128,128]{2,1,0:T(8,128)S(1)} %fusion.94), custom_call_target="InvertDiagBlocksLowerTriangular" | custom-call | tf_op jit(solution)/shard_map/triangular_solve/custom-call.0 | solution.py:32
  527.3 11.7 %cholesky.96 = f32[128,128]{1,0:T(8,128)S(1)} custom-call(f32[128,128]{1,0:T(8,128)S(1)} %fusion.104), custom_call_target="Cholesky" | custom-call | tf_op jit(solution)/shard_map/jit(cholesky)/cholesky | solution.py:31
  540.4 9.8 %custom-call.10 = f32[1,128,128]{1,2,0:T(8,128)S(1)} custom-call(f32[1,128,128]{2,1,0:T(8,128)S(1)} %fusion.95), custom_call_target="InvertDiagBlocksLowerTriangular" | custom-call | tf_op jit(solution)/shard_map/triangular_solve/custom-call.0 | solution.py:32
  556.3 11.7 %cholesky.107 = f32[128,128]{1,0:T(8,128)S(1)} custom-call(f32[128,128]{1,0:T(8,128)S(1)} %fusion.102), custom_call_target="Cholesky" | custom-call | tf_op jit(solution)/shard_map/jit(cholesky)/cholesky | solution.py:31
  569.3 9.8 %custom-call.11 = f32[1,128,128]{1,2,0:T(8,128)S(1)} custom-call(f32[1,128,128]{2,1,0:T(8,128)S(1)} %fusion.96), custom_call_target="InvertDiagBlocksLowerTriangular" | custom-call | tf_op jit(solution)/shard_map/triangular_solve/custom-call.0 | solution.py:32
  592.5 8.7 %collective-permute-done.43 = bf16[32,16,512]{2,0,1:T(8,128)(2,1)S(1)} collective-permute-done((bf16[32,16,512]{2,0,1:T(8,128)(2,1)S(1)}, bf16[32,16,512]{2,0,1:T(8,128)(2,1)S(1)}, u32[]{:S(2)}, u32[]{:S(2)}) %collective-permute-start.43) | collective-permute-done | bytes 524320 | tf_op jit(solution)/shard_map/ppermute | solution.py:138
  604.5 8.8 %collective-permute-done.45 = bf16[32,16,512]{2,0,1:T(8,128)(2,1)S(1)} collective-permute-done((bf16[32,16,512]{2,0,1:T(8,128)(2,1)S(1)}, bf16[32,16,512]{2,0,1:T(8,128)(2,1)S(1)}, u32[]{:S(2)}, u32[]{:S(2)}) %collective-permute-start.45) | collective-permute-done | bytes 524320 | tf_op jit(solution)/shard_map/ppermute | solution.py:138
  616.8 8.6 %collective-permute-done.47 = bf16[32,16,512]{2,0,1:T(8,128)(2,1)S(1)} collective-permute-done((bf16[32,16,512]{2,0,1:T(8,128)(2,1)S(1)}, bf16[32,16,512]{2,0,1:T(8,128)(2,1)S(1)}, u32[]{:S(2)}, u32[]{:S(2)}) %collective-permute-start.47) | collective-permute-done | bytes 524320 | tf_op jit(solution)/shard_map/ppermute | solution.py:138
  628.8 8.6 %collective-permute-done.49 = bf16[32,16,512]{2,0,1:T(8,128)(2,1)S(1)} collective-permute-done((bf16[32,16,512]{2,0,1:T(8,128)(2,1)S(1)}, bf16[32,16,512]{2,0,1:T(8,128)(2,1)S(1)}, u32[]{:S(2)}, u32[]{:S(2)}) %collective-permute-start.49) | collective-permute-done | bytes 524320 | tf_op jit(solution)/shard_map/ppermute | solution.py:138
  640.9 6.0 collective-permute-done.51
  673.0 31.3 %all-reduce.6.cloned.1.call-done = f32[1,512,512]{2,1,0:T(8,128)} async-done(((f32[1,512,512]{2,1,0:T(8,128)}), f32[1,512,512]{2,1,0:T(8,128)}) %all-reduce.6.cloned.1.call-update) | async-done | bytes 1048592 | tf_op jit(solution)/shard_map/psum | solution.py:195
  (269 shorter events, 239.6 us)
Async XLA Ops:
  7.2 303.5 %all-reduce.4.cloned.1.call-start = ((), (), s32[]{:S(2)}) async-start(), calls=%async_computation | async-start | bytes 2097152 | tf_op jit(solution)/shard_map/psum | solution.py:189
  67.5 25.5 %collective-permute-start = (f32[32,16,512]{2,1,0:T(8,128)S(1)}, f32[32,16,512]{2,1,0:T(8,128)S(1)}, u32[]{:S(2)}, u32[]{:S(2)}) collective-permute-start(f32[32,16,512]{2,1,0:T(8,128)S(1)} %constant_dynamic-slice_fusion.20), channel_id=1, source_target_pairs={{0,4},{4,12},{12,20},{20,28},{28,24},{24,16},{16,8},{8,0},{1,5},{5... | collective-permute-start | bytes 3145736 | tf_op jit(solution)/shard_map/ppermute | solution.py:104
  95.8 24.8 %collective-permute-start.1 = (f32[32,16,512]{2,1,0:T(8,128)}, f32[32,16,512]{2,1,0:T(8,128)S(1)}, u32[]{:S(2)}, u32[]{:S(2)}) collective-permute-start(f32[32,16,512]{2,1,0:T(8,128)} %get-tuple-element.18), channel_id=1, source_target_pairs={{0,4},{4,12},{12,20},{20,28},{28,24},{24,16},{16,8},{8,0},{1,5},{5... | collective-permute-start | bytes 3145736 | tf_op jit(solution)/shard_map/ppermute | solution.py:104
  97.4 24.3 %collective-permute-start.7 = (f32[32,16,512]{2,1,0:T(8,128)S(1)}, f32[32,16,512]{2,1,0:T(8,128)S(1)}, u32[]{:S(2)}, u32[]{:S(2)}) collective-permute-start(f32[32,16,512]{2,1,0:T(8,128)S(1)} %get-tuple-element.19), channel_id=1, source_target_pairs={{0,8},{4,0},{12,4},{20,12},{28,20},{24,28},{16,24},{8,16},{1,9},{5... | collective-permute-start | bytes 3145736 | tf_op jit(solution)/shard_map/ppermute | solution.py:105
  124.7 23.6 %collective-permute-start.2 = (f32[32,16,512]{2,1,0:T(8,128)}, f32[32,16,512]{2,1,0:T(8,128)S(1)}, u32[]{:S(2)}, u32[]{:S(2)}) collective-permute-start(f32[32,16,512]{2,1,0:T(8,128)} %get-tuple-element.16), channel_id=1, source_target_pairs={{0,4},{4,12},{12,20},{20,28},{28,24},{24,16},{16,8},{8,0},{1,5},{5... | collective-permute-start | bytes 3145736 | tf_op jit(solution)/shard_map/ppermute | solution.py:104
  126.3 23.1 %collective-permute-start.8 = (f32[32,16,512]{2,1,0:T(8,128)S(1)}, f32[32,16,512]{2,1,0:T(8,128)S(1)}, u32[]{:S(2)}, u32[]{:S(2)}) collective-permute-start(f32[32,16,512]{2,1,0:T(8,128)S(1)} %get-tuple-element.17), channel_id=1, source_target_pairs={{0,8},{4,0},{12,4},{20,12},{28,20},{24,28},{16,24},{8,16},{1,9},{5... | collective-permute-start | bytes 3145736 | tf_op jit(solution)/shard_map/ppermute | solution.py:105
  152.5 22.4 %collective-permute-start.3 = (f32[32,16,512]{2,1,0:T(8,128)}, f32[32,16,512]{2,1,0:T(8,128)S(1)}, u32[]{:S(2)}, u32[]{:S(2)}) collective-permute-start(f32[32,16,512]{2,1,0:T(8,128)} %get-tuple-element.14), channel_id=1, source_target_pairs={{0,4},{4,12},{12,20},{20,28},{28,24},{24,16},{16,8},{8,0},{1,5},{5... | collective-permute-start | bytes 3145736 | tf_op jit(solution)/shard_map/ppermute | solution.py:104
  153.9 22.1 %collective-permute-start.9 = (f32[32,16,512]{2,1,0:T(8,128)S(1)}, f32[32,16,512]{2,1,0:T(8,128)S(1)}, u32[]{:S(2)}, u32[]{:S(2)}) collective-permute-start(f32[32,16,512]{2,1,0:T(8,128)S(1)} %get-tuple-element.15), channel_id=1, source_target_pairs={{0,8},{4,0},{12,4},{20,12},{28,20},{24,28},{16,24},{8,16},{1,9},{5... | collective-permute-start | bytes 3145736 | tf_op jit(solution)/shard_map/ppermute | solution.py:105
  179.0 21.2 %collective-permute-start.10 = (f32[32,16,512]{2,1,0:T(8,128)}, f32[32,16,512]{2,1,0:T(8,128)S(1)}, u32[]{:S(2)}, u32[]{:S(2)}) collective-permute-start(f32[32,16,512]{2,1,0:T(8,128)} %get-tuple-element.13), channel_id=1, source_target_pairs={{0,8},{4,0},{12,4},{20,12},{28,20},{24,28},{16,24},{8,16},{1,9},{5... | collective-permute-start | bytes 3145736 | tf_op jit(solution)/shard_map/ppermute | solution.py:105
  179.5 20.7 %collective-permute-start.4 = (f32[32,16,512]{2,1,0:T(8,128)S(1)}, f32[32,16,512]{2,1,0:T(8,128)S(1)}, u32[]{:S(2)}, u32[]{:S(2)}) collective-permute-start(f32[32,16,512]{2,1,0:T(8,128)S(1)} %get-tuple-element.12), channel_id=1, source_target_pairs={{0,4},{4,12},{12,20},{20,28},{28,24},{24,16},{16,8},{8,0},{1,5},{5... | collective-permute-start | bytes 3145736 | tf_op jit(solution)/shard_map/ppermute | solution.py:104
  203.3 20.2 %collective-permute-start.11 = (f32[32,16,512]{2,1,0:T(8,128)}, f32[32,16,512]{2,1,0:T(8,128)S(1)}, u32[]{:S(2)}, u32[]{:S(2)}) collective-permute-start(f32[32,16,512]{2,1,0:T(8,128)} %get-tuple-element.11), channel_id=1, source_target_pairs={{0,8},{4,0},{12,4},{20,12},{28,20},{24,28},{16,24},{8,16},{1,9},{5... | collective-permute-start | bytes 3145736 | tf_op jit(solution)/shard_map/ppermute | solution.py:105
  204.3 20.2 %collective-permute-start.5 = (f32[32,16,512]{2,1,0:T(8,128)S(1)}, f32[32,16,512]{2,1,0:T(8,128)S(1)}, u32[]{:S(2)}, u32[]{:S(2)}) collective-permute-start(f32[32,16,512]{2,1,0:T(8,128)S(1)} %get-tuple-element.10), channel_id=1, source_target_pairs={{0,4},{4,12},{12,20},{20,28},{28,24},{24,16},{16,8},{8,0},{1,5},{5... | collective-permute-start | bytes 3145736 | tf_op jit(solution)/shard_map/ppermute | solution.py:104
  227.5 19.5 %collective-permute-start.12 = (f32[32,16,512]{2,1,0:T(8,128)}, f32[32,16,512]{2,1,0:T(8,128)S(1)}, u32[]{:S(2)}, u32[]{:S(2)}) collective-permute-start(f32[32,16,512]{2,1,0:T(8,128)} %get-tuple-element.9), channel_id=1, source_target_pairs={{0,8},{4,0},{12,4},{20,12},{28,20},{24,28},{16,24},{8,16},{1,9},{5... | collective-permute-start | bytes 3145736 | tf_op jit(solution)/shard_map/ppermute | solution.py:105
  229.2 19.1 %collective-permute-start.6 = (f32[32,16,512]{2,1,0:T(8,128)S(1)}, f32[32,16,512]{2,1,0:T(8,128)S(1)}, u32[]{:S(2)}, u32[]{:S(2)}) collective-permute-start(f32[32,16,512]{2,1,0:T(8,128)S(1)} %get-tuple-element.8), channel_id=1, source_target_pairs={{0,4},{4,12},{12,20},{20,28},{28,24},{24,16},{16,8},{8,0},{1,5},{5... | collective-permute-start | bytes 3145736 | tf_op jit(solution)/shard_map/ppermute | solution.py:104
  251.2 18.4 %collective-permute-start.13 = (f32[32,16,512]{2,1,0:T(8,128)}, f32[32,16,512]{2,1,0:T(8,128)S(1)}, u32[]{:S(2)}, u32[]{:S(2)}) collective-permute-start(f32[32,16,512]{2,1,0:T(8,128)} %get-tuple-element.7), channel_id=1, source_target_pairs={{0,8},{4,0},{12,4},{20,12},{28,20},{24,28},{16,24},{8,16},{1,9},{5... | collective-permute-start | bytes 3145736 | tf_op jit(solution)/shard_map/ppermute | solution.py:105
  275.6 428.7 %all-reduce.6.cloned.1.call-start = ((), (), s32[]{:S(2)}) async-start(), calls=%async_computation.1 | async-start | bytes 2097152 | tf_op jit(solution)/shard_map/psum | solution.py:195
  406.5 11.8 %collective-permute-start.36 = (f32[32,512]{0,1:T(8,128)S(1)}, f32[32,512]{0,1:T(8,128)}, u32[]{:S(2)}, u32[]{:S(2)}) collective-permute-start(f32[32,512]{0,1:T(8,128)S(1)} %collective-permute-done.34), channel_id=1, source_target_pairs={{0,4},{4,12},{12,20},{20,28},{28,24},{24,16},{16,8},{8,0},{1,5},{5... | collective-permute-start | bytes 196616 | tf_op jit(solution)/shard_map/ppermute | solution.py:165
  407.4 11.7 %collective-permute-start.37 = (f32[32,512]{0,1:T(8,128)}, f32[32,512]{0,1:T(8,128)}, u32[]{:S(2)}, u32[]{:S(2)}) collective-permute-start(f32[32,512]{0,1:T(8,128)} %collective-permute-done.35), channel_id=1, source_target_pairs={{0,8},{4,0},{12,4},{20,12},{28,20},{24,28},{16,24},{8,16},{1,9},{5... | collective-permute-start | bytes 196616 | tf_op jit(solution)/shard_map/ppermute | solution.py:166
  418.3 9.6 %collective-permute-start.38 = (f32[32,512]{0,1:T(8,128)}, f32[32,512]{0,1:T(8,128)}, u32[]{:S(2)}, u32[]{:S(2)}) collective-permute-start(f32[32,512]{0,1:T(8,128)} %collective-permute-done.36), channel_id=1, source_target_pairs={{0,4},{4,12},{12,20},{20,28},{28,24},{24,16},{16,8},{8,0},{1,5},{5... | collective-permute-start | bytes 196616 | tf_op jit(solution)/shard_map/ppermute | solution.py:165
  419.1 9.6 %collective-permute-start.39 = (f32[32,512]{0,1:T(8,128)}, f32[32,512]{0,1:T(8,128)}, u32[]{:S(2)}, u32[]{:S(2)}) collective-permute-start(f32[32,512]{0,1:T(8,128)} %collective-permute-done.37), channel_id=1, source_target_pairs={{0,8},{4,0},{12,4},{20,12},{28,20},{24,28},{16,24},{8,16},{1,9},{5... | collective-permute-start | bytes 196616 | tf_op jit(solution)/shard_map/ppermute | solution.py:166
  428.0 37.6 %collective-permute-start.40 = (f32[32,512]{0,1:T(8,128)}, f32[32,512]{0,1:T(8,128)}, u32[]{:S(2)}, u32[]{:S(2)}) collective-permute-start(f32[32,512]{0,1:T(8,128)} %collective-permute-done.38), channel_id=1, source_target_pairs={{0,4},{4,12},{12,20},{20,28},{28,24},{24,16},{16,8},{8,0},{1,5},{5... | collective-permute-start | bytes 196616 | tf_op jit(solution)/shard_map/ppermute | solution.py:165
  428.8 39.6 %collective-permute-start.41 = (f32[32,512]{0,1:T(8,128)}, f32[32,512]{0,1:T(8,128)}, u32[]{:S(2)}, u32[]{:S(2)}) collective-permute-start(f32[32,512]{0,1:T(8,128)} %collective-permute-done.39), channel_id=1, source_target_pairs={{0,8},{4,0},{12,4},{20,12},{28,20},{24,28},{16,24},{8,16},{1,9},{5... | collective-permute-start | bytes 196616 | tf_op jit(solution)/shard_map/ppermute | solution.py:166
  587.9 13.3 %collective-permute-start.43 = (bf16[32,16,512]{2,0,1:T(8,128)(2,1)S(1)}, bf16[32,16,512]{2,0,1:T(8,128)(2,1)S(1)}, u32[]{:S(2)}, u32[]{:S(2)}) collective-permute-start(bf16[32,16,512]{2,0,1:T(8,128)(2,1)S(1)} %copy.69), channel_id=1, source_target_pairs={{0,8},{4,0},{12,4},{20,12},{28,20},{24,28},{16,24},{8,16},{1,9},{5... | collective-permute-start | bytes 1572872 | tf_op jit(solution)/shard_map/ppermute | solution.py:138
  590.1 13.4 %collective-permute-start.42 = (bf16[32,16,512]{2,0,1:T(8,128)(2,1)S(1)}, bf16[32,16,512]{2,0,1:T(8,128)(2,1)S(1)}, u32[]{:S(2)}, u32[]{:S(2)}) collective-permute-start(bf16[32,16,512]{2,0,1:T(8,128)(2,1)S(1)} %copy.67), channel_id=1, source_target_pairs={{0,4},{4,12},{12,20},{20,28},{28,24},{24,16},{16,8},{8,0},{1,5},{5... | collective-permute-start | bytes 1572872 | tf_op jit(solution)/shard_map/ppermute | solution.py:137
  601.2 12.1 %collective-permute-start.45 = (bf16[32,16,512]{2,0,1:T(8,128)(2,1)S(1)}, bf16[32,16,512]{2,0,1:T(8,128)(2,1)S(1)}, u32[]{:S(2)}, u32[]{:S(2)}) collective-permute-start(bf16[32,16,512]{2,0,1:T(8,128)(2,1)S(1)} %collective-permute-done.43), channel_id=1, source_target_pairs={{0,8},{4,0},{12,4},{20,12},{28,20},{24,28},{16,24},{8,16},{1,9},{5... | collective-permute-start | bytes 1572872 | tf_op jit(solution)/shard_map/ppermute | solution.py:138
  603.5 12.4 %collective-permute-start.44 = (bf16[32,16,512]{2,0,1:T(8,128)(2,1)S(1)}, bf16[32,16,512]{2,0,1:T(8,128)(2,1)S(1)}, u32[]{:S(2)}, u32[]{:S(2)}) collective-permute-start(bf16[32,16,512]{2,0,1:T(8,128)(2,1)S(1)} %collective-permute-done.42), channel_id=1, source_target_pairs={{0,4},{4,12},{12,20},{20,28},{28,24},{24,16},{16,8},{8,0},{1,5},{5... | collective-permute-start | bytes 1572872 | tf_op jit(solution)/shard_map/ppermute | solution.py:137
  613.3 12.1 %collective-permute-start.47 = (bf16[32,16,512]{2,0,1:T(8,128)(2,1)S(1)}, bf16[32,16,512]{2,0,1:T(8,128)(2,1)S(1)}, u32[]{:S(2)}, u32[]{:S(2)}) collective-permute-start(bf16[32,16,512]{2,0,1:T(8,128)(2,1)S(1)} %collective-permute-done.45), channel_id=1, source_target_pairs={{0,8},{4,0},{12,4},{20,12},{28,20},{24,28},{16,24},{8,16},{1,9},{5... | collective-permute-start | bytes 1572872 | tf_op jit(solution)/shard_map/ppermute | solution.py:138
  615.9 12.1 %collective-permute-start.46 = (bf16[32,16,512]{2,0,1:T(8,128)(2,1)S(1)}, bf16[32,16,512]{2,0,1:T(8,128)(2,1)S(1)}, u32[]{:S(2)}, u32[]{:S(2)}) collective-permute-start(bf16[32,16,512]{2,0,1:T(8,128)(2,1)S(1)} %collective-permute-done.44), channel_id=1, source_target_pairs={{0,4},{4,12},{12,20},{20,28},{28,24},{24,16},{16,8},{8,0},{1,5},{5... | collective-permute-start | bytes 1572872 | tf_op jit(solution)/shard_map/ppermute | solution.py:137
  625.4 12.1 %collective-permute-start.49 = (bf16[32,16,512]{2,0,1:T(8,128)(2,1)S(1)}, bf16[32,16,512]{2,0,1:T(8,128)(2,1)S(1)}, u32[]{:S(2)}, u32[]{:S(2)}) collective-permute-start(bf16[32,16,512]{2,0,1:T(8,128)(2,1)S(1)} %collective-permute-done.47), channel_id=1, source_target_pairs={{0,8},{4,0},{12,4},{20,12},{28,20},{24,28},{16,24},{8,16},{1,9},{5... | collective-permute-start | bytes 1572872 | tf_op jit(solution)/shard_map/ppermute | solution.py:138
  628.0 12.1 %collective-permute-start.48 = (bf16[32,16,512]{2,0,1:T(8,128)(2,1)S(1)}, bf16[32,16,512]{2,0,1:T(8,128)(2,1)S(1)}, u32[]{:S(2)}, u32[]{:S(2)}) collective-permute-start(bf16[32,16,512]{2,0,1:T(8,128)(2,1)S(1)} %collective-permute-done.46), channel_id=1, source_target_pairs={{0,4},{4,12},{12,20},{20,28},{28,24},{24,16},{16,8},{8,0},{1,5},{5... | collective-permute-start | bytes 1572872 | tf_op jit(solution)/shard_map/ppermute | solution.py:137
  637.5 9.5 %collective-permute-start.51 = (bf16[32,16,512]{2,0,1:T(8,128)(2,1)S(1)}, bf16[32,16,512]{2,0,1:T(8,128)(2,1)S(1)}, u32[]{:S(2)}, u32[]{:S(2)}) collective-permute-start(bf16[32,16,512]{2,0,1:T(8,128)(2,1)S(1)} %collective-permute-done.49), channel_id=1, source_target_pairs={{0,8},{4,0},{12,4},{20,12},{28,20},{24,28},{16,24},{8,16},{1,9},{5... | collective-permute-start | bytes 1572872 | tf_op jit(solution)/shard_map/ppermute | solution.py:138
  640.0 9.7 %collective-permute-start.50 = (bf16[32,16,512]{2,0,1:T(8,128)(2,1)S(1)}, bf16[32,16,512]{2,0,1:T(8,128)(2,1)S(1)}, u32[]{:S(2)}, u32[]{:S(2)}) collective-permute-start(bf16[32,16,512]{2,0,1:T(8,128)(2,1)S(1)} %collective-permute-done.48), channel_id=1, source_target_pairs={{0,4},{4,12},{12,20},{20,28},{28,24},{24,16},{16,8},{8,0},{1,5},{5... | collective-permute-start | bytes 1572872 | tf_op jit(solution)/shard_map/ppermute | solution.py:137
  (59 other events, 794.6 us)
Sparse Core Ops, SparseCore 0:
  275.7 34.9 all-reduce.3
  669.9 34.3 all-reduce.5

commit v6 on v4

--- a/solution.py
+++ b/solution.py
@@ -46,6 +46,23 @@
             rhs = rhs - mm(done, lrow.T)
         blocks.append(mm(rhs, inverses[k].T))
     return jnp.concatenate(blocks, axis=1)
+
+
+def symmetric_psum(gram_part):
+    n = gram_part.shape[0]
+    b = min(BLOCK, n)
+    nb = n // b
+    lower = [(i, j) for i in range(nb) for j in range(i + 1)]
+    packed = jnp.stack([gram_part[i * b:(i + 1) * b, j * b:(j + 1) * b] for i, j in lower])
+    packed = lax.psum(lax.psum(packed, "mode"), "sum")
+    where = {cell: k for k, cell in enumerate(lower)}
+    rows = []
+    for i in range(nb):
+        row = []
+        for j in range(nb):
+            row.append(packed[where[(i, j)]] if j <= i else packed[where[(j, i)]].T)
+        rows.append(jnp.concatenate(row, axis=1))
+    return jnp.concatenate(rows, axis=0)
 
 
 def ring_order(mesh):
@@ -156,7 +173,7 @@
     share = ring_reduce_scatter(local_sum, ring)
     flat_share = share.reshape(-1, target)
     gram_part = jnp.dot(flat_share.T, flat_share, precision=HI)
-    gram = lax.psum(lax.psum(gram_part, "mode"), "sum")
+    gram = symmetric_psum(gram_part)
     basis = orthonormal(flat_share, gram)
     block = basis.reshape(share.shape)
     rounded = block.astype(jnp.bfloat16)

time: 650 us -> 642 us (0.988)
  waiting for transfers between devices: 350 us -> 343 us
    psum x2, waiting for transfers between devices: 100 us -> 92.5 us  [symmetric_psum(): packed = lax.psum(lax.psum(packed, 'mode'), 'sum')]
where the time goes in v6:
time: 642 us; the launch traced here: 632 us
  waiting for transfers between devices  343 us (53%)
  other arithmetic  114 us (18%)
  matrix products  61.9 us (10%)
  between operations  35.2 us (5%)
  starting transfers between devices  30.4 us (5%)
  blocking collectives  28 us (4%)
  local copies, waits for them, and re-layouts  19.9 us (3%)
    psum x2, waiting for transfers between devices, symmetric_psum(): packed = lax.psum(lax.psum(packed, 'mode'), 'sum')  92.5 us
    ppermute x7, waiting for transfers between devices, ring_reduce_scatter(): acc_f = lax.ppermute(acc_f, 'sum', fwd) + piece(fwd_blocks[t, me], 0, half)  83.4 us
    ppermute x7, waiting for transfers between devices, ring_reduce_scatter(): lax.ppermute(acc_b, 'sum', bwd)  72.7 us
    ppermute x7, waiting for transfers between devices, ring_gather_carries(): hold_b = lax.ppermute(hold_b, 'sum', bwd)  60 us
    another operation x12, other arithmetic, orthonormal(): lkk = jnp.linalg.cholesky(diag)  49.7 us
    another operation x8, other arithmetic, orthonormal(): ikk = lax.linalg.triangular_solve(lkk, eye, left_side=True, lower=True)  41.9 us
    psum x1, waiting for transfers between devices, per_device(): carries = lax.psum(partial_carry, 'mode')  33.2 us
    psum x1, blocking collectives, per_device(): mapped = lax.psum(partial_map, 'mode').astype(jnp.bfloat16)  28 us
  transfers between devices with their start and end apart: 31, of which 24 were waited for; matrix products, arithmetic and copies ran while one was open for 3% of the time, Pallas kernels for 0%

profile of v6, /device:TPU:0, one launch (start us, length us, event | category | flops | bytes accessed | tf_op | source)
XLA Modules:
  0.0 631.8 jit_solution(6416428845070648292)
XLA Ops:
  9.5 17.1 %fusion.9 = f32[1,512,512]{2,1,0:T(8,128)S(1)} fusion(bf16[16,512,512]{2,1,0:T(8,128)(2,1)} %param.12, bf16[512,16,512]{2,1,0:T(8,128)(2,1)} %bitcast.340), kind=kOutput, calls=%fused_computation.29 | convolution fusion | flops 4294967296 | bytes 17825792 | tf_op jit(solution)/shard_map/dot_general | solution.py:164
  26.7 28.0 %all-reduce.10 = bf16[1,512,512]{2,1,0:T(8,128)(2,1)S(1)} all-reduce(f32[1,512,512]{2,1,0:T(8,128)S(1)} %fusion.9), channel_id=1, replica_groups=mesh['sum'=8,'mode'=4] {'mode'}, use_global_device_ids=true, to_apply=%region_0.0 | all-reduce | flops 262144 | bytes 1572864 | tf_op jit(solution)/shard_map/psum | solution.py:167
  54.7 11.7 %convolution_bitcast_fusion = f32[512,16,512]{2,1,0:T(8,128)} fusion(bf16[1,512,16,512]{3,2,1,0:T(8,128)(2,1)} %param.10, bf16[1,512,512]{2,1,0:T(8,128)(2,1)S(1)} %all-reduce.10), kind=kOutput, calls=%fused_computation | convolution fusion | flops 4294967296 | bytes 25690112 | tf_op jit(solution)/shard_map/dot_general | solution.py:168
  70.4 22.8 %collective-permute-done = f32[32,16,512]{2,1,0:T(8,128)S(1)} collective-permute-done((f32[32,16,512]{2,1,0:T(8,128)S(1)}, f32[32,16,512]{2,1,0:T(8,128)S(1)}, u32[]{:S(2)}, u32[]{:S(2)}) %collective-permute-start) | collective-permute-done | bytes 1048608 | tf_op jit(solution)/shard_map/ppermute | solution.py:121
  98.5 21.2 %collective-permute-done.1 = f32[32,16,512]{2,1,0:T(8,128)S(1)} collective-permute-done((f32[32,16,512]{2,1,0:T(8,128)S(1)}, f32[32,16,512]{2,1,0:T(8,128)S(1)}, u32[]{:S(2)}, u32[]{:S(2)}) %collective-permute-start.1) | collective-permute-done | bytes 1048608 | tf_op jit(solution)/shard_map/ppermute | solution.py:121
  126.5 20.2 %collective-permute-done.2 = f32[32,16,512]{2,1,0:T(8,128)S(1)} collective-permute-done((f32[32,16,512]{2,1,0:T(8,128)S(1)}, f32[32,16,512]{2,1,0:T(8,128)S(1)}, u32[]{:S(2)}, u32[]{:S(2)}) %collective-permute-start.2) | collective-permute-done | bytes 1048608 | tf_op jit(solution)/shard_map/ppermute | solution.py:121
  154.1 18.7 %collective-permute-done.3 = f32[32,16,512]{2,1,0:T(8,128)S(1)} collective-permute-done((f32[32,16,512]{2,1,0:T(8,128)S(1)}, f32[32,16,512]{2,1,0:T(8,128)S(1)}, u32[]{:S(2)}, u32[]{:S(2)}) %collective-permute-start.3) | collective-permute-done | bytes 1048608 | tf_op jit(solution)/shard_map/ppermute | solution.py:121
  179.9 17.8 %collective-permute-done.10 = f32[32,16,512]{2,1,0:T(8,128)S(1)} collective-permute-done((f32[32,16,512]{2,1,0:T(8,128)S(1)}, f32[32,16,512]{2,1,0:T(8,128)S(1)}, u32[]{:S(2)}, u32[]{:S(2)}) %collective-permute-start.10) | collective-permute-done | bytes 1048608 | tf_op jit(solution)/shard_map/ppermute | solution.py:122
  203.8 16.6 %collective-permute-done.11 = f32[32,16,512]{2,1,0:T(8,128)S(1)} collective-permute-done((f32[32,16,512]{2,1,0:T(8,128)S(1)}, f32[32,16,512]{2,1,0:T(8,128)S(1)}, u32[]{:S(2)}, u32[]{:S(2)}) %collective-permute-start.11) | collective-permute-done | bytes 1048608 | tf_op jit(solution)/shard_map/ppermute | solution.py:122
  227.2 17.3 %collective-permute-done.12 = f32[32,16,512]{2,1,0:T(8,128)S(1)} collective-permute-done((f32[32,16,512]{2,1,0:T(8,128)}, f32[32,16,512]{2,1,0:T(8,128)S(1)}, u32[]{:S(2)}, u32[]{:S(2)}) %collective-permute-start.12) | collective-permute-done | bytes 1048608 | tf_op jit(solution)/shard_map/ppermute | solution.py:122
  248.7 16.7 %collective-permute-done.13 = f32[32,16,512]{2,1,0:T(8,128)S(1)} collective-permute-done((f32[32,16,512]{2,1,0:T(8,128)S(1)}, f32[32,16,512]{2,1,0:T(8,128)S(1)}, u32[]{:S(2)}, u32[]{:S(2)}) %collective-permute-start.13) | collective-permute-done | bytes 1048608 | tf_op jit(solution)/shard_map/ppermute | solution.py:122
  266.9 3.5 convolution_bitcast_fusion.17
  271.5 33.4 %all-reduce.5.cloned.1.call-done = f32[10,128,128]{1,2,0:T(8,128)} async-done(((f32[10,128,128]{1,2,0:T(8,128)}), f32[10,128,128]{1,2,0:T(8,128)}) %all-reduce.5.cloned.1.call-update) | async-done | bytes 655376 | tf_op jit(solution)/shard_map/psum | solution.py:57
  316.1 6.2 constant_dynamic-slice_fusion.1
  322.6 59.1 %all-reduce.7.cloned.1.call-done = f32[10,128,128]{1,2,0:T(8,128)} async-done(((f32[10,128,128]{1,2,0:T(8,128)}), f32[10,128,128]{1,2,0:T(8,128)}) %all-reduce.7.cloned.1.call-update) | async-done | bytes 655376 | tf_op jit(solution)/shard_map/psum | solution.py:57
  383.8 11.7 %cholesky.74 = f32[128,128]{1,0:T(8,128)S(1)} custom-call(f32[128,128]{1,0:T(8,128)S(1)} %fusion.128), custom_call_target="Cholesky" | custom-call | tf_op jit(solution)/shard_map/jit(cholesky)/cholesky | solution.py:31
  396.9 9.8 %custom-call.8 = f32[1,128,128]{1,2,0:T(8,128)S(1)} custom-call(f32[1,128,128]{2,1,0:T(8,128)S(1)} %fusion.110), custom_call_target="InvertDiagBlocksLowerTriangular" | custom-call | tf_op jit(solution)/shard_map/triangular_solve/custom-call.0 | solution.py:32
  410.4 11.9 %cholesky.85 = f32[128,128]{1,0:T(8,128)S(1)} custom-call(f32[128,128]{1,0:T(8,128)S(1)} %fusion.134), custom_call_target="Cholesky" | custom-call | tf_op jit(solution)/shard_map/jit(cholesky)/cholesky | solution.py:31
  423.6 9.8 %custom-call.9 = f32[1,128,128]{1,2,0:T(8,128)S(1)} custom-call(f32[1,128,128]{2,1,0:T(8,128)S(1)} %fusion.111), custom_call_target="InvertDiagBlocksLowerTriangular" | custom-call | tf_op jit(solution)/shard_map/triangular_solve/custom-call.0 | solution.py:32
  439.3 11.7 %cholesky.96 = f32[128,128]{1,0:T(8,128)S(1)} custom-call(f32[128,128]{1,0:T(8,128)S(1)} %fusion.132), custom_call_target="Cholesky" | custom-call | tf_op jit(solution)/shard_map/jit(cholesky)/cholesky | solution.py:31
  452.4 9.8 %custom-call.10 = f32[1,128,128]{1,2,0:T(8,128)S(1)} custom-call(f32[1,128,128]{2,1,0:T(8,128)S(1)} %fusion.112), custom_call_target="InvertDiagBlocksLowerTriangular" | custom-call | tf_op jit(solution)/shard_map/triangular_solve/custom-call.0 | solution.py:32
  467.4 11.7 %cholesky.107 = f32[128,128]{1,0:T(8,128)S(1)} custom-call(f32[128,128]{1,0:T(8,128)S(1)} %fusion.130), custom_call_target="Cholesky" | custom-call | tf_op jit(solution)/shard_map/jit(cholesky)/cholesky | solution.py:31
  480.5 9.8 %custom-call.11 = f32[1,128,128]{1,2,0:T(8,128)S(1)} custom-call(f32[1,128,128]{2,1,0:T(8,128)S(1)} %fusion.113), custom_call_target="InvertDiagBlocksLowerTriangular" | custom-call | tf_op jit(solution)/shard_map/triangular_solve/custom-call.0 | solution.py:32
  490.6 3.7 fusion.3
  503.3 8.2 %collective-permute-done.15 = bf16[32,16,512]{2,0,1:T(8,128)(2,1)S(1)} collective-permute-done((bf16[32,16,512]{2,0,1:T(8,128)(2,1)S(1)}, bf16[32,16,512]{2,0,1:T(8,128)(2,1)S(1)}, u32[]{:S(2)}, u32[]{:S(2)}) %collective-permute-start.15) | collective-permute-done | bytes 524320 | tf_op jit(solution)/shard_map/ppermute | solution.py:155
  514.8 8.7 %collective-permute-done.17 = bf16[32,16,512]{2,0,1:T(8,128)(2,1)S(1)} collective-permute-done((bf16[32,16,512]{2,0,1:T(8,128)(2,1)S(1)}, bf16[32,16,512]{2,0,1:T(8,128)(2,1)S(1)}, u32[]{:S(2)}, u32[]{:S(2)}) %collective-permute-start.17) | collective-permute-done | bytes 524320 | tf_op jit(solution)/shard_map/ppermute | solution.py:155
  526.8 8.8 %collective-permute-done.19 = bf16[32,16,512]{2,0,1:T(8,128)(2,1)S(1)} collective-permute-done((bf16[32,16,512]{2,0,1:T(8,128)(2,1)S(1)}, bf16[32,16,512]{2,0,1:T(8,128)(2,1)S(1)}, u32[]{:S(2)}, u32[]{:S(2)}) %collective-permute-start.19) | collective-permute-done | bytes 524320 | tf_op jit(solution)/shard_map/ppermute | solution.py:155
  538.9 8.8 %collective-permute-done.21 = bf16[32,16,512]{2,0,1:T(8,128)(2,1)S(1)} collective-permute-done((bf16[32,16,512]{2,0,1:T(8,128)(2,1)S(1)}, bf16[32,16,512]{2,0,1:T(8,128)(2,1)S(1)}, u32[]{:S(2)}, u32[]{:S(2)}) %collective-permute-start.21) | collective-permute-done | bytes 524320 | tf_op jit(solution)/shard_map/ppermute | solution.py:155
  551.0 9.2 %collective-permute-done.23 = bf16[32,16,512]{2,0,1:T(8,128)(2,1)S(1)} collective-permute-done((bf16[32,16,512]{2,0,1:T(8,128)(2,1)S(1)}, bf16[32,16,512]{2,0,1:T(8,128)(2,1)S(1)}, u32[]{:S(2)}, u32[]{:S(2)}) %collective-permute-start.23) | collective-permute-done | bytes 524320 | tf_op jit(solution)/shard_map/ppermute | solution.py:155
  563.5 10.3 %collective-permute-done.25 = bf16[32,16,512]{2,0,1:T(8,128)(2,1)S(1)} collective-permute-done((bf16[32,16,512]{2,0,1:T(8,128)(2,1)S(1)}, bf16[32,16,512]{2,0,1:T(8,128)(2,1)S(1)}, u32[]{:S(2)}, u32[]{:S(2)}) %collective-permute-start.25) | collective-permute-done | bytes 524320 | tf_op jit(solution)/shard_map/ppermute | solution.py:155
  577.1 5.9 collective-permute-done.27
  589.5 33.2 %all-reduce.9.cloned.1.call-done = f32[1,512,512]{2,1,0:T(8,128)} async-done(((f32[1,512,512]{2,1,0:T(8,128)}), f32[1,512,512]{2,1,0:T(8,128)}) %all-reduce.9.cloned.1.call-update) | async-done | bytes 1048592 | tf_op jit(solution)/shard_map/psum | solution.py:181
  (185 shorter events, 103.5 us)
Async XLA Ops:
  7.2 297.8 %all-reduce.5.cloned.1.call-start = ((), (), s32[]{:S(2)}) async-start(), calls=%async_computation | async-start | bytes 1310720 | tf_op jit(solution)/shard_map/psum | solution.py:57
  67.6 25.5 %collective-permute-start = (f32[32,16,512]{2,1,0:T(8,128)S(1)}, f32[32,16,512]{2,1,0:T(8,128)S(1)}, u32[]{:S(2)}, u32[]{:S(2)}) collective-permute-start(f32[32,16,512]{2,1,0:T(8,128)S(1)} %constant_dynamic-slice_fusion.18), channel_id=1, source_target_pairs={{0,4},{4,12},{12,20},{20,28},{28,24},{24,16},{16,8},{8,0},{1,5},{5... | collective-permute-start | bytes 3145736 | tf_op jit(solution)/shard_map/ppermute | solution.py:121
  95.0 24.7 %collective-permute-start.1 = (f32[32,16,512]{2,1,0:T(8,128)S(1)}, f32[32,16,512]{2,1,0:T(8,128)S(1)}, u32[]{:S(2)}, u32[]{:S(2)}) collective-permute-start(f32[32,16,512]{2,1,0:T(8,128)S(1)} %get-tuple-element.18), channel_id=1, source_target_pairs={{0,4},{4,12},{12,20},{20,28},{28,24},{24,16},{16,8},{8,0},{1,5},{5... | collective-permute-start | bytes 3145736 | tf_op jit(solution)/shard_map/ppermute | solution.py:121
  96.4 24.4 %collective-permute-start.7 = (f32[32,16,512]{2,1,0:T(8,128)S(1)}, f32[32,16,512]{2,1,0:T(8,128)}, u32[]{:S(2)}, u32[]{:S(2)}) collective-permute-start(f32[32,16,512]{2,1,0:T(8,128)S(1)} %get-tuple-element.19), channel_id=1, source_target_pairs={{0,8},{4,0},{12,4},{20,12},{28,20},{24,28},{16,24},{8,16},{1,9},{5... | collective-permute-start | bytes 3145736 | tf_op jit(solution)/shard_map/ppermute | solution.py:122
  123.2 23.5 %collective-permute-start.2 = (f32[32,16,512]{2,1,0:T(8,128)S(1)}, f32[32,16,512]{2,1,0:T(8,128)S(1)}, u32[]{:S(2)}, u32[]{:S(2)}) collective-permute-start(f32[32,16,512]{2,1,0:T(8,128)S(1)} %get-tuple-element.16), channel_id=1, source_target_pairs={{0,4},{4,12},{12,20},{20,28},{28,24},{24,16},{16,8},{8,0},{1,5},{5... | collective-permute-start | bytes 3145736 | tf_op jit(solution)/shard_map/ppermute | solution.py:121
  124.9 23.2 %collective-permute-start.8 = (f32[32,16,512]{2,1,0:T(8,128)S(1)}, f32[32,16,512]{2,1,0:T(8,128)}, u32[]{:S(2)}, u32[]{:S(2)}) collective-permute-start(f32[32,16,512]{2,1,0:T(8,128)S(1)} %get-tuple-element.17), channel_id=1, source_target_pairs={{0,8},{4,0},{12,4},{20,12},{28,20},{24,28},{16,24},{8,16},{1,9},{5... | collective-permute-start | bytes 3145736 | tf_op jit(solution)/shard_map/ppermute | solution.py:122
  150.5 22.3 %collective-permute-start.3 = (f32[32,16,512]{2,1,0:T(8,128)S(1)}, f32[32,16,512]{2,1,0:T(8,128)S(1)}, u32[]{:S(2)}, u32[]{:S(2)}) collective-permute-start(f32[32,16,512]{2,1,0:T(8,128)S(1)} %get-tuple-element.14), channel_id=1, source_target_pairs={{0,4},{4,12},{12,20},{20,28},{28,24},{24,16},{16,8},{8,0},{1,5},{5... | collective-permute-start | bytes 3145736 | tf_op jit(solution)/shard_map/ppermute | solution.py:121
  152.1 22.2 %collective-permute-start.9 = (f32[32,16,512]{2,1,0:T(8,128)S(1)}, f32[32,16,512]{2,1,0:T(8,128)}, u32[]{:S(2)}, u32[]{:S(2)}) collective-permute-start(f32[32,16,512]{2,1,0:T(8,128)S(1)} %get-tuple-element.15), channel_id=1, source_target_pairs={{0,8},{4,0},{12,4},{20,12},{28,20},{24,28},{16,24},{8,16},{1,9},{5... | collective-permute-start | bytes 3145736 | tf_op jit(solution)/shard_map/ppermute | solution.py:122
  176.7 21.1 %collective-permute-start.10 = (f32[32,16,512]{2,1,0:T(8,128)S(1)}, f32[32,16,512]{2,1,0:T(8,128)S(1)}, u32[]{:S(2)}, u32[]{:S(2)}) collective-permute-start(f32[32,16,512]{2,1,0:T(8,128)S(1)} %get-tuple-element.13), channel_id=1, source_target_pairs={{0,8},{4,0},{12,4},{20,12},{28,20},{24,28},{16,24},{8,16},{1,9},{5... | collective-permute-start | bytes 3145736 | tf_op jit(solution)/shard_map/ppermute | solution.py:122
  177.2 20.8 %collective-permute-start.4 = (f32[32,16,512]{2,1,0:T(8,128)S(1)}, f32[32,16,512]{2,1,0:T(8,128)}, u32[]{:S(2)}, u32[]{:S(2)}) collective-permute-start(f32[32,16,512]{2,1,0:T(8,128)S(1)} %get-tuple-element.12), channel_id=1, source_target_pairs={{0,4},{4,12},{12,20},{20,28},{28,24},{24,16},{16,8},{8,0},{1,5},{5... | collective-permute-start | bytes 3145736 | tf_op jit(solution)/shard_map/ppermute | solution.py:121
  200.4 20.0 %collective-permute-start.11 = (f32[32,16,512]{2,1,0:T(8,128)S(1)}, f32[32,16,512]{2,1,0:T(8,128)S(1)}, u32[]{:S(2)}, u32[]{:S(2)}) collective-permute-start(f32[32,16,512]{2,1,0:T(8,128)S(1)} %get-tuple-element.11), channel_id=1, source_target_pairs={{0,8},{4,0},{12,4},{20,12},{28,20},{24,28},{16,24},{8,16},{1,9},{5... | collective-permute-start | bytes 3145736 | tf_op jit(solution)/shard_map/ppermute | solution.py:122
  200.8 19.8 %collective-permute-start.5 = (f32[32,16,512]{2,1,0:T(8,128)S(1)}, f32[32,16,512]{2,1,0:T(8,128)}, u32[]{:S(2)}, u32[]{:S(2)}) collective-permute-start(f32[32,16,512]{2,1,0:T(8,128)S(1)} %get-tuple-element.10), channel_id=1, source_target_pairs={{0,4},{4,12},{12,20},{20,28},{28,24},{24,16},{16,8},{8,0},{1,5},{5... | collective-permute-start | bytes 3145736 | tf_op jit(solution)/shard_map/ppermute | solution.py:121
  223.9 20.6 %collective-permute-start.12 = (f32[32,16,512]{2,1,0:T(8,128)}, f32[32,16,512]{2,1,0:T(8,128)S(1)}, u32[]{:S(2)}, u32[]{:S(2)}) collective-permute-start(f32[32,16,512]{2,1,0:T(8,128)} %get-tuple-element.9), channel_id=1, source_target_pairs={{0,8},{4,0},{12,4},{20,12},{28,20},{24,28},{16,24},{8,16},{1,9},{5... | collective-permute-start | bytes 3145736 | tf_op jit(solution)/shard_map/ppermute | solution.py:122
  225.1 19.4 %collective-permute-start.6 = (f32[32,16,512]{2,1,0:T(8,128)S(1)}, f32[32,16,512]{2,1,0:T(8,128)}, u32[]{:S(2)}, u32[]{:S(2)}) collective-permute-start(f32[32,16,512]{2,1,0:T(8,128)S(1)} %get-tuple-element.8), channel_id=1, source_target_pairs={{0,4},{4,12},{12,20},{20,28},{28,24},{24,16},{16,8},{8,0},{1,5},{5... | collective-permute-start | bytes 3145736 | tf_op jit(solution)/shard_map/ppermute | solution.py:121
  246.8 18.6 %collective-permute-start.13 = (f32[32,16,512]{2,1,0:T(8,128)S(1)}, f32[32,16,512]{2,1,0:T(8,128)S(1)}, u32[]{:S(2)}, u32[]{:S(2)}) collective-permute-start(f32[32,16,512]{2,1,0:T(8,128)S(1)} %get-tuple-element.7), channel_id=1, source_target_pairs={{0,8},{4,0},{12,4},{20,12},{28,20},{24,28},{16,24},{8,16},{1,9},{5... | collective-permute-start | bytes 3145736 | tf_op jit(solution)/shard_map/ppermute | solution.py:122
  270.4 35.0 %copy-start.20 = (s32[8,8]{1,0:T(8,128)S(1)}, s32[8,8]{1,0:T(8,128)}, u32[]{:S(2)}) copy-start(s32[8,8]{1,0:T(8,128)} %constant.152.clone) | copy-start | bytes 772
  271.5 110.2 %all-reduce.7.cloned.1.call-start = ((), (), s32[]{:S(2)}) async-start(), calls=%async_computation.1 | async-start | bytes 1310720 | tf_op jit(solution)/shard_map/psum | solution.py:57
  305.0 317.6 %all-reduce.9.cloned.1.call-start = ((), (), s32[]{:S(2)}) async-start(), calls=%async_computation.2 | async-start | bytes 2097152 | tf_op jit(solution)/shard_map/psum | solution.py:181
  499.0 12.5 %collective-permute-start.15 = (bf16[32,16,512]{2,0,1:T(8,128)(2,1)S(1)}, bf16[32,16,512]{2,0,1:T(8,128)(2,1)S(1)}, u32[]{:S(2)}, u32[]{:S(2)}) collective-permute-start(bf16[32,16,512]{2,0,1:T(8,128)(2,1)S(1)} %copy.95), channel_id=1, source_target_pairs={{0,8},{4,0},{12,4},{20,12},{28,20},{24,28},{16,24},{8,16},{1,9},{5... | collective-permute-start | bytes 1572872 | tf_op jit(solution)/shard_map/ppermute | solution.py:155
  500.3 12.9 %collective-permute-start.14 = (bf16[32,16,512]{2,0,1:T(8,128)(2,1)S(1)}, bf16[32,16,512]{2,0,1:T(8,128)(2,1)S(1)}, u32[]{:S(2)}, u32[]{:S(2)}) collective-permute-start(bf16[32,16,512]{2,0,1:T(8,128)(2,1)S(1)} %copy.93), channel_id=1, source_target_pairs={{0,4},{4,12},{12,20},{20,28},{28,24},{24,16},{16,8},{8,0},{1,5},{5... | collective-permute-start | bytes 1572872 | tf_op jit(solution)/shard_map/ppermute | solution.py:154
  511.5 12.0 %collective-permute-start.17 = (bf16[32,16,512]{2,0,1:T(8,128)(2,1)S(1)}, bf16[32,16,512]{2,0,1:T(8,128)(2,1)S(1)}, u32[]{:S(2)}, u32[]{:S(2)}) collective-permute-start(bf16[32,16,512]{2,0,1:T(8,128)(2,1)S(1)} %collective-permute-done.15), channel_id=1, source_target_pairs={{0,8},{4,0},{12,4},{20,12},{28,20},{24,28},{16,24},{8,16},{1,9},{5... | collective-permute-start | bytes 1572872 | tf_op jit(solution)/shard_map/ppermute | solution.py:155
  513.1 12.1 %collective-permute-start.16 = (bf16[32,16,512]{2,0,1:T(8,128)(2,1)S(1)}, bf16[32,16,512]{2,0,1:T(8,128)(2,1)S(1)}, u32[]{:S(2)}, u32[]{:S(2)}) collective-permute-start(bf16[32,16,512]{2,0,1:T(8,128)(2,1)S(1)} %collective-permute-done.14), channel_id=1, source_target_pairs={{0,4},{4,12},{12,20},{20,28},{28,24},{24,16},{16,8},{8,0},{1,5},{5... | collective-permute-start | bytes 1572872 | tf_op jit(solution)/shard_map/ppermute | solution.py:154
  523.5 12.1 %collective-permute-start.19 = (bf16[32,16,512]{2,0,1:T(8,128)(2,1)S(1)}, bf16[32,16,512]{2,0,1:T(8,128)(2,1)S(1)}, u32[]{:S(2)}, u32[]{:S(2)}) collective-permute-start(bf16[32,16,512]{2,0,1:T(8,128)(2,1)S(1)} %collective-permute-done.17), channel_id=1, source_target_pairs={{0,8},{4,0},{12,4},{20,12},{28,20},{24,28},{16,24},{8,16},{1,9},{5... | collective-permute-start | bytes 1572872 | tf_op jit(solution)/shard_map/ppermute | solution.py:155
  525.2 12.1 %collective-permute-start.18 = (bf16[32,16,512]{2,0,1:T(8,128)(2,1)S(1)}, bf16[32,16,512]{2,0,1:T(8,128)(2,1)S(1)}, u32[]{:S(2)}, u32[]{:S(2)}) collective-permute-start(bf16[32,16,512]{2,0,1:T(8,128)(2,1)S(1)} %collective-permute-done.16), channel_id=1, source_target_pairs={{0,4},{4,12},{12,20},{20,28},{28,24},{24,16},{16,8},{8,0},{1,5},{5... | collective-permute-start | bytes 1572872 | tf_op jit(solution)/shard_map/ppermute | solution.py:154
  535.6 12.1 %collective-permute-start.21 = (bf16[32,16,512]{2,0,1:T(8,128)(2,1)S(1)}, bf16[32,16,512]{2,0,1:T(8,128)(2,1)S(1)}, u32[]{:S(2)}, u32[]{:S(2)}) collective-permute-start(bf16[32,16,512]{2,0,1:T(8,128)(2,1)S(1)} %collective-permute-done.19), channel_id=1, source_target_pairs={{0,8},{4,0},{12,4},{20,12},{28,20},{24,28},{16,24},{8,16},{1,9},{5... | collective-permute-start | bytes 1572872 | tf_op jit(solution)/shard_map/ppermute | solution.py:155
  537.3 12.1 %collective-permute-start.20 = (bf16[32,16,512]{2,0,1:T(8,128)(2,1)S(1)}, bf16[32,16,512]{2,0,1:T(8,128)(2,1)S(1)}, u32[]{:S(2)}, u32[]{:S(2)}) collective-permute-start(bf16[32,16,512]{2,0,1:T(8,128)(2,1)S(1)} %collective-permute-done.18), channel_id=1, source_target_pairs={{0,4},{4,12},{12,20},{20,28},{28,24},{24,16},{16,8},{8,0},{1,5},{5... | collective-permute-start | bytes 1572872 | tf_op jit(solution)/shard_map/ppermute | solution.py:154
  547.7 12.5 %collective-permute-start.23 = (bf16[32,16,512]{2,0,1:T(8,128)(2,1)S(1)}, bf16[32,16,512]{2,0,1:T(8,128)(2,1)S(1)}, u32[]{:S(2)}, u32[]{:S(2)}) collective-permute-start(bf16[32,16,512]{2,0,1:T(8,128)(2,1)S(1)} %collective-permute-done.21), channel_id=1, source_target_pairs={{0,8},{4,0},{12,4},{20,12},{28,20},{24,28},{16,24},{8,16},{1,9},{5... | collective-permute-start | bytes 1572872 | tf_op jit(solution)/shard_map/ppermute | solution.py:155
  549.4 12.4 %collective-permute-start.22 = (bf16[32,16,512]{2,0,1:T(8,128)(2,1)S(1)}, bf16[32,16,512]{2,0,1:T(8,128)(2,1)S(1)}, u32[]{:S(2)}, u32[]{:S(2)}) collective-permute-start(bf16[32,16,512]{2,0,1:T(8,128)(2,1)S(1)} %collective-permute-done.20), channel_id=1, source_target_pairs={{0,4},{4,12},{12,20},{20,28},{28,24},{24,16},{16,8},{8,0},{1,5},{5... | collective-permute-start | bytes 1572872 | tf_op jit(solution)/shard_map/ppermute | solution.py:154
  560.2 13.6 %collective-permute-start.25 = (bf16[32,16,512]{2,0,1:T(8,128)(2,1)S(1)}, bf16[32,16,512]{2,0,1:T(8,128)(2,1)S(1)}, u32[]{:S(2)}, u32[]{:S(2)}) collective-permute-start(bf16[32,16,512]{2,0,1:T(8,128)(2,1)S(1)} %collective-permute-done.23), channel_id=1, source_target_pairs={{0,8},{4,0},{12,4},{20,12},{28,20},{24,28},{16,24},{8,16},{1,9},{5... | collective-permute-start | bytes 1572872 | tf_op jit(solution)/shard_map/ppermute | solution.py:155
  561.9 13.5 %collective-permute-start.24 = (bf16[32,16,512]{2,0,1:T(8,128)(2,1)S(1)}, bf16[32,16,512]{2,0,1:T(8,128)(2,1)S(1)}, u32[]{:S(2)}, u32[]{:S(2)}) collective-permute-start(bf16[32,16,512]{2,0,1:T(8,128)(2,1)S(1)} %collective-permute-done.22), channel_id=1, source_target_pairs={{0,4},{4,12},{12,20},{20,28},{28,24},{24,16},{16,8},{8,0},{1,5},{5... | collective-permute-start | bytes 1572872 | tf_op jit(solution)/shard_map/ppermute | solution.py:154
  573.8 9.2 %collective-permute-start.27 = (bf16[32,16,512]{2,0,1:T(8,128)(2,1)S(1)}, bf16[32,16,512]{2,0,1:T(8,128)(2,1)S(1)}, u32[]{:S(2)}, u32[]{:S(2)}) collective-permute-start(bf16[32,16,512]{2,0,1:T(8,128)(2,1)S(1)} %collective-permute-done.25), channel_id=1, source_target_pairs={{0,8},{4,0},{12,4},{20,12},{28,20},{24,28},{16,24},{8,16},{1,9},{5... | collective-permute-start | bytes 1572872 | tf_op jit(solution)/shard_map/ppermute | solution.py:155
  575.3 9.2 %collective-permute-start.26 = (bf16[32,16,512]{2,0,1:T(8,128)(2,1)S(1)}, bf16[32,16,512]{2,0,1:T(8,128)(2,1)S(1)}, u32[]{:S(2)}, u32[]{:S(2)}) collective-permute-start(bf16[32,16,512]{2,0,1:T(8,128)(2,1)S(1)} %collective-permute-done.24), channel_id=1, source_target_pairs={{0,4},{4,12},{12,20},{20,28},{28,24},{24,16},{16,8},{8,0},{1,5},{5... | collective-permute-start | bytes 1572872 | tf_op jit(solution)/shard_map/ppermute | solution.py:154
  (21 other events, 156.3 us)
Sparse Core Ops, SparseCore 0:
  271.6 33.2 all-reduce.4
  308.4 73.2 all-reduce.6
  586.3 36.2 all-reduce.8

commit v7 on v6

--- a/solution.py
+++ b/solution.py
@@ -91,9 +91,9 @@
     return [where[cell] for cell in cells]
 
 
-def ring_reduce_scatter(local, ring):
+def ring_reduce_scatter(local, total_rows, ring):
     n = len(ring)
-    rows = local.shape[0] // n
+    rows = total_rows // n
     half = rows // 2
     pos = [0] * n
     for p, i in enumerate(ring):
@@ -113,7 +113,7 @@
 
     def piece(block, offset, size):
         start = block * rows + offset
-        return lax.dynamic_slice_in_dim(local, start, size, axis=0)
+        return local(start, size)
 
     acc_f = piece(fwd_blocks[0, me], 0, half)
     acc_b = piece(bwd_blocks[0, me], half, rows - half)
@@ -165,12 +165,16 @@
         right_cores, sketch, (((2, 3), (0, 1)), ((), ())), preferred_element_type=jnp.float32
     )
     mapped = lax.psum(partial_map, "mode").astype(jnp.bfloat16)
-    local_sum = lax.dot_general(
-        left_cores, mapped, (((0, 3), (0, 1)), ((), ())), preferred_element_type=jnp.float32
-    )
-    local_sum = with_layout_constraint(local_sum, Layout(major_to_minor=(0, 1, 2)))
+
+    def local_rows(start, size):
+        part = lax.dynamic_slice_in_dim(left_cores, start, size, axis=1)
+        out = lax.dot_general(
+            part, mapped, (((0, 3), (0, 1)), ((), ())), preferred_element_type=jnp.float32
+        )
+        return with_layout_constraint(out, Layout(major_to_minor=(0, 1, 2)))
+
     factor = math.sqrt(R_IN * MODES)
-    share = ring_reduce_scatter(local_sum, ring)
+    share = ring_reduce_scatter(local_rows, rows_in, ring)
     flat_share = share.reshape(-1, target)
     gram_part = jnp.dot(flat_share.T, flat_share, precision=HI)
     gram = symmetric_psum(gram_part)

time: 642 us -> 611 us (0.952)
  waiting for transfers between devices: 343 us -> 296 us
  matrix products: 61.9 us -> 76.3 us
    ppermute x7, waiting for transfers between devices: 72.7 us -> 22.9 us  [ring_reduce_scatter(): lax.ppermute(acc_b, 'sum', bwd)]
    dot_general x1 -> x16, matrix products: 11.7 us -> 26 us  [local_rows(): lax.dot_general(part, mapped, (((0, 3), (0, 1)), ((), ())), preferred_ele...]
    add x7 -> x6, other arithmetic: 16.8 us -> 6.25 us  [ring_reduce_scatter(): acc_f = lax.ppermute(acc_f, 'sum', fwd) + piece(fwd_blocks[t, me], 0, half)]
    add x1 -> x6, other arithmetic: 1.43 us -> 10.5 us  [ring_reduce_scatter(): lax.ppermute(acc_b, 'sum', bwd)]
  transfers between devices with their start and end apart: 31 -> 31, of which waited for: 24 -> 25; matrix products, arithmetic and copies ran while one was open for 3% -> 10% of each run, Pallas kernels for 0% -> 0%
where the time goes in v7:
time: 611 us; the launch traced here: 601 us
  waiting for transfers between devices  296 us (48%)
  other arithmetic  114 us (19%)
  matrix products  76.3 us (12%)
  between operations  35.5 us (6%)
  starting transfers between devices  30 us (5%)
  blocking collectives  28 us (5%)
  local copies, waits for them, and re-layouts  20.1 us (3%)
    psum x2, waiting for transfers between devices, symmetric_psum(): packed = lax.psum(lax.psum(packed, 'mode'), 'sum')  91.1 us
    ppermute x7, waiting for transfers between devices, ring_reduce_scatter(): acc_f = lax.ppermute(acc_f, 'sum', fwd) + piece(fwd_blocks[t, me], 0, half)  88.3 us
    ppermute x7, waiting for transfers between devices, ring_gather_carries(): hold_b = lax.ppermute(hold_b, 'sum', bwd)  59.9 us
    another operation x12, other arithmetic, orthonormal(): lkk = jnp.linalg.cholesky(diag)  49.7 us
    another operation x8, other arithmetic, orthonormal(): ikk = lax.linalg.triangular_solve(lkk, eye, left_side=True, lower=True)  41.9 us
    psum x1, waiting for transfers between devices, per_device(): carries = lax.psum(partial_carry, 'mode')  33.2 us
    psum x1, blocking collectives, per_device(): mapped = lax.psum(partial_map, 'mode').astype(jnp.bfloat16)  28 us
    dot_general x16, matrix products, local_rows(): lax.dot_general(part, mapped, (((0, 3), (0, 1)), ((), ())), preferred_ele...  26 us
  transfers between devices with their start and end apart: 31, of which 25 were waited for; matrix products, arithmetic and copies ran while one was open for 10% of the time, Pallas kernels for 0%

profile of v7, /device:TPU:0, one launch (start us, length us, event | category | flops | bytes accessed | tf_op | source)
XLA Modules:
  0.0 600.8 jit_solution(13190673647253831884)
XLA Ops:
  9.6 17.1 %fusion.8 = f32[1,512,512]{2,1,0:T(8,128)S(1)} fusion(bf16[16,512,512]{2,1,0:T(8,128)(2,1)} %param.12, bf16[512,16,512]{2,1,0:T(8,128)(2,1)} %bitcast.413), kind=kOutput, calls=%fused_computation.29 | convolution fusion | flops 4294967296 | bytes 17825792 | tf_op jit(solution)/shard_map/dot_general | solution.py:164
  26.7 28.0 %all-reduce.10 = bf16[1,512,512]{2,1,0:T(8,128)(2,1)S(1)} all-reduce(f32[1,512,512]{2,1,0:T(8,128)S(1)} %fusion.8), channel_id=1, replica_groups=mesh['sum'=8,'mode'=4] {'mode'}, use_global_device_ids=true, to_apply=%region_0.0 | all-reduce | flops 262144 | bytes 1572864 | tf_op jit(solution)/shard_map/psum | solution.py:167
  62.7 19.0 %collective-permute-done = f32[32,16,512]{2,1,0:T(8,128)S(1)} collective-permute-done((f32[32,16,512]{2,1,0:T(8,128)S(1)}, f32[32,16,512]{2,1,0:T(8,128)S(1)}, u32[]{:S(2)}, u32[]{:S(2)}) %collective-permute-start) | collective-permute-done | bytes 1048608 | tf_op jit(solution)/shard_map/ppermute | solution.py:121
  93.9 14.1 %collective-permute-done.1 = f32[32,16,512]{2,1,0:T(8,128)S(1)} collective-permute-done((f32[32,16,512]{2,1,0:T(8,128)S(1)}, f32[32,16,512]{2,1,0:T(8,128)S(1)}, u32[]{:S(2)}, u32[]{:S(2)}) %collective-permute-start.1) | collective-permute-done | bytes 1048608 | tf_op jit(solution)/shard_map/ppermute | solution.py:121
  109.7 4.0 collective-permute-done.8
  120.0 12.3 %collective-permute-done.2 = f32[32,16,512]{2,1,0:T(8,128)} collective-permute-done((f32[32,16,512]{2,1,0:T(8,128)S(1)}, f32[32,16,512]{2,1,0:T(8,128)}, u32[]{:S(2)}, u32[]{:S(2)}) %collective-permute-start.2) | collective-permute-done | bytes 1048608 | tf_op jit(solution)/shard_map/ppermute | solution.py:121
  144.9 11.9 %collective-permute-done.3 = f32[32,16,512]{2,1,0:T(8,128)} collective-permute-done((f32[32,16,512]{2,1,0:T(8,128)S(1)}, f32[32,16,512]{2,1,0:T(8,128)}, u32[]{:S(2)}, u32[]{:S(2)}) %collective-permute-start.3) | collective-permute-done | bytes 1048608 | tf_op jit(solution)/shard_map/ppermute | solution.py:121
  169.2 11.3 %collective-permute-done.4 = f32[32,16,512]{2,1,0:T(8,128)} collective-permute-done((f32[32,16,512]{2,1,0:T(8,128)S(1)}, f32[32,16,512]{2,1,0:T(8,128)}, u32[]{:S(2)}, u32[]{:S(2)}) %collective-permute-start.4) | collective-permute-done | bytes 1048608 | tf_op jit(solution)/shard_map/ppermute | solution.py:121
  193.2 10.6 %collective-permute-done.5 = f32[32,16,512]{2,1,0:T(8,128)} collective-permute-done((f32[32,16,512]{2,1,0:T(8,128)S(1)}, f32[32,16,512]{2,1,0:T(8,128)}, u32[]{:S(2)}, u32[]{:S(2)}) %collective-permute-start.5) | collective-permute-done | bytes 1048608 | tf_op jit(solution)/shard_map/ppermute | solution.py:121
  216.7 9.0 %collective-permute-done.6 = f32[32,16,512]{2,1,0:T(8,128)S(1)} collective-permute-done((f32[32,16,512]{2,1,0:T(8,128)S(1)}, f32[32,16,512]{2,1,0:T(8,128)S(1)}, u32[]{:S(2)}, u32[]{:S(2)}) %collective-permute-start.6) | collective-permute-done | bytes 1048608 | tf_op jit(solution)/shard_map/ppermute | solution.py:121
  225.9 5.9 collective-permute-done.13
  234.3 3.6 convolution_bitcast_fusion.16
  239.0 33.4 %all-reduce.5.cloned.1.call-done = f32[10,128,128]{1,2,0:T(8,128)} async-done(((f32[10,128,128]{1,2,0:T(8,128)}), f32[10,128,128]{1,2,0:T(8,128)}) %all-reduce.5.cloned.1.call-update) | async-done | bytes 655376 | tf_op jit(solution)/shard_map/psum | solution.py:57
  283.8 6.2 %constant_dynamic-slice_fusion.1 = (bf16[1,32,16,512]{3,2,1,0:T(8,128)(2,1)}, bf16[1,32,16,512]{3,2,1,0:T(8,128)(2,1)}, bf16[1,32,16,512]{3,2,1,0:T(8,128)(2,1)}...) fusion(bf16[1,512,16,512]{3,2,1,0:T(8,128)(2,1)} %param.10, ...), kind=kLoop, calls=%fused_computation.260 | loop fusion | bytes 14680120 | tf_op jit(solution)/shard_map/dynamic_slice | solution.py:145
  291.4 57.7 %all-reduce.7.cloned.1.call-done = f32[10,128,128]{1,2,0:T(8,128)} async-done(((f32[10,128,128]{1,2,0:T(8,128)}), f32[10,128,128]{1,2,0:T(8,128)}) %all-reduce.7.cloned.1.call-update) | async-done | bytes 655376 | tf_op jit(solution)/shard_map/psum | solution.py:57
  351.3 11.7 %cholesky.74 = f32[128,128]{1,0:T(8,128)S(1)} custom-call(f32[128,128]{1,0:T(8,128)S(1)} %fusion.187), custom_call_target="Cholesky" | custom-call | tf_op jit(solution)/shard_map/jit(cholesky)/cholesky | solution.py:31
  364.3 9.8 %custom-call.8 = f32[1,128,128]{1,2,0:T(8,128)S(1)} custom-call(f32[1,128,128]{2,1,0:T(8,128)S(1)} %fusion.169), custom_call_target="InvertDiagBlocksLowerTriangular" | custom-call | tf_op jit(solution)/shard_map/triangular_solve/custom-call.0 | solution.py:32
  377.8 11.9 %cholesky.85 = f32[128,128]{1,0:T(8,128)S(1)} custom-call(f32[128,128]{1,0:T(8,128)S(1)} %fusion.193), custom_call_target="Cholesky" | custom-call | tf_op jit(solution)/shard_map/jit(cholesky)/cholesky | solution.py:31
  391.0 9.8 %custom-call.9 = f32[1,128,128]{1,2,0:T(8,128)S(1)} custom-call(f32[1,128,128]{2,1,0:T(8,128)S(1)} %fusion.170), custom_call_target="InvertDiagBlocksLowerTriangular" | custom-call | tf_op jit(solution)/shard_map/triangular_solve/custom-call.0 | solution.py:32
  406.7 11.7 %cholesky.96 = f32[128,128]{1,0:T(8,128)S(1)} custom-call(f32[128,128]{1,0:T(8,128)S(1)} %fusion.191), custom_call_target="Cholesky" | custom-call | tf_op jit(solution)/shard_map/jit(cholesky)/cholesky | solution.py:31
  419.8 9.8 %custom-call.10 = f32[1,128,128]{1,2,0:T(8,128)S(1)} custom-call(f32[1,128,128]{2,1,0:T(8,128)S(1)} %fusion.171), custom_call_target="InvertDiagBlocksLowerTriangular" | custom-call | tf_op jit(solution)/shard_map/triangular_solve/custom-call.0 | solution.py:32
  434.8 11.7 %cholesky.107 = f32[128,128]{1,0:T(8,128)S(1)} custom-call(f32[128,128]{1,0:T(8,128)S(1)} %fusion.189), custom_call_target="Cholesky" | custom-call | tf_op jit(solution)/shard_map/jit(cholesky)/cholesky | solution.py:31
  447.9 9.8 %custom-call.11 = f32[1,128,128]{1,2,0:T(8,128)S(1)} custom-call(f32[1,128,128]{2,1,0:T(8,128)S(1)} %fusion.172), custom_call_target="InvertDiagBlocksLowerTriangular" | custom-call | tf_op jit(solution)/shard_map/triangular_solve/custom-call.0 | solution.py:32
  458.0 3.7 fusion.2
  472.3 8.2 %collective-permute-done.15 = bf16[32,16,512]{2,0,1:T(8,128)(2,1)S(1)} collective-permute-done((bf16[32,16,512]{2,0,1:T(8,128)(2,1)S(1)}, bf16[32,16,512]{2,0,1:T(8,128)(2,1)S(1)}, u32[]{:S(2)}, u32[]{:S(2)}) %collective-permute-start.15) | collective-permute-done | bytes 524320 | tf_op jit(solution)/shard_map/ppermute | solution.py:155
  483.8 8.7 %collective-permute-done.17 = bf16[32,16,512]{2,0,1:T(8,128)(2,1)S(1)} collective-permute-done((bf16[32,16,512]{2,0,1:T(8,128)(2,1)S(1)}, bf16[32,16,512]{2,0,1:T(8,128)(2,1)S(1)}, u32[]{:S(2)}, u32[]{:S(2)}) %collective-permute-start.17) | collective-permute-done | bytes 524320 | tf_op jit(solution)/shard_map/ppermute | solution.py:155
  495.8 8.8 %collective-permute-done.19 = bf16[32,16,512]{2,0,1:T(8,128)(2,1)S(1)} collective-permute-done((bf16[32,16,512]{2,0,1:T(8,128)(2,1)S(1)}, bf16[32,16,512]{2,0,1:T(8,128)(2,1)S(1)}, u32[]{:S(2)}, u32[]{:S(2)}) %collective-permute-start.19) | collective-permute-done | bytes 524320 | tf_op jit(solution)/shard_map/ppermute | solution.py:155
  507.9 8.8 %collective-permute-done.21 = bf16[32,16,512]{2,0,1:T(8,128)(2,1)S(1)} collective-permute-done((bf16[32,16,512]{2,0,1:T(8,128)(2,1)S(1)}, bf16[32,16,512]{2,0,1:T(8,128)(2,1)S(1)}, u32[]{:S(2)}, u32[]{:S(2)}) %collective-permute-start.21) | collective-permute-done | bytes 524320 | tf_op jit(solution)/shard_map/ppermute | solution.py:155
  520.0 9.2 %collective-permute-done.23 = bf16[32,16,512]{2,0,1:T(8,128)(2,1)S(1)} collective-permute-done((bf16[32,16,512]{2,0,1:T(8,128)(2,1)S(1)}, bf16[32,16,512]{2,0,1:T(8,128)(2,1)S(1)}, u32[]{:S(2)}, u32[]{:S(2)}) %collective-permute-start.23) | collective-permute-done | bytes 524320 | tf_op jit(solution)/shard_map/ppermute | solution.py:155
  532.5 10.3 %collective-permute-done.25 = bf16[32,16,512]{2,0,1:T(8,128)(2,1)S(1)} collective-permute-done((bf16[32,16,512]{2,0,1:T(8,128)(2,1)S(1)}, bf16[32,16,512]{2,0,1:T(8,128)(2,1)S(1)}, u32[]{:S(2)}, u32[]{:S(2)}) %collective-permute-start.25) | collective-permute-done | bytes 524320 | tf_op jit(solution)/shard_map/ppermute | solution.py:155
  546.1 5.9 collective-permute-done.27
  558.5 33.2 %all-reduce.9.cloned.1.call-done = f32[1,512,512]{2,1,0:T(8,128)} async-done(((f32[1,512,512]{2,1,0:T(8,128)}), f32[1,512,512]{2,1,0:T(8,128)}) %all-reduce.9.cloned.1.call-update) | async-done | bytes 1048592 | tf_op jit(solution)/shard_map/psum | solution.py:185
  (199 shorter events, 138.1 us)
Async XLA Ops:
  7.2 265.2 %all-reduce.5.cloned.1.call-start = ((), (), s32[]{:S(2)}) async-start(), calls=%async_computation | async-start | bytes 1310720 | tf_op jit(solution)/shard_map/psum | solution.py:57
  56.2 25.5 %collective-permute-start = (f32[32,16,512]{2,1,0:T(8,128)S(1)}, f32[32,16,512]{2,1,0:T(8,128)S(1)}, u32[]{:S(2)}, u32[]{:S(2)}) collective-permute-start(f32[32,16,512]{2,1,0:T(8,128)S(1)} %fusion.98), channel_id=1, source_target_pairs={{0,4},{4,12},{12,20},{20,28},{28,24},{24,16},{16,8},{8,0},{1,5},{5... | collective-permute-start | bytes 3145736 | tf_op jit(solution)/shard_map/ppermute | solution.py:121
  60.9 25.5 %collective-permute-start.7 = (f32[32,16,512]{2,1,0:T(8,128)}, f32[32,16,512]{2,1,0:T(8,128)}, u32[]{:S(2)}, u32[]{:S(2)}) collective-permute-start(f32[32,16,512]{2,1,0:T(8,128)} %fusion.68), channel_id=1, source_target_pairs={{0,8},{4,0},{12,4},{20,12},{28,20},{24,28},{16,24},{8,16},{1,9},{5... | collective-permute-start | bytes 3145736 | tf_op jit(solution)/shard_map/ppermute | solution.py:122
  83.2 24.8 %collective-permute-start.1 = (f32[32,16,512]{2,1,0:T(8,128)S(1)}, f32[32,16,512]{2,1,0:T(8,128)S(1)}, u32[]{:S(2)}, u32[]{:S(2)}) collective-permute-start(f32[32,16,512]{2,1,0:T(8,128)S(1)} %convolution_add_fusion.1), channel_id=1, source_target_pairs={{0,4},{4,12},{12,20},{20,28},{28,24},{24,16},{16,8},{8,0},{1,5},{5... | collective-permute-start | bytes 3145736 | tf_op jit(solution)/shard_map/ppermute | solution.py:121
  89.1 24.6 %collective-permute-start.8 = (f32[32,16,512]{2,1,0:T(8,128)}, f32[32,16,512]{2,1,0:T(8,128)}, u32[]{:S(2)}, u32[]{:S(2)}) collective-permute-start(f32[32,16,512]{2,1,0:T(8,128)} %convolution_add_fusion), channel_id=1, source_target_pairs={{0,8},{4,0},{12,4},{20,12},{28,20},{24,28},{16,24},{8,16},{1,9},{5... | collective-permute-start | bytes 3145736 | tf_op jit(solution)/shard_map/ppermute | solution.py:122
  108.2 24.1 %collective-permute-start.2 = (f32[32,16,512]{2,1,0:T(8,128)S(1)}, f32[32,16,512]{2,1,0:T(8,128)}, u32[]{:S(2)}, u32[]{:S(2)}) collective-permute-start(f32[32,16,512]{2,1,0:T(8,128)S(1)} %add.429), channel_id=1, source_target_pairs={{0,4},{4,12},{12,20},{20,28},{28,24},{24,16},{16,8},{8,0},{1,5},{5... | collective-permute-start | bytes 3145736 | tf_op jit(solution)/shard_map/ppermute | solution.py:121
  115.2 23.5 %collective-permute-start.9 = (f32[32,16,512]{2,1,0:T(8,128)S(1)}, f32[32,16,512]{2,1,0:T(8,128)}, u32[]{:S(2)}, u32[]{:S(2)}) collective-permute-start(f32[32,16,512]{2,1,0:T(8,128)S(1)} %add.453), channel_id=1, source_target_pairs={{0,8},{4,0},{12,4},{20,12},{28,20},{24,28},{16,24},{8,16},{1,9},{5... | collective-permute-start | bytes 3145736 | tf_op jit(solution)/shard_map/ppermute | solution.py:122
  133.7 23.2 %collective-permute-start.3 = (f32[32,16,512]{2,1,0:T(8,128)S(1)}, f32[32,16,512]{2,1,0:T(8,128)}, u32[]{:S(2)}, u32[]{:S(2)}) collective-permute-start(f32[32,16,512]{2,1,0:T(8,128)S(1)} %add.431), channel_id=1, source_target_pairs={{0,4},{4,12},{12,20},{20,28},{28,24},{24,16},{16,8},{8,0},{1,5},{5... | collective-permute-start | bytes 3145736 | tf_op jit(solution)/shard_map/ppermute | solution.py:121
  140.1 22.6 %collective-permute-start.10 = (f32[32,16,512]{2,1,0:T(8,128)S(1)}, f32[32,16,512]{2,1,0:T(8,128)}, u32[]{:S(2)}, u32[]{:S(2)}) collective-permute-start(f32[32,16,512]{2,1,0:T(8,128)S(1)} %add.458), channel_id=1, source_target_pairs={{0,8},{4,0},{12,4},{20,12},{28,20},{24,28},{16,24},{8,16},{1,9},{5... | collective-permute-start | bytes 3145736 | tf_op jit(solution)/shard_map/ppermute | solution.py:122
  158.3 22.2 %collective-permute-start.4 = (f32[32,16,512]{2,1,0:T(8,128)S(1)}, f32[32,16,512]{2,1,0:T(8,128)}, u32[]{:S(2)}, u32[]{:S(2)}) collective-permute-start(f32[32,16,512]{2,1,0:T(8,128)S(1)} %add.433), channel_id=1, source_target_pairs={{0,4},{4,12},{12,20},{20,28},{28,24},{24,16},{16,8},{8,0},{1,5},{5... | collective-permute-start | bytes 3145736 | tf_op jit(solution)/shard_map/ppermute | solution.py:121
  164.2 21.9 %collective-permute-start.11 = (f32[32,16,512]{2,1,0:T(8,128)S(1)}, f32[32,16,512]{2,1,0:T(8,128)}, u32[]{:S(2)}, u32[]{:S(2)}) collective-permute-start(f32[32,16,512]{2,1,0:T(8,128)S(1)} %add.463), channel_id=1, source_target_pairs={{0,8},{4,0},{12,4},{20,12},{28,20},{24,28},{16,24},{8,16},{1,9},{5... | collective-permute-start | bytes 3145736 | tf_op jit(solution)/shard_map/ppermute | solution.py:122
  182.0 21.9 %collective-permute-start.5 = (f32[32,16,512]{2,1,0:T(8,128)S(1)}, f32[32,16,512]{2,1,0:T(8,128)}, u32[]{:S(2)}, u32[]{:S(2)}) collective-permute-start(f32[32,16,512]{2,1,0:T(8,128)S(1)} %add.435), channel_id=1, source_target_pairs={{0,4},{4,12},{12,20},{20,28},{28,24},{24,16},{16,8},{8,0},{1,5},{5... | collective-permute-start | bytes 3145736 | tf_op jit(solution)/shard_map/ppermute | solution.py:121
  188.5 20.9 %collective-permute-start.12 = (f32[32,16,512]{2,1,0:T(8,128)}, f32[32,16,512]{2,1,0:T(8,128)}, u32[]{:S(2)}, u32[]{:S(2)}) collective-permute-start(f32[32,16,512]{2,1,0:T(8,128)} %add.468), channel_id=1, source_target_pairs={{0,8},{4,0},{12,4},{20,12},{28,20},{24,28},{16,24},{8,16},{1,9},{5... | collective-permute-start | bytes 3145736 | tf_op jit(solution)/shard_map/ppermute | solution.py:122
  205.3 20.4 %collective-permute-start.6 = (f32[32,16,512]{2,1,0:T(8,128)S(1)}, f32[32,16,512]{2,1,0:T(8,128)S(1)}, u32[]{:S(2)}, u32[]{:S(2)}) collective-permute-start(f32[32,16,512]{2,1,0:T(8,128)S(1)} %add.437), channel_id=1, source_target_pairs={{0,4},{4,12},{12,20},{20,28},{28,24},{24,16},{16,8},{8,0},{1,5},{5... | collective-permute-start | bytes 3145736 | tf_op jit(solution)/shard_map/ppermute | solution.py:121
  211.8 61.1 %copy-start.19 = (s32[8,8]{1,0:T(8,128)S(1)}, s32[8,8]{1,0:T(8,128)}, u32[]{:S(2)}) copy-start(s32[8,8]{1,0:T(8,128)} %constant.153.clone) | copy-start | bytes 772
  211.8 20.1 %collective-permute-start.13 = (f32[32,16,512]{2,1,0:T(8,128)}, f32[32,16,512]{2,1,0:T(8,128)}, u32[]{:S(2)}, u32[]{:S(2)}) collective-permute-start(f32[32,16,512]{2,1,0:T(8,128)} %add.473), channel_id=1, source_target_pairs={{0,8},{4,0},{12,4},{20,12},{28,20},{24,28},{16,24},{8,16},{1,9},{5... | collective-permute-start | bytes 3145736 | tf_op jit(solution)/shard_map/ppermute | solution.py:122
  238.9 110.2 %all-reduce.7.cloned.1.call-start = ((), (), s32[]{:S(2)}) async-start(), calls=%async_computation.1 | async-start | bytes 1310720 | tf_op jit(solution)/shard_map/psum | solution.py:57
  272.4 319.2 %all-reduce.9.cloned.1.call-start = ((), (), s32[]{:S(2)}) async-start(), calls=%async_computation.2 | async-start | bytes 2097152 | tf_op jit(solution)/shard_map/psum | solution.py:185
  468.0 12.5 %collective-permute-start.15 = (bf16[32,16,512]{2,0,1:T(8,128)(2,1)S(1)}, bf16[32,16,512]{2,0,1:T(8,128)(2,1)S(1)}, u32[]{:S(2)}, u32[]{:S(2)}) collective-permute-start(bf16[32,16,512]{2,0,1:T(8,128)(2,1)S(1)} %copy.91), channel_id=1, source_target_pairs={{0,8},{4,0},{12,4},{20,12},{28,20},{24,28},{16,24},{8,16},{1,9},{5... | collective-permute-start | bytes 1572872 | tf_op jit(solution)/shard_map/ppermute | solution.py:155
  469.2 12.9 %collective-permute-start.14 = (bf16[32,16,512]{2,0,1:T(8,128)(2,1)S(1)}, bf16[32,16,512]{2,0,1:T(8,128)(2,1)S(1)}, u32[]{:S(2)}, u32[]{:S(2)}) collective-permute-start(bf16[32,16,512]{2,0,1:T(8,128)(2,1)S(1)} %copy.89), channel_id=1, source_target_pairs={{0,4},{4,12},{12,20},{20,28},{28,24},{24,16},{16,8},{8,0},{1,5},{5... | collective-permute-start | bytes 1572872 | tf_op jit(solution)/shard_map/ppermute | solution.py:154
  480.4 12.1 %collective-permute-start.17 = (bf16[32,16,512]{2,0,1:T(8,128)(2,1)S(1)}, bf16[32,16,512]{2,0,1:T(8,128)(2,1)S(1)}, u32[]{:S(2)}, u32[]{:S(2)}) collective-permute-start(bf16[32,16,512]{2,0,1:T(8,128)(2,1)S(1)} %collective-permute-done.15), channel_id=1, source_target_pairs={{0,8},{4,0},{12,4},{20,12},{28,20},{24,28},{16,24},{8,16},{1,9},{5... | collective-permute-start | bytes 1572872 | tf_op jit(solution)/shard_map/ppermute | solution.py:155
  482.1 12.1 %collective-permute-start.16 = (bf16[32,16,512]{2,0,1:T(8,128)(2,1)S(1)}, bf16[32,16,512]{2,0,1:T(8,128)(2,1)S(1)}, u32[]{:S(2)}, u32[]{:S(2)}) collective-permute-start(bf16[32,16,512]{2,0,1:T(8,128)(2,1)S(1)} %collective-permute-done.14), channel_id=1, source_target_pairs={{0,4},{4,12},{12,20},{20,28},{28,24},{24,16},{16,8},{8,0},{1,5},{5... | collective-permute-start | bytes 1572872 | tf_op jit(solution)/shard_map/ppermute | solution.py:154
  492.5 12.1 %collective-permute-start.19 = (bf16[32,16,512]{2,0,1:T(8,128)(2,1)S(1)}, bf16[32,16,512]{2,0,1:T(8,128)(2,1)S(1)}, u32[]{:S(2)}, u32[]{:S(2)}) collective-permute-start(bf16[32,16,512]{2,0,1:T(8,128)(2,1)S(1)} %collective-permute-done.17), channel_id=1, source_target_pairs={{0,8},{4,0},{12,4},{20,12},{28,20},{24,28},{16,24},{8,16},{1,9},{5... | collective-permute-start | bytes 1572872 | tf_op jit(solution)/shard_map/ppermute | solution.py:155
  494.2 12.1 %collective-permute-start.18 = (bf16[32,16,512]{2,0,1:T(8,128)(2,1)S(1)}, bf16[32,16,512]{2,0,1:T(8,128)(2,1)S(1)}, u32[]{:S(2)}, u32[]{:S(2)}) collective-permute-start(bf16[32,16,512]{2,0,1:T(8,128)(2,1)S(1)} %collective-permute-done.16), channel_id=1, source_target_pairs={{0,4},{4,12},{12,20},{20,28},{28,24},{24,16},{16,8},{8,0},{1,5},{5... | collective-permute-start | bytes 1572872 | tf_op jit(solution)/shard_map/ppermute | solution.py:154
  504.6 12.1 %collective-permute-start.21 = (bf16[32,16,512]{2,0,1:T(8,128)(2,1)S(1)}, bf16[32,16,512]{2,0,1:T(8,128)(2,1)S(1)}, u32[]{:S(2)}, u32[]{:S(2)}) collective-permute-start(bf16[32,16,512]{2,0,1:T(8,128)(2,1)S(1)} %collective-permute-done.19), channel_id=1, source_target_pairs={{0,8},{4,0},{12,4},{20,12},{28,20},{24,28},{16,24},{8,16},{1,9},{5... | collective-permute-start | bytes 1572872 | tf_op jit(solution)/shard_map/ppermute | solution.py:155
  506.3 12.1 %collective-permute-start.20 = (bf16[32,16,512]{2,0,1:T(8,128)(2,1)S(1)}, bf16[32,16,512]{2,0,1:T(8,128)(2,1)S(1)}, u32[]{:S(2)}, u32[]{:S(2)}) collective-permute-start(bf16[32,16,512]{2,0,1:T(8,128)(2,1)S(1)} %collective-permute-done.18), channel_id=1, source_target_pairs={{0,4},{4,12},{12,20},{20,28},{28,24},{24,16},{16,8},{8,0},{1,5},{5... | collective-permute-start | bytes 1572872 | tf_op jit(solution)/shard_map/ppermute | solution.py:154
  516.7 12.5 %collective-permute-start.23 = (bf16[32,16,512]{2,0,1:T(8,128)(2,1)S(1)}, bf16[32,16,512]{2,0,1:T(8,128)(2,1)S(1)}, u32[]{:S(2)}, u32[]{:S(2)}) collective-permute-start(bf16[32,16,512]{2,0,1:T(8,128)(2,1)S(1)} %collective-permute-done.21), channel_id=1, source_target_pairs={{0,8},{4,0},{12,4},{20,12},{28,20},{24,28},{16,24},{8,16},{1,9},{5... | collective-permute-start | bytes 1572872 | tf_op jit(solution)/shard_map/ppermute | solution.py:155
  518.4 12.5 %collective-permute-start.22 = (bf16[32,16,512]{2,0,1:T(8,128)(2,1)S(1)}, bf16[32,16,512]{2,0,1:T(8,128)(2,1)S(1)}, u32[]{:S(2)}, u32[]{:S(2)}) collective-permute-start(bf16[32,16,512]{2,0,1:T(8,128)(2,1)S(1)} %collective-permute-done.20), channel_id=1, source_target_pairs={{0,4},{4,12},{12,20},{20,28},{28,24},{24,16},{16,8},{8,0},{1,5},{5... | collective-permute-start | bytes 1572872 | tf_op jit(solution)/shard_map/ppermute | solution.py:154
  529.2 13.6 %collective-permute-start.25 = (bf16[32,16,512]{2,0,1:T(8,128)(2,1)S(1)}, bf16[32,16,512]{2,0,1:T(8,128)(2,1)S(1)}, u32[]{:S(2)}, u32[]{:S(2)}) collective-permute-start(bf16[32,16,512]{2,0,1:T(8,128)(2,1)S(1)} %collective-permute-done.23), channel_id=1, source_target_pairs={{0,8},{4,0},{12,4},{20,12},{28,20},{24,28},{16,24},{8,16},{1,9},{5... | collective-permute-start | bytes 1572872 | tf_op jit(solution)/shard_map/ppermute | solution.py:155
  530.8 13.5 %collective-permute-start.24 = (bf16[32,16,512]{2,0,1:T(8,128)(2,1)S(1)}, bf16[32,16,512]{2,0,1:T(8,128)(2,1)S(1)}, u32[]{:S(2)}, u32[]{:S(2)}) collective-permute-start(bf16[32,16,512]{2,0,1:T(8,128)(2,1)S(1)} %collective-permute-done.22), channel_id=1, source_target_pairs={{0,4},{4,12},{12,20},{20,28},{28,24},{24,16},{16,8},{8,0},{1,5},{5... | collective-permute-start | bytes 1572872 | tf_op jit(solution)/shard_map/ppermute | solution.py:154
  542.8 9.2 %collective-permute-start.27 = (bf16[32,16,512]{2,0,1:T(8,128)(2,1)S(1)}, bf16[32,16,512]{2,0,1:T(8,128)(2,1)S(1)}, u32[]{:S(2)}, u32[]{:S(2)}) collective-permute-start(bf16[32,16,512]{2,0,1:T(8,128)(2,1)S(1)} %collective-permute-done.25), channel_id=1, source_target_pairs={{0,8},{4,0},{12,4},{20,12},{28,20},{24,28},{16,24},{8,16},{1,9},{5... | collective-permute-start | bytes 1572872 | tf_op jit(solution)/shard_map/ppermute | solution.py:155
  544.3 9.2 %collective-permute-start.26 = (bf16[32,16,512]{2,0,1:T(8,128)(2,1)S(1)}, bf16[32,16,512]{2,0,1:T(8,128)(2,1)S(1)}, u32[]{:S(2)}, u32[]{:S(2)}) collective-permute-start(bf16[32,16,512]{2,0,1:T(8,128)(2,1)S(1)} %collective-permute-done.24), channel_id=1, source_target_pairs={{0,4},{4,12},{12,20},{20,28},{28,24},{24,16},{16,8},{8,0},{1,5},{5... | collective-permute-start | bytes 1572872 | tf_op jit(solution)/shard_map/ppermute | solution.py:154
  (19 other events, 298.7 us)
Sparse Core Ops, SparseCore 0:
  239.0 33.2 all-reduce.4
  275.8 73.2 all-reduce.6
  555.3 36.2 all-reduce.8

commit v8 on v7

--- a/solution.py
+++ b/solution.py
@@ -16,6 +16,17 @@
 
 def mm(a, b):
     return jnp.dot(a, b, precision=HI, preferred_element_type=jnp.float32)
+
+
+def tri_inverse(lower):
+    n = lower.shape[0]
+    h = n // 2
+    diag = jnp.stack([lower[:h, :h], lower[h:, h:]])
+    eye = jnp.broadcast_to(jnp.eye(h, dtype=jnp.float32), diag.shape)
+    inv = lax.linalg.triangular_solve(diag, eye, left_side=True, lower=True)
+    corner = -mm(inv[1], mm(lower[h:, :h], inv[0]))
+    top = jnp.concatenate([inv[0], jnp.zeros((h, n - h), jnp.float32)], axis=1)
+    return jnp.concatenate([top, jnp.concatenate([corner, inv[1]], axis=1)], axis=0)
 
 
 def orthonormal(sketched, gram):
@@ -29,7 +40,7 @@
     for k in range(nb):
         diag = trailing[:b, :b]
         lkk = jnp.linalg.cholesky(diag)
-        ikk = lax.linalg.triangular_solve(lkk, eye, left_side=True, lower=True)
+        ikk = tri_inverse(lkk)
         inverses.append(ikk)
         if k < nb - 1:
             panel = mm(trailing[b:, :b], ikk.T)

time: 611 us -> 609 us (level)
    another operation x8 -> x9, other arithmetic: 41.9 us -> 40 us  [tri_inverse(): inv = lax.linalg.triangular_solve(diag, eye, left_side=True, lower=True)]
    dot_general x13 -> x21, matrix products: 14.9 us -> 13.5 us  [mm(): return jnp.dot(a, b, precision=HI, preferred_element_type=jnp.float32)]
where the time goes in v8:
time: 609 us; the launch traced here: 598 us
  waiting for transfers between devices  297 us (49%)
  other arithmetic  114 us (19%)
  matrix products  75 us (12%)
  between operations  35.1 us (6%)
  starting transfers between devices  29.8 us (5%)
  blocking collectives  28 us (5%)
  local copies, waits for them, and re-layouts  19.4 us (3%)
    psum x2, waiting for transfers between devices, symmetric_psum(): packed = lax.psum(lax.psum(packed, 'mode'), 'sum')  91.9 us
    ppermute x7, waiting for transfers between devices, ring_reduce_scatter(): acc_f = lax.ppermute(acc_f, 'sum', fwd) + piece(fwd_blocks[t, me], 0, half)  88.5 us
    ppermute x7, waiting for transfers between devices, ring_gather_carries(): hold_b = lax.ppermute(hold_b, 'sum', bwd)  59.6 us
    another operation x12, other arithmetic, orthonormal(): lkk = jnp.linalg.cholesky(diag)  49.6 us
    another operation x9, other arithmetic, tri_inverse(): inv = lax.linalg.triangular_solve(diag, eye, left_side=True, lower=True)  40 us
    psum x1, waiting for transfers between devices, per_device(): carries = lax.psum(partial_carry, 'mode')  33 us
    psum x1, blocking collectives, per_device(): mapped = lax.psum(partial_map, 'mode').astype(jnp.bfloat16)  28 us
    dot_general x16, matrix products, local_rows(): lax.dot_general(part, mapped, (((0, 3), (0, 1)), ((), ())), preferred_ele...  26 us
  transfers between devices with their start and end apart: 31, of which 25 were waited for; matrix products, arithmetic and copies ran while one was open for 10% of the time, Pallas kernels for 0%

profile of v8, /device:TPU:0, one launch (start us, length us, event | category | flops | bytes accessed | tf_op | source)
XLA Modules:
  0.0 598.3 jit_solution(6445833536353612595)
XLA Ops:
  9.6 17.1 %fusion.8 = f32[1,512,512]{2,1,0:T(8,128)S(1)} fusion(bf16[16,512,512]{2,1,0:T(8,128)(2,1)} %param.12, bf16[512,16,512]{2,1,0:T(8,128)(2,1)} %bitcast.450), kind=kOutput, calls=%fused_computation.29 | convolution fusion | flops 4294967296 | bytes 17825792 | tf_op jit(solution)/shard_map/dot_general | solution.py:175
  26.7 28.0 %all-reduce.14 = bf16[1,512,512]{2,1,0:T(8,128)(2,1)S(1)} all-reduce(f32[1,512,512]{2,1,0:T(8,128)S(1)} %fusion.8), channel_id=1, replica_groups=mesh['sum'=8,'mode'=4] {'mode'}, use_global_device_ids=true, to_apply=%region_0.0 | all-reduce | flops 262144 | bytes 1572864 | tf_op jit(solution)/shard_map/psum | solution.py:178
  62.6 19.1 %collective-permute-done = f32[32,16,512]{2,1,0:T(8,128)S(1)} collective-permute-done((f32[32,16,512]{2,1,0:T(8,128)S(1)}, f32[32,16,512]{2,1,0:T(8,128)S(1)}, u32[]{:S(2)}, u32[]{:S(2)}) %collective-permute-start) | collective-permute-done | bytes 1048608 | tf_op jit(solution)/shard_map/ppermute | solution.py:132
  93.8 14.1 %collective-permute-done.1 = f32[32,16,512]{2,1,0:T(8,128)S(1)} collective-permute-done((f32[32,16,512]{2,1,0:T(8,128)S(1)}, f32[32,16,512]{2,1,0:T(8,128)S(1)}, u32[]{:S(2)}, u32[]{:S(2)}) %collective-permute-start.1) | collective-permute-done | bytes 1048608 | tf_op jit(solution)/shard_map/ppermute | solution.py:132
  109.7 4.0 collective-permute-done.8
  120.0 12.3 %collective-permute-done.2 = f32[32,16,512]{2,1,0:T(8,128)} collective-permute-done((f32[32,16,512]{2,1,0:T(8,128)S(1)}, f32[32,16,512]{2,1,0:T(8,128)}, u32[]{:S(2)}, u32[]{:S(2)}) %collective-permute-start.2) | collective-permute-done | bytes 1048608 | tf_op jit(solution)/shard_map/ppermute | solution.py:132
  135.2 3.4 collective-permute-done.9
  144.9 12.0 %collective-permute-done.3 = f32[32,16,512]{2,1,0:T(8,128)} collective-permute-done((f32[32,16,512]{2,1,0:T(8,128)S(1)}, f32[32,16,512]{2,1,0:T(8,128)}, u32[]{:S(2)}, u32[]{:S(2)}) %collective-permute-start.3) | collective-permute-done | bytes 1048608 | tf_op jit(solution)/shard_map/ppermute | solution.py:132
  169.2 11.3 %collective-permute-done.4 = f32[32,16,512]{2,1,0:T(8,128)} collective-permute-done((f32[32,16,512]{2,1,0:T(8,128)S(1)}, f32[32,16,512]{2,1,0:T(8,128)}, u32[]{:S(2)}, u32[]{:S(2)}) %collective-permute-start.4) | collective-permute-done | bytes 1048608 | tf_op jit(solution)/shard_map/ppermute | solution.py:132
  193.2 10.7 %collective-permute-done.5 = f32[32,16,512]{2,1,0:T(8,128)} collective-permute-done((f32[32,16,512]{2,1,0:T(8,128)S(1)}, f32[32,16,512]{2,1,0:T(8,128)}, u32[]{:S(2)}, u32[]{:S(2)}) %collective-permute-start.5) | collective-permute-done | bytes 1048608 | tf_op jit(solution)/shard_map/ppermute | solution.py:132
  216.6 9.0 %collective-permute-done.6 = f32[32,16,512]{2,1,0:T(8,128)S(1)} collective-permute-done((f32[32,16,512]{2,1,0:T(8,128)S(1)}, f32[32,16,512]{2,1,0:T(8,128)S(1)}, u32[]{:S(2)}, u32[]{:S(2)}) %collective-permute-start.6) | collective-permute-done | bytes 1048608 | tf_op jit(solution)/shard_map/ppermute | solution.py:132
  225.9 5.9 collective-permute-done.13
  234.3 3.6 convolution_bitcast_fusion.16
  249.6 22.7 %all-reduce.9.cloned.1.call-done = f32[10,128,128]{1,2,0:T(8,128)} async-done(((f32[10,128,128]{1,2,0:T(8,128)}), f32[10,128,128]{1,2,0:T(8,128)}) %all-reduce.9.cloned.1.call-update) | async-done | bytes 655376 | tf_op jit(solution)/shard_map/psum | solution.py:68
  272.5 6.1 %constant_dynamic-slice_fusion.1 = (bf16[1,32,16,512]{3,2,1,0:T(8,128)(2,1)}, bf16[1,32,16,512]{3,2,1,0:T(8,128)(2,1)}, bf16[1,32,16,512]{3,2,1,0:T(8,128)(2,1)}...) fusion(bf16[1,512,16,512]{3,2,1,0:T(8,128)(2,1)} %param.10, ...), kind=kLoop, calls=%fused_computation.306 | loop fusion | bytes 14680120 | tf_op jit(solution)/shard_map/dynamic_slice | solution.py:156
  280.0 69.1 %all-reduce.11.cloned.1.call-done = f32[10,128,128]{1,2,0:T(8,128)} async-done(((f32[10,128,128]{1,2,0:T(8,128)}), f32[10,128,128]{1,2,0:T(8,128)}) %all-reduce.11.cloned.1.call-update) | async-done | bytes 655376 | tf_op jit(solution)/shard_map/psum | solution.py:68
  351.3 11.7 %cholesky.74 = f32[128,128]{1,0:T(8,128)S(1)} custom-call(f32[128,128]{1,0:T(8,128)S(1)} %fusion.183), custom_call_target="Cholesky" | custom-call | tf_op jit(solution)/shard_map/jit(cholesky)/cholesky | solution.py:42
  364.4 10.3 %custom-call.8 = f32[2,1,64,64]{2,3,1,0:T(8,128)S(1)} custom-call(f32[2,1,64,64]{3,2,1,0:T(8,128)S(1)} %fusion.176), custom_call_target="InvertDiagBlocksLowerTriangular" | custom-call | tf_op jit(solution)/shard_map/triangular_solve/custom-call.0 | solution.py:26
  378.8 11.7 %cholesky.85 = f32[128,128]{1,0:T(8,128)S(1)} custom-call(f32[128,128]{1,0:T(8,128)S(1)} %fusion.192), custom_call_target="Cholesky" | custom-call | tf_op jit(solution)/shard_map/jit(cholesky)/cholesky | solution.py:42
  391.9 9.8 %custom-call.9 = f32[2,1,64,64]{2,3,1,0:T(8,128)S(1)} custom-call(f32[2,1,64,64]{3,2,1,0:T(8,128)S(1)} %fusion.177), custom_call_target="InvertDiagBlocksLowerTriangular" | custom-call | tf_op jit(solution)/shard_map/triangular_solve/custom-call.0 | solution.py:26
  405.1 11.7 %cholesky.96 = f32[128,128]{1,0:T(8,128)S(1)} custom-call(f32[128,128]{1,0:T(8,128)S(1)} %fusion.189), custom_call_target="Cholesky" | custom-call | tf_op jit(solution)/shard_map/jit(cholesky)/cholesky | solution.py:42
  418.3 10.0 %custom-call.10 = f32[2,1,64,64]{2,3,1,0:T(8,128)S(1)} custom-call(f32[2,1,64,64]{3,2,1,0:T(8,128)S(1)} %fusion.178), custom_call_target="InvertDiagBlocksLowerTriangular" | custom-call | tf_op jit(solution)/shard_map/triangular_solve/custom-call.0 | solution.py:26
  429.6 11.7 %cholesky.107 = f32[128,128]{1,0:T(8,128)S(1)} custom-call(f32[128,128]{1,0:T(8,128)S(1)} %fusion.186), custom_call_target="Cholesky" | custom-call | tf_op jit(solution)/shard_map/jit(cholesky)/cholesky | solution.py:42
  442.8 9.8 %custom-call.11 = f32[2,1,64,64]{2,3,1,0:T(8,128)S(1)} custom-call(f32[2,1,64,64]{3,2,1,0:T(8,128)S(1)} %fusion.179), custom_call_target="InvertDiagBlocksLowerTriangular" | custom-call | tf_op jit(solution)/shard_map/triangular_solve/custom-call.0 | solution.py:26
  469.9 8.2 %collective-permute-done.15 = bf16[32,16,512]{2,0,1:T(8,128)(2,1)S(1)} collective-permute-done((bf16[32,16,512]{2,0,1:T(8,128)(2,1)S(1)}, bf16[32,16,512]{2,0,1:T(8,128)(2,1)S(1)}, u32[]{:S(2)}, u32[]{:S(2)}) %collective-permute-start.15) | collective-permute-done | bytes 524320 | tf_op jit(solution)/shard_map/ppermute | solution.py:166
  481.3 8.5 %collective-permute-done.17 = bf16[32,16,512]{2,0,1:T(8,128)(2,1)S(1)} collective-permute-done((bf16[32,16,512]{2,0,1:T(8,128)(2,1)S(1)}, bf16[32,16,512]{2,0,1:T(8,128)(2,1)S(1)}, u32[]{:S(2)}, u32[]{:S(2)}) %collective-permute-start.17) | collective-permute-done | bytes 524320 | tf_op jit(solution)/shard_map/ppermute | solution.py:166
  493.4 8.8 %collective-permute-done.19 = bf16[32,16,512]{2,0,1:T(8,128)(2,1)S(1)} collective-permute-done((bf16[32,16,512]{2,0,1:T(8,128)(2,1)S(1)}, bf16[32,16,512]{2,0,1:T(8,128)(2,1)S(1)}, u32[]{:S(2)}, u32[]{:S(2)}) %collective-permute-start.19) | collective-permute-done | bytes 524320 | tf_op jit(solution)/shard_map/ppermute | solution.py:166
  505.5 8.8 %collective-permute-done.21 = bf16[32,16,512]{2,0,1:T(8,128)(2,1)S(1)} collective-permute-done((bf16[32,16,512]{2,0,1:T(8,128)(2,1)S(1)}, bf16[32,16,512]{2,0,1:T(8,128)(2,1)S(1)}, u32[]{:S(2)}, u32[]{:S(2)}) %collective-permute-start.21) | collective-permute-done | bytes 524320 | tf_op jit(solution)/shard_map/ppermute | solution.py:166
  517.5 9.2 %collective-permute-done.23 = bf16[32,16,512]{2,0,1:T(8,128)(2,1)S(1)} collective-permute-done((bf16[32,16,512]{2,0,1:T(8,128)(2,1)S(1)}, bf16[32,16,512]{2,0,1:T(8,128)(2,1)S(1)}, u32[]{:S(2)}, u32[]{:S(2)}) %collective-permute-start.23) | collective-permute-done | bytes 524320 | tf_op jit(solution)/shard_map/ppermute | solution.py:166
  530.0 10.3 %collective-permute-done.25 = bf16[32,16,512]{2,0,1:T(8,128)(2,1)S(1)} collective-permute-done((bf16[32,16,512]{2,0,1:T(8,128)(2,1)S(1)}, bf16[32,16,512]{2,0,1:T(8,128)(2,1)S(1)}, u32[]{:S(2)}, u32[]{:S(2)}) %collective-permute-start.25) | collective-permute-done | bytes 524320 | tf_op jit(solution)/shard_map/ppermute | solution.py:166
  543.6 5.9 collective-permute-done.27
  556.1 33.0 %all-reduce.13.cloned.1.call-done = f32[1,512,512]{2,1,0:T(8,128)} async-done(((f32[1,512,512]{2,1,0:T(8,128)}), f32[1,512,512]{2,1,0:T(8,128)}) %all-reduce.13.cloned.1.call-update) | async-done | bytes 1048592 | tf_op jit(solution)/shard_map/psum | solution.py:196
  (223 shorter events, 135.2 us)
Async XLA Ops:
  7.2 265.2 %all-reduce.9.cloned.1.call-start = ((), (), s32[]{:S(2)}) async-start(), calls=%async_computation | async-start | bytes 1310720 | tf_op jit(solution)/shard_map/psum | solution.py:68
  56.2 25.5 %collective-permute-start = (f32[32,16,512]{2,1,0:T(8,128)S(1)}, f32[32,16,512]{2,1,0:T(8,128)S(1)}, u32[]{:S(2)}, u32[]{:S(2)}) collective-permute-start(f32[32,16,512]{2,1,0:T(8,128)S(1)} %fusion.98), channel_id=1, source_target_pairs={{0,4},{4,12},{12,20},{20,28},{28,24},{24,16},{16,8},{8,0},{1,5},{5... | collective-permute-start | bytes 3145736 | tf_op jit(solution)/shard_map/ppermute | solution.py:132
  60.8 25.5 %collective-permute-start.7 = (f32[32,16,512]{2,1,0:T(8,128)}, f32[32,16,512]{2,1,0:T(8,128)}, u32[]{:S(2)}, u32[]{:S(2)}) collective-permute-start(f32[32,16,512]{2,1,0:T(8,128)} %fusion.68), channel_id=1, source_target_pairs={{0,8},{4,0},{12,4},{20,12},{28,20},{24,28},{16,24},{8,16},{1,9},{5... | collective-permute-start | bytes 3145736 | tf_op jit(solution)/shard_map/ppermute | solution.py:133
  83.1 24.8 %collective-permute-start.1 = (f32[32,16,512]{2,1,0:T(8,128)S(1)}, f32[32,16,512]{2,1,0:T(8,128)S(1)}, u32[]{:S(2)}, u32[]{:S(2)}) collective-permute-start(f32[32,16,512]{2,1,0:T(8,128)S(1)} %convolution_add_fusion.1), channel_id=1, source_target_pairs={{0,4},{4,12},{12,20},{20,28},{28,24},{24,16},{16,8},{8,0},{1,5},{5... | collective-permute-start | bytes 3145736 | tf_op jit(solution)/shard_map/ppermute | solution.py:132
  89.1 24.6 %collective-permute-start.8 = (f32[32,16,512]{2,1,0:T(8,128)}, f32[32,16,512]{2,1,0:T(8,128)}, u32[]{:S(2)}, u32[]{:S(2)}) collective-permute-start(f32[32,16,512]{2,1,0:T(8,128)} %convolution_add_fusion), channel_id=1, source_target_pairs={{0,8},{4,0},{12,4},{20,12},{28,20},{24,28},{16,24},{8,16},{1,9},{5... | collective-permute-start | bytes 3145736 | tf_op jit(solution)/shard_map/ppermute | solution.py:133
  108.2 24.1 %collective-permute-start.2 = (f32[32,16,512]{2,1,0:T(8,128)S(1)}, f32[32,16,512]{2,1,0:T(8,128)}, u32[]{:S(2)}, u32[]{:S(2)}) collective-permute-start(f32[32,16,512]{2,1,0:T(8,128)S(1)} %add.437), channel_id=1, source_target_pairs={{0,4},{4,12},{12,20},{20,28},{28,24},{24,16},{16,8},{8,0},{1,5},{5... | collective-permute-start | bytes 3145736 | tf_op jit(solution)/shard_map/ppermute | solution.py:132
  115.1 23.5 %collective-permute-start.9 = (f32[32,16,512]{2,1,0:T(8,128)S(1)}, f32[32,16,512]{2,1,0:T(8,128)}, u32[]{:S(2)}, u32[]{:S(2)}) collective-permute-start(f32[32,16,512]{2,1,0:T(8,128)S(1)} %add.461), channel_id=1, source_target_pairs={{0,8},{4,0},{12,4},{20,12},{28,20},{24,28},{16,24},{8,16},{1,9},{5... | collective-permute-start | bytes 3145736 | tf_op jit(solution)/shard_map/ppermute | solution.py:133
  133.7 23.2 %collective-permute-start.3 = (f32[32,16,512]{2,1,0:T(8,128)S(1)}, f32[32,16,512]{2,1,0:T(8,128)}, u32[]{:S(2)}, u32[]{:S(2)}) collective-permute-start(f32[32,16,512]{2,1,0:T(8,128)S(1)} %add.439), channel_id=1, source_target_pairs={{0,4},{4,12},{12,20},{20,28},{28,24},{24,16},{16,8},{8,0},{1,5},{5... | collective-permute-start | bytes 3145736 | tf_op jit(solution)/shard_map/ppermute | solution.py:132
  140.1 22.6 %collective-permute-start.10 = (f32[32,16,512]{2,1,0:T(8,128)S(1)}, f32[32,16,512]{2,1,0:T(8,128)}, u32[]{:S(2)}, u32[]{:S(2)}) collective-permute-start(f32[32,16,512]{2,1,0:T(8,128)S(1)} %add.466), channel_id=1, source_target_pairs={{0,8},{4,0},{12,4},{20,12},{28,20},{24,28},{16,24},{8,16},{1,9},{5... | collective-permute-start | bytes 3145736 | tf_op jit(solution)/shard_map/ppermute | solution.py:133
  158.3 22.2 %collective-permute-start.4 = (f32[32,16,512]{2,1,0:T(8,128)S(1)}, f32[32,16,512]{2,1,0:T(8,128)}, u32[]{:S(2)}, u32[]{:S(2)}) collective-permute-start(f32[32,16,512]{2,1,0:T(8,128)S(1)} %add.441), channel_id=1, source_target_pairs={{0,4},{4,12},{12,20},{20,28},{28,24},{24,16},{16,8},{8,0},{1,5},{5... | collective-permute-start | bytes 3145736 | tf_op jit(solution)/shard_map/ppermute | solution.py:132
  164.1 21.9 %collective-permute-start.11 = (f32[32,16,512]{2,1,0:T(8,128)S(1)}, f32[32,16,512]{2,1,0:T(8,128)}, u32[]{:S(2)}, u32[]{:S(2)}) collective-permute-start(f32[32,16,512]{2,1,0:T(8,128)S(1)} %add.471), channel_id=1, source_target_pairs={{0,8},{4,0},{12,4},{20,12},{28,20},{24,28},{16,24},{8,16},{1,9},{5... | collective-permute-start | bytes 3145736 | tf_op jit(solution)/shard_map/ppermute | solution.py:133
  182.0 21.9 %collective-permute-start.5 = (f32[32,16,512]{2,1,0:T(8,128)S(1)}, f32[32,16,512]{2,1,0:T(8,128)}, u32[]{:S(2)}, u32[]{:S(2)}) collective-permute-start(f32[32,16,512]{2,1,0:T(8,128)S(1)} %add.443), channel_id=1, source_target_pairs={{0,4},{4,12},{12,20},{20,28},{28,24},{24,16},{16,8},{8,0},{1,5},{5... | collective-permute-start | bytes 3145736 | tf_op jit(solution)/shard_map/ppermute | solution.py:132
  188.4 20.9 %collective-permute-start.12 = (f32[32,16,512]{2,1,0:T(8,128)}, f32[32,16,512]{2,1,0:T(8,128)}, u32[]{:S(2)}, u32[]{:S(2)}) collective-permute-start(f32[32,16,512]{2,1,0:T(8,128)} %add.476), channel_id=1, source_target_pairs={{0,8},{4,0},{12,4},{20,12},{28,20},{24,28},{16,24},{8,16},{1,9},{5... | collective-permute-start | bytes 3145736 | tf_op jit(solution)/shard_map/ppermute | solution.py:133
  205.3 20.4 %collective-permute-start.6 = (f32[32,16,512]{2,1,0:T(8,128)S(1)}, f32[32,16,512]{2,1,0:T(8,128)S(1)}, u32[]{:S(2)}, u32[]{:S(2)}) collective-permute-start(f32[32,16,512]{2,1,0:T(8,128)S(1)} %add.445), channel_id=1, source_target_pairs={{0,4},{4,12},{12,20},{20,28},{28,24},{24,16},{16,8},{8,0},{1,5},{5... | collective-permute-start | bytes 3145736 | tf_op jit(solution)/shard_map/ppermute | solution.py:132
  211.8 27.2 %copy-start.20 = (s32[8,8]{1,0:T(8,128)S(1)}, s32[8,8]{1,0:T(8,128)}, u32[]{:S(2)}) copy-start(s32[8,8]{1,0:T(8,128)} %constant.155.clone) | copy-start | bytes 772
  211.8 20.1 %collective-permute-start.13 = (f32[32,16,512]{2,1,0:T(8,128)}, f32[32,16,512]{2,1,0:T(8,128)}, u32[]{:S(2)}, u32[]{:S(2)}) collective-permute-start(f32[32,16,512]{2,1,0:T(8,128)} %add.481), channel_id=1, source_target_pairs={{0,8},{4,0},{12,4},{20,12},{28,20},{24,28},{16,24},{8,16},{1,9},{5... | collective-permute-start | bytes 3145736 | tf_op jit(solution)/shard_map/ppermute | solution.py:133
  238.9 110.2 %all-reduce.11.cloned.1.call-start = ((), (), s32[]{:S(2)}) async-start(), calls=%async_computation.1 | async-start | bytes 1310720 | tf_op jit(solution)/shard_map/psum | solution.py:68
  272.4 316.7 %all-reduce.13.cloned.1.call-start = ((), (), s32[]{:S(2)}) async-start(), calls=%async_computation.2 | async-start | bytes 2097152 | tf_op jit(solution)/shard_map/psum | solution.py:196
  465.6 12.5 %collective-permute-start.15 = (bf16[32,16,512]{2,0,1:T(8,128)(2,1)S(1)}, bf16[32,16,512]{2,0,1:T(8,128)(2,1)S(1)}, u32[]{:S(2)}, u32[]{:S(2)}) collective-permute-start(bf16[32,16,512]{2,0,1:T(8,128)(2,1)S(1)} %copy.99), channel_id=1, source_target_pairs={{0,8},{4,0},{12,4},{20,12},{28,20},{24,28},{16,24},{8,16},{1,9},{5... | collective-permute-start | bytes 1572872 | tf_op jit(solution)/shard_map/ppermute | solution.py:166
  466.8 12.9 %collective-permute-start.14 = (bf16[32,16,512]{2,0,1:T(8,128)(2,1)S(1)}, bf16[32,16,512]{2,0,1:T(8,128)(2,1)S(1)}, u32[]{:S(2)}, u32[]{:S(2)}) collective-permute-start(bf16[32,16,512]{2,0,1:T(8,128)(2,1)S(1)} %copy.97), channel_id=1, source_target_pairs={{0,4},{4,12},{12,20},{20,28},{28,24},{24,16},{16,8},{8,0},{1,5},{5... | collective-permute-start | bytes 1572872 | tf_op jit(solution)/shard_map/ppermute | solution.py:165
  478.0 11.8 %collective-permute-start.17 = (bf16[32,16,512]{2,0,1:T(8,128)(2,1)S(1)}, bf16[32,16,512]{2,0,1:T(8,128)(2,1)S(1)}, u32[]{:S(2)}, u32[]{:S(2)}) collective-permute-start(bf16[32,16,512]{2,0,1:T(8,128)(2,1)S(1)} %collective-permute-done.15), channel_id=1, source_target_pairs={{0,8},{4,0},{12,4},{20,12},{28,20},{24,28},{16,24},{8,16},{1,9},{5... | collective-permute-start | bytes 1572872 | tf_op jit(solution)/shard_map/ppermute | solution.py:166
  479.7 12.1 %collective-permute-start.16 = (bf16[32,16,512]{2,0,1:T(8,128)(2,1)S(1)}, bf16[32,16,512]{2,0,1:T(8,128)(2,1)S(1)}, u32[]{:S(2)}, u32[]{:S(2)}) collective-permute-start(bf16[32,16,512]{2,0,1:T(8,128)(2,1)S(1)} %collective-permute-done.14), channel_id=1, source_target_pairs={{0,4},{4,12},{12,20},{20,28},{28,24},{24,16},{16,8},{8,0},{1,5},{5... | collective-permute-start | bytes 1572872 | tf_op jit(solution)/shard_map/ppermute | solution.py:165
  489.9 12.3 %collective-permute-start.19 = (bf16[32,16,512]{2,0,1:T(8,128)(2,1)S(1)}, bf16[32,16,512]{2,0,1:T(8,128)(2,1)S(1)}, u32[]{:S(2)}, u32[]{:S(2)}) collective-permute-start(bf16[32,16,512]{2,0,1:T(8,128)(2,1)S(1)} %collective-permute-done.17), channel_id=1, source_target_pairs={{0,8},{4,0},{12,4},{20,12},{28,20},{24,28},{16,24},{8,16},{1,9},{5... | collective-permute-start | bytes 1572872 | tf_op jit(solution)/shard_map/ppermute | solution.py:166
  491.8 12.1 %collective-permute-start.18 = (bf16[32,16,512]{2,0,1:T(8,128)(2,1)S(1)}, bf16[32,16,512]{2,0,1:T(8,128)(2,1)S(1)}, u32[]{:S(2)}, u32[]{:S(2)}) collective-permute-start(bf16[32,16,512]{2,0,1:T(8,128)(2,1)S(1)} %collective-permute-done.16), channel_id=1, source_target_pairs={{0,4},{4,12},{12,20},{20,28},{28,24},{24,16},{16,8},{8,0},{1,5},{5... | collective-permute-start | bytes 1572872 | tf_op jit(solution)/shard_map/ppermute | solution.py:165
  502.1 12.1 %collective-permute-start.21 = (bf16[32,16,512]{2,0,1:T(8,128)(2,1)S(1)}, bf16[32,16,512]{2,0,1:T(8,128)(2,1)S(1)}, u32[]{:S(2)}, u32[]{:S(2)}) collective-permute-start(bf16[32,16,512]{2,0,1:T(8,128)(2,1)S(1)} %collective-permute-done.19), channel_id=1, source_target_pairs={{0,8},{4,0},{12,4},{20,12},{28,20},{24,28},{16,24},{8,16},{1,9},{5... | collective-permute-start | bytes 1572872 | tf_op jit(solution)/shard_map/ppermute | solution.py:166
  503.9 12.1 %collective-permute-start.20 = (bf16[32,16,512]{2,0,1:T(8,128)(2,1)S(1)}, bf16[32,16,512]{2,0,1:T(8,128)(2,1)S(1)}, u32[]{:S(2)}, u32[]{:S(2)}) collective-permute-start(bf16[32,16,512]{2,0,1:T(8,128)(2,1)S(1)} %collective-permute-done.18), channel_id=1, source_target_pairs={{0,4},{4,12},{12,20},{20,28},{28,24},{24,16},{16,8},{8,0},{1,5},{5... | collective-permute-start | bytes 1572872 | tf_op jit(solution)/shard_map/ppermute | solution.py:165
  514.2 12.5 %collective-permute-start.23 = (bf16[32,16,512]{2,0,1:T(8,128)(2,1)S(1)}, bf16[32,16,512]{2,0,1:T(8,128)(2,1)S(1)}, u32[]{:S(2)}, u32[]{:S(2)}) collective-permute-start(bf16[32,16,512]{2,0,1:T(8,128)(2,1)S(1)} %collective-permute-done.21), channel_id=1, source_target_pairs={{0,8},{4,0},{12,4},{20,12},{28,20},{24,28},{16,24},{8,16},{1,9},{5... | collective-permute-start | bytes 1572872 | tf_op jit(solution)/shard_map/ppermute | solution.py:166
  516.0 12.5 %collective-permute-start.22 = (bf16[32,16,512]{2,0,1:T(8,128)(2,1)S(1)}, bf16[32,16,512]{2,0,1:T(8,128)(2,1)S(1)}, u32[]{:S(2)}, u32[]{:S(2)}) collective-permute-start(bf16[32,16,512]{2,0,1:T(8,128)(2,1)S(1)} %collective-permute-done.20), channel_id=1, source_target_pairs={{0,4},{4,12},{12,20},{20,28},{28,24},{24,16},{16,8},{8,0},{1,5},{5... | collective-permute-start | bytes 1572872 | tf_op jit(solution)/shard_map/ppermute | solution.py:165
  526.7 13.6 %collective-permute-start.25 = (bf16[32,16,512]{2,0,1:T(8,128)(2,1)S(1)}, bf16[32,16,512]{2,0,1:T(8,128)(2,1)S(1)}, u32[]{:S(2)}, u32[]{:S(2)}) collective-permute-start(bf16[32,16,512]{2,0,1:T(8,128)(2,1)S(1)} %collective-permute-done.23), channel_id=1, source_target_pairs={{0,8},{4,0},{12,4},{20,12},{28,20},{24,28},{16,24},{8,16},{1,9},{5... | collective-permute-start | bytes 1572872 | tf_op jit(solution)/shard_map/ppermute | solution.py:166
  528.4 13.5 %collective-permute-start.24 = (bf16[32,16,512]{2,0,1:T(8,128)(2,1)S(1)}, bf16[32,16,512]{2,0,1:T(8,128)(2,1)S(1)}, u32[]{:S(2)}, u32[]{:S(2)}) collective-permute-start(bf16[32,16,512]{2,0,1:T(8,128)(2,1)S(1)} %collective-permute-done.22), channel_id=1, source_target_pairs={{0,4},{4,12},{12,20},{20,28},{28,24},{24,16},{16,8},{8,0},{1,5},{5... | collective-permute-start | bytes 1572872 | tf_op jit(solution)/shard_map/ppermute | solution.py:165
  540.3 9.2 %collective-permute-start.27 = (bf16[32,16,512]{2,0,1:T(8,128)(2,1)S(1)}, bf16[32,16,512]{2,0,1:T(8,128)(2,1)S(1)}, u32[]{:S(2)}, u32[]{:S(2)}) collective-permute-start(bf16[32,16,512]{2,0,1:T(8,128)(2,1)S(1)} %collective-permute-done.25), channel_id=1, source_target_pairs={{0,8},{4,0},{12,4},{20,12},{28,20},{24,28},{16,24},{8,16},{1,9},{5... | collective-permute-start | bytes 1572872 | tf_op jit(solution)/shard_map/ppermute | solution.py:166
  541.9 9.2 %collective-permute-start.26 = (bf16[32,16,512]{2,0,1:T(8,128)(2,1)S(1)}, bf16[32,16,512]{2,0,1:T(8,128)(2,1)S(1)}, u32[]{:S(2)}, u32[]{:S(2)}) collective-permute-start(bf16[32,16,512]{2,0,1:T(8,128)(2,1)S(1)} %collective-permute-done.24), channel_id=1, source_target_pairs={{0,4},{4,12},{12,20},{20,28},{28,24},{24,16},{16,8},{8,0},{1,5},{5... | collective-permute-start | bytes 1572872 | tf_op jit(solution)/shard_map/ppermute | solution.py:165
  (20 other events, 268.0 us)
Sparse Core Ops, SparseCore 0:
  239.0 33.2 all-reduce.8
  275.8 73.3 all-reduce.10
  552.9 36.1 all-reduce.12

commit v9 on v8

--- a/solution.py
+++ b/solution.py
@@ -59,13 +59,23 @@
     return jnp.concatenate(blocks, axis=1)
 
 
-def symmetric_psum(gram_part):
+def butterfly_sum(x, n):
+    if n & (n - 1):
+        return lax.psum(x, "sum")
+    d = 1
+    while d < n:
+        x = x + lax.ppermute(x, "sum", [(i, i ^ d) for i in range(n)])
+        d *= 2
+    return x
+
+
+def symmetric_psum(gram_part, n_sum):
     n = gram_part.shape[0]
     b = min(BLOCK, n)
     nb = n // b
     lower = [(i, j) for i in range(nb) for j in range(i + 1)]
     packed = jnp.stack([gram_part[i * b:(i + 1) * b, j * b:(j + 1) * b] for i, j in lower])
-    packed = lax.psum(lax.psum(packed, "mode"), "sum")
+    packed = butterfly_sum(lax.psum(packed, "mode"), n_sum)
     where = {cell: k for k, cell in enumerate(lower)}
     rows = []
     for i in range(nb):
@@ -188,7 +198,7 @@
     share = ring_reduce_scatter(local_rows, rows_in, ring)
     flat_share = share.reshape(-1, target)
     gram_part = jnp.dot(flat_share.T, flat_share, precision=HI)
-    gram = symmetric_psum(gram_part)
+    gram = symmetric_psum(gram_part, len(ring))
     basis = orthonormal(flat_share, gram)
     block = basis.reshape(share.shape)
     rounded = block.astype(jnp.bfloat16)

time: 609 us -> 597 us (0.980)
  waiting for transfers between devices: 297 us -> 274 us
  starting transfers between devices: 29.8 us -> 37.7 us
    psum x2 -> x1, waiting for transfers between devices: 91.9 us -> 33.3 us  [symmetric_psum(): packed = butterfly_sum(lax.psum(packed, 'mode'), n_sum)]
    ppermute x0 -> x3, waiting for transfers between devices: none -> 34.5 us  [butterfly_sum(): x = x + lax.ppermute(x, 'sum', [(i, i ^ d) for i in range(n)])]
    ppermute x0 -> x3, starting transfers between devices: none -> 6.17 us  [butterfly_sum(): x = x + lax.ppermute(x, 'sum', [(i, i ^ d) for i in range(n)])]
  transfers between devices with their start and end apart: 31 -> 33, of which waited for: 25 -> 28; matrix products, arithmetic and copies ran while one was open for 10% -> 10% of each run, Pallas kernels for 0% -> 0%
where the time goes in v9:
time: 597 us; the launch traced here: 587 us
  waiting for transfers between devices  274 us (46%)
  other arithmetic  117 us (20%)
  matrix products  75 us (13%)
  starting transfers between devices  37.7 us (6%)
  between operations  35.2 us (6%)
  blocking collectives  28 us (5%)
  local copies, waits for them, and re-layouts  20.6 us (3%)
    ppermute x7, waiting for transfers between devices, ring_reduce_scatter(): acc_f = lax.ppermute(acc_f, 'sum', fwd) + piece(fwd_blocks[t, me], 0, half)  87.8 us
    ppermute x7, waiting for transfers between devices, ring_gather_carries(): hold_b = lax.ppermute(hold_b, 'sum', bwd)  59.3 us
    another operation x12, other arithmetic, orthonormal(): lkk = jnp.linalg.cholesky(diag)  50.5 us
    another operation x9, other arithmetic, tri_inverse(): inv = lax.linalg.triangular_solve(diag, eye, left_side=True, lower=True)  40 us
    psum x1, waiting for transfers between devices, per_device(): carries = lax.psum(partial_carry, 'mode')  34.9 us
    ppermute x3, waiting for transfers between devices, butterfly_sum(): x = x + lax.ppermute(x, 'sum', [(i, i ^ d) for i in range(n)])  34.5 us
    psum x1, waiting for transfers between devices, symmetric_psum(): packed = butterfly_sum(lax.psum(packed, 'mode'), n_sum)  33.3 us
    psum x1, blocking collectives, per_device(): mapped = lax.psum(partial_map, 'mode').astype(jnp.bfloat16)  28 us
  transfers between devices with their start and end apart: 33, of which 28 were waited for; matrix products, arithmetic and copies ran while one was open for 10% of the time, Pallas kernels for 0%

profile of v9, /device:TPU:0, one launch (start us, length us, event | category | flops | bytes accessed | tf_op | source)
XLA Modules:
  0.0 586.8 jit_solution(11660515464830579468)
XLA Ops:
  9.5 17.1 %fusion.8 = f32[1,512,512]{2,1,0:T(8,128)S(1)} fusion(bf16[16,512,512]{2,1,0:T(8,128)(2,1)} %param.12, bf16[512,16,512]{2,1,0:T(8,128)(2,1)} %bitcast.450), kind=kOutput, calls=%fused_computation.29 | convolution fusion | flops 4294967296 | bytes 17825792 | tf_op jit(solution)/shard_map/dot_general | solution.py:185
  26.6 28.0 %all-reduce.11 = bf16[1,512,512]{2,1,0:T(8,128)(2,1)S(1)} all-reduce(f32[1,512,512]{2,1,0:T(8,128)S(1)} %fusion.8), channel_id=1, replica_groups=mesh['sum'=8,'mode'=4] {'mode'}, use_global_device_ids=true, to_apply=%region_0.0 | all-reduce | flops 262144 | bytes 1572864 | tf_op jit(solution)/shard_map/psum | solution.py:188
  62.6 19.0 %collective-permute-done = f32[32,16,512]{2,1,0:T(8,128)S(1)} collective-permute-done((f32[32,16,512]{2,1,0:T(8,128)S(1)}, f32[32,16,512]{2,1,0:T(8,128)S(1)}, u32[]{:S(2)}, u32[]{:S(2)}) %collective-permute-start) | collective-permute-done | bytes 1048608 | tf_op jit(solution)/shard_map/ppermute | solution.py:142
  93.6 14.2 %collective-permute-done.1 = f32[32,16,512]{2,1,0:T(8,128)S(1)} collective-permute-done((f32[32,16,512]{2,1,0:T(8,128)S(1)}, f32[32,16,512]{2,1,0:T(8,128)S(1)}, u32[]{:S(2)}, u32[]{:S(2)}) %collective-permute-start.1) | collective-permute-done | bytes 1048608 | tf_op jit(solution)/shard_map/ppermute | solution.py:142
  109.6 4.0 collective-permute-done.8
  119.8 12.4 %collective-permute-done.2 = f32[32,16,512]{2,1,0:T(8,128)} collective-permute-done((f32[32,16,512]{2,1,0:T(8,128)S(1)}, f32[32,16,512]{2,1,0:T(8,128)}, u32[]{:S(2)}, u32[]{:S(2)}) %collective-permute-start.2) | collective-permute-done | bytes 1048608 | tf_op jit(solution)/shard_map/ppermute | solution.py:142
  144.8 11.9 %collective-permute-done.3 = f32[32,16,512]{2,1,0:T(8,128)} collective-permute-done((f32[32,16,512]{2,1,0:T(8,128)S(1)}, f32[32,16,512]{2,1,0:T(8,128)}, u32[]{:S(2)}, u32[]{:S(2)}) %collective-permute-start.3) | collective-permute-done | bytes 1048608 | tf_op jit(solution)/shard_map/ppermute | solution.py:142
  169.3 11.2 %collective-permute-done.4 = f32[32,16,512]{2,1,0:T(8,128)} collective-permute-done((f32[32,16,512]{2,1,0:T(8,128)S(1)}, f32[32,16,512]{2,1,0:T(8,128)}, u32[]{:S(2)}, u32[]{:S(2)}) %collective-permute-start.4) | collective-permute-done | bytes 1048608 | tf_op jit(solution)/shard_map/ppermute | solution.py:142
  193.4 10.4 %collective-permute-done.5 = f32[32,16,512]{2,1,0:T(8,128)} collective-permute-done((f32[32,16,512]{2,1,0:T(8,128)S(1)}, f32[32,16,512]{2,1,0:T(8,128)}, u32[]{:S(2)}, u32[]{:S(2)}) %collective-permute-start.5) | collective-permute-done | bytes 1048608 | tf_op jit(solution)/shard_map/ppermute | solution.py:142
  216.7 8.8 %collective-permute-done.6 = f32[32,16,512]{2,1,0:T(8,128)S(1)} collective-permute-done((f32[32,16,512]{2,1,0:T(8,128)S(1)}, f32[32,16,512]{2,1,0:T(8,128)S(1)}, u32[]{:S(2)}, u32[]{:S(2)}) %collective-permute-start.6) | collective-permute-done | bytes 1048608 | tf_op jit(solution)/shard_map/ppermute | solution.py:142
  225.8 6.2 %collective-permute-done.13 = f32[32,16,512]{2,1,0:T(8,128)} collective-permute-done((f32[32,16,512]{2,1,0:T(8,128)}, f32[32,16,512]{2,1,0:T(8,128)}, u32[]{:S(2)}, u32[]{:S(2)}) %collective-permute-start.13) | collective-permute-done | bytes 1048608 | tf_op jit(solution)/shard_map/ppermute | solution.py:143
  234.4 3.6 convolution_bitcast_fusion.16
  239.1 33.3 %all-reduce.8.cloned.1.call-done = f32[10,128,128]{1,2,0:T(8,128)} async-done(((f32[10,128,128]{1,2,0:T(8,128)}), f32[10,128,128]{1,2,0:T(8,128)}) %all-reduce.8.cloned.1.call-update) | async-done | bytes 655376 | tf_op jit(solution)/shard_map/psum | solution.py:78
  273.9 14.0 %collective-permute-done.14 = f32[10,128,128]{1,2,0:T(8,128)S(1)} collective-permute-done((f32[10,128,128]{1,2,0:T(8,128)}, f32[10,128,128]{1,2,0:T(8,128)S(1)}, u32[]{:S(2)}, u32[]{:S(2)}) %collective-permute-start.14) | collective-permute-done | bytes 655392 | tf_op jit(solution)/shard_map/ppermute | solution.py:67
  306.8 6.0 %constant_dynamic-slice_fusion.1 = (bf16[1,32,16,512]{3,2,1,0:T(8,128)(2,1)}, bf16[1,32,16,512]{3,2,1,0:T(8,128)(2,1)}, bf16[1,32,16,512]{3,2,1,0:T(8,128)(2,1)}...) fusion(bf16[1,512,16,512]{3,2,1,0:T(8,128)(2,1)} %param.10, ...), kind=kLoop, calls=%fused_computation.306 | loop fusion | bytes 14680120 | tf_op jit(solution)/shard_map/dynamic_slice | solution.py:166
  314.3 18.3 %collective-permute-done.16 = f32[10,128,128]{1,2,0:T(8,128)S(1)} collective-permute-done((f32[10,128,128]{1,2,0:T(8,128)S(1)}, f32[10,128,128]{1,2,0:T(8,128)S(1)}, u32[]{:S(2)}, u32[]{:S(2)}) %collective-permute-start.16) | collective-permute-done | bytes 655392 | tf_op jit(solution)/shard_map/ppermute | solution.py:67
  334.2 12.5 %cholesky.74 = f32[128,128]{1,0:T(8,128)S(1)} custom-call(f32[128,128]{1,0:T(8,128)} %fusion.183), custom_call_target="Cholesky" | custom-call | tf_op jit(solution)/shard_map/jit(cholesky)/cholesky | solution.py:42
  348.3 10.0 %custom-call.8 = f32[2,1,64,64]{2,3,1,0:T(8,128)S(1)} custom-call(f32[2,1,64,64]{3,2,1,0:T(8,128)S(1)} %fusion.176), custom_call_target="InvertDiagBlocksLowerTriangular" | custom-call | tf_op jit(solution)/shard_map/triangular_solve/custom-call.0 | solution.py:26
  364.9 11.7 %cholesky.85 = f32[128,128]{1,0:T(8,128)S(1)} custom-call(f32[128,128]{1,0:T(8,128)S(1)} %fusion.192), custom_call_target="Cholesky" | custom-call | tf_op jit(solution)/shard_map/jit(cholesky)/cholesky | solution.py:42
  378.0 9.8 %custom-call.9 = f32[2,1,64,64]{2,3,1,0:T(8,128)S(1)} custom-call(f32[2,1,64,64]{3,2,1,0:T(8,128)S(1)} %fusion.177), custom_call_target="InvertDiagBlocksLowerTriangular" | custom-call | tf_op jit(solution)/shard_map/triangular_solve/custom-call.0 | solution.py:26
  391.2 11.7 %cholesky.96 = f32[128,128]{1,0:T(8,128)S(1)} custom-call(f32[128,128]{1,0:T(8,128)S(1)} %fusion.189), custom_call_target="Cholesky" | custom-call | tf_op jit(solution)/shard_map/jit(cholesky)/cholesky | solution.py:42
  404.4 10.2 %custom-call.10 = f32[2,1,64,64]{2,3,1,0:T(8,128)S(1)} custom-call(f32[2,1,64,64]{3,2,1,0:T(8,128)S(1)} %fusion.178), custom_call_target="InvertDiagBlocksLowerTriangular" | custom-call | tf_op jit(solution)/shard_map/triangular_solve/custom-call.0 | solution.py:26
  416.0 11.7 %cholesky.107 = f32[128,128]{1,0:T(8,128)S(1)} custom-call(f32[128,128]{1,0:T(8,128)S(1)} %fusion.186), custom_call_target="Cholesky" | custom-call | tf_op jit(solution)/shard_map/jit(cholesky)/cholesky | solution.py:42
  429.1 9.8 %custom-call.11 = f32[2,1,64,64]{2,3,1,0:T(8,128)S(1)} custom-call(f32[2,1,64,64]{3,2,1,0:T(8,128)S(1)} %fusion.179), custom_call_target="InvertDiagBlocksLowerTriangular" | custom-call | tf_op jit(solution)/shard_map/triangular_solve/custom-call.0 | solution.py:26
  456.2 8.3 %collective-permute-done.18 = bf16[32,16,512]{2,0,1:T(8,128)(2,1)S(1)} collective-permute-done((bf16[32,16,512]{2,0,1:T(8,128)(2,1)S(1)}, bf16[32,16,512]{2,0,1:T(8,128)(2,1)S(1)}, u32[]{:S(2)}, u32[]{:S(2)}) %collective-permute-start.18) | collective-permute-done | bytes 524320 | tf_op jit(solution)/shard_map/ppermute | solution.py:176
  467.8 9.2 %collective-permute-done.20 = bf16[32,16,512]{2,0,1:T(8,128)(2,1)S(1)} collective-permute-done((bf16[32,16,512]{2,0,1:T(8,128)(2,1)S(1)}, bf16[32,16,512]{2,0,1:T(8,128)(2,1)S(1)}, u32[]{:S(2)}, u32[]{:S(2)}) %collective-permute-start.20) | collective-permute-done | bytes 524320 | tf_op jit(solution)/shard_map/ppermute | solution.py:176
  481.0 8.7 %collective-permute-done.22 = bf16[32,16,512]{2,0,1:T(8,128)(2,1)S(1)} collective-permute-done((bf16[32,16,512]{2,0,1:T(8,128)(2,1)S(1)}, bf16[32,16,512]{2,0,1:T(8,128)(2,1)S(1)}, u32[]{:S(2)}, u32[]{:S(2)}) %collective-permute-start.22) | collective-permute-done | bytes 524320 | tf_op jit(solution)/shard_map/ppermute | solution.py:176
  494.1 9.0 %collective-permute-done.24 = bf16[32,16,512]{2,0,1:T(8,128)(2,1)S(1)} collective-permute-done((bf16[32,16,512]{2,0,1:T(8,128)(2,1)S(1)}, bf16[32,16,512]{2,0,1:T(8,128)(2,1)S(1)}, u32[]{:S(2)}, u32[]{:S(2)}) %collective-permute-start.24) | collective-permute-done | bytes 524320 | tf_op jit(solution)/shard_map/ppermute | solution.py:176
  506.5 8.8 %collective-permute-done.26 = bf16[32,16,512]{2,0,1:T(8,128)(2,1)S(1)} collective-permute-done((bf16[32,16,512]{2,0,1:T(8,128)(2,1)S(1)}, bf16[32,16,512]{2,0,1:T(8,128)(2,1)S(1)}, u32[]{:S(2)}, u32[]{:S(2)}) %collective-permute-start.26) | collective-permute-done | bytes 524320 | tf_op jit(solution)/shard_map/ppermute | solution.py:176
  518.6 8.8 %collective-permute-done.28 = bf16[32,16,512]{2,0,1:T(8,128)(2,1)S(1)} collective-permute-done((bf16[32,16,512]{2,0,1:T(8,128)(2,1)S(1)}, bf16[32,16,512]{2,0,1:T(8,128)(2,1)S(1)}, u32[]{:S(2)}, u32[]{:S(2)}) %collective-permute-start.28) | collective-permute-done | bytes 524320 | tf_op jit(solution)/shard_map/ppermute | solution.py:176
  530.7 6.4 %collective-permute-done.30 = bf16[32,16,512]{2,0,1:T(8,128)(2,1)S(1)} collective-permute-done((bf16[32,16,512]{2,0,1:T(8,128)(2,1)S(1)}, bf16[32,16,512]{2,0,1:T(8,128)(2,1)S(1)}, u32[]{:S(2)}, u32[]{:S(2)}) %collective-permute-start.30) | collective-permute-done | bytes 524320 | tf_op jit(solution)/shard_map/ppermute | solution.py:176
  542.6 34.9 %all-reduce.10.cloned.1.call-done = f32[1,512,512]{2,1,0:T(8,128)} async-done(((f32[1,512,512]{2,1,0:T(8,128)}), f32[1,512,512]{2,1,0:T(8,128)}) %all-reduce.10.cloned.1.call-update) | async-done | bytes 1048592 | tf_op jit(solution)/shard_map/psum | solution.py:206
  (229 shorter events, 151.4 us)
Async XLA Ops:
  7.2 265.3 %all-reduce.8.cloned.1.call-start = ((), (), s32[]{:S(2)}) async-start(), calls=%async_computation | async-start | bytes 1310720 | tf_op jit(solution)/shard_map/psum | solution.py:78
  56.1 25.5 %collective-permute-start = (f32[32,16,512]{2,1,0:T(8,128)S(1)}, f32[32,16,512]{2,1,0:T(8,128)S(1)}, u32[]{:S(2)}, u32[]{:S(2)}) collective-permute-start(f32[32,16,512]{2,1,0:T(8,128)S(1)} %fusion.98), channel_id=1, source_target_pairs={{0,4},{4,12},{12,20},{20,28},{28,24},{24,16},{16,8},{8,0},{1,5},{5... | collective-permute-start | bytes 3145736 | tf_op jit(solution)/shard_map/ppermute | solution.py:142
  60.8 25.5 %collective-permute-start.7 = (f32[32,16,512]{2,1,0:T(8,128)}, f32[32,16,512]{2,1,0:T(8,128)}, u32[]{:S(2)}, u32[]{:S(2)}) collective-permute-start(f32[32,16,512]{2,1,0:T(8,128)} %fusion.68), channel_id=1, source_target_pairs={{0,8},{4,0},{12,4},{20,12},{28,20},{24,28},{16,24},{8,16},{1,9},{5... | collective-permute-start | bytes 3145736 | tf_op jit(solution)/shard_map/ppermute | solution.py:143
  83.0 24.8 %collective-permute-start.1 = (f32[32,16,512]{2,1,0:T(8,128)S(1)}, f32[32,16,512]{2,1,0:T(8,128)S(1)}, u32[]{:S(2)}, u32[]{:S(2)}) collective-permute-start(f32[32,16,512]{2,1,0:T(8,128)S(1)} %convolution_add_fusion.1), channel_id=1, source_target_pairs={{0,4},{4,12},{12,20},{20,28},{28,24},{24,16},{16,8},{8,0},{1,5},{5... | collective-permute-start | bytes 3145736 | tf_op jit(solution)/shard_map/ppermute | solution.py:142
  89.0 24.6 %collective-permute-start.8 = (f32[32,16,512]{2,1,0:T(8,128)}, f32[32,16,512]{2,1,0:T(8,128)}, u32[]{:S(2)}, u32[]{:S(2)}) collective-permute-start(f32[32,16,512]{2,1,0:T(8,128)} %convolution_add_fusion), channel_id=1, source_target_pairs={{0,8},{4,0},{12,4},{20,12},{28,20},{24,28},{16,24},{8,16},{1,9},{5... | collective-permute-start | bytes 3145736 | tf_op jit(solution)/shard_map/ppermute | solution.py:143
  108.1 24.1 %collective-permute-start.2 = (f32[32,16,512]{2,1,0:T(8,128)S(1)}, f32[32,16,512]{2,1,0:T(8,128)}, u32[]{:S(2)}, u32[]{:S(2)}) collective-permute-start(f32[32,16,512]{2,1,0:T(8,128)S(1)} %add.444), channel_id=1, source_target_pairs={{0,4},{4,12},{12,20},{20,28},{28,24},{24,16},{16,8},{8,0},{1,5},{5... | collective-permute-start | bytes 3145736 | tf_op jit(solution)/shard_map/ppermute | solution.py:142
  115.1 23.5 %collective-permute-start.9 = (f32[32,16,512]{2,1,0:T(8,128)S(1)}, f32[32,16,512]{2,1,0:T(8,128)}, u32[]{:S(2)}, u32[]{:S(2)}) collective-permute-start(f32[32,16,512]{2,1,0:T(8,128)S(1)} %add.468), channel_id=1, source_target_pairs={{0,8},{4,0},{12,4},{20,12},{28,20},{24,28},{16,24},{8,16},{1,9},{5... | collective-permute-start | bytes 3145736 | tf_op jit(solution)/shard_map/ppermute | solution.py:143
  133.6 23.2 %collective-permute-start.3 = (f32[32,16,512]{2,1,0:T(8,128)S(1)}, f32[32,16,512]{2,1,0:T(8,128)}, u32[]{:S(2)}, u32[]{:S(2)}) collective-permute-start(f32[32,16,512]{2,1,0:T(8,128)S(1)} %add.446), channel_id=1, source_target_pairs={{0,4},{4,12},{12,20},{20,28},{28,24},{24,16},{16,8},{8,0},{1,5},{5... | collective-permute-start | bytes 3145736 | tf_op jit(solution)/shard_map/ppermute | solution.py:142
  140.0 22.6 %collective-permute-start.10 = (f32[32,16,512]{2,1,0:T(8,128)S(1)}, f32[32,16,512]{2,1,0:T(8,128)}, u32[]{:S(2)}, u32[]{:S(2)}) collective-permute-start(f32[32,16,512]{2,1,0:T(8,128)S(1)} %add.473), channel_id=1, source_target_pairs={{0,8},{4,0},{12,4},{20,12},{28,20},{24,28},{16,24},{8,16},{1,9},{5... | collective-permute-start | bytes 3145736 | tf_op jit(solution)/shard_map/ppermute | solution.py:143
  158.2 22.2 %collective-permute-start.4 = (f32[32,16,512]{2,1,0:T(8,128)S(1)}, f32[32,16,512]{2,1,0:T(8,128)}, u32[]{:S(2)}, u32[]{:S(2)}) collective-permute-start(f32[32,16,512]{2,1,0:T(8,128)S(1)} %add.448), channel_id=1, source_target_pairs={{0,4},{4,12},{12,20},{20,28},{28,24},{24,16},{16,8},{8,0},{1,5},{5... | collective-permute-start | bytes 3145736 | tf_op jit(solution)/shard_map/ppermute | solution.py:142
  164.1 22.2 %collective-permute-start.11 = (f32[32,16,512]{2,1,0:T(8,128)S(1)}, f32[32,16,512]{2,1,0:T(8,128)}, u32[]{:S(2)}, u32[]{:S(2)}) collective-permute-start(f32[32,16,512]{2,1,0:T(8,128)S(1)} %add.478), channel_id=1, source_target_pairs={{0,8},{4,0},{12,4},{20,12},{28,20},{24,28},{16,24},{8,16},{1,9},{5... | collective-permute-start | bytes 3145736 | tf_op jit(solution)/shard_map/ppermute | solution.py:143
  181.9 21.9 %collective-permute-start.5 = (f32[32,16,512]{2,1,0:T(8,128)S(1)}, f32[32,16,512]{2,1,0:T(8,128)}, u32[]{:S(2)}, u32[]{:S(2)}) collective-permute-start(f32[32,16,512]{2,1,0:T(8,128)S(1)} %add.450), channel_id=1, source_target_pairs={{0,4},{4,12},{12,20},{20,28},{28,24},{24,16},{16,8},{8,0},{1,5},{5... | collective-permute-start | bytes 3145736 | tf_op jit(solution)/shard_map/ppermute | solution.py:142
  188.6 20.9 %collective-permute-start.12 = (f32[32,16,512]{2,1,0:T(8,128)}, f32[32,16,512]{2,1,0:T(8,128)}, u32[]{:S(2)}, u32[]{:S(2)}) collective-permute-start(f32[32,16,512]{2,1,0:T(8,128)} %add.483), channel_id=1, source_target_pairs={{0,8},{4,0},{12,4},{20,12},{28,20},{24,28},{16,24},{8,16},{1,9},{5... | collective-permute-start | bytes 3145736 | tf_op jit(solution)/shard_map/ppermute | solution.py:143
  205.2 20.4 %collective-permute-start.6 = (f32[32,16,512]{2,1,0:T(8,128)S(1)}, f32[32,16,512]{2,1,0:T(8,128)S(1)}, u32[]{:S(2)}, u32[]{:S(2)}) collective-permute-start(f32[32,16,512]{2,1,0:T(8,128)S(1)} %add.452), channel_id=1, source_target_pairs={{0,4},{4,12},{12,20},{20,28},{28,24},{24,16},{16,8},{8,0},{1,5},{5... | collective-permute-start | bytes 3145736 | tf_op jit(solution)/shard_map/ppermute | solution.py:142
  211.9 20.1 %collective-permute-start.13 = (f32[32,16,512]{2,1,0:T(8,128)}, f32[32,16,512]{2,1,0:T(8,128)}, u32[]{:S(2)}, u32[]{:S(2)}) collective-permute-start(f32[32,16,512]{2,1,0:T(8,128)} %add.488), channel_id=1, source_target_pairs={{0,8},{4,0},{12,4},{20,12},{28,20},{24,28},{16,24},{8,16},{1,9},{5... | collective-permute-start | bytes 3145736 | tf_op jit(solution)/shard_map/ppermute | solution.py:143
  239.1 338.5 %all-reduce.10.cloned.1.call-start = ((), (), s32[]{:S(2)}) async-start(), calls=%async_computation.1 | async-start | bytes 2097152 | tf_op jit(solution)/shard_map/psum | solution.py:206
  272.5 15.5 %collective-permute-start.14 = (f32[10,128,128]{1,2,0:T(8,128)}, f32[10,128,128]{1,2,0:T(8,128)S(1)}, u32[]{:S(2)}, u32[]{:S(2)}) collective-permute-start(f32[10,128,128]{1,2,0:T(8,128)} %all-reduce.8.cloned.1.call-done), channel_id=1, source_target_pairs={{0,4},{4,0},{8,12},{12,8},{16,20},{20,16},{24,28},{28,24},{1,5},{5... | collective-permute-start | bytes 1966088 | tf_op jit(solution)/shard_map/ppermute | solution.py:67
  289.1 14.7 %collective-permute-start.15 = (f32[10,128,128]{1,2,0:T(8,128)S(1)}, f32[10,128,128]{1,2,0:T(8,128)S(1)}, u32[]{:S(2)}, u32[]{:S(2)}) collective-permute-start(f32[10,128,128]{1,2,0:T(8,128)S(1)} %add.494), channel_id=1, source_target_pairs={{0,8},{4,12},{8,0},{12,4},{16,24},{20,28},{24,16},{28,20},{1,9},{5... | collective-permute-start | bytes 1966088 | tf_op jit(solution)/shard_map/ppermute | solution.py:67
  303.9 28.7 %collective-permute-start.16 = (f32[10,128,128]{1,2,0:T(8,128)S(1)}, f32[10,128,128]{1,2,0:T(8,128)S(1)}, u32[]{:S(2)}, u32[]{:S(2)}) collective-permute-start(f32[10,128,128]{1,2,0:T(8,128)S(1)} %add.495), channel_id=1, source_target_pairs={{0,16},{4,20},{8,24},{12,28},{16,0},{20,4},{24,8},{28,12},{1,17},{... | collective-permute-start | bytes 1966088 | tf_op jit(solution)/shard_map/ppermute | solution.py:67
  451.9 12.6 %collective-permute-start.18 = (bf16[32,16,512]{2,0,1:T(8,128)(2,1)S(1)}, bf16[32,16,512]{2,0,1:T(8,128)(2,1)S(1)}, u32[]{:S(2)}, u32[]{:S(2)}) collective-permute-start(bf16[32,16,512]{2,0,1:T(8,128)(2,1)S(1)} %copy.99), channel_id=1, source_target_pairs={{0,8},{4,0},{12,4},{20,12},{28,20},{24,28},{16,24},{8,16},{1,9},{5... | collective-permute-start | bytes 1572872 | tf_op jit(solution)/shard_map/ppermute | solution.py:176
  453.0 14.1 %collective-permute-start.17 = (bf16[32,16,512]{2,0,1:T(8,128)(2,1)S(1)}, bf16[32,16,512]{2,0,1:T(8,128)(2,1)S(1)}, u32[]{:S(2)}, u32[]{:S(2)}) collective-permute-start(bf16[32,16,512]{2,0,1:T(8,128)(2,1)S(1)} %copy.97), channel_id=1, source_target_pairs={{0,4},{4,12},{12,20},{20,28},{28,24},{24,16},{16,8},{8,0},{1,5},{5... | collective-permute-start | bytes 1572872 | tf_op jit(solution)/shard_map/ppermute | solution.py:175
  464.5 12.5 %collective-permute-start.20 = (bf16[32,16,512]{2,0,1:T(8,128)(2,1)S(1)}, bf16[32,16,512]{2,0,1:T(8,128)(2,1)S(1)}, u32[]{:S(2)}, u32[]{:S(2)}) collective-permute-start(bf16[32,16,512]{2,0,1:T(8,128)(2,1)S(1)} %collective-permute-done.18), channel_id=1, source_target_pairs={{0,8},{4,0},{12,4},{20,12},{28,20},{24,28},{16,24},{8,16},{1,9},{5... | collective-permute-start | bytes 1572872 | tf_op jit(solution)/shard_map/ppermute | solution.py:176
  467.1 13.1 %collective-permute-start.19 = (bf16[32,16,512]{2,0,1:T(8,128)(2,1)S(1)}, bf16[32,16,512]{2,0,1:T(8,128)(2,1)S(1)}, u32[]{:S(2)}, u32[]{:S(2)}) collective-permute-start(bf16[32,16,512]{2,0,1:T(8,128)(2,1)S(1)} %collective-permute-done.17), channel_id=1, source_target_pairs={{0,4},{4,12},{12,20},{20,28},{28,24},{24,16},{16,8},{8,0},{1,5},{5... | collective-permute-start | bytes 1572872 | tf_op jit(solution)/shard_map/ppermute | solution.py:175
  477.0 12.7 %collective-permute-start.22 = (bf16[32,16,512]{2,0,1:T(8,128)(2,1)S(1)}, bf16[32,16,512]{2,0,1:T(8,128)(2,1)S(1)}, u32[]{:S(2)}, u32[]{:S(2)}) collective-permute-start(bf16[32,16,512]{2,0,1:T(8,128)(2,1)S(1)} %collective-permute-done.20), channel_id=1, source_target_pairs={{0,8},{4,0},{12,4},{20,12},{28,20},{24,28},{16,24},{8,16},{1,9},{5... | collective-permute-start | bytes 1572872 | tf_op jit(solution)/shard_map/ppermute | solution.py:176
  480.3 12.2 %collective-permute-start.21 = (bf16[32,16,512]{2,0,1:T(8,128)(2,1)S(1)}, bf16[32,16,512]{2,0,1:T(8,128)(2,1)S(1)}, u32[]{:S(2)}, u32[]{:S(2)}) collective-permute-start(bf16[32,16,512]{2,0,1:T(8,128)(2,1)S(1)} %collective-permute-done.19), channel_id=1, source_target_pairs={{0,4},{4,12},{12,20},{20,28},{28,24},{24,16},{16,8},{8,0},{1,5},{5... | collective-permute-start | bytes 1572872 | tf_op jit(solution)/shard_map/ppermute | solution.py:175
  489.7 13.5 %collective-permute-start.24 = (bf16[32,16,512]{2,0,1:T(8,128)(2,1)S(1)}, bf16[32,16,512]{2,0,1:T(8,128)(2,1)S(1)}, u32[]{:S(2)}, u32[]{:S(2)}) collective-permute-start(bf16[32,16,512]{2,0,1:T(8,128)(2,1)S(1)} %collective-permute-done.22), channel_id=1, source_target_pairs={{0,8},{4,0},{12,4},{20,12},{28,20},{24,28},{16,24},{8,16},{1,9},{5... | collective-permute-start | bytes 1572872 | tf_op jit(solution)/shard_map/ppermute | solution.py:176
  492.4 11.4 %collective-permute-start.23 = (bf16[32,16,512]{2,0,1:T(8,128)(2,1)S(1)}, bf16[32,16,512]{2,0,1:T(8,128)(2,1)S(1)}, u32[]{:S(2)}, u32[]{:S(2)}) collective-permute-start(bf16[32,16,512]{2,0,1:T(8,128)(2,1)S(1)} %collective-permute-done.21), channel_id=1, source_target_pairs={{0,4},{4,12},{12,20},{20,28},{28,24},{24,16},{16,8},{8,0},{1,5},{5... | collective-permute-start | bytes 1572872 | tf_op jit(solution)/shard_map/ppermute | solution.py:175
  503.2 12.1 %collective-permute-start.26 = (bf16[32,16,512]{2,0,1:T(8,128)(2,1)S(1)}, bf16[32,16,512]{2,0,1:T(8,128)(2,1)S(1)}, u32[]{:S(2)}, u32[]{:S(2)}) collective-permute-start(bf16[32,16,512]{2,0,1:T(8,128)(2,1)S(1)} %collective-permute-done.24), channel_id=1, source_target_pairs={{0,8},{4,0},{12,4},{20,12},{28,20},{24,28},{16,24},{8,16},{1,9},{5... | collective-permute-start | bytes 1572872 | tf_op jit(solution)/shard_map/ppermute | solution.py:176
  503.8 12.1 %collective-permute-start.25 = (bf16[32,16,512]{2,0,1:T(8,128)(2,1)S(1)}, bf16[32,16,512]{2,0,1:T(8,128)(2,1)S(1)}, u32[]{:S(2)}, u32[]{:S(2)}) collective-permute-start(bf16[32,16,512]{2,0,1:T(8,128)(2,1)S(1)} %collective-permute-done.23), channel_id=1, source_target_pairs={{0,4},{4,12},{12,20},{20,28},{28,24},{24,16},{16,8},{8,0},{1,5},{5... | collective-permute-start | bytes 1572872 | tf_op jit(solution)/shard_map/ppermute | solution.py:175
  515.3 12.1 %collective-permute-start.28 = (bf16[32,16,512]{2,0,1:T(8,128)(2,1)S(1)}, bf16[32,16,512]{2,0,1:T(8,128)(2,1)S(1)}, u32[]{:S(2)}, u32[]{:S(2)}) collective-permute-start(bf16[32,16,512]{2,0,1:T(8,128)(2,1)S(1)} %collective-permute-done.26), channel_id=1, source_target_pairs={{0,8},{4,0},{12,4},{20,12},{28,20},{24,28},{16,24},{8,16},{1,9},{5... | collective-permute-start | bytes 1572872 | tf_op jit(solution)/shard_map/ppermute | solution.py:176
  515.9 12.1 %collective-permute-start.27 = (bf16[32,16,512]{2,0,1:T(8,128)(2,1)S(1)}, bf16[32,16,512]{2,0,1:T(8,128)(2,1)S(1)}, u32[]{:S(2)}, u32[]{:S(2)}) collective-permute-start(bf16[32,16,512]{2,0,1:T(8,128)(2,1)S(1)} %collective-permute-done.25), channel_id=1, source_target_pairs={{0,4},{4,12},{12,20},{20,28},{28,24},{24,16},{16,8},{8,0},{1,5},{5... | collective-permute-start | bytes 1572872 | tf_op jit(solution)/shard_map/ppermute | solution.py:175
  528.0 9.8 %collective-permute-start.29 = (bf16[32,16,512]{2,0,1:T(8,128)(2,1)S(1)}, bf16[32,16,512]{2,0,1:T(8,128)(2,1)S(1)}, u32[]{:S(2)}, u32[]{:S(2)}) collective-permute-start(bf16[32,16,512]{2,0,1:T(8,128)(2,1)S(1)} %collective-permute-done.27), channel_id=1, source_target_pairs={{0,4},{4,12},{12,20},{20,28},{28,24},{24,16},{16,8},{8,0},{1,5},{5... | collective-permute-start | bytes 1572872 | tf_op jit(solution)/shard_map/ppermute | solution.py:175
  (22 other events, 404.5 us)
Sparse Core Ops, SparseCore 0:
  239.2 33.2 all-reduce.7
  539.5 38.0 all-reduce.9

commit v10 on v9

--- a/solution.py
+++ b/solution.py
@@ -59,23 +59,23 @@
     return jnp.concatenate(blocks, axis=1)
 
 
-def butterfly_sum(x, n):
+def butterfly_sum(x, n, axis="sum"):
     if n & (n - 1):
-        return lax.psum(x, "sum")
+        return lax.psum(x, axis)
     d = 1
     while d < n:
-        x = x + lax.ppermute(x, "sum", [(i, i ^ d) for i in range(n)])
+        x = x + lax.ppermute(x, axis, [(i, i ^ d) for i in range(n)])
         d *= 2
     return x
 
 
-def symmetric_psum(gram_part, n_sum):
+def symmetric_psum(gram_part, n_sum, n_mode):
     n = gram_part.shape[0]
     b = min(BLOCK, n)
     nb = n // b
     lower = [(i, j) for i in range(nb) for j in range(i + 1)]
     packed = jnp.stack([gram_part[i * b:(i + 1) * b, j * b:(j + 1) * b] for i, j in lower])
-    packed = butterfly_sum(lax.psum(packed, "mode"), n_sum)
+    packed = butterfly_sum(butterfly_sum(packed, n_mode, "mode"), n_sum)
     where = {cell: k for k, cell in enumerate(lower)}
     rows = []
     for i in range(nb):
@@ -179,7 +179,7 @@
     return jnp.transpose(total, (1, 0, 2))
 
 
-def per_device(ring, left_cores, right_cores, sketch):
+def per_device(ring, n_mode, left_cores, right_cores, sketch):
     sum_local, rows_in, mode_local, rank_width = left_cores.shape
     target = sketch.shape[2]
     partial_map = lax.dot_general(
@@ -198,12 +198,12 @@
     share = ring_reduce_scatter(local_rows, rows_in, ring)
     flat_share = share.reshape(-1, target)
     gram_part = jnp.dot(flat_share.T, flat_share, precision=HI)
-    gram = symmetric_psum(gram_part, len(ring))
+    gram = symmetric_psum(gram_part, len(ring), n_mode)
     basis = orthonormal(flat_share, gram)
     block = basis.reshape(share.shape)
     rounded = block.astype(jnp.bfloat16)
     partial_carry = ring_gather_carries(rounded, left_cores, ring)
-    carries = lax.psum(partial_carry, "mode")
+    carries = butterfly_sum(partial_carry, n_mode, "mode")
     return (block * factor, carries)
 
 
@@ -212,5 +212,5 @@
     out_specs = (P("sum", "mode", None), P("sum", None, None))
     ring = ring_order(mesh)
     return jax.shard_map(
-        functools.partial(per_device, ring), mesh=mesh, in_specs=in_specs, out_specs=out_specs, check_vma=False
-    )
+        functools.partial(per_device, ring, mesh.shape["mode"]), mesh=mesh, in_specs=in_specs, out_specs=out_specs, check_vma=False
+    )

time: 597 us -> 556 us (0.931)
  waiting for transfers between devices: 274 us -> 251 us
  between operations: 35.2 us -> 21.9 us
    psum x2 -> x0, waiting for transfers between devices: 68.3 us -> none  [the longest x1 34.9 us: per_device(): carries = lax.psum(partial_carry, 'mode')]
    ppermute x3 -> x7, waiting for transfers between devices: 34.5 us -> 79.7 us  [butterfly_sum(): x = x + lax.ppermute(x, axis, [(i, i ^ d) for i in range(n)])]
  transfers between devices with their start and end apart: 33 -> 35, of which waited for: 28 -> 29; matrix products, arithmetic and copies ran while one was open for 10% -> 11% of each run, Pallas kernels for 0% -> 0%
where the time goes in v10:
time: 556 us; the launch traced here: 546 us
  waiting for transfers between devices  251 us (45%)
  other arithmetic  116 us (21%)
  matrix products  75.7 us (14%)
  starting transfers between devices  37.6 us (7%)
  blocking collectives  27.9 us (5%)
  between operations  21.9 us (4%)
  local copies, waits for them, and re-layouts  15.8 us (3%)
    ppermute x7, waiting for transfers between devices, ring_reduce_scatter(): acc_f = lax.ppermute(acc_f, 'sum', fwd) + piece(fwd_blocks[t, me], 0, half)  87.7 us
    ppermute x7, waiting for transfers between devices, butterfly_sum(): x = x + lax.ppermute(x, axis, [(i, i ^ d) for i in range(n)])  79.7 us
    ppermute x7, waiting for transfers between devices, ring_gather_carries(): hold_b = lax.ppermute(hold_b, 'sum', bwd)  59.1 us
    another operation x12, other arithmetic, orthonormal(): lkk = jnp.linalg.cholesky(diag)  49.6 us
    another operation x9, other arithmetic, tri_inverse(): inv = lax.linalg.triangular_solve(diag, eye, left_side=True, lower=True)  40 us
    psum x1, blocking collectives, per_device(): mapped = lax.psum(partial_map, 'mode').astype(jnp.bfloat16)  27.9 us
    dot_general x16, matrix products, local_rows(): lax.dot_general(part, mapped, (((0, 3), (0, 1)), ((), ())), preferred_ele...  26 us
    ppermute x7, waiting for transfers between devices, ring_reduce_scatter(): lax.ppermute(acc_b, 'sum', bwd)  23.7 us
  transfers between devices with their start and end apart: 35, of which 29 were waited for; matrix products, arithmetic and copies ran while one was open for 11% of the time, Pallas kernels for 0%

profile of v10, /device:TPU:0, one launch (start us, length us, event | category | flops | bytes accessed | tf_op | source)
XLA Modules:
  0.0 545.8 jit_solution(16958446937507955141)
XLA Ops:
  2.9 17.1 %fusion.8 = f32[1,512,512]{2,1,0:T(8,128)S(1)} fusion(bf16[16,512,512]{2,1,0:T(8,128)(2,1)} %param.12, bf16[512,16,512]{2,1,0:T(8,128)(2,1)} %bitcast.440), kind=kOutput, calls=%fused_computation.29 | convolution fusion | flops 4294967296 | bytes 17825792 | tf_op jit(solution)/shard_map/dot_general | solution.py:185
  20.0 27.9 %all-reduce.5 = bf16[1,512,512]{2,1,0:T(8,128)(2,1)S(1)} all-reduce(f32[1,512,512]{2,1,0:T(8,128)S(1)} %fusion.8), channel_id=1, replica_groups=mesh['sum'=8,'mode'=4] {'mode'}, use_global_device_ids=true, to_apply=%region_0.0 | all-reduce | flops 262144 | bytes 1572864 | tf_op jit(solution)/shard_map/psum | solution.py:188
  55.8 19.1 %collective-permute-done = f32[32,16,512]{2,1,0:T(8,128)S(1)} collective-permute-done((f32[32,16,512]{2,1,0:T(8,128)S(1)}, f32[32,16,512]{2,1,0:T(8,128)S(1)}, u32[]{:S(2)}, u32[]{:S(2)}) %collective-permute-start) | collective-permute-done | bytes 1048608 | tf_op jit(solution)/shard_map/ppermute | solution.py:142
  87.1 14.0 %collective-permute-done.1 = f32[32,16,512]{2,1,0:T(8,128)S(1)} collective-permute-done((f32[32,16,512]{2,1,0:T(8,128)S(1)}, f32[32,16,512]{2,1,0:T(8,128)S(1)}, u32[]{:S(2)}, u32[]{:S(2)}) %collective-permute-start.1) | collective-permute-done | bytes 1048608 | tf_op jit(solution)/shard_map/ppermute | solution.py:142
  103.0 4.0 collective-permute-done.8
  113.2 12.3 %collective-permute-done.2 = f32[32,16,512]{2,1,0:T(8,128)} collective-permute-done((f32[32,16,512]{2,1,0:T(8,128)S(1)}, f32[32,16,512]{2,1,0:T(8,128)}, u32[]{:S(2)}, u32[]{:S(2)}) %collective-permute-start.2) | collective-permute-done | bytes 1048608 | tf_op jit(solution)/shard_map/ppermute | solution.py:142
  138.1 12.0 %collective-permute-done.3 = f32[32,16,512]{2,1,0:T(8,128)} collective-permute-done((f32[32,16,512]{2,1,0:T(8,128)S(1)}, f32[32,16,512]{2,1,0:T(8,128)}, u32[]{:S(2)}, u32[]{:S(2)}) %collective-permute-start.3) | collective-permute-done | bytes 1048608 | tf_op jit(solution)/shard_map/ppermute | solution.py:142
  162.7 11.1 %collective-permute-done.4 = f32[32,16,512]{2,1,0:T(8,128)} collective-permute-done((f32[32,16,512]{2,1,0:T(8,128)S(1)}, f32[32,16,512]{2,1,0:T(8,128)}, u32[]{:S(2)}, u32[]{:S(2)}) %collective-permute-start.4) | collective-permute-done | bytes 1048608 | tf_op jit(solution)/shard_map/ppermute | solution.py:142
  186.8 10.3 %collective-permute-done.5 = f32[32,16,512]{2,1,0:T(8,128)} collective-permute-done((f32[32,16,512]{2,1,0:T(8,128)S(1)}, f32[32,16,512]{2,1,0:T(8,128)}, u32[]{:S(2)}, u32[]{:S(2)}) %collective-permute-start.5) | collective-permute-done | bytes 1048608 | tf_op jit(solution)/shard_map/ppermute | solution.py:142
  210.1 8.8 %collective-permute-done.6 = f32[32,16,512]{2,1,0:T(8,128)S(1)} collective-permute-done((f32[32,16,512]{2,1,0:T(8,128)S(1)}, f32[32,16,512]{2,1,0:T(8,128)S(1)}, u32[]{:S(2)}, u32[]{:S(2)}) %collective-permute-start.6) | collective-permute-done | bytes 1048608 | tf_op jit(solution)/shard_map/ppermute | solution.py:142
  219.2 6.3 %collective-permute-done.13 = f32[32,16,512]{2,1,0:T(8,128)} collective-permute-done((f32[32,16,512]{2,1,0:T(8,128)}, f32[32,16,512]{2,1,0:T(8,128)}, u32[]{:S(2)}, u32[]{:S(2)}) %collective-permute-start.13) | collective-permute-done | bytes 1048608 | tf_op jit(solution)/shard_map/ppermute | solution.py:143
  227.8 3.6 convolution_bitcast_fusion.16
  234.7 16.0 %collective-permute-done.15 = f32[10,128,128]{1,2,0:T(8,128)S(1)} collective-permute-done((f32[10,128,128]{1,2,0:T(8,128)S(1)}, f32[10,128,128]{1,2,0:T(8,128)S(1)}, u32[]{:S(2)}, u32[]{:S(2)}) %collective-permute-start.15) | collective-permute-done | bytes 655392 | tf_op jit(solution)/shard_map/ppermute | solution.py:67
  252.4 14.3 %collective-permute-done.16 = f32[10,128,128]{1,2,0:T(8,128)S(1)} collective-permute-done((f32[10,128,128]{1,2,0:T(8,128)S(1)}, f32[10,128,128]{1,2,0:T(8,128)S(1)}, u32[]{:S(2)}, u32[]{:S(2)}) %collective-permute-start.16) | collective-permute-done | bytes 655392 | tf_op jit(solution)/shard_map/ppermute | solution.py:67
  284.8 6.0 %constant_dynamic-slice_fusion.1 = (bf16[1,32,16,512]{3,2,1,0:T(8,128)(2,1)}, bf16[1,32,16,512]{3,2,1,0:T(8,128)(2,1)}, bf16[1,32,16,512]{3,2,1,0:T(8,128)(2,1)}...) fusion(bf16[1,512,16,512]{3,2,1,0:T(8,128)(2,1)} %param.10, ...), kind=kLoop, calls=%fused_computation.306 | loop fusion | bytes 14680120 | tf_op jit(solution)/shard_map/dynamic_slice | solution.py:166
  292.3 19.2 %collective-permute-done.18 = f32[10,128,128]{1,2,0:T(8,128)S(1)} collective-permute-done((f32[10,128,128]{1,2,0:T(8,128)S(1)}, f32[10,128,128]{1,2,0:T(8,128)S(1)}, u32[]{:S(2)}, u32[]{:S(2)}) %collective-permute-start.18) | collective-permute-done | bytes 655392 | tf_op jit(solution)/shard_map/ppermute | solution.py:67
  312.4 11.7 %cholesky.74 = f32[128,128]{1,0:T(8,128)S(1)} custom-call(f32[128,128]{1,0:T(8,128)S(1)} %fusion.183), custom_call_target="Cholesky" | custom-call | tf_op jit(solution)/shard_map/jit(cholesky)/cholesky | solution.py:42
  325.7 10.0 %custom-call.8 = f32[2,1,64,64]{2,3,1,0:T(8,128)S(1)} custom-call(f32[2,1,64,64]{3,2,1,0:T(8,128)S(1)} %fusion.176), custom_call_target="InvertDiagBlocksLowerTriangular" | custom-call | tf_op jit(solution)/shard_map/triangular_solve/custom-call.0 | solution.py:26
  341.4 11.7 %cholesky.85 = f32[128,128]{1,0:T(8,128)S(1)} custom-call(f32[128,128]{1,0:T(8,128)S(1)} %fusion.192), custom_call_target="Cholesky" | custom-call | tf_op jit(solution)/shard_map/jit(cholesky)/cholesky | solution.py:42
  354.6 9.8 %custom-call.9 = f32[2,1,64,64]{2,3,1,0:T(8,128)S(1)} custom-call(f32[2,1,64,64]{3,2,1,0:T(8,128)S(1)} %fusion.177), custom_call_target="InvertDiagBlocksLowerTriangular" | custom-call | tf_op jit(solution)/shard_map/triangular_solve/custom-call.0 | solution.py:26
  367.8 11.7 %cholesky.96 = f32[128,128]{1,0:T(8,128)S(1)} custom-call(f32[128,128]{1,0:T(8,128)S(1)} %fusion.189), custom_call_target="Cholesky" | custom-call | tf_op jit(solution)/shard_map/jit(cholesky)/cholesky | solution.py:42
  380.9 9.8 %custom-call.10 = f32[2,1,64,64]{2,3,1,0:T(8,128)S(1)} custom-call(f32[2,1,64,64]{3,2,1,0:T(8,128)S(1)} %fusion.178), custom_call_target="InvertDiagBlocksLowerTriangular" | custom-call | tf_op jit(solution)/shard_map/triangular_solve/custom-call.0 | solution.py:26
  392.1 11.7 %cholesky.107 = f32[128,128]{1,0:T(8,128)S(1)} custom-call(f32[128,128]{1,0:T(8,128)S(1)} %fusion.186), custom_call_target="Cholesky" | custom-call | tf_op jit(solution)/shard_map/jit(cholesky)/cholesky | solution.py:42
  405.3 10.2 %custom-call.11 = f32[2,1,64,64]{2,3,1,0:T(8,128)S(1)} custom-call(f32[2,1,64,64]{3,2,1,0:T(8,128)S(1)} %fusion.179), custom_call_target="InvertDiagBlocksLowerTriangular" | custom-call | tf_op jit(solution)/shard_map/triangular_solve/custom-call.0 | solution.py:26
  432.7 8.5 %collective-permute-done.20 = bf16[32,16,512]{2,0,1:T(8,128)(2,1)S(1)} collective-permute-done((bf16[32,16,512]{2,0,1:T(8,128)(2,1)S(1)}, bf16[32,16,512]{2,0,1:T(8,128)(2,1)S(1)}, u32[]{:S(2)}, u32[]{:S(2)}) %collective-permute-start.20) | collective-permute-done | bytes 524320 | tf_op jit(solution)/shard_map/ppermute | solution.py:176
  444.6 8.6 %collective-permute-done.22 = bf16[32,16,512]{2,0,1:T(8,128)(2,1)S(1)} collective-permute-done((bf16[32,16,512]{2,0,1:T(8,128)(2,1)S(1)}, bf16[32,16,512]{2,0,1:T(8,128)(2,1)S(1)}, u32[]{:S(2)}, u32[]{:S(2)}) %collective-permute-start.22) | collective-permute-done | bytes 524320 | tf_op jit(solution)/shard_map/ppermute | solution.py:176
  456.7 8.8 %collective-permute-done.24 = bf16[32,16,512]{2,0,1:T(8,128)(2,1)S(1)} collective-permute-done((bf16[32,16,512]{2,0,1:T(8,128)(2,1)S(1)}, bf16[32,16,512]{2,0,1:T(8,128)(2,1)S(1)}, u32[]{:S(2)}, u32[]{:S(2)}) %collective-permute-start.24) | collective-permute-done | bytes 524320 | tf_op jit(solution)/shard_map/ppermute | solution.py:176
  468.8 8.8 %collective-permute-done.26 = bf16[32,16,512]{2,0,1:T(8,128)(2,1)S(1)} collective-permute-done((bf16[32,16,512]{2,0,1:T(8,128)(2,1)S(1)}, bf16[32,16,512]{2,0,1:T(8,128)(2,1)S(1)}, u32[]{:S(2)}, u32[]{:S(2)}) %collective-permute-start.26) | collective-permute-done | bytes 524320 | tf_op jit(solution)/shard_map/ppermute | solution.py:176
  480.9 8.8 %collective-permute-done.28 = bf16[32,16,512]{2,0,1:T(8,128)(2,1)S(1)} collective-permute-done((bf16[32,16,512]{2,0,1:T(8,128)(2,1)S(1)}, bf16[32,16,512]{2,0,1:T(8,128)(2,1)S(1)}, u32[]{:S(2)}, u32[]{:S(2)}) %collective-permute-start.28) | collective-permute-done | bytes 524320 | tf_op jit(solution)/shard_map/ppermute | solution.py:176
  493.0 9.7 %collective-permute-done.30 = bf16[32,16,512]{2,0,1:T(8,128)(2,1)S(1)} collective-permute-done((bf16[32,16,512]{2,0,1:T(8,128)(2,1)S(1)}, bf16[32,16,512]{2,0,1:T(8,128)(2,1)S(1)}, u32[]{:S(2)}, u32[]{:S(2)}) %collective-permute-start.30) | collective-permute-done | bytes 524320 | tf_op jit(solution)/shard_map/ppermute | solution.py:176
  506.0 5.9 %collective-permute-done.32 = bf16[32,16,512]{2,0,1:T(8,128)(2,1)S(1)} collective-permute-done((bf16[32,16,512]{2,0,1:T(8,128)(2,1)S(1)}, bf16[32,16,512]{2,0,1:T(8,128)(2,1)S(1)}, u32[]{:S(2)}, u32[]{:S(2)}) %collective-permute-start.32) | collective-permute-done | bytes 524320 | tf_op jit(solution)/shard_map/ppermute | solution.py:176
  520.3 22.5 %collective-permute-done.34 = f32[1,512,512]{2,1,0:T(8,128)} collective-permute-done((f32[1,512,512]{2,1,0:T(8,128)}, f32[1,512,512]{2,1,0:T(8,128)}, u32[]{:S(2)}, u32[]{:S(2)}) %collective-permute-start.34) | collective-permute-done | bytes 1048608 | tf_op jit(solution)/shard_map/ppermute | solution.py:67
  (236 shorter events, 153.3 us)
Async XLA Ops:
  49.4 25.5 %collective-permute-start = (f32[32,16,512]{2,1,0:T(8,128)S(1)}, f32[32,16,512]{2,1,0:T(8,128)S(1)}, u32[]{:S(2)}, u32[]{:S(2)}) collective-permute-start(f32[32,16,512]{2,1,0:T(8,128)S(1)} %fusion.98), channel_id=1, source_target_pairs={{0,4},{4,12},{12,20},{20,28},{28,24},{24,16},{16,8},{8,0},{1,5},{5... | collective-permute-start | bytes 3145736 | tf_op jit(solution)/shard_map/ppermute | solution.py:142
  54.1 25.5 %collective-permute-start.7 = (f32[32,16,512]{2,1,0:T(8,128)}, f32[32,16,512]{2,1,0:T(8,128)}, u32[]{:S(2)}, u32[]{:S(2)}) collective-permute-start(f32[32,16,512]{2,1,0:T(8,128)} %fusion.68), channel_id=1, source_target_pairs={{0,8},{4,0},{12,4},{20,12},{28,20},{24,28},{16,24},{8,16},{1,9},{5... | collective-permute-start | bytes 3145736 | tf_op jit(solution)/shard_map/ppermute | solution.py:143
  76.4 24.8 %collective-permute-start.1 = (f32[32,16,512]{2,1,0:T(8,128)S(1)}, f32[32,16,512]{2,1,0:T(8,128)S(1)}, u32[]{:S(2)}, u32[]{:S(2)}) collective-permute-start(f32[32,16,512]{2,1,0:T(8,128)S(1)} %convolution_add_fusion.1), channel_id=1, source_target_pairs={{0,4},{4,12},{12,20},{20,28},{28,24},{24,16},{16,8},{8,0},{1,5},{5... | collective-permute-start | bytes 3145736 | tf_op jit(solution)/shard_map/ppermute | solution.py:142
  82.4 24.6 %collective-permute-start.8 = (f32[32,16,512]{2,1,0:T(8,128)}, f32[32,16,512]{2,1,0:T(8,128)}, u32[]{:S(2)}, u32[]{:S(2)}) collective-permute-start(f32[32,16,512]{2,1,0:T(8,128)} %convolution_add_fusion), channel_id=1, source_target_pairs={{0,8},{4,0},{12,4},{20,12},{28,20},{24,28},{16,24},{8,16},{1,9},{5... | collective-permute-start | bytes 3145736 | tf_op jit(solution)/shard_map/ppermute | solution.py:143
  101.4 24.1 %collective-permute-start.2 = (f32[32,16,512]{2,1,0:T(8,128)S(1)}, f32[32,16,512]{2,1,0:T(8,128)}, u32[]{:S(2)}, u32[]{:S(2)}) collective-permute-start(f32[32,16,512]{2,1,0:T(8,128)S(1)} %add.452), channel_id=1, source_target_pairs={{0,4},{4,12},{12,20},{20,28},{28,24},{24,16},{16,8},{8,0},{1,5},{5... | collective-permute-start | bytes 3145736 | tf_op jit(solution)/shard_map/ppermute | solution.py:142
  108.4 23.5 %collective-permute-start.9 = (f32[32,16,512]{2,1,0:T(8,128)S(1)}, f32[32,16,512]{2,1,0:T(8,128)}, u32[]{:S(2)}, u32[]{:S(2)}) collective-permute-start(f32[32,16,512]{2,1,0:T(8,128)S(1)} %add.476), channel_id=1, source_target_pairs={{0,8},{4,0},{12,4},{20,12},{28,20},{24,28},{16,24},{8,16},{1,9},{5... | collective-permute-start | bytes 3145736 | tf_op jit(solution)/shard_map/ppermute | solution.py:143
  126.9 23.2 %collective-permute-start.3 = (f32[32,16,512]{2,1,0:T(8,128)S(1)}, f32[32,16,512]{2,1,0:T(8,128)}, u32[]{:S(2)}, u32[]{:S(2)}) collective-permute-start(f32[32,16,512]{2,1,0:T(8,128)S(1)} %add.454), channel_id=1, source_target_pairs={{0,4},{4,12},{12,20},{20,28},{28,24},{24,16},{16,8},{8,0},{1,5},{5... | collective-permute-start | bytes 3145736 | tf_op jit(solution)/shard_map/ppermute | solution.py:142
  133.4 22.6 %collective-permute-start.10 = (f32[32,16,512]{2,1,0:T(8,128)S(1)}, f32[32,16,512]{2,1,0:T(8,128)}, u32[]{:S(2)}, u32[]{:S(2)}) collective-permute-start(f32[32,16,512]{2,1,0:T(8,128)S(1)} %add.481), channel_id=1, source_target_pairs={{0,8},{4,0},{12,4},{20,12},{28,20},{24,28},{16,24},{8,16},{1,9},{5... | collective-permute-start | bytes 3145736 | tf_op jit(solution)/shard_map/ppermute | solution.py:143
  151.5 22.2 %collective-permute-start.4 = (f32[32,16,512]{2,1,0:T(8,128)S(1)}, f32[32,16,512]{2,1,0:T(8,128)}, u32[]{:S(2)}, u32[]{:S(2)}) collective-permute-start(f32[32,16,512]{2,1,0:T(8,128)S(1)} %add.456), channel_id=1, source_target_pairs={{0,4},{4,12},{12,20},{20,28},{28,24},{24,16},{16,8},{8,0},{1,5},{5... | collective-permute-start | bytes 3145736 | tf_op jit(solution)/shard_map/ppermute | solution.py:142
  157.5 22.2 %collective-permute-start.11 = (f32[32,16,512]{2,1,0:T(8,128)S(1)}, f32[32,16,512]{2,1,0:T(8,128)}, u32[]{:S(2)}, u32[]{:S(2)}) collective-permute-start(f32[32,16,512]{2,1,0:T(8,128)S(1)} %add.486), channel_id=1, source_target_pairs={{0,8},{4,0},{12,4},{20,12},{28,20},{24,28},{16,24},{8,16},{1,9},{5... | collective-permute-start | bytes 3145736 | tf_op jit(solution)/shard_map/ppermute | solution.py:143
  175.2 21.9 %collective-permute-start.5 = (f32[32,16,512]{2,1,0:T(8,128)S(1)}, f32[32,16,512]{2,1,0:T(8,128)}, u32[]{:S(2)}, u32[]{:S(2)}) collective-permute-start(f32[32,16,512]{2,1,0:T(8,128)S(1)} %add.458), channel_id=1, source_target_pairs={{0,4},{4,12},{12,20},{20,28},{28,24},{24,16},{16,8},{8,0},{1,5},{5... | collective-permute-start | bytes 3145736 | tf_op jit(solution)/shard_map/ppermute | solution.py:142
  182.0 20.9 %collective-permute-start.12 = (f32[32,16,512]{2,1,0:T(8,128)}, f32[32,16,512]{2,1,0:T(8,128)}, u32[]{:S(2)}, u32[]{:S(2)}) collective-permute-start(f32[32,16,512]{2,1,0:T(8,128)} %add.491), channel_id=1, source_target_pairs={{0,8},{4,0},{12,4},{20,12},{28,20},{24,28},{16,24},{8,16},{1,9},{5... | collective-permute-start | bytes 3145736 | tf_op jit(solution)/shard_map/ppermute | solution.py:143
  198.5 20.4 %collective-permute-start.6 = (f32[32,16,512]{2,1,0:T(8,128)S(1)}, f32[32,16,512]{2,1,0:T(8,128)S(1)}, u32[]{:S(2)}, u32[]{:S(2)}) collective-permute-start(f32[32,16,512]{2,1,0:T(8,128)S(1)} %add.460), channel_id=1, source_target_pairs={{0,4},{4,12},{12,20},{20,28},{28,24},{24,16},{16,8},{8,0},{1,5},{5... | collective-permute-start | bytes 3145736 | tf_op jit(solution)/shard_map/ppermute | solution.py:142
  205.3 20.1 %collective-permute-start.13 = (f32[32,16,512]{2,1,0:T(8,128)}, f32[32,16,512]{2,1,0:T(8,128)}, u32[]{:S(2)}, u32[]{:S(2)}) collective-permute-start(f32[32,16,512]{2,1,0:T(8,128)} %add.496), channel_id=1, source_target_pairs={{0,8},{4,0},{12,4},{20,12},{28,20},{24,28},{16,24},{8,16},{1,9},{5... | collective-permute-start | bytes 3145736 | tf_op jit(solution)/shard_map/ppermute | solution.py:143
  233.8 16.8 %collective-permute-start.15 = (f32[10,128,128]{1,2,0:T(8,128)S(1)}, f32[10,128,128]{1,2,0:T(8,128)S(1)}, u32[]{:S(2)}, u32[]{:S(2)}) collective-permute-start(f32[10,128,128]{1,2,0:T(8,128)S(1)} %add.502), channel_id=1, source_target_pairs={{0,2},{1,3},{2,0},{3,1},{4,6},{5,7},{6,4},{7,5},{8,10},{9,11},{10,... | collective-permute-start | bytes 1966088 | tf_op jit(solution)/shard_map/ppermute | solution.py:67
  250.8 16.0 %collective-permute-start.16 = (f32[10,128,128]{1,2,0:T(8,128)S(1)}, f32[10,128,128]{1,2,0:T(8,128)S(1)}, u32[]{:S(2)}, u32[]{:S(2)}) collective-permute-start(f32[10,128,128]{1,2,0:T(8,128)S(1)} %add.503), channel_id=1, source_target_pairs={{0,4},{4,0},{8,12},{12,8},{16,20},{20,16},{24,28},{28,24},{1,5},{5... | collective-permute-start | bytes 1966088 | tf_op jit(solution)/shard_map/ppermute | solution.py:67
  266.8 15.1 %collective-permute-start.17 = (f32[10,128,128]{1,2,0:T(8,128)S(1)}, f32[10,128,128]{1,2,0:T(8,128)S(1)}, u32[]{:S(2)}, u32[]{:S(2)}) collective-permute-start(f32[10,128,128]{1,2,0:T(8,128)S(1)} %add.504), channel_id=1, source_target_pairs={{0,8},{4,12},{8,0},{12,4},{16,24},{20,28},{24,16},{28,20},{1,9},{5... | collective-permute-start | bytes 1966088 | tf_op jit(solution)/shard_map/ppermute | solution.py:67
  282.0 29.5 %collective-permute-start.18 = (f32[10,128,128]{1,2,0:T(8,128)S(1)}, f32[10,128,128]{1,2,0:T(8,128)S(1)}, u32[]{:S(2)}, u32[]{:S(2)}) collective-permute-start(f32[10,128,128]{1,2,0:T(8,128)S(1)} %add.505), channel_id=1, source_target_pairs={{0,16},{4,20},{8,24},{12,28},{16,0},{20,4},{24,8},{28,12},{1,17},{... | collective-permute-start | bytes 1966088 | tf_op jit(solution)/shard_map/ppermute | solution.py:67
  428.4 12.8 %collective-permute-start.20 = (bf16[32,16,512]{2,0,1:T(8,128)(2,1)S(1)}, bf16[32,16,512]{2,0,1:T(8,128)(2,1)S(1)}, u32[]{:S(2)}, u32[]{:S(2)}) collective-permute-start(bf16[32,16,512]{2,0,1:T(8,128)(2,1)S(1)} %copy.79), channel_id=1, source_target_pairs={{0,8},{4,0},{12,4},{20,12},{28,20},{24,28},{16,24},{8,16},{1,9},{5... | collective-permute-start | bytes 1572872 | tf_op jit(solution)/shard_map/ppermute | solution.py:176
  428.8 13.4 %collective-permute-start.19 = (bf16[32,16,512]{2,0,1:T(8,128)(2,1)S(1)}, bf16[32,16,512]{2,0,1:T(8,128)(2,1)S(1)}, u32[]{:S(2)}, u32[]{:S(2)}) collective-permute-start(bf16[32,16,512]{2,0,1:T(8,128)(2,1)S(1)} %copy.77), channel_id=1, source_target_pairs={{0,4},{4,12},{12,20},{20,28},{28,24},{24,16},{16,8},{8,0},{1,5},{5... | collective-permute-start | bytes 1572872 | tf_op jit(solution)/shard_map/ppermute | solution.py:175
  441.3 11.9 %collective-permute-start.22 = (bf16[32,16,512]{2,0,1:T(8,128)(2,1)S(1)}, bf16[32,16,512]{2,0,1:T(8,128)(2,1)S(1)}, u32[]{:S(2)}, u32[]{:S(2)}) collective-permute-start(bf16[32,16,512]{2,0,1:T(8,128)(2,1)S(1)} %collective-permute-done.20), channel_id=1, source_target_pairs={{0,8},{4,0},{12,4},{20,12},{28,20},{24,28},{16,24},{8,16},{1,9},{5... | collective-permute-start | bytes 1572872 | tf_op jit(solution)/shard_map/ppermute | solution.py:176
  442.2 12.3 %collective-permute-start.21 = (bf16[32,16,512]{2,0,1:T(8,128)(2,1)S(1)}, bf16[32,16,512]{2,0,1:T(8,128)(2,1)S(1)}, u32[]{:S(2)}, u32[]{:S(2)}) collective-permute-start(bf16[32,16,512]{2,0,1:T(8,128)(2,1)S(1)} %collective-permute-done.19), channel_id=1, source_target_pairs={{0,4},{4,12},{12,20},{20,28},{28,24},{24,16},{16,8},{8,0},{1,5},{5... | collective-permute-start | bytes 1572872 | tf_op jit(solution)/shard_map/ppermute | solution.py:175
  453.2 12.2 %collective-permute-start.24 = (bf16[32,16,512]{2,0,1:T(8,128)(2,1)S(1)}, bf16[32,16,512]{2,0,1:T(8,128)(2,1)S(1)}, u32[]{:S(2)}, u32[]{:S(2)}) collective-permute-start(bf16[32,16,512]{2,0,1:T(8,128)(2,1)S(1)} %collective-permute-done.22), channel_id=1, source_target_pairs={{0,8},{4,0},{12,4},{20,12},{28,20},{24,28},{16,24},{8,16},{1,9},{5... | collective-permute-start | bytes 1572872 | tf_op jit(solution)/shard_map/ppermute | solution.py:176
  454.5 12.1 %collective-permute-start.23 = (bf16[32,16,512]{2,0,1:T(8,128)(2,1)S(1)}, bf16[32,16,512]{2,0,1:T(8,128)(2,1)S(1)}, u32[]{:S(2)}, u32[]{:S(2)}) collective-permute-start(bf16[32,16,512]{2,0,1:T(8,128)(2,1)S(1)} %collective-permute-done.21), channel_id=1, source_target_pairs={{0,4},{4,12},{12,20},{20,28},{28,24},{24,16},{16,8},{8,0},{1,5},{5... | collective-permute-start | bytes 1572872 | tf_op jit(solution)/shard_map/ppermute | solution.py:175
  465.5 12.1 %collective-permute-start.26 = (bf16[32,16,512]{2,0,1:T(8,128)(2,1)S(1)}, bf16[32,16,512]{2,0,1:T(8,128)(2,1)S(1)}, u32[]{:S(2)}, u32[]{:S(2)}) collective-permute-start(bf16[32,16,512]{2,0,1:T(8,128)(2,1)S(1)} %collective-permute-done.24), channel_id=1, source_target_pairs={{0,8},{4,0},{12,4},{20,12},{28,20},{24,28},{16,24},{8,16},{1,9},{5... | collective-permute-start | bytes 1572872 | tf_op jit(solution)/shard_map/ppermute | solution.py:176
  466.6 12.1 %collective-permute-start.25 = (bf16[32,16,512]{2,0,1:T(8,128)(2,1)S(1)}, bf16[32,16,512]{2,0,1:T(8,128)(2,1)S(1)}, u32[]{:S(2)}, u32[]{:S(2)}) collective-permute-start(bf16[32,16,512]{2,0,1:T(8,128)(2,1)S(1)} %collective-permute-done.23), channel_id=1, source_target_pairs={{0,4},{4,12},{12,20},{20,28},{28,24},{24,16},{16,8},{8,0},{1,5},{5... | collective-permute-start | bytes 1572872 | tf_op jit(solution)/shard_map/ppermute | solution.py:175
  477.5 12.1 %collective-permute-start.28 = (bf16[32,16,512]{2,0,1:T(8,128)(2,1)S(1)}, bf16[32,16,512]{2,0,1:T(8,128)(2,1)S(1)}, u32[]{:S(2)}, u32[]{:S(2)}) collective-permute-start(bf16[32,16,512]{2,0,1:T(8,128)(2,1)S(1)} %collective-permute-done.26), channel_id=1, source_target_pairs={{0,8},{4,0},{12,4},{20,12},{28,20},{24,28},{16,24},{8,16},{1,9},{5... | collective-permute-start | bytes 1572872 | tf_op jit(solution)/shard_map/ppermute | solution.py:176
  478.7 12.1 %collective-permute-start.27 = (bf16[32,16,512]{2,0,1:T(8,128)(2,1)S(1)}, bf16[32,16,512]{2,0,1:T(8,128)(2,1)S(1)}, u32[]{:S(2)}, u32[]{:S(2)}) collective-permute-start(bf16[32,16,512]{2,0,1:T(8,128)(2,1)S(1)} %collective-permute-done.25), channel_id=1, source_target_pairs={{0,4},{4,12},{12,20},{20,28},{28,24},{24,16},{16,8},{8,0},{1,5},{5... | collective-permute-start | bytes 1572872 | tf_op jit(solution)/shard_map/ppermute | solution.py:175
  489.6 13.0 %collective-permute-start.30 = (bf16[32,16,512]{2,0,1:T(8,128)(2,1)S(1)}, bf16[32,16,512]{2,0,1:T(8,128)(2,1)S(1)}, u32[]{:S(2)}, u32[]{:S(2)}) collective-permute-start(bf16[32,16,512]{2,0,1:T(8,128)(2,1)S(1)} %collective-permute-done.28), channel_id=1, source_target_pairs={{0,8},{4,0},{12,4},{20,12},{28,20},{24,28},{16,24},{8,16},{1,9},{5... | collective-permute-start | bytes 1572872 | tf_op jit(solution)/shard_map/ppermute | solution.py:176
  490.8 12.9 %collective-permute-start.29 = (bf16[32,16,512]{2,0,1:T(8,128)(2,1)S(1)}, bf16[32,16,512]{2,0,1:T(8,128)(2,1)S(1)}, u32[]{:S(2)}, u32[]{:S(2)}) collective-permute-start(bf16[32,16,512]{2,0,1:T(8,128)(2,1)S(1)} %collective-permute-done.27), channel_id=1, source_target_pairs={{0,4},{4,12},{12,20},{20,28},{28,24},{24,16},{16,8},{8,0},{1,5},{5... | collective-permute-start | bytes 1572872 | tf_op jit(solution)/shard_map/ppermute | solution.py:175
  503.6 9.2 %collective-permute-start.31 = (bf16[32,16,512]{2,0,1:T(8,128)(2,1)S(1)}, bf16[32,16,512]{2,0,1:T(8,128)(2,1)S(1)}, u32[]{:S(2)}, u32[]{:S(2)}) collective-permute-start(bf16[32,16,512]{2,0,1:T(8,128)(2,1)S(1)} %collective-permute-done.29), channel_id=1, source_target_pairs={{0,4},{4,12},{12,20},{20,28},{28,24},{24,16},{16,8},{8,0},{1,5},{5... | collective-permute-start | bytes 1572872 | tf_op jit(solution)/shard_map/ppermute | solution.py:175
  517.3 25.5 %collective-permute-start.34 = (f32[1,512,512]{2,1,0:T(8,128)}, f32[1,512,512]{2,1,0:T(8,128)}, u32[]{:S(2)}, u32[]{:S(2)}) collective-permute-start(f32[1,512,512]{2,1,0:T(8,128)} %add.562), channel_id=1, source_target_pairs={{0,2},{1,3},{2,0},{3,1},{4,6},{5,7},{6,4},{7,5},{8,10},{9,11},{10,... | collective-permute-start | bytes 3145736 | tf_op jit(solution)/shard_map/ppermute | solution.py:67
  (25 other events, 382.6 us)

commit v11 on v10

--- a/solution.py
+++ b/solution.py
@@ -185,7 +185,7 @@
     partial_map = lax.dot_general(
         right_cores, sketch, (((2, 3), (0, 1)), ((), ())), preferred_element_type=jnp.float32
     )
-    mapped = lax.psum(partial_map, "mode").astype(jnp.bfloat16)
+    mapped = butterfly_sum(partial_map, n_mode, "mode").astype(jnp.bfloat16)
 
     def local_rows(start, size):
         part = lax.dynamic_slice_in_dim(left_cores, start, size, axis=1)

time: 556 us -> 547 us (0.984)
  blocking collectives: 27.9 us -> 0 us
  waiting for transfers between devices: 251 us -> 264 us
    psum x1 -> x0, blocking collectives: 27.9 us -> none  [per_device(): mapped = lax.psum(partial_map, 'mode').astype(jnp.bfloat16)]
    ppermute x7 -> x9, waiting for transfers between devices: 79.7 us -> 101 us  [butterfly_sum(): x = x + lax.ppermute(x, axis, [(i, i ^ d) for i in range(n)])]
    ppermute x7, waiting for transfers between devices: 23.7 us -> 8.26 us  [ring_reduce_scatter(): lax.ppermute(acc_b, 'sum', bwd)]
    ppermute x7, waiting for transfers between devices: 87.7 us -> 94.2 us  [ring_reduce_scatter(): acc_f = lax.ppermute(acc_f, 'sum', fwd) + piece(fwd_blocks[t, me], 0, half)]
    ppermute x7 -> x9, starting transfers between devices: 7.74 us -> 13 us  [butterfly_sum(): x = x + lax.ppermute(x, axis, [(i, i ^ d) for i in range(n)])]
    add x6 -> x7, other arithmetic: 10.5 us -> 12 us  [ring_reduce_scatter(): lax.ppermute(acc_b, 'sum', bwd)]
  transfers between devices with their start and end apart: 35 -> 37, of which waited for: 29 -> 30; matrix products, arithmetic and copies ran while one was open for 11% -> 12% of each run, Pallas kernels for 0% -> 0%
where the time goes in v11:
time: 547 us; the launch traced here: 537 us
  waiting for transfers between devices  264 us (48%)
  other arithmetic  119 us (22%)
  matrix products  74.4 us (14%)
  starting transfers between devices  42.5 us (8%)
  between operations  22.2 us (4%)
  local copies, waits for them, and re-layouts  14.8 us (3%)
    ppermute x9, waiting for transfers between devices, butterfly_sum(): x = x + lax.ppermute(x, axis, [(i, i ^ d) for i in range(n)])  101 us
    ppermute x7, waiting for transfers between devices, ring_reduce_scatter(): acc_f = lax.ppermute(acc_f, 'sum', fwd) + piece(fwd_blocks[t, me], 0, half)  94.2 us
    ppermute x7, waiting for transfers between devices, ring_gather_carries(): hold_b = lax.ppermute(hold_b, 'sum', bwd)  59.3 us
    another operation x12, other arithmetic, orthonormal(): lkk = jnp.linalg.cholesky(diag)  49.6 us
    another operation x9, other arithmetic, tri_inverse(): inv = lax.linalg.triangular_solve(diag, eye, left_side=True, lower=True)  40 us
    dot_general x16, matrix products, local_rows(): lax.dot_general(part, mapped, (((0, 3), (0, 1)), ((), ())), preferred_ele...  24.6 us
    dot_general x1, matrix products, per_device(): lax.dot_general(right_cores, sketch, (((2, 3), (0, 1)), ((), ())), prefer...  17.1 us
    dot_general x21, matrix products, mm(): return jnp.dot(a, b, precision=HI, preferred_element_type=jnp.float32)  15.2 us
  transfers between devices with their start and end apart: 37, of which 30 were waited for; matrix products, arithmetic and copies ran while one was open for 12% of the time, Pallas kernels for 0%

profile of v11, /device:TPU:0, one launch (start us, length us, event | category | flops | bytes accessed | tf_op | source)
XLA Modules:
  0.0 537.0 jit_solution(3802370323519002974)
XLA Ops:
  0.7 17.1 %fusion.8 = f32[1,512,512]{2,1,0:T(8,128)S(1)} fusion(bf16[16,512,512]{2,1,0:T(8,128)(2,1)} %param.12, bf16[512,16,512]{2,1,0:T(8,128)(2,1)} %bitcast.425), kind=kOutput, calls=%fused_computation.27 | convolution fusion | flops 4294967296 | bytes 17825792 | tf_op jit(solution)/shard_map/dot_general | solution.py:185
  20.8 3.0 collective-permute-start.1
  25.8 21.4 %collective-permute-done.1 = f32[1,512,512]{2,1,0:T(8,128)S(1)} collective-permute-done((f32[1,512,512]{2,1,0:T(8,128)S(1)}, f32[1,512,512]{2,1,0:T(8,128)S(1)}, u32[]{:S(2)}, u32[]{:S(2)}) %collective-permute-start.1) | collective-permute-done | bytes 1048608 | tf_op jit(solution)/shard_map/ppermute | solution.py:67
  57.7 16.0 %collective-permute-done.2 = f32[32,16,512]{2,1,0:T(8,128)S(1)} collective-permute-done((f32[32,16,512]{2,1,0:T(8,128)S(1)}, f32[32,16,512]{2,1,0:T(8,128)S(1)}, u32[]{:S(2)}, u32[]{:S(2)}) %collective-permute-start.2) | collective-permute-done | bytes 1048608 | tf_op jit(solution)/shard_map/ppermute | solution.py:142
  83.9 14.2 %collective-permute-done.3 = f32[32,16,512]{2,1,0:T(8,128)} collective-permute-done((f32[32,16,512]{2,1,0:T(8,128)S(1)}, f32[32,16,512]{2,1,0:T(8,128)}, u32[]{:S(2)}, u32[]{:S(2)}) %collective-permute-start.3) | collective-permute-done | bytes 1048608 | tf_op jit(solution)/shard_map/ppermute | solution.py:142
  109.0 13.6 %collective-permute-done.4 = f32[32,16,512]{2,1,0:T(8,128)} collective-permute-done((f32[32,16,512]{2,1,0:T(8,128)S(1)}, f32[32,16,512]{2,1,0:T(8,128)}, u32[]{:S(2)}, u32[]{:S(2)}) %collective-permute-start.4) | collective-permute-done | bytes 1048608 | tf_op jit(solution)/shard_map/ppermute | solution.py:142
  133.1 13.1 %collective-permute-done.5 = f32[32,16,512]{2,1,0:T(8,128)} collective-permute-done((f32[32,16,512]{2,1,0:T(8,128)S(1)}, f32[32,16,512]{2,1,0:T(8,128)}, u32[]{:S(2)}, u32[]{:S(2)}) %collective-permute-start.5) | collective-permute-done | bytes 1048608 | tf_op jit(solution)/shard_map/ppermute | solution.py:142
  156.5 13.5 %collective-permute-done.6 = f32[32,16,512]{2,1,0:T(8,128)} collective-permute-done((f32[32,16,512]{2,1,0:T(8,128)S(1)}, f32[32,16,512]{2,1,0:T(8,128)}, u32[]{:S(2)}, u32[]{:S(2)}) %collective-permute-start.6) | collective-permute-done | bytes 1048608 | tf_op jit(solution)/shard_map/ppermute | solution.py:142
  180.2 13.1 %collective-permute-done.7 = f32[32,16,512]{2,1,0:T(8,128)} collective-permute-done((f32[32,16,512]{2,1,0:T(8,128)S(1)}, f32[32,16,512]{2,1,0:T(8,128)}, u32[]{:S(2)}, u32[]{:S(2)}) %collective-permute-start.7) | collective-permute-done | bytes 1048608 | tf_op jit(solution)/shard_map/ppermute | solution.py:142
  203.6 10.7 %collective-permute-done.8 = f32[32,16,512]{2,1,0:T(8,128)S(1)} collective-permute-done((f32[32,16,512]{2,1,0:T(8,128)S(1)}, f32[32,16,512]{2,1,0:T(8,128)S(1)}, u32[]{:S(2)}, u32[]{:S(2)}) %collective-permute-start.8) | collective-permute-done | bytes 1048608 | tf_op jit(solution)/shard_map/ppermute | solution.py:142
  218.9 3.6 convolution_bitcast_fusion.16
  226.5 15.3 %collective-permute-done.17 = f32[10,128,128]{1,2,0:T(8,128)S(1)} collective-permute-done((f32[10,128,128]{1,2,0:T(8,128)S(1)}, f32[10,128,128]{1,2,0:T(8,128)S(1)}, u32[]{:S(2)}, u32[]{:S(2)}) %collective-permute-start.17) | collective-permute-done | bytes 655392 | tf_op jit(solution)/shard_map/ppermute | solution.py:67
  243.5 14.4 %collective-permute-done.18 = f32[10,128,128]{1,2,0:T(8,128)S(1)} collective-permute-done((f32[10,128,128]{1,2,0:T(8,128)S(1)}, f32[10,128,128]{1,2,0:T(8,128)S(1)}, u32[]{:S(2)}, u32[]{:S(2)}) %collective-permute-start.18) | collective-permute-done | bytes 655392 | tf_op jit(solution)/shard_map/ppermute | solution.py:67
  273.1 2.8 collective-permute-start.20
  275.9 6.0 %constant_dynamic-slice_fusion.1 = (bf16[1,32,16,512]{3,2,1,0:T(8,128)(2,1)}, bf16[1,32,16,512]{3,2,1,0:T(8,128)(2,1)}, bf16[1,32,16,512]{3,2,1,0:T(8,128)(2,1)}...) fusion(bf16[1,512,16,512]{3,2,1,0:T(8,128)(2,1)} %param.10, ...), kind=kLoop, calls=%fused_computation.292 | loop fusion | bytes 14680120 | tf_op jit(solution)/shard_map/dynamic_slice | solution.py:166
  283.4 19.2 %collective-permute-done.20 = f32[10,128,128]{1,2,0:T(8,128)S(1)} collective-permute-done((f32[10,128,128]{1,2,0:T(8,128)S(1)}, f32[10,128,128]{1,2,0:T(8,128)S(1)}, u32[]{:S(2)}, u32[]{:S(2)}) %collective-permute-start.20) | collective-permute-done | bytes 655392 | tf_op jit(solution)/shard_map/ppermute | solution.py:67
  303.5 11.7 %cholesky.74 = f32[128,128]{1,0:T(8,128)S(1)} custom-call(f32[128,128]{1,0:T(8,128)S(1)} %fusion.170), custom_call_target="Cholesky" | custom-call | tf_op jit(solution)/shard_map/jit(cholesky)/cholesky | solution.py:42
  316.8 10.0 %custom-call.8 = f32[2,1,64,64]{2,3,1,0:T(8,128)S(1)} custom-call(f32[2,1,64,64]{3,2,1,0:T(8,128)S(1)} %fusion.163), custom_call_target="InvertDiagBlocksLowerTriangular" | custom-call | tf_op jit(solution)/shard_map/triangular_solve/custom-call.0 | solution.py:26
  332.5 11.7 %cholesky.85 = f32[128,128]{1,0:T(8,128)S(1)} custom-call(f32[128,128]{1,0:T(8,128)S(1)} %fusion.179), custom_call_target="Cholesky" | custom-call | tf_op jit(solution)/shard_map/jit(cholesky)/cholesky | solution.py:42
  345.7 9.8 %custom-call.9 = f32[2,1,64,64]{2,3,1,0:T(8,128)S(1)} custom-call(f32[2,1,64,64]{3,2,1,0:T(8,128)S(1)} %fusion.164), custom_call_target="InvertDiagBlocksLowerTriangular" | custom-call | tf_op jit(solution)/shard_map/triangular_solve/custom-call.0 | solution.py:26
  358.9 11.7 %cholesky.96 = f32[128,128]{1,0:T(8,128)S(1)} custom-call(f32[128,128]{1,0:T(8,128)S(1)} %fusion.176), custom_call_target="Cholesky" | custom-call | tf_op jit(solution)/shard_map/jit(cholesky)/cholesky | solution.py:42
  372.0 9.8 %custom-call.10 = f32[2,1,64,64]{2,3,1,0:T(8,128)S(1)} custom-call(f32[2,1,64,64]{3,2,1,0:T(8,128)S(1)} %fusion.165), custom_call_target="InvertDiagBlocksLowerTriangular" | custom-call | tf_op jit(solution)/shard_map/triangular_solve/custom-call.0 | solution.py:26
  383.2 11.7 %cholesky.107 = f32[128,128]{1,0:T(8,128)S(1)} custom-call(f32[128,128]{1,0:T(8,128)S(1)} %fusion.173), custom_call_target="Cholesky" | custom-call | tf_op jit(solution)/shard_map/jit(cholesky)/cholesky | solution.py:42
  396.4 10.2 %custom-call.11 = f32[2,1,64,64]{2,3,1,0:T(8,128)S(1)} custom-call(f32[2,1,64,64]{3,2,1,0:T(8,128)S(1)} %fusion.166), custom_call_target="InvertDiagBlocksLowerTriangular" | custom-call | tf_op jit(solution)/shard_map/triangular_solve/custom-call.0 | solution.py:26
  423.8 8.7 %collective-permute-done.22 = bf16[32,16,512]{2,0,1:T(8,128)(2,1)S(1)} collective-permute-done((bf16[32,16,512]{2,0,1:T(8,128)(2,1)S(1)}, bf16[32,16,512]{2,0,1:T(8,128)(2,1)S(1)}, u32[]{:S(2)}, u32[]{:S(2)}) %collective-permute-start.22) | collective-permute-done | bytes 524320 | tf_op jit(solution)/shard_map/ppermute | solution.py:176
  435.8 8.7 %collective-permute-done.24 = bf16[32,16,512]{2,0,1:T(8,128)(2,1)S(1)} collective-permute-done((bf16[32,16,512]{2,0,1:T(8,128)(2,1)S(1)}, bf16[32,16,512]{2,0,1:T(8,128)(2,1)S(1)}, u32[]{:S(2)}, u32[]{:S(2)}) %collective-permute-start.24) | collective-permute-done | bytes 524320 | tf_op jit(solution)/shard_map/ppermute | solution.py:176
  448.0 8.8 %collective-permute-done.26 = bf16[32,16,512]{2,0,1:T(8,128)(2,1)S(1)} collective-permute-done((bf16[32,16,512]{2,0,1:T(8,128)(2,1)S(1)}, bf16[32,16,512]{2,0,1:T(8,128)(2,1)S(1)}, u32[]{:S(2)}, u32[]{:S(2)}) %collective-permute-start.26) | collective-permute-done | bytes 524320 | tf_op jit(solution)/shard_map/ppermute | solution.py:176
  460.1 8.8 %collective-permute-done.28 = bf16[32,16,512]{2,0,1:T(8,128)(2,1)S(1)} collective-permute-done((bf16[32,16,512]{2,0,1:T(8,128)(2,1)S(1)}, bf16[32,16,512]{2,0,1:T(8,128)(2,1)S(1)}, u32[]{:S(2)}, u32[]{:S(2)}) %collective-permute-start.28) | collective-permute-done | bytes 524320 | tf_op jit(solution)/shard_map/ppermute | solution.py:176
  472.2 8.8 %collective-permute-done.30 = bf16[32,16,512]{2,0,1:T(8,128)(2,1)S(1)} collective-permute-done((bf16[32,16,512]{2,0,1:T(8,128)(2,1)S(1)}, bf16[32,16,512]{2,0,1:T(8,128)(2,1)S(1)}, u32[]{:S(2)}, u32[]{:S(2)}) %collective-permute-start.30) | collective-permute-done | bytes 524320 | tf_op jit(solution)/shard_map/ppermute | solution.py:176
  484.3 9.6 %collective-permute-done.32 = bf16[32,16,512]{2,0,1:T(8,128)(2,1)S(1)} collective-permute-done((bf16[32,16,512]{2,0,1:T(8,128)(2,1)S(1)}, bf16[32,16,512]{2,0,1:T(8,128)(2,1)S(1)}, u32[]{:S(2)}, u32[]{:S(2)}) %collective-permute-start.32) | collective-permute-done | bytes 524320 | tf_op jit(solution)/shard_map/ppermute | solution.py:176
  497.2 5.9 %collective-permute-done.34 = bf16[32,16,512]{2,0,1:T(8,128)(2,1)S(1)} collective-permute-done((bf16[32,16,512]{2,0,1:T(8,128)(2,1)S(1)}, bf16[32,16,512]{2,0,1:T(8,128)(2,1)S(1)}, u32[]{:S(2)}, u32[]{:S(2)}) %collective-permute-start.34) | collective-permute-done | bytes 524320 | tf_op jit(solution)/shard_map/ppermute | solution.py:176
  512.3 21.8 %collective-permute-done.36 = f32[1,512,512]{2,1,0:T(8,128)} collective-permute-done((f32[1,512,512]{2,1,0:T(8,128)}, f32[1,512,512]{2,1,0:T(8,128)}, u32[]{:S(2)}, u32[]{:S(2)}) %collective-permute-start.36) | collective-permute-done | bytes 1048608 | tf_op jit(solution)/shard_map/ppermute | solution.py:67
  (247 shorter events, 150.1 us)
Async XLA Ops:
  20.8 26.4 %collective-permute-start.1 = (f32[1,512,512]{2,1,0:T(8,128)S(1)}, f32[1,512,512]{2,1,0:T(8,128)S(1)}, u32[]{:S(2)}, u32[]{:S(2)}) collective-permute-start(f32[1,512,512]{2,1,0:T(8,128)S(1)} %add.453), channel_id=1, source_target_pairs={{0,2},{1,3},{2,0},{3,1},{4,6},{5,7},{6,4},{7,5},{8,10},{9,11},{10,... | collective-permute-start | bytes 3145736 | tf_op jit(solution)/shard_map/ppermute | solution.py:67
  49.0 24.7 %collective-permute-start.2 = (f32[32,16,512]{2,1,0:T(8,128)S(1)}, f32[32,16,512]{2,1,0:T(8,128)S(1)}, u32[]{:S(2)}, u32[]{:S(2)}) collective-permute-start(f32[32,16,512]{2,1,0:T(8,128)S(1)} %fusion.86), channel_id=1, source_target_pairs={{0,4},{4,12},{12,20},{20,28},{28,24},{24,16},{16,8},{8,0},{1,5},{5... | collective-permute-start | bytes 3145736 | tf_op jit(solution)/shard_map/ppermute | solution.py:142
  53.2 24.4 %collective-permute-start.9 = (f32[32,16,512]{2,1,0:T(8,128)}, f32[32,16,512]{2,1,0:T(8,128)}, u32[]{:S(2)}, u32[]{:S(2)}) collective-permute-start(f32[32,16,512]{2,1,0:T(8,128)} %fusion.70), channel_id=1, source_target_pairs={{0,8},{4,0},{12,4},{20,12},{28,20},{24,28},{16,24},{8,16},{1,9},{5... | collective-permute-start | bytes 3145736 | tf_op jit(solution)/shard_map/ppermute | solution.py:143
  74.0 24.1 %collective-permute-start.3 = (f32[32,16,512]{2,1,0:T(8,128)S(1)}, f32[32,16,512]{2,1,0:T(8,128)}, u32[]{:S(2)}, u32[]{:S(2)}) collective-permute-start(f32[32,16,512]{2,1,0:T(8,128)S(1)} %add.456), channel_id=1, source_target_pairs={{0,4},{4,12},{12,20},{20,28},{28,24},{24,16},{16,8},{8,0},{1,5},{5... | collective-permute-start | bytes 3145736 | tf_op jit(solution)/shard_map/ppermute | solution.py:142
  79.0 23.3 %collective-permute-start.10 = (f32[32,16,512]{2,1,0:T(8,128)S(1)}, f32[32,16,512]{2,1,0:T(8,128)}, u32[]{:S(2)}, u32[]{:S(2)}) collective-permute-start(f32[32,16,512]{2,1,0:T(8,128)S(1)} %add.477), channel_id=1, source_target_pairs={{0,8},{4,0},{12,4},{20,12},{28,20},{24,28},{16,24},{8,16},{1,9},{5... | collective-permute-start | bytes 3145736 | tf_op jit(solution)/shard_map/ppermute | solution.py:143
  99.5 23.1 %collective-permute-start.4 = (f32[32,16,512]{2,1,0:T(8,128)S(1)}, f32[32,16,512]{2,1,0:T(8,128)}, u32[]{:S(2)}, u32[]{:S(2)}) collective-permute-start(f32[32,16,512]{2,1,0:T(8,128)S(1)} %add.458), channel_id=1, source_target_pairs={{0,4},{4,12},{12,20},{20,28},{28,24},{24,16},{16,8},{8,0},{1,5},{5... | collective-permute-start | bytes 3145736 | tf_op jit(solution)/shard_map/ppermute | solution.py:142
  103.8 22.4 %collective-permute-start.11 = (f32[32,16,512]{2,1,0:T(8,128)S(1)}, f32[32,16,512]{2,1,0:T(8,128)}, u32[]{:S(2)}, u32[]{:S(2)}) collective-permute-start(f32[32,16,512]{2,1,0:T(8,128)S(1)} %add.482), channel_id=1, source_target_pairs={{0,8},{4,0},{12,4},{20,12},{28,20},{24,28},{16,24},{8,16},{1,9},{5... | collective-permute-start | bytes 3145736 | tf_op jit(solution)/shard_map/ppermute | solution.py:143
  124.0 22.2 %collective-permute-start.5 = (f32[32,16,512]{2,1,0:T(8,128)S(1)}, f32[32,16,512]{2,1,0:T(8,128)}, u32[]{:S(2)}, u32[]{:S(2)}) collective-permute-start(f32[32,16,512]{2,1,0:T(8,128)S(1)} %add.460), channel_id=1, source_target_pairs={{0,4},{4,12},{12,20},{20,28},{28,24},{24,16},{16,8},{8,0},{1,5},{5... | collective-permute-start | bytes 3145736 | tf_op jit(solution)/shard_map/ppermute | solution.py:142
  127.6 21.9 %collective-permute-start.12 = (f32[32,16,512]{2,1,0:T(8,128)S(1)}, f32[32,16,512]{2,1,0:T(8,128)}, u32[]{:S(2)}, u32[]{:S(2)}) collective-permute-start(f32[32,16,512]{2,1,0:T(8,128)S(1)} %add.487), channel_id=1, source_target_pairs={{0,8},{4,0},{12,4},{20,12},{28,20},{24,28},{16,24},{8,16},{1,9},{5... | collective-permute-start | bytes 3145736 | tf_op jit(solution)/shard_map/ppermute | solution.py:143
  147.7 22.4 %collective-permute-start.6 = (f32[32,16,512]{2,1,0:T(8,128)S(1)}, f32[32,16,512]{2,1,0:T(8,128)}, u32[]{:S(2)}, u32[]{:S(2)}) collective-permute-start(f32[32,16,512]{2,1,0:T(8,128)S(1)} %add.462), channel_id=1, source_target_pairs={{0,4},{4,12},{12,20},{20,28},{28,24},{24,16},{16,8},{8,0},{1,5},{5... | collective-permute-start | bytes 3145736 | tf_op jit(solution)/shard_map/ppermute | solution.py:142
  150.9 20.9 %collective-permute-start.13 = (f32[32,16,512]{2,1,0:T(8,128)S(1)}, f32[32,16,512]{2,1,0:T(8,128)}, u32[]{:S(2)}, u32[]{:S(2)}) collective-permute-start(f32[32,16,512]{2,1,0:T(8,128)S(1)} %add.492), channel_id=1, source_target_pairs={{0,8},{4,0},{12,4},{20,12},{28,20},{24,28},{16,24},{8,16},{1,9},{5... | collective-permute-start | bytes 3145736 | tf_op jit(solution)/shard_map/ppermute | solution.py:143
  171.5 21.9 %collective-permute-start.7 = (f32[32,16,512]{2,1,0:T(8,128)S(1)}, f32[32,16,512]{2,1,0:T(8,128)}, u32[]{:S(2)}, u32[]{:S(2)}) collective-permute-start(f32[32,16,512]{2,1,0:T(8,128)S(1)} %add.464), channel_id=1, source_target_pairs={{0,4},{4,12},{12,20},{20,28},{28,24},{24,16},{16,8},{8,0},{1,5},{5... | collective-permute-start | bytes 3145736 | tf_op jit(solution)/shard_map/ppermute | solution.py:142
  174.2 20.9 %collective-permute-start.14 = (f32[32,16,512]{2,1,0:T(8,128)}, f32[32,16,512]{2,1,0:T(8,128)}, u32[]{:S(2)}, u32[]{:S(2)}) collective-permute-start(f32[32,16,512]{2,1,0:T(8,128)} %add.497), channel_id=1, source_target_pairs={{0,8},{4,0},{12,4},{20,12},{28,20},{24,28},{16,24},{8,16},{1,9},{5... | collective-permute-start | bytes 3145736 | tf_op jit(solution)/shard_map/ppermute | solution.py:143
  194.8 19.5 %collective-permute-start.8 = (f32[32,16,512]{2,1,0:T(8,128)S(1)}, f32[32,16,512]{2,1,0:T(8,128)S(1)}, u32[]{:S(2)}, u32[]{:S(2)}) collective-permute-start(f32[32,16,512]{2,1,0:T(8,128)S(1)} %add.466), channel_id=1, source_target_pairs={{0,4},{4,12},{12,20},{20,28},{28,24},{24,16},{16,8},{8,0},{1,5},{5... | collective-permute-start | bytes 3145736 | tf_op jit(solution)/shard_map/ppermute | solution.py:142
  197.5 19.0 %collective-permute-start.15 = (f32[32,16,512]{2,1,0:T(8,128)}, f32[32,16,512]{2,1,0:T(8,128)}, u32[]{:S(2)}, u32[]{:S(2)}) collective-permute-start(f32[32,16,512]{2,1,0:T(8,128)} %add.502), channel_id=1, source_target_pairs={{0,8},{4,0},{12,4},{20,12},{28,20},{24,28},{16,24},{8,16},{1,9},{5... | collective-permute-start | bytes 3145736 | tf_op jit(solution)/shard_map/ppermute | solution.py:143
  224.9 16.8 %collective-permute-start.17 = (f32[10,128,128]{1,2,0:T(8,128)S(1)}, f32[10,128,128]{1,2,0:T(8,128)S(1)}, u32[]{:S(2)}, u32[]{:S(2)}) collective-permute-start(f32[10,128,128]{1,2,0:T(8,128)S(1)} %add.508), channel_id=1, source_target_pairs={{0,2},{1,3},{2,0},{3,1},{4,6},{5,7},{6,4},{7,5},{8,10},{9,11},{10,... | collective-permute-start | bytes 1966088 | tf_op jit(solution)/shard_map/ppermute | solution.py:67
  241.9 16.0 %collective-permute-start.18 = (f32[10,128,128]{1,2,0:T(8,128)S(1)}, f32[10,128,128]{1,2,0:T(8,128)S(1)}, u32[]{:S(2)}, u32[]{:S(2)}) collective-permute-start(f32[10,128,128]{1,2,0:T(8,128)S(1)} %add.509), channel_id=1, source_target_pairs={{0,4},{4,0},{8,12},{12,8},{16,20},{20,16},{24,28},{28,24},{1,5},{5... | collective-permute-start | bytes 1966088 | tf_op jit(solution)/shard_map/ppermute | solution.py:67
  257.9 15.1 %collective-permute-start.19 = (f32[10,128,128]{1,2,0:T(8,128)S(1)}, f32[10,128,128]{1,2,0:T(8,128)S(1)}, u32[]{:S(2)}, u32[]{:S(2)}) collective-permute-start(f32[10,128,128]{1,2,0:T(8,128)S(1)} %add.510), channel_id=1, source_target_pairs={{0,8},{4,12},{8,0},{12,4},{16,24},{20,28},{24,16},{28,20},{1,9},{5... | collective-permute-start | bytes 1966088 | tf_op jit(solution)/shard_map/ppermute | solution.py:67
  273.1 29.5 %collective-permute-start.20 = (f32[10,128,128]{1,2,0:T(8,128)S(1)}, f32[10,128,128]{1,2,0:T(8,128)S(1)}, u32[]{:S(2)}, u32[]{:S(2)}) collective-permute-start(f32[10,128,128]{1,2,0:T(8,128)S(1)} %add.511), channel_id=1, source_target_pairs={{0,16},{4,20},{8,24},{12,28},{16,0},{20,4},{24,8},{28,12},{1,17},{... | collective-permute-start | bytes 1966088 | tf_op jit(solution)/shard_map/ppermute | solution.py:67
  419.5 13.0 %collective-permute-start.22 = (bf16[32,16,512]{2,0,1:T(8,128)(2,1)S(1)}, bf16[32,16,512]{2,0,1:T(8,128)(2,1)S(1)}, u32[]{:S(2)}, u32[]{:S(2)}) collective-permute-start(bf16[32,16,512]{2,0,1:T(8,128)(2,1)S(1)} %copy.79), channel_id=1, source_target_pairs={{0,8},{4,0},{12,4},{20,12},{28,20},{24,28},{16,24},{8,16},{1,9},{5... | collective-permute-start | bytes 1572872 | tf_op jit(solution)/shard_map/ppermute | solution.py:176
  419.9 13.5 %collective-permute-start.21 = (bf16[32,16,512]{2,0,1:T(8,128)(2,1)S(1)}, bf16[32,16,512]{2,0,1:T(8,128)(2,1)S(1)}, u32[]{:S(2)}, u32[]{:S(2)}) collective-permute-start(bf16[32,16,512]{2,0,1:T(8,128)(2,1)S(1)} %copy.77), channel_id=1, source_target_pairs={{0,4},{4,12},{12,20},{20,28},{28,24},{24,16},{16,8},{8,0},{1,5},{5... | collective-permute-start | bytes 1572872 | tf_op jit(solution)/shard_map/ppermute | solution.py:175
  432.5 12.0 %collective-permute-start.24 = (bf16[32,16,512]{2,0,1:T(8,128)(2,1)S(1)}, bf16[32,16,512]{2,0,1:T(8,128)(2,1)S(1)}, u32[]{:S(2)}, u32[]{:S(2)}) collective-permute-start(bf16[32,16,512]{2,0,1:T(8,128)(2,1)S(1)} %collective-permute-done.22), channel_id=1, source_target_pairs={{0,8},{4,0},{12,4},{20,12},{28,20},{24,28},{16,24},{8,16},{1,9},{5... | collective-permute-start | bytes 1572872 | tf_op jit(solution)/shard_map/ppermute | solution.py:176
  433.4 12.5 %collective-permute-start.23 = (bf16[32,16,512]{2,0,1:T(8,128)(2,1)S(1)}, bf16[32,16,512]{2,0,1:T(8,128)(2,1)S(1)}, u32[]{:S(2)}, u32[]{:S(2)}) collective-permute-start(bf16[32,16,512]{2,0,1:T(8,128)(2,1)S(1)} %collective-permute-done.21), channel_id=1, source_target_pairs={{0,4},{4,12},{12,20},{20,28},{28,24},{24,16},{16,8},{8,0},{1,5},{5... | collective-permute-start | bytes 1572872 | tf_op jit(solution)/shard_map/ppermute | solution.py:175
  444.6 12.2 %collective-permute-start.26 = (bf16[32,16,512]{2,0,1:T(8,128)(2,1)S(1)}, bf16[32,16,512]{2,0,1:T(8,128)(2,1)S(1)}, u32[]{:S(2)}, u32[]{:S(2)}) collective-permute-start(bf16[32,16,512]{2,0,1:T(8,128)(2,1)S(1)} %collective-permute-done.24), channel_id=1, source_target_pairs={{0,8},{4,0},{12,4},{20,12},{28,20},{24,28},{16,24},{8,16},{1,9},{5... | collective-permute-start | bytes 1572872 | tf_op jit(solution)/shard_map/ppermute | solution.py:176
  445.9 12.1 %collective-permute-start.25 = (bf16[32,16,512]{2,0,1:T(8,128)(2,1)S(1)}, bf16[32,16,512]{2,0,1:T(8,128)(2,1)S(1)}, u32[]{:S(2)}, u32[]{:S(2)}) collective-permute-start(bf16[32,16,512]{2,0,1:T(8,128)(2,1)S(1)} %collective-permute-done.23), channel_id=1, source_target_pairs={{0,4},{4,12},{12,20},{20,28},{28,24},{24,16},{16,8},{8,0},{1,5},{5... | collective-permute-start | bytes 1572872 | tf_op jit(solution)/shard_map/ppermute | solution.py:175
  456.8 12.1 %collective-permute-start.28 = (bf16[32,16,512]{2,0,1:T(8,128)(2,1)S(1)}, bf16[32,16,512]{2,0,1:T(8,128)(2,1)S(1)}, u32[]{:S(2)}, u32[]{:S(2)}) collective-permute-start(bf16[32,16,512]{2,0,1:T(8,128)(2,1)S(1)} %collective-permute-done.26), channel_id=1, source_target_pairs={{0,8},{4,0},{12,4},{20,12},{28,20},{24,28},{16,24},{8,16},{1,9},{5... | collective-permute-start | bytes 1572872 | tf_op jit(solution)/shard_map/ppermute | solution.py:176
  458.0 12.1 %collective-permute-start.27 = (bf16[32,16,512]{2,0,1:T(8,128)(2,1)S(1)}, bf16[32,16,512]{2,0,1:T(8,128)(2,1)S(1)}, u32[]{:S(2)}, u32[]{:S(2)}) collective-permute-start(bf16[32,16,512]{2,0,1:T(8,128)(2,1)S(1)} %collective-permute-done.25), channel_id=1, source_target_pairs={{0,4},{4,12},{12,20},{20,28},{28,24},{24,16},{16,8},{8,0},{1,5},{5... | collective-permute-start | bytes 1572872 | tf_op jit(solution)/shard_map/ppermute | solution.py:175
  468.9 12.1 %collective-permute-start.30 = (bf16[32,16,512]{2,0,1:T(8,128)(2,1)S(1)}, bf16[32,16,512]{2,0,1:T(8,128)(2,1)S(1)}, u32[]{:S(2)}, u32[]{:S(2)}) collective-permute-start(bf16[32,16,512]{2,0,1:T(8,128)(2,1)S(1)} %collective-permute-done.28), channel_id=1, source_target_pairs={{0,8},{4,0},{12,4},{20,12},{28,20},{24,28},{16,24},{8,16},{1,9},{5... | collective-permute-start | bytes 1572872 | tf_op jit(solution)/shard_map/ppermute | solution.py:176
  470.1 12.1 %collective-permute-start.29 = (bf16[32,16,512]{2,0,1:T(8,128)(2,1)S(1)}, bf16[32,16,512]{2,0,1:T(8,128)(2,1)S(1)}, u32[]{:S(2)}, u32[]{:S(2)}) collective-permute-start(bf16[32,16,512]{2,0,1:T(8,128)(2,1)S(1)} %collective-permute-done.27), channel_id=1, source_target_pairs={{0,4},{4,12},{12,20},{20,28},{28,24},{24,16},{16,8},{8,0},{1,5},{5... | collective-permute-start | bytes 1572872 | tf_op jit(solution)/shard_map/ppermute | solution.py:175
  481.0 12.9 %collective-permute-start.32 = (bf16[32,16,512]{2,0,1:T(8,128)(2,1)S(1)}, bf16[32,16,512]{2,0,1:T(8,128)(2,1)S(1)}, u32[]{:S(2)}, u32[]{:S(2)}) collective-permute-start(bf16[32,16,512]{2,0,1:T(8,128)(2,1)S(1)} %collective-permute-done.30), channel_id=1, source_target_pairs={{0,8},{4,0},{12,4},{20,12},{28,20},{24,28},{16,24},{8,16},{1,9},{5... | collective-permute-start | bytes 1572872 | tf_op jit(solution)/shard_map/ppermute | solution.py:176
  482.2 12.7 %collective-permute-start.31 = (bf16[32,16,512]{2,0,1:T(8,128)(2,1)S(1)}, bf16[32,16,512]{2,0,1:T(8,128)(2,1)S(1)}, u32[]{:S(2)}, u32[]{:S(2)}) collective-permute-start(bf16[32,16,512]{2,0,1:T(8,128)(2,1)S(1)} %collective-permute-done.29), channel_id=1, source_target_pairs={{0,4},{4,12},{12,20},{20,28},{28,24},{24,16},{16,8},{8,0},{1,5},{5... | collective-permute-start | bytes 1572872 | tf_op jit(solution)/shard_map/ppermute | solution.py:175
  508.6 25.5 %collective-permute-start.36 = (f32[1,512,512]{2,1,0:T(8,128)}, f32[1,512,512]{2,1,0:T(8,128)}, u32[]{:S(2)}, u32[]{:S(2)}) collective-permute-start(f32[1,512,512]{2,1,0:T(8,128)} %add.568), channel_id=1, source_target_pairs={{0,2},{1,3},{2,0},{3,1},{4,6},{5,7},{6,4},{7,5},{8,10},{9,11},{10,... | collective-permute-start | bytes 3145736 | tf_op jit(solution)/shard_map/ppermute | solution.py:67
  (29 other events, 438.8 us)

commit v12 on v11

--- a/solution.py
+++ b/solution.py
@@ -182,10 +182,15 @@
 def per_device(ring, n_mode, left_cores, right_cores, sketch):
     sum_local, rows_in, mode_local, rank_width = left_cores.shape
     target = sketch.shape[2]
-    partial_map = lax.dot_general(
-        right_cores, sketch, (((2, 3), (0, 1)), ((), ())), preferred_element_type=jnp.float32
-    )
-    mapped = butterfly_sum(partial_map, n_mode, "mode").astype(jnp.bfloat16)
+    cut = rank_width // 2
+    halves = []
+    for lo, hi in ((0, cut), (cut, rank_width)):
+        part = lax.dot_general(
+            right_cores[:, lo:hi], sketch, (((2, 3), (0, 1)), ((), ())),
+            preferred_element_type=jnp.float32,
+        )
+        halves.append(butterfly_sum(part, n_mode, "mode"))
+    mapped = jnp.concatenate(halves, axis=1).astype(jnp.bfloat16)
 
     def local_rows(start, size):
         part = lax.dynamic_slice_in_dim(left_cores, start, size, axis=1)

time: 547 us -> 544 us (level)
  matrix products: 74.4 us -> 66.9 us
    ppermute x7, waiting for transfers between devices: 8.26 us -> 22.2 us  [ring_reduce_scatter(): lax.ppermute(acc_b, 'sum', bwd)]
    ppermute x7, waiting for transfers between devices: 94.2 us -> 84 us  [ring_reduce_scatter(): acc_f = lax.ppermute(acc_f, 'sum', fwd) + piece(fwd_blocks[t, me], 0, half)]
    dot_general x1 -> x2, matrix products: 17.1 us -> 9.95 us  [per_device(): lax.dot_general(right_cores[:, lo:hi], sketch, (((2, 3), (0, 1)), ((), ()...]
    ppermute x9 -> x11, waiting for transfers between devices: 101 us -> 99.4 us  [butterfly_sum(): x = x + lax.ppermute(x, axis, [(i, i ^ d) for i in range(n)])]
    add x7 -> x6, other arithmetic: 12 us -> 10.5 us  [ring_reduce_scatter(): lax.ppermute(acc_b, 'sum', bwd)]
    ppermute x9 -> x11, starting transfers between devices: 13 us -> 14.4 us  [butterfly_sum(): x = x + lax.ppermute(x, axis, [(i, i ^ d) for i in range(n)])]
  transfers between devices with their start and end apart: 37 -> 39, of which waited for: 30 -> 31; matrix products, arithmetic and copies ran while one was open for 12% -> 12% of each run, Pallas kernels for 0% -> 0%
where the time goes in v12:
time: 544 us; the launch traced here: 533 us
  waiting for transfers between devices  266 us (49%)
  other arithmetic  115 us (21%)
  matrix products  66.9 us (12%)
  starting transfers between devices  43.1 us (8%)
  between operations  22.1 us (4%)
  local copies, waits for them, and re-layouts  20.2 us (4%)
    ppermute x11, waiting for transfers between devices, butterfly_sum(): x = x + lax.ppermute(x, axis, [(i, i ^ d) for i in range(n)])  99.4 us
    ppermute x7, waiting for transfers between devices, ring_reduce_scatter(): acc_f = lax.ppermute(acc_f, 'sum', fwd) + piece(fwd_blocks[t, me], 0, half)  84 us
    ppermute x7, waiting for transfers between devices, ring_gather_carries(): hold_b = lax.ppermute(hold_b, 'sum', bwd)  59.5 us
    another operation x12, other arithmetic, orthonormal(): lkk = jnp.linalg.cholesky(diag)  49.6 us
    another operation x9, other arithmetic, tri_inverse(): inv = lax.linalg.triangular_solve(diag, eye, left_side=True, lower=True)  40 us
    dot_general x16, matrix products, local_rows(): lax.dot_general(part, mapped, (((0, 3), (0, 1)), ((), ())), preferred_ele...  26 us
    ppermute x7, waiting for transfers between devices, ring_reduce_scatter(): lax.ppermute(acc_b, 'sum', bwd)  22.2 us
    ppermute x11, starting transfers between devices, butterfly_sum(): x = x + lax.ppermute(x, axis, [(i, i ^ d) for i in range(n)])  14.4 us
  transfers between devices with their start and end apart: 39, of which 31 were waited for; matrix products, arithmetic and copies ran while one was open for 12% of the time, Pallas kernels for 0%

profile of v12, /device:TPU:0, one launch (start us, length us, event | category | flops | bytes accessed | tf_op | source)
XLA Modules:
  0.0 533.2 jit_solution(13009653006308133298)
XLA Ops:
  6.5 5.0 fusion.24
  12.0 5.0 fusion.25
  23.1 9.8 %collective-permute-done.1 = f32[1,256,512]{2,1,0:T(8,128)S(1)} collective-permute-done((f32[1,256,512]{2,1,0:T(8,128)S(1)}, f32[1,256,512]{2,1,0:T(8,128)S(1)}, u32[]{:S(2)}, u32[]{:S(2)}) %collective-permute-start.1) | collective-permute-done | bytes 524320 | tf_op jit(solution)/shard_map/ppermute | solution.py:67
  33.0 10.5 %collective-permute-done.3 = f32[1,256,512]{2,1,0:T(8,128)S(1)} collective-permute-done((f32[1,256,512]{2,1,0:T(8,128)S(1)}, f32[1,256,512]{2,1,0:T(8,128)S(1)}, u32[]{:S(2)}, u32[]{:S(2)}) %collective-permute-start.3) | collective-permute-done | bytes 524320 | tf_op jit(solution)/shard_map/ppermute | solution.py:67
  51.8 18.2 %collective-permute-done.4 = f32[32,16,512]{2,1,0:T(8,128)S(1)} collective-permute-done((f32[32,16,512]{2,1,0:T(8,128)S(1)}, f32[32,16,512]{2,1,0:T(8,128)S(1)}, u32[]{:S(2)}, u32[]{:S(2)}) %collective-permute-start.4) | collective-permute-done | bytes 1048608 | tf_op jit(solution)/shard_map/ppermute | solution.py:142
  82.1 13.2 %collective-permute-done.5 = f32[32,16,512]{2,1,0:T(8,128)S(1)} collective-permute-done((f32[32,16,512]{2,1,0:T(8,128)S(1)}, f32[32,16,512]{2,1,0:T(8,128)S(1)}, u32[]{:S(2)}, u32[]{:S(2)}) %collective-permute-start.5) | collective-permute-done | bytes 1048608 | tf_op jit(solution)/shard_map/ppermute | solution.py:142
  107.2 11.3 %collective-permute-done.6 = f32[32,16,512]{2,1,0:T(8,128)} collective-permute-done((f32[32,16,512]{2,1,0:T(8,128)S(1)}, f32[32,16,512]{2,1,0:T(8,128)}, u32[]{:S(2)}, u32[]{:S(2)}) %collective-permute-start.6) | collective-permute-done | bytes 1048608 | tf_op jit(solution)/shard_map/ppermute | solution.py:142
  131.3 10.9 %collective-permute-done.7 = f32[32,16,512]{2,1,0:T(8,128)} collective-permute-done((f32[32,16,512]{2,1,0:T(8,128)S(1)}, f32[32,16,512]{2,1,0:T(8,128)}, u32[]{:S(2)}, u32[]{:S(2)}) %collective-permute-start.7) | collective-permute-done | bytes 1048608 | tf_op jit(solution)/shard_map/ppermute | solution.py:142
  154.6 10.9 %collective-permute-done.8 = f32[32,16,512]{2,1,0:T(8,128)} collective-permute-done((f32[32,16,512]{2,1,0:T(8,128)S(1)}, f32[32,16,512]{2,1,0:T(8,128)}, u32[]{:S(2)}, u32[]{:S(2)}) %collective-permute-start.8) | collective-permute-done | bytes 1048608 | tf_op jit(solution)/shard_map/ppermute | solution.py:142
  177.8 11.0 %collective-permute-done.9 = f32[32,16,512]{2,1,0:T(8,128)} collective-permute-done((f32[32,16,512]{2,1,0:T(8,128)S(1)}, f32[32,16,512]{2,1,0:T(8,128)}, u32[]{:S(2)}, u32[]{:S(2)}) %collective-permute-start.9) | collective-permute-done | bytes 1048608 | tf_op jit(solution)/shard_map/ppermute | solution.py:142
  201.2 8.5 %collective-permute-done.10 = f32[32,16,512]{2,1,0:T(8,128)S(1)} collective-permute-done((f32[32,16,512]{2,1,0:T(8,128)S(1)}, f32[32,16,512]{2,1,0:T(8,128)S(1)}, u32[]{:S(2)}, u32[]{:S(2)}) %collective-permute-start.10) | collective-permute-done | bytes 1048608 | tf_op jit(solution)/shard_map/ppermute | solution.py:142
  209.9 4.6 collective-permute-done.17
  223.7 15.3 %collective-permute-done.19 = f32[10,128,128]{1,2,0:T(8,128)S(1)} collective-permute-done((f32[10,128,128]{1,2,0:T(8,128)S(1)}, f32[10,128,128]{1,2,0:T(8,128)S(1)}, u32[]{:S(2)}, u32[]{:S(2)}) %collective-permute-start.19) | collective-permute-done | bytes 655392 | tf_op jit(solution)/shard_map/ppermute | solution.py:67
  240.7 14.3 %collective-permute-done.20 = f32[10,128,128]{1,2,0:T(8,128)S(1)} collective-permute-done((f32[10,128,128]{1,2,0:T(8,128)S(1)}, f32[10,128,128]{1,2,0:T(8,128)S(1)}, u32[]{:S(2)}, u32[]{:S(2)}) %collective-permute-start.20) | collective-permute-done | bytes 655392 | tf_op jit(solution)/shard_map/ppermute | solution.py:67
  273.1 6.2 %constant_dynamic-slice_fusion.1 = (bf16[1,32,16,512]{3,2,1,0:T(8,128)(2,1)}, bf16[1,32,16,512]{3,2,1,0:T(8,128)(2,1)}, bf16[1,32,16,512]{3,2,1,0:T(8,128)(2,1)}...) fusion(bf16[1,512,16,512]{3,2,1,0:T(8,128)(2,1)} %param.10, ...), kind=kLoop, calls=%fused_computation.298 | loop fusion | bytes 14680120 | tf_op jit(solution)/shard_map/dynamic_slice | solution.py:166
  279.7 20.1 %collective-permute-done.22 = f32[10,128,128]{1,2,0:T(8,128)S(1)} collective-permute-done((f32[10,128,128]{1,2,0:T(8,128)S(1)}, f32[10,128,128]{1,2,0:T(8,128)S(1)}, u32[]{:S(2)}, u32[]{:S(2)}) %collective-permute-start.22) | collective-permute-done | bytes 655392 | tf_op jit(solution)/shard_map/ppermute | solution.py:67
  300.7 11.7 %cholesky.74 = f32[128,128]{1,0:T(8,128)S(1)} custom-call(f32[128,128]{1,0:T(8,128)S(1)} %fusion.168), custom_call_target="Cholesky" | custom-call | tf_op jit(solution)/shard_map/jit(cholesky)/cholesky | solution.py:42
  314.0 10.3 %custom-call.8 = f32[2,1,64,64]{2,3,1,0:T(8,128)S(1)} custom-call(f32[2,1,64,64]{3,2,1,0:T(8,128)S(1)} %fusion.161), custom_call_target="InvertDiagBlocksLowerTriangular" | custom-call | tf_op jit(solution)/shard_map/triangular_solve/custom-call.0 | solution.py:26
  329.4 11.7 %cholesky.85 = f32[128,128]{1,0:T(8,128)S(1)} custom-call(f32[128,128]{1,0:T(8,128)S(1)} %fusion.177), custom_call_target="Cholesky" | custom-call | tf_op jit(solution)/shard_map/jit(cholesky)/cholesky | solution.py:42
  342.5 9.8 %custom-call.9 = f32[2,1,64,64]{2,3,1,0:T(8,128)S(1)} custom-call(f32[2,1,64,64]{3,2,1,0:T(8,128)S(1)} %fusion.162), custom_call_target="InvertDiagBlocksLowerTriangular" | custom-call | tf_op jit(solution)/shard_map/triangular_solve/custom-call.0 | solution.py:26
  354.9 11.7 %cholesky.96 = f32[128,128]{1,0:T(8,128)S(1)} custom-call(f32[128,128]{1,0:T(8,128)S(1)} %fusion.174), custom_call_target="Cholesky" | custom-call | tf_op jit(solution)/shard_map/jit(cholesky)/cholesky | solution.py:42
  368.0 9.8 %custom-call.10 = f32[2,1,64,64]{2,3,1,0:T(8,128)S(1)} custom-call(f32[2,1,64,64]{3,2,1,0:T(8,128)S(1)} %fusion.163), custom_call_target="InvertDiagBlocksLowerTriangular" | custom-call | tf_op jit(solution)/shard_map/triangular_solve/custom-call.0 | solution.py:26
  379.2 11.7 %cholesky.107 = f32[128,128]{1,0:T(8,128)S(1)} custom-call(f32[128,128]{1,0:T(8,128)S(1)} %fusion.171), custom_call_target="Cholesky" | custom-call | tf_op jit(solution)/shard_map/jit(cholesky)/cholesky | solution.py:42
  392.4 10.0 %custom-call.11 = f32[2,1,64,64]{2,3,1,0:T(8,128)S(1)} custom-call(f32[2,1,64,64]{3,2,1,0:T(8,128)S(1)} %fusion.164), custom_call_target="InvertDiagBlocksLowerTriangular" | custom-call | tf_op jit(solution)/shard_map/triangular_solve/custom-call.0 | solution.py:26
  419.8 8.8 %collective-permute-done.24 = bf16[32,16,512]{2,0,1:T(8,128)(2,1)S(1)} collective-permute-done((bf16[32,16,512]{2,0,1:T(8,128)(2,1)S(1)}, bf16[32,16,512]{2,0,1:T(8,128)(2,1)S(1)}, u32[]{:S(2)}, u32[]{:S(2)}) %collective-permute-start.24) | collective-permute-done | bytes 524320 | tf_op jit(solution)/shard_map/ppermute | solution.py:176
  432.0 8.9 %collective-permute-done.26 = bf16[32,16,512]{2,0,1:T(8,128)(2,1)S(1)} collective-permute-done((bf16[32,16,512]{2,0,1:T(8,128)(2,1)S(1)}, bf16[32,16,512]{2,0,1:T(8,128)(2,1)S(1)}, u32[]{:S(2)}, u32[]{:S(2)}) %collective-permute-start.26) | collective-permute-done | bytes 524320 | tf_op jit(solution)/shard_map/ppermute | solution.py:176
  444.3 8.8 %collective-permute-done.28 = bf16[32,16,512]{2,0,1:T(8,128)(2,1)S(1)} collective-permute-done((bf16[32,16,512]{2,0,1:T(8,128)(2,1)S(1)}, bf16[32,16,512]{2,0,1:T(8,128)(2,1)S(1)}, u32[]{:S(2)}, u32[]{:S(2)}) %collective-permute-start.28) | collective-permute-done | bytes 524320 | tf_op jit(solution)/shard_map/ppermute | solution.py:176
  456.4 8.8 %collective-permute-done.30 = bf16[32,16,512]{2,0,1:T(8,128)(2,1)S(1)} collective-permute-done((bf16[32,16,512]{2,0,1:T(8,128)(2,1)S(1)}, bf16[32,16,512]{2,0,1:T(8,128)(2,1)S(1)}, u32[]{:S(2)}, u32[]{:S(2)}) %collective-permute-start.30) | collective-permute-done | bytes 524320 | tf_op jit(solution)/shard_map/ppermute | solution.py:176
  468.5 8.8 %collective-permute-done.32 = bf16[32,16,512]{2,0,1:T(8,128)(2,1)S(1)} collective-permute-done((bf16[32,16,512]{2,0,1:T(8,128)(2,1)S(1)}, bf16[32,16,512]{2,0,1:T(8,128)(2,1)S(1)}, u32[]{:S(2)}, u32[]{:S(2)}) %collective-permute-start.32) | collective-permute-done | bytes 524320 | tf_op jit(solution)/shard_map/ppermute | solution.py:176
  480.6 9.5 %collective-permute-done.34 = bf16[32,16,512]{2,0,1:T(8,128)(2,1)S(1)} collective-permute-done((bf16[32,16,512]{2,0,1:T(8,128)(2,1)S(1)}, bf16[32,16,512]{2,0,1:T(8,128)(2,1)S(1)}, u32[]{:S(2)}, u32[]{:S(2)}) %collective-permute-start.34) | collective-permute-done | bytes 524320 | tf_op jit(solution)/shard_map/ppermute | solution.py:176
  493.4 5.9 %collective-permute-done.36 = bf16[32,16,512]{2,0,1:T(8,128)(2,1)S(1)} collective-permute-done((bf16[32,16,512]{2,0,1:T(8,128)(2,1)S(1)}, bf16[32,16,512]{2,0,1:T(8,128)(2,1)S(1)}, u32[]{:S(2)}, u32[]{:S(2)}) %collective-permute-start.36) | collective-permute-done | bytes 524320 | tf_op jit(solution)/shard_map/ppermute | solution.py:176
  508.3 22.0 %collective-permute-done.38 = f32[1,512,512]{2,1,0:T(8,128)} collective-permute-done((f32[1,512,512]{2,1,0:T(8,128)}, f32[1,512,512]{2,1,0:T(8,128)}, u32[]{:S(2)}, u32[]{:S(2)}) %collective-permute-start.38) | collective-permute-done | bytes 1048608 | tf_op jit(solution)/shard_map/ppermute | solution.py:67
  (281 shorter events, 168.0 us)
Async XLA Ops:
  17.1 15.8 %collective-permute-start.1 = (f32[1,256,512]{2,1,0:T(8,128)S(1)}, f32[1,256,512]{2,1,0:T(8,128)S(1)}, u32[]{:S(2)}, u32[]{:S(2)}) collective-permute-start(f32[1,256,512]{2,1,0:T(8,128)S(1)} %add.459), channel_id=1, source_target_pairs={{0,2},{1,3},{2,0},{3,1},{4,6},{5,7},{6,4},{7,5},{8,10},{9,11},{10,... | collective-permute-start | bytes 1572872 | tf_op jit(solution)/shard_map/ppermute | solution.py:67
  20.3 23.3 %collective-permute-start.3 = (f32[1,256,512]{2,1,0:T(8,128)S(1)}, f32[1,256,512]{2,1,0:T(8,128)S(1)}, u32[]{:S(2)}, u32[]{:S(2)}) collective-permute-start(f32[1,256,512]{2,1,0:T(8,128)S(1)} %add.461), channel_id=1, source_target_pairs={{0,2},{1,3},{2,0},{3,1},{4,6},{5,7},{6,4},{7,5},{8,10},{9,11},{10,... | collective-permute-start | bytes 1572872 | tf_op jit(solution)/shard_map/ppermute | solution.py:67
  45.1 24.8 %collective-permute-start.4 = (f32[32,16,512]{2,1,0:T(8,128)S(1)}, f32[32,16,512]{2,1,0:T(8,128)S(1)}, u32[]{:S(2)}, u32[]{:S(2)}) collective-permute-start(f32[32,16,512]{2,1,0:T(8,128)S(1)} %fusion.82), channel_id=1, source_target_pairs={{0,4},{4,12},{12,20},{20,28},{28,24},{24,16},{16,8},{8,0},{1,5},{5... | collective-permute-start | bytes 3145736 | tf_op jit(solution)/shard_map/ppermute | solution.py:142
  50.2 24.3 %collective-permute-start.11 = (f32[32,16,512]{2,1,0:T(8,128)}, f32[32,16,512]{2,1,0:T(8,128)}, u32[]{:S(2)}, u32[]{:S(2)}) collective-permute-start(f32[32,16,512]{2,1,0:T(8,128)} %fusion.67), channel_id=1, source_target_pairs={{0,8},{4,0},{12,4},{20,12},{28,20},{24,28},{16,24},{8,16},{1,9},{5... | collective-permute-start | bytes 3145736 | tf_op jit(solution)/shard_map/ppermute | solution.py:143
  71.4 23.8 %collective-permute-start.5 = (f32[32,16,512]{2,1,0:T(8,128)S(1)}, f32[32,16,512]{2,1,0:T(8,128)S(1)}, u32[]{:S(2)}, u32[]{:S(2)}) collective-permute-start(f32[32,16,512]{2,1,0:T(8,128)S(1)} %convolution_add_fusion.1), channel_id=1, source_target_pairs={{0,4},{4,12},{12,20},{20,28},{28,24},{24,16},{16,8},{8,0},{1,5},{5... | collective-permute-start | bytes 3145736 | tf_op jit(solution)/shard_map/ppermute | solution.py:142
  77.2 23.4 %collective-permute-start.12 = (f32[32,16,512]{2,1,0:T(8,128)}, f32[32,16,512]{2,1,0:T(8,128)}, u32[]{:S(2)}, u32[]{:S(2)}) collective-permute-start(f32[32,16,512]{2,1,0:T(8,128)} %convolution_add_fusion), channel_id=1, source_target_pairs={{0,8},{4,0},{12,4},{20,12},{28,20},{24,28},{16,24},{8,16},{1,9},{5... | collective-permute-start | bytes 3145736 | tf_op jit(solution)/shard_map/ppermute | solution.py:143
  95.5 23.1 %collective-permute-start.6 = (f32[32,16,512]{2,1,0:T(8,128)S(1)}, f32[32,16,512]{2,1,0:T(8,128)}, u32[]{:S(2)}, u32[]{:S(2)}) collective-permute-start(f32[32,16,512]{2,1,0:T(8,128)S(1)} %add.466), channel_id=1, source_target_pairs={{0,4},{4,12},{12,20},{20,28},{28,24},{24,16},{16,8},{8,0},{1,5},{5... | collective-permute-start | bytes 3145736 | tf_op jit(solution)/shard_map/ppermute | solution.py:142
  102.0 22.3 %collective-permute-start.13 = (f32[32,16,512]{2,1,0:T(8,128)S(1)}, f32[32,16,512]{2,1,0:T(8,128)}, u32[]{:S(2)}, u32[]{:S(2)}) collective-permute-start(f32[32,16,512]{2,1,0:T(8,128)S(1)} %add.490), channel_id=1, source_target_pairs={{0,8},{4,0},{12,4},{20,12},{28,20},{24,28},{16,24},{8,16},{1,9},{5... | collective-permute-start | bytes 3145736 | tf_op jit(solution)/shard_map/ppermute | solution.py:143
  120.0 22.2 %collective-permute-start.7 = (f32[32,16,512]{2,1,0:T(8,128)S(1)}, f32[32,16,512]{2,1,0:T(8,128)}, u32[]{:S(2)}, u32[]{:S(2)}) collective-permute-start(f32[32,16,512]{2,1,0:T(8,128)S(1)} %add.468), channel_id=1, source_target_pairs={{0,4},{4,12},{12,20},{20,28},{28,24},{24,16},{16,8},{8,0},{1,5},{5... | collective-permute-start | bytes 3145736 | tf_op jit(solution)/shard_map/ppermute | solution.py:142
  125.8 21.9 %collective-permute-start.14 = (f32[32,16,512]{2,1,0:T(8,128)S(1)}, f32[32,16,512]{2,1,0:T(8,128)}, u32[]{:S(2)}, u32[]{:S(2)}) collective-permute-start(f32[32,16,512]{2,1,0:T(8,128)S(1)} %add.495), channel_id=1, source_target_pairs={{0,8},{4,0},{12,4},{20,12},{28,20},{24,28},{16,24},{8,16},{1,9},{5... | collective-permute-start | bytes 3145736 | tf_op jit(solution)/shard_map/ppermute | solution.py:143
  143.6 21.9 %collective-permute-start.8 = (f32[32,16,512]{2,1,0:T(8,128)S(1)}, f32[32,16,512]{2,1,0:T(8,128)}, u32[]{:S(2)}, u32[]{:S(2)}) collective-permute-start(f32[32,16,512]{2,1,0:T(8,128)S(1)} %add.470), channel_id=1, source_target_pairs={{0,4},{4,12},{12,20},{20,28},{28,24},{24,16},{16,8},{8,0},{1,5},{5... | collective-permute-start | bytes 3145736 | tf_op jit(solution)/shard_map/ppermute | solution.py:142
  149.1 20.8 %collective-permute-start.15 = (f32[32,16,512]{2,1,0:T(8,128)S(1)}, f32[32,16,512]{2,1,0:T(8,128)}, u32[]{:S(2)}, u32[]{:S(2)}) collective-permute-start(f32[32,16,512]{2,1,0:T(8,128)S(1)} %add.500), channel_id=1, source_target_pairs={{0,8},{4,0},{12,4},{20,12},{28,20},{24,28},{16,24},{8,16},{1,9},{5... | collective-permute-start | bytes 3145736 | tf_op jit(solution)/shard_map/ppermute | solution.py:143
  167.0 21.9 %collective-permute-start.9 = (f32[32,16,512]{2,1,0:T(8,128)S(1)}, f32[32,16,512]{2,1,0:T(8,128)}, u32[]{:S(2)}, u32[]{:S(2)}) collective-permute-start(f32[32,16,512]{2,1,0:T(8,128)S(1)} %add.472), channel_id=1, source_target_pairs={{0,4},{4,12},{12,20},{20,28},{28,24},{24,16},{16,8},{8,0},{1,5},{5... | collective-permute-start | bytes 3145736 | tf_op jit(solution)/shard_map/ppermute | solution.py:142
  172.3 20.7 %collective-permute-start.16 = (f32[32,16,512]{2,1,0:T(8,128)}, f32[32,16,512]{2,1,0:T(8,128)}, u32[]{:S(2)}, u32[]{:S(2)}) collective-permute-start(f32[32,16,512]{2,1,0:T(8,128)} %add.505), channel_id=1, source_target_pairs={{0,8},{4,0},{12,4},{20,12},{28,20},{24,28},{16,24},{8,16},{1,9},{5... | collective-permute-start | bytes 3145736 | tf_op jit(solution)/shard_map/ppermute | solution.py:143
  190.3 19.4 %collective-permute-start.10 = (f32[32,16,512]{2,1,0:T(8,128)S(1)}, f32[32,16,512]{2,1,0:T(8,128)S(1)}, u32[]{:S(2)}, u32[]{:S(2)}) collective-permute-start(f32[32,16,512]{2,1,0:T(8,128)S(1)} %add.474), channel_id=1, source_target_pairs={{0,4},{4,12},{12,20},{20,28},{28,24},{24,16},{16,8},{8,0},{1,5},{5... | collective-permute-start | bytes 3145736 | tf_op jit(solution)/shard_map/ppermute | solution.py:142
  195.4 19.2 %collective-permute-start.17 = (f32[32,16,512]{2,1,0:T(8,128)}, f32[32,16,512]{2,1,0:T(8,128)}, u32[]{:S(2)}, u32[]{:S(2)}) collective-permute-start(f32[32,16,512]{2,1,0:T(8,128)} %add.510), channel_id=1, source_target_pairs={{0,8},{4,0},{12,4},{20,12},{28,20},{24,28},{16,24},{8,16},{1,9},{5... | collective-permute-start | bytes 3145736 | tf_op jit(solution)/shard_map/ppermute | solution.py:143
  222.1 16.8 %collective-permute-start.19 = (f32[10,128,128]{1,2,0:T(8,128)S(1)}, f32[10,128,128]{1,2,0:T(8,128)S(1)}, u32[]{:S(2)}, u32[]{:S(2)}) collective-permute-start(f32[10,128,128]{1,2,0:T(8,128)S(1)} %add.516), channel_id=1, source_target_pairs={{0,2},{1,3},{2,0},{3,1},{4,6},{5,7},{6,4},{7,5},{8,10},{9,11},{10,... | collective-permute-start | bytes 1966088 | tf_op jit(solution)/shard_map/ppermute | solution.py:67
  239.0 16.0 %collective-permute-start.20 = (f32[10,128,128]{1,2,0:T(8,128)S(1)}, f32[10,128,128]{1,2,0:T(8,128)S(1)}, u32[]{:S(2)}, u32[]{:S(2)}) collective-permute-start(f32[10,128,128]{1,2,0:T(8,128)S(1)} %add.517), channel_id=1, source_target_pairs={{0,4},{4,0},{8,12},{12,8},{16,20},{20,16},{24,28},{28,24},{1,5},{5... | collective-permute-start | bytes 1966088 | tf_op jit(solution)/shard_map/ppermute | solution.py:67
  255.1 15.1 %collective-permute-start.21 = (f32[10,128,128]{1,2,0:T(8,128)S(1)}, f32[10,128,128]{1,2,0:T(8,128)S(1)}, u32[]{:S(2)}, u32[]{:S(2)}) collective-permute-start(f32[10,128,128]{1,2,0:T(8,128)S(1)} %add.518), channel_id=1, source_target_pairs={{0,8},{4,12},{8,0},{12,4},{16,24},{20,28},{24,16},{28,20},{1,9},{5... | collective-permute-start | bytes 1966088 | tf_op jit(solution)/shard_map/ppermute | solution.py:67
  270.3 29.5 %collective-permute-start.22 = (f32[10,128,128]{1,2,0:T(8,128)S(1)}, f32[10,128,128]{1,2,0:T(8,128)S(1)}, u32[]{:S(2)}, u32[]{:S(2)}) collective-permute-start(f32[10,128,128]{1,2,0:T(8,128)S(1)} %add.519), channel_id=1, source_target_pairs={{0,16},{4,20},{8,24},{12,28},{16,0},{20,4},{24,8},{28,12},{1,17},{... | collective-permute-start | bytes 1966088 | tf_op jit(solution)/shard_map/ppermute | solution.py:67
  415.5 13.1 %collective-permute-start.24 = (bf16[32,16,512]{2,0,1:T(8,128)(2,1)S(1)}, bf16[32,16,512]{2,0,1:T(8,128)(2,1)S(1)}, u32[]{:S(2)}, u32[]{:S(2)}) collective-permute-start(bf16[32,16,512]{2,0,1:T(8,128)(2,1)S(1)} %copy.81), channel_id=1, source_target_pairs={{0,8},{4,0},{12,4},{20,12},{28,20},{24,28},{16,24},{8,16},{1,9},{5... | collective-permute-start | bytes 1572872 | tf_op jit(solution)/shard_map/ppermute | solution.py:176
  415.9 13.7 %collective-permute-start.23 = (bf16[32,16,512]{2,0,1:T(8,128)(2,1)S(1)}, bf16[32,16,512]{2,0,1:T(8,128)(2,1)S(1)}, u32[]{:S(2)}, u32[]{:S(2)}) collective-permute-start(bf16[32,16,512]{2,0,1:T(8,128)(2,1)S(1)} %copy.79), channel_id=1, source_target_pairs={{0,4},{4,12},{12,20},{20,28},{28,24},{24,16},{16,8},{8,0},{1,5},{5... | collective-permute-start | bytes 1572872 | tf_op jit(solution)/shard_map/ppermute | solution.py:175
  428.7 12.2 %collective-permute-start.26 = (bf16[32,16,512]{2,0,1:T(8,128)(2,1)S(1)}, bf16[32,16,512]{2,0,1:T(8,128)(2,1)S(1)}, u32[]{:S(2)}, u32[]{:S(2)}) collective-permute-start(bf16[32,16,512]{2,0,1:T(8,128)(2,1)S(1)} %collective-permute-done.24), channel_id=1, source_target_pairs={{0,8},{4,0},{12,4},{20,12},{28,20},{24,28},{16,24},{8,16},{1,9},{5... | collective-permute-start | bytes 1572872 | tf_op jit(solution)/shard_map/ppermute | solution.py:176
  429.5 12.6 %collective-permute-start.25 = (bf16[32,16,512]{2,0,1:T(8,128)(2,1)S(1)}, bf16[32,16,512]{2,0,1:T(8,128)(2,1)S(1)}, u32[]{:S(2)}, u32[]{:S(2)}) collective-permute-start(bf16[32,16,512]{2,0,1:T(8,128)(2,1)S(1)} %collective-permute-done.23), channel_id=1, source_target_pairs={{0,4},{4,12},{12,20},{20,28},{28,24},{24,16},{16,8},{8,0},{1,5},{5... | collective-permute-start | bytes 1572872 | tf_op jit(solution)/shard_map/ppermute | solution.py:175
  440.8 12.3 %collective-permute-start.28 = (bf16[32,16,512]{2,0,1:T(8,128)(2,1)S(1)}, bf16[32,16,512]{2,0,1:T(8,128)(2,1)S(1)}, u32[]{:S(2)}, u32[]{:S(2)}) collective-permute-start(bf16[32,16,512]{2,0,1:T(8,128)(2,1)S(1)} %collective-permute-done.26), channel_id=1, source_target_pairs={{0,8},{4,0},{12,4},{20,12},{28,20},{24,28},{16,24},{8,16},{1,9},{5... | collective-permute-start | bytes 1572872 | tf_op jit(solution)/shard_map/ppermute | solution.py:176
  453.1 12.1 %collective-permute-start.30 = (bf16[32,16,512]{2,0,1:T(8,128)(2,1)S(1)}, bf16[32,16,512]{2,0,1:T(8,128)(2,1)S(1)}, u32[]{:S(2)}, u32[]{:S(2)}) collective-permute-start(bf16[32,16,512]{2,0,1:T(8,128)(2,1)S(1)} %collective-permute-done.28), channel_id=1, source_target_pairs={{0,8},{4,0},{12,4},{20,12},{28,20},{24,28},{16,24},{8,16},{1,9},{5... | collective-permute-start | bytes 1572872 | tf_op jit(solution)/shard_map/ppermute | solution.py:176
  454.3 12.1 %collective-permute-start.29 = (bf16[32,16,512]{2,0,1:T(8,128)(2,1)S(1)}, bf16[32,16,512]{2,0,1:T(8,128)(2,1)S(1)}, u32[]{:S(2)}, u32[]{:S(2)}) collective-permute-start(bf16[32,16,512]{2,0,1:T(8,128)(2,1)S(1)} %collective-permute-done.27), channel_id=1, source_target_pairs={{0,4},{4,12},{12,20},{20,28},{28,24},{24,16},{16,8},{8,0},{1,5},{5... | collective-permute-start | bytes 1572872 | tf_op jit(solution)/shard_map/ppermute | solution.py:175
  465.2 12.1 %collective-permute-start.32 = (bf16[32,16,512]{2,0,1:T(8,128)(2,1)S(1)}, bf16[32,16,512]{2,0,1:T(8,128)(2,1)S(1)}, u32[]{:S(2)}, u32[]{:S(2)}) collective-permute-start(bf16[32,16,512]{2,0,1:T(8,128)(2,1)S(1)} %collective-permute-done.30), channel_id=1, source_target_pairs={{0,8},{4,0},{12,4},{20,12},{28,20},{24,28},{16,24},{8,16},{1,9},{5... | collective-permute-start | bytes 1572872 | tf_op jit(solution)/shard_map/ppermute | solution.py:176
  466.4 12.1 %collective-permute-start.31 = (bf16[32,16,512]{2,0,1:T(8,128)(2,1)S(1)}, bf16[32,16,512]{2,0,1:T(8,128)(2,1)S(1)}, u32[]{:S(2)}, u32[]{:S(2)}) collective-permute-start(bf16[32,16,512]{2,0,1:T(8,128)(2,1)S(1)} %collective-permute-done.29), channel_id=1, source_target_pairs={{0,4},{4,12},{12,20},{20,28},{28,24},{24,16},{16,8},{8,0},{1,5},{5... | collective-permute-start | bytes 1572872 | tf_op jit(solution)/shard_map/ppermute | solution.py:175
  477.3 12.8 %collective-permute-start.34 = (bf16[32,16,512]{2,0,1:T(8,128)(2,1)S(1)}, bf16[32,16,512]{2,0,1:T(8,128)(2,1)S(1)}, u32[]{:S(2)}, u32[]{:S(2)}) collective-permute-start(bf16[32,16,512]{2,0,1:T(8,128)(2,1)S(1)} %collective-permute-done.32), channel_id=1, source_target_pairs={{0,8},{4,0},{12,4},{20,12},{28,20},{24,28},{16,24},{8,16},{1,9},{5... | collective-permute-start | bytes 1572872 | tf_op jit(solution)/shard_map/ppermute | solution.py:176
  478.5 12.6 %collective-permute-start.33 = (bf16[32,16,512]{2,0,1:T(8,128)(2,1)S(1)}, bf16[32,16,512]{2,0,1:T(8,128)(2,1)S(1)}, u32[]{:S(2)}, u32[]{:S(2)}) collective-permute-start(bf16[32,16,512]{2,0,1:T(8,128)(2,1)S(1)} %collective-permute-done.31), channel_id=1, source_target_pairs={{0,4},{4,12},{12,20},{20,28},{28,24},{24,16},{16,8},{8,0},{1,5},{5... | collective-permute-start | bytes 1572872 | tf_op jit(solution)/shard_map/ppermute | solution.py:175
  504.7 25.5 %collective-permute-start.38 = (f32[1,512,512]{2,1,0:T(8,128)}, f32[1,512,512]{2,1,0:T(8,128)}, u32[]{:S(2)}, u32[]{:S(2)}) collective-permute-start(f32[1,512,512]{2,1,0:T(8,128)} %add.576), channel_id=1, source_target_pairs={{0,2},{1,3},{2,0},{3,1},{4,6},{5,7},{6,4},{7,5},{8,10},{9,11},{10,... | collective-permute-start | bytes 3145736 | tf_op jit(solution)/shard_map/ppermute | solution.py:67
  (45 other events, 623.2 us)

commit v13 on v12

--- a/solution.py
+++ b/solution.py
@@ -29,7 +29,7 @@
     return jnp.concatenate([top, jnp.concatenate([corner, inv[1]], axis=1)], axis=0)
 
 
-def orthonormal(sketched, gram):
+def orthonormal(sketched, gram, first):
     n = gram.shape[0]
     b = min(BLOCK, n)
     nb = n // b
@@ -38,7 +38,7 @@
     panels = []
     trailing = gram
     for k in range(nb):
-        diag = trailing[:b, :b]
+        diag = first if k == 0 else trailing[:b, :b]
         lkk = jnp.linalg.cholesky(diag)
         ikk = tri_inverse(lkk)
         inverses.append(ikk)
@@ -73,17 +73,22 @@
     n = gram_part.shape[0]
     b = min(BLOCK, n)
     nb = n // b
-    lower = [(i, j) for i in range(nb) for j in range(i + 1)]
+    first = gram_part[:b, :b]
+    first = butterfly_sum(butterfly_sum(first, n_mode, "mode"), n_sum)
+    if nb == 1:
+        return first, first
+    lower = [(i, j) for i in range(nb) for j in range(i + 1)][1:]
     packed = jnp.stack([gram_part[i * b:(i + 1) * b, j * b:(j + 1) * b] for i, j in lower])
     packed = butterfly_sum(butterfly_sum(packed, n_mode, "mode"), n_sum)
     where = {cell: k for k, cell in enumerate(lower)}
-    rows = []
-    for i in range(nb):
-        row = []
-        for j in range(nb):
-            row.append(packed[where[(i, j)]] if j <= i else packed[where[(j, i)]].T)
-        rows.append(jnp.concatenate(row, axis=1))
-    return jnp.concatenate(rows, axis=0)
+
+    def cell(i, j):
+        if (i, j) == (0, 0):
+            return first
+        return packed[where[(i, j)]] if j <= i else packed[where[(j, i)]].T
+
+    rows = [jnp.concatenate([cell(i, j) for j in range(nb)], axis=1) for i in range(nb)]
+    return jnp.concatenate(rows, axis=0), first
 
 
 def ring_order(mesh):
@@ -203,8 +208,8 @@
     share = ring_reduce_scatter(local_rows, rows_in, ring)
     flat_share = share.reshape(-1, target)
     gram_part = jnp.dot(flat_share.T, flat_share, precision=HI)
-    gram = symmetric_psum(gram_part, len(ring), n_mode)
-    basis = orthonormal(flat_share, gram)
+    gram, first = symmetric_psum(gram_part, len(ring), n_mode)
+    basis = orthonormal(flat_share, gram, first)
     block = basis.reshape(share.shape)
     rounded = block.astype(jnp.bfloat16)
     partial_carry = ring_gather_carries(rounded, left_cores, ring)

time: 544 us -> 539 us (level)
  waiting for transfers between devices: 266 us -> 249 us
    ppermute x11 -> x16, waiting for transfers between devices: 99.4 us -> 83 us  [butterfly_sum(): x = x + lax.ppermute(x, axis, [(i, i ^ d) for i in range(n)])]
    ppermute x11 -> x16, starting transfers between devices: 14.4 us -> 18.7 us  [butterfly_sum(): x = x + lax.ppermute(x, axis, [(i, i ^ d) for i in range(n)])]
  transfers between devices with their start and end apart: 39 -> 44, of which waited for: 31 -> 34; matrix products, arithmetic and copies ran while one was open for 12% -> 17% of each run, Pallas kernels for 0% -> 0%
where the time goes in v13:
time: 539 us; the launch traced here: 528 us
  waiting for transfers between devices  249 us (46%)
  other arithmetic  119 us (22%)
  matrix products  70.3 us (13%)
  starting transfers between devices  46.8 us (9%)
  between operations  22.2 us (4%)
  local copies, waits for them, and re-layouts  20.6 us (4%)
    ppermute x7, waiting for transfers between devices, ring_reduce_scatter(): acc_f = lax.ppermute(acc_f, 'sum', fwd) + piece(fwd_blocks[t, me], 0, half)  83.8 us
    ppermute x16, waiting for transfers between devices, butterfly_sum(): x = x + lax.ppermute(x, axis, [(i, i ^ d) for i in range(n)])  83 us
    ppermute x7, waiting for transfers between devices, ring_gather_carries(): hold_b = lax.ppermute(hold_b, 'sum', bwd)  58.3 us
    another operation x12, other arithmetic, orthonormal(): lkk = jnp.linalg.cholesky(diag)  49.5 us
    another operation x9, other arithmetic, tri_inverse(): inv = lax.linalg.triangular_solve(diag, eye, left_side=True, lower=True)  40.3 us
    dot_general x16, matrix products, local_rows(): lax.dot_general(part, mapped, (((0, 3), (0, 1)), ((), ())), preferred_ele...  26 us
    ppermute x7, waiting for transfers between devices, ring_reduce_scatter(): lax.ppermute(acc_b, 'sum', bwd)  22.2 us
    ppermute x16, starting transfers between devices, butterfly_sum(): x = x + lax.ppermute(x, axis, [(i, i ^ d) for i in range(n)])  18.7 us
  transfers between devices with their start and end apart: 44, of which 34 were waited for; matrix products, arithmetic and copies ran while one was open for 17% of the time, Pallas kernels for 0%

profile of v13, /device:TPU:0, one launch (start us, length us, event | category | flops | bytes accessed | tf_op | source)
XLA Modules:
  0.0 528.3 jit_solution(14941630101903909007)
XLA Ops:
  0.6 4.1 fusion.235
  6.5 5.0 fusion.24
  12.0 5.0 fusion.25
  23.0 9.9 %collective-permute-done.1 = f32[1,256,512]{2,1,0:T(8,128)S(1)} collective-permute-done((f32[1,256,512]{2,1,0:T(8,128)S(1)}, f32[1,256,512]{2,1,0:T(8,128)S(1)}, u32[]{:S(2)}, u32[]{:S(2)}) %collective-permute-start.1) | collective-permute-done | bytes 524320 | tf_op jit(solution)/shard_map/ppermute | solution.py:67
  33.0 10.5 %collective-permute-done.3 = f32[1,256,512]{2,1,0:T(8,128)S(1)} collective-permute-done((f32[1,256,512]{2,1,0:T(8,128)S(1)}, f32[1,256,512]{2,1,0:T(8,128)S(1)}, u32[]{:S(2)}, u32[]{:S(2)}) %collective-permute-start.3) | collective-permute-done | bytes 524320 | tf_op jit(solution)/shard_map/ppermute | solution.py:67
  51.7 18.2 %collective-permute-done.4 = f32[32,16,512]{2,1,0:T(8,128)S(1)} collective-permute-done((f32[32,16,512]{2,1,0:T(8,128)S(1)}, f32[32,16,512]{2,1,0:T(8,128)S(1)}, u32[]{:S(2)}, u32[]{:S(2)}) %collective-permute-start.4) | collective-permute-done | bytes 1048608 | tf_op jit(solution)/shard_map/ppermute | solution.py:147
  82.1 13.1 %collective-permute-done.5 = f32[32,16,512]{2,1,0:T(8,128)S(1)} collective-permute-done((f32[32,16,512]{2,1,0:T(8,128)S(1)}, f32[32,16,512]{2,1,0:T(8,128)S(1)}, u32[]{:S(2)}, u32[]{:S(2)}) %collective-permute-start.5) | collective-permute-done | bytes 1048608 | tf_op jit(solution)/shard_map/ppermute | solution.py:147
  107.3 11.3 %collective-permute-done.6 = f32[32,16,512]{2,1,0:T(8,128)} collective-permute-done((f32[32,16,512]{2,1,0:T(8,128)S(1)}, f32[32,16,512]{2,1,0:T(8,128)}, u32[]{:S(2)}, u32[]{:S(2)}) %collective-permute-start.6) | collective-permute-done | bytes 1048608 | tf_op jit(solution)/shard_map/ppermute | solution.py:147
  131.3 10.8 %collective-permute-done.7 = f32[32,16,512]{2,1,0:T(8,128)} collective-permute-done((f32[32,16,512]{2,1,0:T(8,128)S(1)}, f32[32,16,512]{2,1,0:T(8,128)}, u32[]{:S(2)}, u32[]{:S(2)}) %collective-permute-start.7) | collective-permute-done | bytes 1048608 | tf_op jit(solution)/shard_map/ppermute | solution.py:147
  154.7 10.8 %collective-permute-done.8 = f32[32,16,512]{2,1,0:T(8,128)} collective-permute-done((f32[32,16,512]{2,1,0:T(8,128)S(1)}, f32[32,16,512]{2,1,0:T(8,128)}, u32[]{:S(2)}, u32[]{:S(2)}) %collective-permute-start.8) | collective-permute-done | bytes 1048608 | tf_op jit(solution)/shard_map/ppermute | solution.py:147
  177.9 11.0 %collective-permute-done.9 = f32[32,16,512]{2,1,0:T(8,128)} collective-permute-done((f32[32,16,512]{2,1,0:T(8,128)S(1)}, f32[32,16,512]{2,1,0:T(8,128)}, u32[]{:S(2)}, u32[]{:S(2)}) %collective-permute-start.9) | collective-permute-done | bytes 1048608 | tf_op jit(solution)/shard_map/ppermute | solution.py:147
  201.1 8.6 %collective-permute-done.10 = f32[32,16,512]{2,1,0:T(8,128)S(1)} collective-permute-done((f32[32,16,512]{2,1,0:T(8,128)S(1)}, f32[32,16,512]{2,1,0:T(8,128)S(1)}, u32[]{:S(2)}, u32[]{:S(2)}) %collective-permute-start.10) | collective-permute-done | bytes 1048608 | tf_op jit(solution)/shard_map/ppermute | solution.py:147
  210.0 4.6 collective-permute-done.17
  231.7 6.0 %constant_dynamic-slice_fusion.1 = (bf16[1,32,16,512]{3,2,1,0:T(8,128)(2,1)}, bf16[1,32,16,512]{3,2,1,0:T(8,128)(2,1)}, bf16[1,32,16,512]{3,2,1,0:T(8,128)(2,1)}...) fusion(bf16[1,512,16,512]{3,2,1,0:T(8,128)(2,1)} %param.10, ...), kind=kLoop, calls=%fused_computation.295 | loop fusion | bytes 14680120 | tf_op jit(solution)/shard_map/dynamic_slice | solution.py:171
  253.8 11.7 %cholesky.74 = f32[128,128]{1,0:T(8,128)S(1)} custom-call(f32[128,128]{1,0:T(8,128)S(1)} %fusion.178), custom_call_target="Cholesky" | custom-call | tf_op jit(solution)/shard_map/jit(cholesky)/cholesky | solution.py:42
  269.0 9.0 %collective-permute-done.25 = f32[9,128,128]{1,2,0:T(8,128)S(1)} collective-permute-done((f32[9,128,128]{1,2,0:T(8,128)S(1)}, f32[9,128,128]{1,2,0:T(8,128)S(1)}, u32[]{:S(2)}, u32[]{:S(2)}) %collective-permute-start.25) | collective-permute-done | bytes 589856 | tf_op jit(solution)/shard_map/ppermute | solution.py:67
  279.5 10.1 %custom-call.8 = f32[2,1,64,64]{2,3,1,0:T(8,128)S(1)} custom-call(f32[2,1,64,64]{3,2,1,0:T(8,128)S(1)} %fusion.160), custom_call_target="InvertDiagBlocksLowerTriangular" | custom-call | tf_op jit(solution)/shard_map/triangular_solve/custom-call.0 | solution.py:26
  294.6 21.1 %collective-permute-done.27 = f32[9,128,128]{1,2,0:T(8,128)S(1)} collective-permute-done((f32[9,128,128]{1,2,0:T(8,128)S(1)}, f32[9,128,128]{1,2,0:T(8,128)S(1)}, u32[]{:S(2)}, u32[]{:S(2)}) %collective-permute-start.27) | collective-permute-done | bytes 589856 | tf_op jit(solution)/shard_map/ppermute | solution.py:67
  322.5 11.7 %cholesky.85 = f32[128,128]{1,0:T(8,128)S(1)} custom-call(f32[128,128]{1,0:T(8,128)S(1)} %fusion.175), custom_call_target="Cholesky" | custom-call | tf_op jit(solution)/shard_map/jit(cholesky)/cholesky | solution.py:42
  335.6 10.3 %custom-call.9 = f32[2,1,64,64]{2,3,1,0:T(8,128)S(1)} custom-call(f32[2,1,64,64]{3,2,1,0:T(8,128)S(1)} %fusion.161), custom_call_target="InvertDiagBlocksLowerTriangular" | custom-call | tf_op jit(solution)/shard_map/triangular_solve/custom-call.0 | solution.py:26
  349.9 11.7 %cholesky.96 = f32[128,128]{1,0:T(8,128)S(1)} custom-call(f32[128,128]{1,0:T(8,128)S(1)} %fusion.172), custom_call_target="Cholesky" | custom-call | tf_op jit(solution)/shard_map/jit(cholesky)/cholesky | solution.py:42
  363.1 9.8 %custom-call.10 = f32[2,1,64,64]{2,3,1,0:T(8,128)S(1)} custom-call(f32[2,1,64,64]{3,2,1,0:T(8,128)S(1)} %fusion.162), custom_call_target="InvertDiagBlocksLowerTriangular" | custom-call | tf_op jit(solution)/shard_map/triangular_solve/custom-call.0 | solution.py:26
  374.2 11.7 %cholesky.107 = f32[128,128]{1,0:T(8,128)S(1)} custom-call(f32[128,128]{1,0:T(8,128)S(1)} %fusion.169), custom_call_target="Cholesky" | custom-call | tf_op jit(solution)/shard_map/jit(cholesky)/cholesky | solution.py:42
  387.4 10.0 %custom-call.11 = f32[2,1,64,64]{2,3,1,0:T(8,128)S(1)} custom-call(f32[2,1,64,64]{3,2,1,0:T(8,128)S(1)} %fusion.163), custom_call_target="InvertDiagBlocksLowerTriangular" | custom-call | tf_op jit(solution)/shard_map/triangular_solve/custom-call.0 | solution.py:26
  415.0 8.8 %collective-permute-done.29 = bf16[32,16,512]{2,0,1:T(8,128)(2,1)S(1)} collective-permute-done((bf16[32,16,512]{2,0,1:T(8,128)(2,1)S(1)}, bf16[32,16,512]{2,0,1:T(8,128)(2,1)S(1)}, u32[]{:S(2)}, u32[]{:S(2)}) %collective-permute-start.29) | collective-permute-done | bytes 524320 | tf_op jit(solution)/shard_map/ppermute | solution.py:181
  427.1 8.8 %collective-permute-done.31 = bf16[32,16,512]{2,0,1:T(8,128)(2,1)S(1)} collective-permute-done((bf16[32,16,512]{2,0,1:T(8,128)(2,1)S(1)}, bf16[32,16,512]{2,0,1:T(8,128)(2,1)S(1)}, u32[]{:S(2)}, u32[]{:S(2)}) %collective-permute-start.31) | collective-permute-done | bytes 524320 | tf_op jit(solution)/shard_map/ppermute | solution.py:181
  439.4 7.7 %collective-permute-done.33 = bf16[32,16,512]{2,0,1:T(8,128)(2,1)S(1)} collective-permute-done((bf16[32,16,512]{2,0,1:T(8,128)(2,1)S(1)}, bf16[32,16,512]{2,0,1:T(8,128)(2,1)S(1)}, u32[]{:S(2)}, u32[]{:S(2)}) %collective-permute-start.33) | collective-permute-done | bytes 524320 | tf_op jit(solution)/shard_map/ppermute | solution.py:181
  451.9 9.0 %collective-permute-done.35 = bf16[32,16,512]{2,0,1:T(8,128)(2,1)S(1)} collective-permute-done((bf16[32,16,512]{2,0,1:T(8,128)(2,1)S(1)}, bf16[32,16,512]{2,0,1:T(8,128)(2,1)S(1)}, u32[]{:S(2)}, u32[]{:S(2)}) %collective-permute-start.35) | collective-permute-done | bytes 524320 | tf_op jit(solution)/shard_map/ppermute | solution.py:181
  464.1 8.8 %collective-permute-done.37 = bf16[32,16,512]{2,0,1:T(8,128)(2,1)S(1)} collective-permute-done((bf16[32,16,512]{2,0,1:T(8,128)(2,1)S(1)}, bf16[32,16,512]{2,0,1:T(8,128)(2,1)S(1)}, u32[]{:S(2)}, u32[]{:S(2)}) %collective-permute-start.37) | collective-permute-done | bytes 524320 | tf_op jit(solution)/shard_map/ppermute | solution.py:181
  476.2 8.8 %collective-permute-done.39 = bf16[32,16,512]{2,0,1:T(8,128)(2,1)S(1)} collective-permute-done((bf16[32,16,512]{2,0,1:T(8,128)(2,1)S(1)}, bf16[32,16,512]{2,0,1:T(8,128)(2,1)S(1)}, u32[]{:S(2)}, u32[]{:S(2)}) %collective-permute-start.39) | collective-permute-done | bytes 524320 | tf_op jit(solution)/shard_map/ppermute | solution.py:181
  488.3 6.3 %collective-permute-done.41 = bf16[32,16,512]{2,0,1:T(8,128)(2,1)S(1)} collective-permute-done((bf16[32,16,512]{2,0,1:T(8,128)(2,1)S(1)}, bf16[32,16,512]{2,0,1:T(8,128)(2,1)S(1)}, u32[]{:S(2)}, u32[]{:S(2)}) %collective-permute-start.41) | collective-permute-done | bytes 524320 | tf_op jit(solution)/shard_map/ppermute | solution.py:181
  502.6 22.7 %collective-permute-done.43 = f32[1,512,512]{2,1,0:T(8,128)} collective-permute-done((f32[1,512,512]{2,1,0:T(8,128)}, f32[1,512,512]{2,1,0:T(8,128)}, u32[]{:S(2)}, u32[]{:S(2)}) %collective-permute-start.43) | collective-permute-done | bytes 1048608 | tf_op jit(solution)/shard_map/ppermute | solution.py:67
  (276 shorter events, 179.1 us)
Async XLA Ops:
  17.1 15.8 %collective-permute-start.1 = (f32[1,256,512]{2,1,0:T(8,128)S(1)}, f32[1,256,512]{2,1,0:T(8,128)S(1)}, u32[]{:S(2)}, u32[]{:S(2)}) collective-permute-start(f32[1,256,512]{2,1,0:T(8,128)S(1)} %add.474), channel_id=1, source_target_pairs={{0,2},{1,3},{2,0},{3,1},{4,6},{5,7},{6,4},{7,5},{8,10},{9,11},{10,... | collective-permute-start | bytes 1572872 | tf_op jit(solution)/shard_map/ppermute | solution.py:67
  20.3 23.3 %collective-permute-start.3 = (f32[1,256,512]{2,1,0:T(8,128)S(1)}, f32[1,256,512]{2,1,0:T(8,128)S(1)}, u32[]{:S(2)}, u32[]{:S(2)}) collective-permute-start(f32[1,256,512]{2,1,0:T(8,128)S(1)} %add.476), channel_id=1, source_target_pairs={{0,2},{1,3},{2,0},{3,1},{4,6},{5,7},{6,4},{7,5},{8,10},{9,11},{10,... | collective-permute-start | bytes 1572872 | tf_op jit(solution)/shard_map/ppermute | solution.py:67
  45.1 24.8 %collective-permute-start.4 = (f32[32,16,512]{2,1,0:T(8,128)S(1)}, f32[32,16,512]{2,1,0:T(8,128)S(1)}, u32[]{:S(2)}, u32[]{:S(2)}) collective-permute-start(f32[32,16,512]{2,1,0:T(8,128)S(1)} %fusion.82), channel_id=1, source_target_pairs={{0,4},{4,12},{12,20},{20,28},{28,24},{24,16},{16,8},{8,0},{1,5},{5... | collective-permute-start | bytes 3145736 | tf_op jit(solution)/shard_map/ppermute | solution.py:147
  50.2 24.3 %collective-permute-start.11 = (f32[32,16,512]{2,1,0:T(8,128)}, f32[32,16,512]{2,1,0:T(8,128)}, u32[]{:S(2)}, u32[]{:S(2)}) collective-permute-start(f32[32,16,512]{2,1,0:T(8,128)} %fusion.67), channel_id=1, source_target_pairs={{0,8},{4,0},{12,4},{20,12},{28,20},{24,28},{16,24},{8,16},{1,9},{5... | collective-permute-start | bytes 3145736 | tf_op jit(solution)/shard_map/ppermute | solution.py:148
  71.4 23.8 %collective-permute-start.5 = (f32[32,16,512]{2,1,0:T(8,128)S(1)}, f32[32,16,512]{2,1,0:T(8,128)S(1)}, u32[]{:S(2)}, u32[]{:S(2)}) collective-permute-start(f32[32,16,512]{2,1,0:T(8,128)S(1)} %convolution_add_fusion.1), channel_id=1, source_target_pairs={{0,4},{4,12},{12,20},{20,28},{28,24},{24,16},{16,8},{8,0},{1,5},{5... | collective-permute-start | bytes 3145736 | tf_op jit(solution)/shard_map/ppermute | solution.py:147
  77.2 23.4 %collective-permute-start.12 = (f32[32,16,512]{2,1,0:T(8,128)}, f32[32,16,512]{2,1,0:T(8,128)}, u32[]{:S(2)}, u32[]{:S(2)}) collective-permute-start(f32[32,16,512]{2,1,0:T(8,128)} %convolution_add_fusion), channel_id=1, source_target_pairs={{0,8},{4,0},{12,4},{20,12},{28,20},{24,28},{16,24},{8,16},{1,9},{5... | collective-permute-start | bytes 3145736 | tf_op jit(solution)/shard_map/ppermute | solution.py:148
  95.5 23.1 %collective-permute-start.6 = (f32[32,16,512]{2,1,0:T(8,128)S(1)}, f32[32,16,512]{2,1,0:T(8,128)}, u32[]{:S(2)}, u32[]{:S(2)}) collective-permute-start(f32[32,16,512]{2,1,0:T(8,128)S(1)} %add.481), channel_id=1, source_target_pairs={{0,4},{4,12},{12,20},{20,28},{28,24},{24,16},{16,8},{8,0},{1,5},{5... | collective-permute-start | bytes 3145736 | tf_op jit(solution)/shard_map/ppermute | solution.py:147
  102.0 22.3 %collective-permute-start.13 = (f32[32,16,512]{2,1,0:T(8,128)S(1)}, f32[32,16,512]{2,1,0:T(8,128)}, u32[]{:S(2)}, u32[]{:S(2)}) collective-permute-start(f32[32,16,512]{2,1,0:T(8,128)S(1)} %add.505), channel_id=1, source_target_pairs={{0,8},{4,0},{12,4},{20,12},{28,20},{24,28},{16,24},{8,16},{1,9},{5... | collective-permute-start | bytes 3145736 | tf_op jit(solution)/shard_map/ppermute | solution.py:148
  120.0 22.2 %collective-permute-start.7 = (f32[32,16,512]{2,1,0:T(8,128)S(1)}, f32[32,16,512]{2,1,0:T(8,128)}, u32[]{:S(2)}, u32[]{:S(2)}) collective-permute-start(f32[32,16,512]{2,1,0:T(8,128)S(1)} %add.483), channel_id=1, source_target_pairs={{0,4},{4,12},{12,20},{20,28},{28,24},{24,16},{16,8},{8,0},{1,5},{5... | collective-permute-start | bytes 3145736 | tf_op jit(solution)/shard_map/ppermute | solution.py:147
  125.8 21.9 %collective-permute-start.14 = (f32[32,16,512]{2,1,0:T(8,128)S(1)}, f32[32,16,512]{2,1,0:T(8,128)}, u32[]{:S(2)}, u32[]{:S(2)}) collective-permute-start(f32[32,16,512]{2,1,0:T(8,128)S(1)} %add.510), channel_id=1, source_target_pairs={{0,8},{4,0},{12,4},{20,12},{28,20},{24,28},{16,24},{8,16},{1,9},{5... | collective-permute-start | bytes 3145736 | tf_op jit(solution)/shard_map/ppermute | solution.py:148
  143.6 21.9 %collective-permute-start.8 = (f32[32,16,512]{2,1,0:T(8,128)S(1)}, f32[32,16,512]{2,1,0:T(8,128)}, u32[]{:S(2)}, u32[]{:S(2)}) collective-permute-start(f32[32,16,512]{2,1,0:T(8,128)S(1)} %add.485), channel_id=1, source_target_pairs={{0,4},{4,12},{12,20},{20,28},{28,24},{24,16},{16,8},{8,0},{1,5},{5... | collective-permute-start | bytes 3145736 | tf_op jit(solution)/shard_map/ppermute | solution.py:147
  149.1 20.8 %collective-permute-start.15 = (f32[32,16,512]{2,1,0:T(8,128)S(1)}, f32[32,16,512]{2,1,0:T(8,128)}, u32[]{:S(2)}, u32[]{:S(2)}) collective-permute-start(f32[32,16,512]{2,1,0:T(8,128)S(1)} %add.515), channel_id=1, source_target_pairs={{0,8},{4,0},{12,4},{20,12},{28,20},{24,28},{16,24},{8,16},{1,9},{5... | collective-permute-start | bytes 3145736 | tf_op jit(solution)/shard_map/ppermute | solution.py:148
  167.0 21.9 %collective-permute-start.9 = (f32[32,16,512]{2,1,0:T(8,128)S(1)}, f32[32,16,512]{2,1,0:T(8,128)}, u32[]{:S(2)}, u32[]{:S(2)}) collective-permute-start(f32[32,16,512]{2,1,0:T(8,128)S(1)} %add.487), channel_id=1, source_target_pairs={{0,4},{4,12},{12,20},{20,28},{28,24},{24,16},{16,8},{8,0},{1,5},{5... | collective-permute-start | bytes 3145736 | tf_op jit(solution)/shard_map/ppermute | solution.py:147
  172.3 20.7 %collective-permute-start.16 = (f32[32,16,512]{2,1,0:T(8,128)}, f32[32,16,512]{2,1,0:T(8,128)}, u32[]{:S(2)}, u32[]{:S(2)}) collective-permute-start(f32[32,16,512]{2,1,0:T(8,128)} %add.520), channel_id=1, source_target_pairs={{0,8},{4,0},{12,4},{20,12},{28,20},{24,28},{16,24},{8,16},{1,9},{5... | collective-permute-start | bytes 3145736 | tf_op jit(solution)/shard_map/ppermute | solution.py:148
  190.3 19.4 %collective-permute-start.10 = (f32[32,16,512]{2,1,0:T(8,128)S(1)}, f32[32,16,512]{2,1,0:T(8,128)S(1)}, u32[]{:S(2)}, u32[]{:S(2)}) collective-permute-start(f32[32,16,512]{2,1,0:T(8,128)S(1)} %add.489), channel_id=1, source_target_pairs={{0,4},{4,12},{12,20},{20,28},{28,24},{24,16},{16,8},{8,0},{1,5},{5... | collective-permute-start | bytes 3145736 | tf_op jit(solution)/shard_map/ppermute | solution.py:147
  195.4 19.2 %collective-permute-start.17 = (f32[32,16,512]{2,1,0:T(8,128)}, f32[32,16,512]{2,1,0:T(8,128)}, u32[]{:S(2)}, u32[]{:S(2)}) collective-permute-start(f32[32,16,512]{2,1,0:T(8,128)} %add.525), channel_id=1, source_target_pairs={{0,8},{4,0},{12,4},{20,12},{28,20},{24,28},{16,24},{8,16},{1,9},{5... | collective-permute-start | bytes 3145736 | tf_op jit(solution)/shard_map/ppermute | solution.py:148
  219.9 20.7 %collective-permute-start.23 = (f32[9,128,128]{1,2,0:T(8,128)S(1)}, f32[9,128,128]{1,2,0:T(8,128)S(1)}, u32[]{:S(2)}, u32[]{:S(2)}) collective-permute-start(f32[9,128,128]{1,2,0:T(8,128)S(1)} %fusion.151), channel_id=1, source_target_pairs={{0,1},{1,0},{2,3},{3,2},{4,5},{5,4},{6,7},{7,6},{8,9},{9,8},{10,11... | collective-permute-start | bytes 1769480 | tf_op jit(solution)/shard_map/ppermute | solution.py:67
  240.7 24.8 %collective-permute-start.24 = (f32[9,128,128]{1,2,0:T(8,128)S(1)}, f32[9,128,128]{1,2,0:T(8,128)}, u32[]{:S(2)}, u32[]{:S(2)}) collective-permute-start(f32[9,128,128]{1,2,0:T(8,128)S(1)} %add.536), channel_id=1, source_target_pairs={{0,2},{1,3},{2,0},{3,1},{4,6},{5,7},{6,4},{7,5},{8,10},{9,11},{10,... | collective-permute-start | bytes 1769480 | tf_op jit(solution)/shard_map/ppermute | solution.py:67
  278.0 12.1 %collective-permute-start.26 = (f32[9,128,128]{1,2,0:T(8,128)S(1)}, f32[9,128,128]{1,2,0:T(8,128)}, u32[]{:S(2)}, u32[]{:S(2)}) collective-permute-start(f32[9,128,128]{1,2,0:T(8,128)S(1)} %add.538), channel_id=1, source_target_pairs={{0,8},{4,12},{8,0},{12,4},{16,24},{20,28},{24,16},{28,20},{1,9},{5... | collective-permute-start | bytes 1769480 | tf_op jit(solution)/shard_map/ppermute | solution.py:67
  291.2 24.5 %collective-permute-start.27 = (f32[9,128,128]{1,2,0:T(8,128)S(1)}, f32[9,128,128]{1,2,0:T(8,128)S(1)}, u32[]{:S(2)}, u32[]{:S(2)}) collective-permute-start(f32[9,128,128]{1,2,0:T(8,128)S(1)} %add.539), channel_id=1, source_target_pairs={{0,16},{4,20},{8,24},{12,28},{16,0},{20,4},{24,8},{28,12},{1,17},{... | collective-permute-start | bytes 1769480 | tf_op jit(solution)/shard_map/ppermute | solution.py:67
  410.7 13.1 %collective-permute-start.29 = (bf16[32,16,512]{2,0,1:T(8,128)(2,1)S(1)}, bf16[32,16,512]{2,0,1:T(8,128)(2,1)S(1)}, u32[]{:S(2)}, u32[]{:S(2)}) collective-permute-start(bf16[32,16,512]{2,0,1:T(8,128)(2,1)S(1)} %copy.81), channel_id=1, source_target_pairs={{0,8},{4,0},{12,4},{20,12},{28,20},{24,28},{16,24},{8,16},{1,9},{5... | collective-permute-start | bytes 1572872 | tf_op jit(solution)/shard_map/ppermute | solution.py:181
  411.1 13.6 %collective-permute-start.28 = (bf16[32,16,512]{2,0,1:T(8,128)(2,1)S(1)}, bf16[32,16,512]{2,0,1:T(8,128)(2,1)S(1)}, u32[]{:S(2)}, u32[]{:S(2)}) collective-permute-start(bf16[32,16,512]{2,0,1:T(8,128)(2,1)S(1)} %copy.79), channel_id=1, source_target_pairs={{0,4},{4,12},{12,20},{20,28},{28,24},{24,16},{16,8},{8,0},{1,5},{5... | collective-permute-start | bytes 1572872 | tf_op jit(solution)/shard_map/ppermute | solution.py:180
  423.8 12.1 %collective-permute-start.31 = (bf16[32,16,512]{2,0,1:T(8,128)(2,1)S(1)}, bf16[32,16,512]{2,0,1:T(8,128)(2,1)S(1)}, u32[]{:S(2)}, u32[]{:S(2)}) collective-permute-start(bf16[32,16,512]{2,0,1:T(8,128)(2,1)S(1)} %collective-permute-done.29), channel_id=1, source_target_pairs={{0,8},{4,0},{12,4},{20,12},{28,20},{24,28},{16,24},{8,16},{1,9},{5... | collective-permute-start | bytes 1572872 | tf_op jit(solution)/shard_map/ppermute | solution.py:181
  424.7 12.9 %collective-permute-start.30 = (bf16[32,16,512]{2,0,1:T(8,128)(2,1)S(1)}, bf16[32,16,512]{2,0,1:T(8,128)(2,1)S(1)}, u32[]{:S(2)}, u32[]{:S(2)}) collective-permute-start(bf16[32,16,512]{2,0,1:T(8,128)(2,1)S(1)} %collective-permute-done.28), channel_id=1, source_target_pairs={{0,4},{4,12},{12,20},{20,28},{28,24},{24,16},{16,8},{8,0},{1,5},{5... | collective-permute-start | bytes 1572872 | tf_op jit(solution)/shard_map/ppermute | solution.py:180
  437.6 12.6 %collective-permute-start.32 = (bf16[32,16,512]{2,0,1:T(8,128)(2,1)S(1)}, bf16[32,16,512]{2,0,1:T(8,128)(2,1)S(1)}, u32[]{:S(2)}, u32[]{:S(2)}) collective-permute-start(bf16[32,16,512]{2,0,1:T(8,128)(2,1)S(1)} %collective-permute-done.30), channel_id=1, source_target_pairs={{0,4},{4,12},{12,20},{20,28},{28,24},{24,16},{16,8},{8,0},{1,5},{5... | collective-permute-start | bytes 1572872 | tf_op jit(solution)/shard_map/ppermute | solution.py:180
  447.2 13.6 %collective-permute-start.35 = (bf16[32,16,512]{2,0,1:T(8,128)(2,1)S(1)}, bf16[32,16,512]{2,0,1:T(8,128)(2,1)S(1)}, u32[]{:S(2)}, u32[]{:S(2)}) collective-permute-start(bf16[32,16,512]{2,0,1:T(8,128)(2,1)S(1)} %collective-permute-done.33), channel_id=1, source_target_pairs={{0,8},{4,0},{12,4},{20,12},{28,20},{24,28},{16,24},{8,16},{1,9},{5... | collective-permute-start | bytes 1572872 | tf_op jit(solution)/shard_map/ppermute | solution.py:181
  450.1 11.4 %collective-permute-start.34 = (bf16[32,16,512]{2,0,1:T(8,128)(2,1)S(1)}, bf16[32,16,512]{2,0,1:T(8,128)(2,1)S(1)}, u32[]{:S(2)}, u32[]{:S(2)}) collective-permute-start(bf16[32,16,512]{2,0,1:T(8,128)(2,1)S(1)} %collective-permute-done.32), channel_id=1, source_target_pairs={{0,4},{4,12},{12,20},{20,28},{28,24},{24,16},{16,8},{8,0},{1,5},{5... | collective-permute-start | bytes 1572872 | tf_op jit(solution)/shard_map/ppermute | solution.py:180
  460.8 12.1 %collective-permute-start.37 = (bf16[32,16,512]{2,0,1:T(8,128)(2,1)S(1)}, bf16[32,16,512]{2,0,1:T(8,128)(2,1)S(1)}, u32[]{:S(2)}, u32[]{:S(2)}) collective-permute-start(bf16[32,16,512]{2,0,1:T(8,128)(2,1)S(1)} %collective-permute-done.35), channel_id=1, source_target_pairs={{0,8},{4,0},{12,4},{20,12},{28,20},{24,28},{16,24},{8,16},{1,9},{5... | collective-permute-start | bytes 1572872 | tf_op jit(solution)/shard_map/ppermute | solution.py:181
  461.6 11.9 %collective-permute-start.36 = (bf16[32,16,512]{2,0,1:T(8,128)(2,1)S(1)}, bf16[32,16,512]{2,0,1:T(8,128)(2,1)S(1)}, u32[]{:S(2)}, u32[]{:S(2)}) collective-permute-start(bf16[32,16,512]{2,0,1:T(8,128)(2,1)S(1)} %collective-permute-done.34), channel_id=1, source_target_pairs={{0,4},{4,12},{12,20},{20,28},{28,24},{24,16},{16,8},{8,0},{1,5},{5... | collective-permute-start | bytes 1572872 | tf_op jit(solution)/shard_map/ppermute | solution.py:180
  472.9 12.1 %collective-permute-start.39 = (bf16[32,16,512]{2,0,1:T(8,128)(2,1)S(1)}, bf16[32,16,512]{2,0,1:T(8,128)(2,1)S(1)}, u32[]{:S(2)}, u32[]{:S(2)}) collective-permute-start(bf16[32,16,512]{2,0,1:T(8,128)(2,1)S(1)} %collective-permute-done.37), channel_id=1, source_target_pairs={{0,8},{4,0},{12,4},{20,12},{28,20},{24,28},{16,24},{8,16},{1,9},{5... | collective-permute-start | bytes 1572872 | tf_op jit(solution)/shard_map/ppermute | solution.py:181
  473.5 12.1 %collective-permute-start.38 = (bf16[32,16,512]{2,0,1:T(8,128)(2,1)S(1)}, bf16[32,16,512]{2,0,1:T(8,128)(2,1)S(1)}, u32[]{:S(2)}, u32[]{:S(2)}) collective-permute-start(bf16[32,16,512]{2,0,1:T(8,128)(2,1)S(1)} %collective-permute-done.36), channel_id=1, source_target_pairs={{0,4},{4,12},{12,20},{20,28},{28,24},{24,16},{16,8},{8,0},{1,5},{5... | collective-permute-start | bytes 1572872 | tf_op jit(solution)/shard_map/ppermute | solution.py:180
  499.8 25.5 %collective-permute-start.43 = (f32[1,512,512]{2,1,0:T(8,128)}, f32[1,512,512]{2,1,0:T(8,128)}, u32[]{:S(2)}, u32[]{:S(2)}) collective-permute-start(f32[1,512,512]{2,1,0:T(8,128)} %add.596), channel_id=1, source_target_pairs={{0,2},{1,3},{2,0},{3,1},{4,6},{5,7},{6,4},{7,5},{8,10},{9,11},{10,... | collective-permute-start | bytes 3145736 | tf_op jit(solution)/shard_map/ppermute | solution.py:67
  (40 other events, 305.3 us)

commit v14 on v12

--- a/solution.py
+++ b/solution.py
@@ -29,34 +29,28 @@
     return jnp.concatenate([top, jnp.concatenate([corner, inv[1]], axis=1)], axis=0)
 
 
-def orthonormal(sketched, gram):
-    n = gram.shape[0]
-    b = min(BLOCK, n)
-    nb = n // b
-    eye = jnp.eye(b, dtype=jnp.float32)
+def orthonormal(sketched, blocks_of, nb, b):
+    lower = {}
     inverses = []
-    panels = []
-    trailing = gram
-    for k in range(nb):
-        diag = trailing[:b, :b]
-        lkk = jnp.linalg.cholesky(diag)
-        ikk = tri_inverse(lkk)
-        inverses.append(ikk)
-        if k < nb - 1:
-            panel = mm(trailing[b:, :b], ikk.T)
-            panels.append(panel)
-            trailing = trailing[b:, b:] - mm(panel, panel.T)
-    blocks = []
+    for j in range(nb):
+        for i in range(j, nb):
+            acc = blocks_of[(i, j)]
+            if j:
+                lhs = jnp.concatenate([lower[(i, k)] for k in range(j)], axis=1)
+                rhs = jnp.concatenate([lower[(j, k)] for k in range(j)], axis=1)
+                acc = acc - mm(lhs, rhs.T)
+            if i == j:
+                inverses.append(tri_inverse(jnp.linalg.cholesky(acc)))
+            else:
+                lower[(i, j)] = mm(acc, inverses[j].T)
+    done = []
     for k in range(nb):
         rhs = sketched[:, k * b:(k + 1) * b]
-        if k > 0:
-            done = jnp.concatenate(blocks, axis=1)
-            lrow = jnp.concatenate(
-                [panels[j][(k - j - 1) * b:(k - j) * b] for j in range(k)], axis=1
-            )
-            rhs = rhs - mm(done, lrow.T)
-        blocks.append(mm(rhs, inverses[k].T))
-    return jnp.concatenate(blocks, axis=1)
+        if k:
+            lrow = jnp.concatenate([lower[(k, j)] for j in range(k)], axis=1)
+            rhs = rhs - mm(jnp.concatenate(done, axis=1), lrow.T)
+        done.append(mm(rhs, inverses[k].T))
+    return jnp.concatenate(done, axis=1)
 
 
 def butterfly_sum(x, n, axis="sum"):
@@ -73,17 +67,17 @@
     n = gram_part.shape[0]
     b = min(BLOCK, n)
     nb = n // b
-    lower = [(i, j) for i in range(nb) for j in range(i + 1)]
-    packed = jnp.stack([gram_part[i * b:(i + 1) * b, j * b:(j + 1) * b] for i, j in lower])
-    packed = butterfly_sum(butterfly_sum(packed, n_mode, "mode"), n_sum)
-    where = {cell: k for k, cell in enumerate(lower)}
-    rows = []
-    for i in range(nb):
-        row = []
-        for j in range(nb):
-            row.append(packed[where[(i, j)]] if j <= i else packed[where[(j, i)]].T)
-        rows.append(jnp.concatenate(row, axis=1))
-    return jnp.concatenate(rows, axis=0)
+    cells = [(i, j) for i in range(nb) for j in range(i + 1)]
+    groups = [cells[:1], cells[1:3], cells[3:]]
+    blocks_of = {}
+    for group in groups:
+        if not group:
+            continue
+        packed = jnp.stack([gram_part[i * b:(i + 1) * b, j * b:(j + 1) * b] for i, j in group])
+        packed = butterfly_sum(butterfly_sum(packed, n_mode, "mode"), n_sum)
+        for k, cell in enumerate(group):
+            blocks_of[cell] = packed[k]
+    return blocks_of, nb, b
 
 
 def ring_order(mesh):
@@ -203,8 +197,8 @@
     share = ring_reduce_scatter(local_rows, rows_in, ring)
     flat_share = share.reshape(-1, target)
     gram_part = jnp.dot(flat_share.T, flat_share, precision=HI)
-    gram = symmetric_psum(gram_part, len(ring), n_mode)
-    basis = orthonormal(flat_share, gram)
+    blocks_of, nb, b = symmetric_psum(gram_part, len(ring), n_mode)
+    basis = orthonormal(flat_share, blocks_of, nb, b)
     block = basis.reshape(share.shape)
     rounded = block.astype(jnp.bfloat16)
     partial_carry = ring_gather_carries(rounded, left_cores, ring)

time: 544 us -> 547 us (level)
  waiting for transfers between devices: 266 us -> 239 us
  other arithmetic: 115 us -> 129 us
  starting transfers between devices: 43.1 us -> 53.3 us
    ppermute x11 -> x21, waiting for transfers between devices: 99.4 us -> 83.9 us  [butterfly_sum(): x = x + lax.ppermute(x, axis, [(i, i ^ d) for i in range(n)])]
    ppermute x11 -> x21, starting transfers between devices: 14.4 us -> 23.6 us  [butterfly_sum(): x = x + lax.ppermute(x, axis, [(i, i ^ d) for i in range(n)])]
    ppermute x7, waiting for transfers between devices: 84 us -> 75.3 us  [ring_reduce_scatter(): acc_f = lax.ppermute(acc_f, 'sum', fwd) + piece(fwd_blocks[t, me], 0, half)]
    dot_general x21 -> x27, matrix products: 13.5 us -> 17.1 us  [mm(): return jnp.dot(a, b, precision=HI, preferred_element_type=jnp.float32)]
    another operation x12 -> x14, other arithmetic: 49.6 us -> 51.3 us  [the longest x12 51.2 us: orthonormal(): inverses.append(tri_inverse(jnp.linalg.cholesky(acc)))]
  transfers between devices with their start and end apart: 39 -> 49, of which waited for: 31 -> 37; matrix products, arithmetic and copies ran while one was open for 12% -> 22% of each run, Pallas kernels for 0% -> 0%
where the time goes in v14:
time: 547 us; the launch traced here: 536 us
  waiting for transfers between devices  239 us (44%)
  other arithmetic  129 us (24%)
  matrix products  72.1 us (13%)
  starting transfers between devices  53.3 us (10%)
  between operations  22.1 us (4%)
  local copies, waits for them, and re-layouts  21.1 us (4%)
    ppermute x21, waiting for transfers between devices, butterfly_sum(): x = x + lax.ppermute(x, axis, [(i, i ^ d) for i in range(n)])  83.9 us
    ppermute x7, waiting for transfers between devices, ring_reduce_scatter(): acc_f = lax.ppermute(acc_f, 'sum', fwd) + piece(fwd_blocks[t, me], 0, half)  75.3 us
    ppermute x7, waiting for transfers between devices, ring_gather_carries(): hold_b = lax.ppermute(hold_b, 'sum', bwd)  59.5 us
    another operation x12, other arithmetic, orthonormal(): inverses.append(tri_inverse(jnp.linalg.cholesky(acc)))  51.2 us
    another operation x9, other arithmetic, tri_inverse(): inv = lax.linalg.triangular_solve(diag, eye, left_side=True, lower=True)  44.4 us
    dot_general x16, matrix products, local_rows(): lax.dot_general(part, mapped, (((0, 3), (0, 1)), ((), ())), preferred_ele...  26 us
    ppermute x21, starting transfers between devices, butterfly_sum(): x = x + lax.ppermute(x, axis, [(i, i ^ d) for i in range(n)])  23.6 us
    ppermute x7, waiting for transfers between devices, ring_reduce_scatter(): lax.ppermute(acc_b, 'sum', bwd)  17.3 us
  transfers between devices with their start and end apart: 49, of which 37 were waited for; matrix products, arithmetic and copies ran while one was open for 22% of the time, Pallas kernels for 0%

profile of v14, /device:TPU:0, one launch (start us, length us, event | category | flops | bytes accessed | tf_op | source)
XLA Modules:
  0.0 536.2 jit_solution(6391741876623173858)
XLA Ops:
  0.6 4.1 fusion.214
  6.5 5.0 fusion.24
  12.0 5.0 fusion.25
  23.0 9.9 %collective-permute-done.1 = f32[1,256,512]{2,1,0:T(8,128)S(1)} collective-permute-done((f32[1,256,512]{2,1,0:T(8,128)S(1)}, f32[1,256,512]{2,1,0:T(8,128)S(1)}, u32[]{:S(2)}, u32[]{:S(2)}) %collective-permute-start.1) | collective-permute-done | bytes 524320 | tf_op jit(solution)/shard_map/ppermute | solution.py:61
  33.0 10.5 %collective-permute-done.3 = f32[1,256,512]{2,1,0:T(8,128)S(1)} collective-permute-done((f32[1,256,512]{2,1,0:T(8,128)S(1)}, f32[1,256,512]{2,1,0:T(8,128)S(1)}, u32[]{:S(2)}, u32[]{:S(2)}) %collective-permute-start.3) | collective-permute-done | bytes 524320 | tf_op jit(solution)/shard_map/ppermute | solution.py:61
  51.9 18.2 %collective-permute-done.4 = f32[32,16,512]{2,1,0:T(8,128)S(1)} collective-permute-done((f32[32,16,512]{2,1,0:T(8,128)S(1)}, f32[32,16,512]{2,1,0:T(8,128)S(1)}, u32[]{:S(2)}, u32[]{:S(2)}) %collective-permute-start.4) | collective-permute-done | bytes 1048608 | tf_op jit(solution)/shard_map/ppermute | solution.py:136
  82.2 13.1 %collective-permute-done.5 = f32[32,16,512]{2,1,0:T(8,128)S(1)} collective-permute-done((f32[32,16,512]{2,1,0:T(8,128)S(1)}, f32[32,16,512]{2,1,0:T(8,128)S(1)}, u32[]{:S(2)}, u32[]{:S(2)}) %collective-permute-start.5) | collective-permute-done | bytes 1048608 | tf_op jit(solution)/shard_map/ppermute | solution.py:136
  107.4 11.3 %collective-permute-done.6 = f32[32,16,512]{2,1,0:T(8,128)} collective-permute-done((f32[32,16,512]{2,1,0:T(8,128)S(1)}, f32[32,16,512]{2,1,0:T(8,128)}, u32[]{:S(2)}, u32[]{:S(2)}) %collective-permute-start.6) | collective-permute-done | bytes 1048608 | tf_op jit(solution)/shard_map/ppermute | solution.py:136
  131.5 10.9 %collective-permute-done.7 = f32[32,16,512]{2,1,0:T(8,128)} collective-permute-done((f32[32,16,512]{2,1,0:T(8,128)S(1)}, f32[32,16,512]{2,1,0:T(8,128)}, u32[]{:S(2)}, u32[]{:S(2)}) %collective-permute-start.7) | collective-permute-done | bytes 1048608 | tf_op jit(solution)/shard_map/ppermute | solution.py:136
  154.8 10.9 %collective-permute-done.8 = f32[32,16,512]{2,1,0:T(8,128)} collective-permute-done((f32[32,16,512]{2,1,0:T(8,128)S(1)}, f32[32,16,512]{2,1,0:T(8,128)}, u32[]{:S(2)}, u32[]{:S(2)}) %collective-permute-start.8) | collective-permute-done | bytes 1048608 | tf_op jit(solution)/shard_map/ppermute | solution.py:136
  178.0 11.0 %collective-permute-done.9 = f32[32,16,512]{2,1,0:T(8,128)} collective-permute-done((f32[32,16,512]{2,1,0:T(8,128)S(1)}, f32[32,16,512]{2,1,0:T(8,128)}, u32[]{:S(2)}, u32[]{:S(2)}) %collective-permute-start.9) | collective-permute-done | bytes 1048608 | tf_op jit(solution)/shard_map/ppermute | solution.py:136
  209.1 6.2 %constant_dynamic-slice_fusion.1 = (bf16[1,32,16,512]{3,2,1,0:T(8,128)(2,1)}, bf16[1,32,16,512]{3,2,1,0:T(8,128)(2,1)}, bf16[1,32,16,512]{3,2,1,0:T(8,128)(2,1)}...) fusion(bf16[1,512,16,512]{3,2,1,0:T(8,128)(2,1)} %param.10, ...), kind=kLoop, calls=%fused_computation.275 | loop fusion | bytes 14680120 | tf_op jit(solution)/shard_map/dynamic_slice | solution.py:160
  244.2 11.7 %cholesky.74 = f32[128,128]{1,0:T(8,128)S(1)} custom-call(f32[128,128]{1,0:T(8,128)S(1)} %fusion.153), custom_call_target="Cholesky" | custom-call | tf_op jit(solution)/shard_map/jit(cholesky)/cholesky | solution.py:43
  257.3 10.0 %custom-call.8 = f32[2,1,64,64]{2,3,1,0:T(8,128)S(1)} custom-call(f32[2,1,64,64]{3,2,1,0:T(8,128)S(1)} %fusion.146), custom_call_target="InvertDiagBlocksLowerTriangular" | custom-call | tf_op jit(solution)/shard_map/triangular_solve/custom-call.0 | solution.py:26
  268.2 5.3 collective-permute-done.26
  281.2 11.7 %cholesky.85 = f32[128,128]{1,0:T(8,128)S(1)} custom-call(f32[128,128]{1,0:T(8,128)S(1)} %fusion.162), custom_call_target="Cholesky" | custom-call | tf_op jit(solution)/shard_map/jit(cholesky)/cholesky | solution.py:43
  296.2 10.0 %custom-call.9 = f32[2,1,64,64]{2,3,1,0:T(8,128)S(1)} custom-call(f32[2,1,64,64]{3,2,1,0:T(8,128)S(1)} %fusion.147), custom_call_target="InvertDiagBlocksLowerTriangular" | custom-call | tf_op jit(solution)/shard_map/triangular_solve/custom-call.0 | solution.py:26
  310.2 9.2 %collective-permute-done.31 = f32[7,128,128]{1,2,0:T(8,128)S(1)} collective-permute-done((f32[7,128,128]{1,2,0:T(8,128)S(1)}, f32[7,128,128]{1,2,0:T(8,128)S(1)}, u32[]{:S(2)}, u32[]{:S(2)}) %collective-permute-start.31) | collective-permute-done | bytes 458784 | tf_op jit(solution)/shard_map/ppermute | solution.py:61
  319.5 4.3 collective-permute-start.32
  324.6 10.5 %collective-permute-done.32 = f32[7,128,128]{1,2,0:T(8,128)S(1)} collective-permute-done((f32[7,128,128]{1,2,0:T(8,128)S(1)}, f32[7,128,128]{1,2,0:T(8,128)S(1)}, u32[]{:S(2)}, u32[]{:S(2)}) %collective-permute-start.32) | collective-permute-done | bytes 458784 | tf_op jit(solution)/shard_map/ppermute | solution.py:61
  338.9 12.5 %cholesky.96 = f32[128,128]{1,0:T(8,128)S(1)} custom-call(f32[128,128]{1,0:T(8,128)} %fusion.159), custom_call_target="Cholesky" | custom-call | tf_op jit(solution)/shard_map/jit(cholesky)/cholesky | solution.py:43
  354.9 11.4 %custom-call.10 = f32[2,1,64,64]{2,3,1,0:T(8,128)} custom-call(f32[2,1,64,64]{3,2,1,0:T(8,128)} %fusion.148), custom_call_target="InvertDiagBlocksLowerTriangular" | custom-call | tf_op jit(solution)/shard_map/triangular_solve/custom-call.0 | solution.py:26
  374.8 12.5 %cholesky.107 = f32[128,128]{1,0:T(8,128)S(1)} custom-call(f32[128,128]{1,0:T(8,128)} %fusion.156), custom_call_target="Cholesky" | custom-call | tf_op jit(solution)/shard_map/jit(cholesky)/cholesky | solution.py:43
  390.8 11.6 %custom-call.11 = f32[2,1,64,64]{2,3,1,0:T(8,128)} custom-call(f32[2,1,64,64]{3,2,1,0:T(8,128)} %fusion.149), custom_call_target="InvertDiagBlocksLowerTriangular" | custom-call | tf_op jit(solution)/shard_map/triangular_solve/custom-call.0 | solution.py:26
  420.0 7.8 %collective-permute-done.34 = bf16[32,16,512]{2,0,1:T(8,128)(2,1)S(1)} collective-permute-done((bf16[32,16,512]{2,0,1:T(8,128)(2,1)S(1)}, bf16[32,16,512]{2,0,1:T(8,128)(2,1)S(1)}, u32[]{:S(2)}, u32[]{:S(2)}) %collective-permute-start.34) | collective-permute-done | bytes 524320 | tf_op jit(solution)/shard_map/ppermute | solution.py:170
  431.3 9.6 %collective-permute-done.36 = bf16[32,16,512]{2,0,1:T(8,128)(2,1)S(1)} collective-permute-done((bf16[32,16,512]{2,0,1:T(8,128)(2,1)S(1)}, bf16[32,16,512]{2,0,1:T(8,128)(2,1)S(1)}, u32[]{:S(2)}, u32[]{:S(2)}) %collective-permute-start.36) | collective-permute-done | bytes 524320 | tf_op jit(solution)/shard_map/ppermute | solution.py:170
  446.6 10.3 %collective-permute-done.38 = bf16[32,16,512]{2,0,1:T(8,128)(2,1)S(1)} collective-permute-done((bf16[32,16,512]{2,0,1:T(8,128)(2,1)S(1)}, bf16[32,16,512]{2,0,1:T(8,128)(2,1)S(1)}, u32[]{:S(2)}, u32[]{:S(2)}) %collective-permute-start.38) | collective-permute-done | bytes 524320 | tf_op jit(solution)/shard_map/ppermute | solution.py:170
  460.5 10.4 %collective-permute-done.40 = bf16[32,16,512]{2,0,1:T(8,128)(2,1)S(1)} collective-permute-done((bf16[32,16,512]{2,0,1:T(8,128)(2,1)S(1)}, bf16[32,16,512]{2,0,1:T(8,128)(2,1)S(1)}, u32[]{:S(2)}, u32[]{:S(2)}) %collective-permute-start.40) | collective-permute-done | bytes 524320 | tf_op jit(solution)/shard_map/ppermute | solution.py:170
  474.3 9.6 %collective-permute-done.42 = bf16[32,16,512]{2,0,1:T(8,128)(2,1)S(1)} collective-permute-done((bf16[32,16,512]{2,0,1:T(8,128)(2,1)S(1)}, bf16[32,16,512]{2,0,1:T(8,128)(2,1)S(1)}, u32[]{:S(2)}, u32[]{:S(2)}) %collective-permute-start.42) | collective-permute-done | bytes 524320 | tf_op jit(solution)/shard_map/ppermute | solution.py:170
  487.3 5.9 %collective-permute-done.44 = bf16[32,16,512]{2,0,1:T(8,128)(2,1)S(1)} collective-permute-done((bf16[32,16,512]{2,0,1:T(8,128)(2,1)S(1)}, bf16[32,16,512]{2,0,1:T(8,128)(2,1)S(1)}, u32[]{:S(2)}, u32[]{:S(2)}) %collective-permute-start.44) | collective-permute-done | bytes 524320 | tf_op jit(solution)/shard_map/ppermute | solution.py:170
  496.4 5.9 %collective-permute-done.46 = bf16[32,16,512]{2,0,1:T(8,128)(2,1)S(1)} collective-permute-done((bf16[32,16,512]{2,0,1:T(8,128)(2,1)S(1)}, bf16[32,16,512]{2,0,1:T(8,128)(2,1)S(1)}, u32[]{:S(2)}, u32[]{:S(2)}) %collective-permute-start.46) | collective-permute-done | bytes 524320 | tf_op jit(solution)/shard_map/ppermute | solution.py:170
  511.6 21.7 %collective-permute-done.48 = f32[1,512,512]{2,1,0:T(8,128)} collective-permute-done((f32[1,512,512]{2,1,0:T(8,128)}, f32[1,512,512]{2,1,0:T(8,128)}, u32[]{:S(2)}, u32[]{:S(2)}) %collective-permute-start.48) | collective-permute-done | bytes 1048608 | tf_op jit(solution)/shard_map/ppermute | solution.py:61
  (294 shorter events, 196.0 us)
Async XLA Ops:
  17.1 15.8 %collective-permute-start.1 = (f32[1,256,512]{2,1,0:T(8,128)S(1)}, f32[1,256,512]{2,1,0:T(8,128)S(1)}, u32[]{:S(2)}, u32[]{:S(2)}) collective-permute-start(f32[1,256,512]{2,1,0:T(8,128)S(1)} %add.489), channel_id=1, source_target_pairs={{0,2},{1,3},{2,0},{3,1},{4,6},{5,7},{6,4},{7,5},{8,10},{9,11},{10,... | collective-permute-start | bytes 1572872 | tf_op jit(solution)/shard_map/ppermute | solution.py:61
  20.3 23.3 %collective-permute-start.3 = (f32[1,256,512]{2,1,0:T(8,128)S(1)}, f32[1,256,512]{2,1,0:T(8,128)S(1)}, u32[]{:S(2)}, u32[]{:S(2)}) collective-permute-start(f32[1,256,512]{2,1,0:T(8,128)S(1)} %add.491), channel_id=1, source_target_pairs={{0,2},{1,3},{2,0},{3,1},{4,6},{5,7},{6,4},{7,5},{8,10},{9,11},{10,... | collective-permute-start | bytes 1572872 | tf_op jit(solution)/shard_map/ppermute | solution.py:61
  45.1 24.9 %collective-permute-start.4 = (f32[32,16,512]{2,1,0:T(8,128)S(1)}, f32[32,16,512]{2,1,0:T(8,128)S(1)}, u32[]{:S(2)}, u32[]{:S(2)}) collective-permute-start(f32[32,16,512]{2,1,0:T(8,128)S(1)} %fusion.81), channel_id=1, source_target_pairs={{0,4},{4,12},{12,20},{20,28},{28,24},{24,16},{16,8},{8,0},{1,5},{5... | collective-permute-start | bytes 3145736 | tf_op jit(solution)/shard_map/ppermute | solution.py:136
  50.3 24.3 %collective-permute-start.11 = (f32[32,16,512]{2,1,0:T(8,128)}, f32[32,16,512]{2,1,0:T(8,128)}, u32[]{:S(2)}, u32[]{:S(2)}) collective-permute-start(f32[32,16,512]{2,1,0:T(8,128)} %fusion.66), channel_id=1, source_target_pairs={{0,8},{4,0},{12,4},{20,12},{28,20},{24,28},{16,24},{8,16},{1,9},{5... | collective-permute-start | bytes 3145736 | tf_op jit(solution)/shard_map/ppermute | solution.py:137
  71.5 23.8 %collective-permute-start.5 = (f32[32,16,512]{2,1,0:T(8,128)S(1)}, f32[32,16,512]{2,1,0:T(8,128)S(1)}, u32[]{:S(2)}, u32[]{:S(2)}) collective-permute-start(f32[32,16,512]{2,1,0:T(8,128)S(1)} %convolution_add_fusion.1), channel_id=1, source_target_pairs={{0,4},{4,12},{12,20},{20,28},{28,24},{24,16},{16,8},{8,0},{1,5},{5... | collective-permute-start | bytes 3145736 | tf_op jit(solution)/shard_map/ppermute | solution.py:136
  77.4 23.4 %collective-permute-start.12 = (f32[32,16,512]{2,1,0:T(8,128)}, f32[32,16,512]{2,1,0:T(8,128)}, u32[]{:S(2)}, u32[]{:S(2)}) collective-permute-start(f32[32,16,512]{2,1,0:T(8,128)} %convolution_add_fusion), channel_id=1, source_target_pairs={{0,8},{4,0},{12,4},{20,12},{28,20},{24,28},{16,24},{8,16},{1,9},{5... | collective-permute-start | bytes 3145736 | tf_op jit(solution)/shard_map/ppermute | solution.py:137
  95.6 23.1 %collective-permute-start.6 = (f32[32,16,512]{2,1,0:T(8,128)S(1)}, f32[32,16,512]{2,1,0:T(8,128)}, u32[]{:S(2)}, u32[]{:S(2)}) collective-permute-start(f32[32,16,512]{2,1,0:T(8,128)S(1)} %add.496), channel_id=1, source_target_pairs={{0,4},{4,12},{12,20},{20,28},{28,24},{24,16},{16,8},{8,0},{1,5},{5... | collective-permute-start | bytes 3145736 | tf_op jit(solution)/shard_map/ppermute | solution.py:136
  102.2 22.3 %collective-permute-start.13 = (f32[32,16,512]{2,1,0:T(8,128)S(1)}, f32[32,16,512]{2,1,0:T(8,128)}, u32[]{:S(2)}, u32[]{:S(2)}) collective-permute-start(f32[32,16,512]{2,1,0:T(8,128)S(1)} %add.520), channel_id=1, source_target_pairs={{0,8},{4,0},{12,4},{20,12},{28,20},{24,28},{16,24},{8,16},{1,9},{5... | collective-permute-start | bytes 3145736 | tf_op jit(solution)/shard_map/ppermute | solution.py:137
  120.1 22.2 %collective-permute-start.7 = (f32[32,16,512]{2,1,0:T(8,128)S(1)}, f32[32,16,512]{2,1,0:T(8,128)}, u32[]{:S(2)}, u32[]{:S(2)}) collective-permute-start(f32[32,16,512]{2,1,0:T(8,128)S(1)} %add.498), channel_id=1, source_target_pairs={{0,4},{4,12},{12,20},{20,28},{28,24},{24,16},{16,8},{8,0},{1,5},{5... | collective-permute-start | bytes 3145736 | tf_op jit(solution)/shard_map/ppermute | solution.py:136
  125.9 21.9 %collective-permute-start.14 = (f32[32,16,512]{2,1,0:T(8,128)S(1)}, f32[32,16,512]{2,1,0:T(8,128)}, u32[]{:S(2)}, u32[]{:S(2)}) collective-permute-start(f32[32,16,512]{2,1,0:T(8,128)S(1)} %add.525), channel_id=1, source_target_pairs={{0,8},{4,0},{12,4},{20,12},{28,20},{24,28},{16,24},{8,16},{1,9},{5... | collective-permute-start | bytes 3145736 | tf_op jit(solution)/shard_map/ppermute | solution.py:137
  143.8 21.9 %collective-permute-start.8 = (f32[32,16,512]{2,1,0:T(8,128)S(1)}, f32[32,16,512]{2,1,0:T(8,128)}, u32[]{:S(2)}, u32[]{:S(2)}) collective-permute-start(f32[32,16,512]{2,1,0:T(8,128)S(1)} %add.500), channel_id=1, source_target_pairs={{0,4},{4,12},{12,20},{20,28},{28,24},{24,16},{16,8},{8,0},{1,5},{5... | collective-permute-start | bytes 3145736 | tf_op jit(solution)/shard_map/ppermute | solution.py:136
  149.2 20.8 %collective-permute-start.15 = (f32[32,16,512]{2,1,0:T(8,128)S(1)}, f32[32,16,512]{2,1,0:T(8,128)}, u32[]{:S(2)}, u32[]{:S(2)}) collective-permute-start(f32[32,16,512]{2,1,0:T(8,128)S(1)} %add.530), channel_id=1, source_target_pairs={{0,8},{4,0},{12,4},{20,12},{28,20},{24,28},{16,24},{8,16},{1,9},{5... | collective-permute-start | bytes 3145736 | tf_op jit(solution)/shard_map/ppermute | solution.py:137
  167.1 21.9 %collective-permute-start.9 = (f32[32,16,512]{2,1,0:T(8,128)S(1)}, f32[32,16,512]{2,1,0:T(8,128)}, u32[]{:S(2)}, u32[]{:S(2)}) collective-permute-start(f32[32,16,512]{2,1,0:T(8,128)S(1)} %add.502), channel_id=1, source_target_pairs={{0,4},{4,12},{12,20},{20,28},{28,24},{24,16},{16,8},{8,0},{1,5},{5... | collective-permute-start | bytes 3145736 | tf_op jit(solution)/shard_map/ppermute | solution.py:136
  172.4 20.4 %collective-permute-start.16 = (f32[32,16,512]{2,1,0:T(8,128)}, f32[32,16,512]{2,1,0:T(8,128)}, u32[]{:S(2)}, u32[]{:S(2)}) collective-permute-start(f32[32,16,512]{2,1,0:T(8,128)} %add.535), channel_id=1, source_target_pairs={{0,8},{4,0},{12,4},{20,12},{28,20},{24,28},{16,24},{8,16},{1,9},{5... | collective-permute-start | bytes 3145736 | tf_op jit(solution)/shard_map/ppermute | solution.py:137
  190.4 27.9 %collective-permute-start.10 = (f32[32,16,512]{2,1,0:T(8,128)S(1)}, f32[32,16,512]{2,1,0:T(8,128)S(1)}, u32[]{:S(2)}, u32[]{:S(2)}) collective-permute-start(f32[32,16,512]{2,1,0:T(8,128)S(1)} %add.504), channel_id=1, source_target_pairs={{0,4},{4,12},{12,20},{20,28},{28,24},{24,16},{16,8},{8,0},{1,5},{5... | collective-permute-start | bytes 3145736 | tf_op jit(solution)/shard_map/ppermute | solution.py:136
  195.2 23.3 %collective-permute-start.17 = (f32[32,16,512]{2,1,0:T(8,128)}, f32[32,16,512]{2,1,0:T(8,128)}, u32[]{:S(2)}, u32[]{:S(2)}) collective-permute-start(f32[32,16,512]{2,1,0:T(8,128)} %add.540), channel_id=1, source_target_pairs={{0,8},{4,0},{12,4},{20,12},{28,20},{24,28},{16,24},{8,16},{1,9},{5... | collective-permute-start | bytes 3145736 | tf_op jit(solution)/shard_map/ppermute | solution.py:137
  234.7 40.9 %collective-permute-start.28 = (f32[7,128,128]{1,2,0:T(8,128)S(1)}, f32[7,128,128]{1,2,0:T(8,128)}, u32[]{:S(2)}, u32[]{:S(2)}) collective-permute-start(f32[7,128,128]{1,2,0:T(8,128)S(1)} %get-tuple-element.24), channel_id=1, source_target_pairs={{0,1},{1,0},{2,3},{3,2},{4,5},{5,4},{6,7},{7,6},{8,9},{9,8},{10,11... | collective-permute-start | bytes 1376264 | tf_op jit(solution)/shard_map/ppermute | solution.py:61
  240.0 27.8 %collective-permute-start.25 = (f32[2,128,128]{1,2,0:T(8,128)S(1)}, f32[2,128,128]{1,2,0:T(8,128)S(1)}, u32[]{:S(2)}, u32[]{:S(2)}) collective-permute-start(f32[2,128,128]{1,2,0:T(8,128)S(1)} %fusion.249), channel_id=1, source_target_pairs={{0,4},{4,0},{8,12},{12,8},{16,20},{20,16},{24,28},{28,24},{1,5},{5... | collective-permute-start | bytes 393224 | tf_op jit(solution)/shard_map/ppermute | solution.py:61
  276.8 17.6 %collective-permute-start.29 = (f32[7,128,128]{1,2,0:T(8,128)S(1)}, f32[7,128,128]{1,2,0:T(8,128)}, u32[]{:S(2)}, u32[]{:S(2)}) collective-permute-start(f32[7,128,128]{1,2,0:T(8,128)S(1)} %add.556), channel_id=1, source_target_pairs={{0,2},{1,3},{2,0},{3,1},{4,6},{5,7},{6,4},{7,5},{8,10},{9,11},{10,... | collective-permute-start | bytes 1376264 | tf_op jit(solution)/shard_map/ppermute | solution.py:61
  308.0 11.5 %collective-permute-start.31 = (f32[7,128,128]{1,2,0:T(8,128)S(1)}, f32[7,128,128]{1,2,0:T(8,128)S(1)}, u32[]{:S(2)}, u32[]{:S(2)}) collective-permute-start(f32[7,128,128]{1,2,0:T(8,128)S(1)} %add.558), channel_id=1, source_target_pairs={{0,8},{4,12},{8,0},{12,4},{16,24},{20,28},{24,16},{28,20},{1,9},{5... | collective-permute-start | bytes 1376264 | tf_op jit(solution)/shard_map/ppermute | solution.py:61
  319.5 15.6 %collective-permute-start.32 = (f32[7,128,128]{1,2,0:T(8,128)S(1)}, f32[7,128,128]{1,2,0:T(8,128)S(1)}, u32[]{:S(2)}, u32[]{:S(2)}) collective-permute-start(f32[7,128,128]{1,2,0:T(8,128)S(1)} %add.559), channel_id=1, source_target_pairs={{0,16},{4,20},{8,24},{12,28},{16,0},{20,4},{24,8},{28,12},{1,17},{... | collective-permute-start | bytes 1376264 | tf_op jit(solution)/shard_map/ppermute | solution.py:61
  415.7 12.1 %collective-permute-start.34 = (bf16[32,16,512]{2,0,1:T(8,128)(2,1)S(1)}, bf16[32,16,512]{2,0,1:T(8,128)(2,1)S(1)}, u32[]{:S(2)}, u32[]{:S(2)}) collective-permute-start(bf16[32,16,512]{2,0,1:T(8,128)(2,1)S(1)} %copy.89), channel_id=1, source_target_pairs={{0,8},{4,0},{12,4},{20,12},{28,20},{24,28},{16,24},{8,16},{1,9},{5... | collective-permute-start | bytes 1572872 | tf_op jit(solution)/shard_map/ppermute | solution.py:170
  417.0 12.0 %collective-permute-start.33 = (bf16[32,16,512]{2,0,1:T(8,128)(2,1)S(1)}, bf16[32,16,512]{2,0,1:T(8,128)(2,1)S(1)}, u32[]{:S(2)}, u32[]{:S(2)}) collective-permute-start(bf16[32,16,512]{2,0,1:T(8,128)(2,1)S(1)} %copy.87), channel_id=1, source_target_pairs={{0,4},{4,12},{12,20},{20,28},{28,24},{24,16},{16,8},{8,0},{1,5},{5... | collective-permute-start | bytes 1572872 | tf_op jit(solution)/shard_map/ppermute | solution.py:169
  427.8 13.0 %collective-permute-start.36 = (bf16[32,16,512]{2,0,1:T(8,128)(2,1)S(1)}, bf16[32,16,512]{2,0,1:T(8,128)(2,1)S(1)}, u32[]{:S(2)}, u32[]{:S(2)}) collective-permute-start(bf16[32,16,512]{2,0,1:T(8,128)(2,1)S(1)} %collective-permute-done.34), channel_id=1, source_target_pairs={{0,8},{4,0},{12,4},{20,12},{28,20},{24,28},{16,24},{8,16},{1,9},{5... | collective-permute-start | bytes 1572872 | tf_op jit(solution)/shard_map/ppermute | solution.py:170
  429.0 16.9 %collective-permute-start.35 = (bf16[32,16,512]{2,0,1:T(8,128)(2,1)S(1)}, bf16[32,16,512]{2,0,1:T(8,128)(2,1)S(1)}, u32[]{:S(2)}, u32[]{:S(2)}) collective-permute-start(bf16[32,16,512]{2,0,1:T(8,128)(2,1)S(1)} %collective-permute-done.33), channel_id=1, source_target_pairs={{0,4},{4,12},{12,20},{20,28},{28,24},{24,16},{16,8},{8,0},{1,5},{5... | collective-permute-start | bytes 1572872 | tf_op jit(solution)/shard_map/ppermute | solution.py:169
  440.9 16.0 %collective-permute-start.38 = (bf16[32,16,512]{2,0,1:T(8,128)(2,1)S(1)}, bf16[32,16,512]{2,0,1:T(8,128)(2,1)S(1)}, u32[]{:S(2)}, u32[]{:S(2)}) collective-permute-start(bf16[32,16,512]{2,0,1:T(8,128)(2,1)S(1)} %collective-permute-done.36), channel_id=1, source_target_pairs={{0,8},{4,0},{12,4},{20,12},{28,20},{24,28},{16,24},{8,16},{1,9},{5... | collective-permute-start | bytes 1572872 | tf_op jit(solution)/shard_map/ppermute | solution.py:170
  446.0 13.6 %collective-permute-start.37 = (bf16[32,16,512]{2,0,1:T(8,128)(2,1)S(1)}, bf16[32,16,512]{2,0,1:T(8,128)(2,1)S(1)}, u32[]{:S(2)}, u32[]{:S(2)}) collective-permute-start(bf16[32,16,512]{2,0,1:T(8,128)(2,1)S(1)} %collective-permute-done.35), channel_id=1, source_target_pairs={{0,4},{4,12},{12,20},{20,28},{28,24},{24,16},{16,8},{8,0},{1,5},{5... | collective-permute-start | bytes 1572872 | tf_op jit(solution)/shard_map/ppermute | solution.py:169
  456.9 13.9 %collective-permute-start.40 = (bf16[32,16,512]{2,0,1:T(8,128)(2,1)S(1)}, bf16[32,16,512]{2,0,1:T(8,128)(2,1)S(1)}, u32[]{:S(2)}, u32[]{:S(2)}) collective-permute-start(bf16[32,16,512]{2,0,1:T(8,128)(2,1)S(1)} %collective-permute-done.38), channel_id=1, source_target_pairs={{0,8},{4,0},{12,4},{20,12},{28,20},{24,28},{16,24},{8,16},{1,9},{5... | collective-permute-start | bytes 1572872 | tf_op jit(solution)/shard_map/ppermute | solution.py:170
  459.6 12.7 %collective-permute-start.39 = (bf16[32,16,512]{2,0,1:T(8,128)(2,1)S(1)}, bf16[32,16,512]{2,0,1:T(8,128)(2,1)S(1)}, u32[]{:S(2)}, u32[]{:S(2)}) collective-permute-start(bf16[32,16,512]{2,0,1:T(8,128)(2,1)S(1)} %collective-permute-done.37), channel_id=1, source_target_pairs={{0,4},{4,12},{12,20},{20,28},{28,24},{24,16},{16,8},{8,0},{1,5},{5... | collective-permute-start | bytes 1572872 | tf_op jit(solution)/shard_map/ppermute | solution.py:169
  470.9 13.1 %collective-permute-start.42 = (bf16[32,16,512]{2,0,1:T(8,128)(2,1)S(1)}, bf16[32,16,512]{2,0,1:T(8,128)(2,1)S(1)}, u32[]{:S(2)}, u32[]{:S(2)}) collective-permute-start(bf16[32,16,512]{2,0,1:T(8,128)(2,1)S(1)} %collective-permute-done.40), channel_id=1, source_target_pairs={{0,8},{4,0},{12,4},{20,12},{28,20},{24,28},{16,24},{8,16},{1,9},{5... | collective-permute-start | bytes 1572872 | tf_op jit(solution)/shard_map/ppermute | solution.py:170
  472.3 12.6 %collective-permute-start.41 = (bf16[32,16,512]{2,0,1:T(8,128)(2,1)S(1)}, bf16[32,16,512]{2,0,1:T(8,128)(2,1)S(1)}, u32[]{:S(2)}, u32[]{:S(2)}) collective-permute-start(bf16[32,16,512]{2,0,1:T(8,128)(2,1)S(1)} %collective-permute-done.39), channel_id=1, source_target_pairs={{0,4},{4,12},{12,20},{20,28},{28,24},{24,16},{16,8},{8,0},{1,5},{5... | collective-permute-start | bytes 1572872 | tf_op jit(solution)/shard_map/ppermute | solution.py:169
  507.8 25.5 %collective-permute-start.48 = (f32[1,512,512]{2,1,0:T(8,128)}, f32[1,512,512]{2,1,0:T(8,128)}, u32[]{:S(2)}, u32[]{:S(2)}) collective-permute-start(f32[1,512,512]{2,1,0:T(8,128)} %add.616), channel_id=1, source_target_pairs={{0,2},{1,3},{2,0},{3,1},{4,6},{5,7},{6,4},{7,5},{8,10},{9,11},{10,... | collective-permute-start | bytes 3145736 | tf_op jit(solution)/shard_map/ppermute | solution.py:61
  (50 other events, 471.9 us)
